TPU v7x, 32 devices: a whole 2x2x4 slice. The times are simulated.
32 devices in a mesh: node: 8 (over z, y), head: 4 (over x, core).
Axes of the slice: x: 2, y: 2, z: 4, core: 2. Of those that a mesh axis runs over, the one named last changes fastest.
Arguments:
- node_states: bfloat16 [3072, 1024], P('node'), may hold values from -12 to 12
- w_qkv: bfloat16 [1024, 3, 1024], P(None, None, 'head'), may hold values from -1 to 1
- w_out: bfloat16 [1024, 1024], P('head'), may hold values from -4 to 4
- ln_gain: float32 [1024], P('head'), may hold values from 0.5 to 1.5
- ln_bias: float32 [1024], P('head'), may hold values from -4 to 4
- local_mask: int32 [24, 7], P('node'), may hold values 0 or 1
- matchings: int32 [4, 24], P(None, 'node'), may hold values from 0 to 23, as said below
Outputs:
- layer_out: bfloat16 [3072, 1024], P('node', 'head')
Inputs may be any that keep to these rules, and one draw needn't show every extreme that they name: Each row of matchings is a perfect matching of the 24 blocks: matchings[m, matchings[m, b]] = b and matchings[m, b] differs from b. The blocks fall into groups of 3 consecutive blocks, and the number of groups is a power of two; for each m there is one number s_m, 1 <= s_m < 8, such that every block of group g is matched with a block of group g XOR s_m.
All inputs are finite; a program needn't handle non-finite values. No bound on the sum of `local_mask` on one device may be relied on, other than what follows from the above.
Results may differ from a plain program's by a relative error of at most 0.0077.
Values may be sent and summed in bfloat16 or wider, within the bound.
No kernel may reach another device: no remote copies, remote signals or barrier semaphores. Data moves between devices by JAX's collectives and lax.ppermute only.
A program may use at most 64 MiB of HBM per device.

v0:
```python
import math

import jax
import jax.numpy as jnp
from jax import lax
from jax.experimental import pallas as pl
from jax.experimental.pallas import tpu as pltpu
from jax.sharding import PartitionSpec as P

HEAD_DIM = 64
ROWS = 128
REACH = 3
GATHER_GROUPS = 16


NORM_EPS = 1e-05


def partner(array, axis, bit):
    return lax.ppermute(array, axis, [(i, i ^ 1 << bit) for i in range(lax.axis_size(axis))])


def with_halo(array, sides, width):
    for axis, dim in sides:
        devices, length = (lax.axis_size(axis), array.shape[dim])
        up = [(i, (i + 1) % devices) for i in range(devices - 1)]
        down = [(j, i) for i, j in up]
        last = lax.slice_in_dim(array, length - width, length, axis=dim)
        first = lax.slice_in_dim(array, 0, width, axis=dim)
        before = lax.ppermute(last, axis, up)
        after = lax.ppermute(first, axis, down)
        array = jnp.concatenate([before, array, after], axis=dim)
    return array


def shift_heads(array, step, devices):
    return lax.ppermute(array, "head", [(i, (i + step) % devices) for i in range(devices)])


def flip_heads(array, flip, devices):
    return lax.ppermute(array, "head", [(i, i ^ flip) for i in range(devices)])


def spread_slots(piece, heads_axis):
    slots = {0: piece}
    for bit in reversed(range(heads_axis.bit_length() - 1)):
        flip = 1 << bit
        held = sorted(slots)
        other = flip_heads(jnp.stack([slots[k] for k in held]), flip, heads_axis)
        for pos, k in enumerate(held):
            slots[k ^ flip] = other[pos]
    return slots


def keep_same(current):
    return current


def route_direct(payload, shift_val, digits):
    for bit_pos in range(digits):

        def moved(current, bit_pos=bit_pos):
            return partner(current, "node", bit_pos)

        taken = jnp.bitwise_and(jnp.right_shift(shift_val, bit_pos), 1) == 1
        payload = lax.cond(taken, moved, keep_same, payload)
    return payload


def select_partner(received, matchings, blocks_here, pair_feats):
    matches = matchings.shape[0]
    received = received.reshape(matches, blocks_here, ROWS, pair_feats)
    sources = matchings % blocks_here
    selector = (sources[:, :, None] == jnp.arange(blocks_here)[None, None, :]).astype(jnp.bfloat16)
    picked = jnp.einsum("mjs,msrf->mjrf", selector, received, preferred_element_type=jnp.float32)
    return picked.astype(jnp.bfloat16)


def routed_keys(keyvals, matchings, my_index, groups, blocks_here):
    matches = matchings.shape[0]
    digits = groups.bit_length() - 1
    up = [(i, i + 1) for i in range(groups - 1)]
    down = [(i + 1, i) for i in range(groups - 1)]
    before = lax.ppermute(keyvals, "node", up)
    after = lax.ppermute(keyvals, "node", down)
    targets = jnp.bitwise_xor(matchings[:, 0] // blocks_here, my_index)
    received = [route_direct(keyvals, targets[match_pos], digits) for match_pos in range(matches)]
    return jnp.stack([before, after] + received)


def switched_send(payload, shift_val, groups):
    def branch(shift):
        def moved(current):
            return lax.ppermute(current, "node", [(i, i ^ shift) for i in range(groups)])

        return moved

    branches = [branch(shift) for shift in range(1, groups)]
    return lax.switch(jnp.clip(shift_val - 1, 0, groups - 2), branches, payload)


def switched_keys(keyvals, matchings, my_index, groups, blocks_here, window):
    total_rows, pair_feats = keyvals.shape
    matches = matchings.shape[0]
    padded = with_halo(keyvals, (("node", 0),), REACH * ROWS)
    windows = jnp.stack(
        [padded[block_pos * ROWS : (block_pos + window) * ROWS] for block_pos in range(blocks_here)]
    )
    targets = jnp.bitwise_xor(matchings[:, 0] // blocks_here, my_index)
    picked = []
    for match_pos in range(matches):
        received = switched_send(keyvals, targets[match_pos], groups)
        received = received.reshape(blocks_here, ROWS, pair_feats)
        picked.append(jnp.take(received, matchings[match_pos] % blocks_here, axis=0, mode="clip"))
    partner_rows = jnp.stack(picked, axis=1).reshape(blocks_here, matches * ROWS, pair_feats)
    return jnp.concatenate([windows, partner_rows], axis=1)


def quarter_keys(node_states, w_qkv, matchings, my_index, groups, blocks_here):
    total_rows = node_states.shape[0]
    matches = matchings.shape[0]
    heads_axis = lax.axis_size("head")
    part_rows = total_rows // heads_axis
    me = lax.axis_index("head")
    mine = lax.dynamic_slice_in_dim(node_states, me * part_rows, part_rows, 0)
    up = [(i, i + 1) for i in range(groups - 1)]
    down = [(i + 1, i) for i in range(groups - 1)]
    before = lax.ppermute(mine, "node", up)
    after = lax.ppermute(mine, "node", down)
    targets = jnp.bitwise_xor(matchings[:, 0] // blocks_here, my_index)
    matched = [switched_send(mine, targets[match_pos], groups) for match_pos in range(matches)]
    spread = [spread_slots(piece, heads_axis) for piece in [before, after] + matched]
    slots = jnp.stack([jnp.stack([one[k] for one in spread]) for k in range(heads_axis)])
    slot_kv = jnp.einsum(
        "kprd,dtf->kprtf", slots, w_qkv[:, 1:], preferred_element_type=jnp.float32
    ).astype(jnp.bfloat16)
    order = jnp.bitwise_xor(jnp.arange(heads_axis, dtype=jnp.int32), me.astype(jnp.int32))
    ordered = jnp.take(slot_kv, order, axis=0, mode="clip")
    count = len(spread)
    ordered = jnp.transpose(ordered, (1, 0, 2, 3, 4))
    return ordered.reshape(count, total_rows, -1)


def gathered_keys(keyvals, chosen):
    total_rows, pair_feats = keyvals.shape
    blocks_here, key_blocks = chosen.shape
    everyone = lax.all_gather(keyvals, "node", axis=0, tiled=True)
    everyone = everyone.reshape(-1, ROWS, pair_feats)
    picked = jnp.take(everyone, chosen.reshape(-1), axis=0, mode="clip")
    return picked.reshape(blocks_here, key_blocks * ROWS, pair_feats)


def attention_kernel(live_ref, pick_ref, q_ref, own_ref, part_ref, out_ref, score_ref):
    blocks_here = q_ref.shape[0]
    heads_here = q_ref.shape[2] // HEAD_DIM
    head_feats = q_ref.shape[2]
    window = 2 * REACH + 1
    matches = part_ref.shape[0] - 2
    key_blocks = window + matches
    inv_root = 1.0 / math.sqrt(HEAD_DIM)
    for j in range(blocks_here):
        def key_block(t, cols, j=j):
            if t < window:
                pos = j + t - REACH
                if pos < 0:
                    return part_ref[0, pos + blocks_here, :, cols]
                if pos < blocks_here:
                    return own_ref[pos, :, cols]
                return part_ref[1, pos - blocks_here, :, cols]
            match_pos = t - window
            return part_ref[2 + match_pos, pick_ref[match_pos, j], :, cols]
        for h in range(heads_here):
            kcols = pl.ds(h * HEAD_DIM, HEAD_DIM)
            vcols = pl.ds(head_feats + h * HEAD_DIM, HEAD_DIM)
            query = q_ref[j, :, kcols]
            highest = jnp.full((ROWS, 1), -jnp.inf, jnp.float32)
            for t in range(key_blocks):
                scores = lax.dot_general(query, key_block(t, kcols), (((1,), (1,)), ((), ())),
                                         preferred_element_type=jnp.float32) * inv_root
                scores = jnp.where(live_ref[j, t] != 0, scores, -jnp.inf)
                score_ref[t] = scores
                highest = jnp.maximum(highest, jnp.max(scores, axis=1, keepdims=True))
            total = jnp.zeros((ROWS, 1), jnp.float32)
            for t in range(key_blocks):
                weights = jnp.exp(score_ref[t] - highest)
                score_ref[t] = weights
                total = total + jnp.sum(weights, axis=1, keepdims=True)
            context = jnp.zeros((ROWS, HEAD_DIM), jnp.float32)
            for t in range(key_blocks):
                probs = (score_ref[t] / total).astype(jnp.bfloat16)
                context = context + jnp.dot(probs, key_block(t, vcols), preferred_element_type=jnp.float32)
            out_ref[j, :, kcols] = context.astype(jnp.bfloat16)


def attention(live, pick, query, own, part):
    blocks_here, rows, head_feats = query.shape
    key_blocks = live.shape[1]
    vmem = pltpu.VMEM
    flops = 4 * blocks_here * rows * key_blocks * rows * head_feats
    moved = 2 * (query.size * 2 + own.size + part.size)
    return pl.pallas_call(
        attention_kernel,
        out_shape=jax.ShapeDtypeStruct(query.shape, jnp.bfloat16),
        in_specs=[pl.BlockSpec(memory_space=pltpu.SMEM), pl.BlockSpec(memory_space=pltpu.SMEM),
                  pl.BlockSpec(memory_space=vmem), pl.BlockSpec(memory_space=vmem), pl.BlockSpec(memory_space=vmem)],
        out_specs=pl.BlockSpec(memory_space=vmem),
        scratch_shapes=[pltpu.VMEM((key_blocks, ROWS, ROWS), jnp.float32)],
        cost_estimate=pl.CostEstimate(
            flops=flops, transcendentals=blocks_here * rows * key_blocks * rows * 4, bytes_accessed=moved
        ),
    )(live, pick, query, own, part)


def local(node_states, w_qkv, w_out, ln_gain, ln_bias, local_mask, matchings):
    total_rows, model_width = node_states.shape
    blocks_here = total_rows // ROWS
    head_feats = w_qkv.shape[2]
    heads_here = head_feats // HEAD_DIM
    window = 2 * REACH + 1
    matches = matchings.shape[0]
    inv_root = 1.0 / math.sqrt(HEAD_DIM)
    my_index = lax.axis_index("node")
    groups = lax.axis_size("node")
    all_blocks = groups * blocks_here
    heads_axis = lax.axis_size("head")
    head_index = lax.axis_index("head")
    out_cols = ln_gain.shape[0]
    w_parts = [lax.dynamic_slice_in_dim(w_out, head_index * out_cols, out_cols, 1)] + [
        flip_heads(
            lax.dynamic_slice_in_dim(w_out, (head_index ^ flip) * out_cols, out_cols, 1),
            flip,
            heads_axis,
        )
        for flip in range(1, heads_axis)
    ]
    projected = jnp.einsum(
        "nd,dtf->ntf", node_states, w_qkv, preferred_element_type=jnp.float32
    ).astype(jnp.bfloat16)
    queries = projected[:, 0]
    keyvals = projected[:, 1:].reshape(total_rows, 2 * head_feats)
    global_blocks = my_index * blocks_here + jnp.arange(blocks_here, dtype=jnp.int32)
    offsets = jnp.arange(window, dtype=jnp.int32) - REACH
    neighbour = global_blocks[:, None] + offsets[None, :]
    if groups <= GATHER_GROUPS:
        part = quarter_keys(node_states, w_qkv, matchings, my_index, groups, blocks_here)
    else:
        part = routed_keys(keyvals, matchings, my_index, groups, blocks_here)
    local_ok = (
        (neighbour >= 0) & (neighbour < all_blocks) & ((offsets[None, :] == 0) | (local_mask == 1))
    )
    block_ok = jnp.concatenate([local_ok, jnp.ones((blocks_here, matches), dtype=bool)], axis=1)
    context = attention(
        block_ok.astype(jnp.int32),
        (matchings % blocks_here).astype(jnp.int32),
        queries.reshape(blocks_here, ROWS, head_feats),
        keyvals.reshape(blocks_here, ROWS, 2 * head_feats),
        part.reshape(part.shape[0], blocks_here, ROWS, 2 * head_feats),
    ).reshape(total_rows, head_feats)
    context_slots = spread_slots(context, heads_axis)
    own_cols = lax.dynamic_slice_in_dim(node_states, head_index * out_cols, out_cols, 1)
    mixed_rows = own_cols.astype(jnp.float32) + jnp.einsum(
        "srf,sfo->ro",
        jnp.stack([context_slots[flip] for flip in range(heads_axis)]),
        jnp.stack(w_parts),
        preferred_element_type=jnp.float32,
    )
    part_mean = jnp.mean(mixed_rows, axis=1, keepdims=True)
    part_square = jnp.sum(jnp.square(mixed_rows - part_mean), axis=1, keepdims=True)
    stats = jnp.concatenate([part_mean, part_square], axis=1)
    all_stats = jnp.stack(
        [stats] + [flip_heads(stats, flip, heads_axis) for flip in range(1, heads_axis)]
    )
    centre = jnp.mean(all_stats[:, :, 0:1], axis=0)
    spread = (
        jnp.sum(all_stats[:, :, 1:2], axis=0)
        + out_cols * jnp.sum(jnp.square(all_stats[:, :, 0:1] - centre), axis=0)
    ) / (heads_axis * out_cols)
    normed = (mixed_rows - centre) * lax.rsqrt(spread + NORM_EPS)
    return (normed * ln_gain + ln_bias).astype(jnp.bfloat16)


def solution(mesh):
    placed = (
        P("node", None),
        P(None, None, "head"),
        P("head", None),
        P("head"),
        P("head"),
        P("node", None),
        P(None, "node"),
    )
    return jax.shard_map(
        local, mesh=mesh, in_specs=placed, out_specs=P("node", "head"), check_vma=False
    )
```

profile of v0, /device:TPU:9, one launch (start us, length us, event | category | flops | bytes accessed | tf_op | source)
XLA Modules:
  0.0 130.6 jit_solution(15354027074352452530)
XLA Ops:
  0.0 1.1 copy-done
  1.8 3.1 %collective-permute-start.28 = (bf16[96,1024]{1,0:T(8,128)(2,1)}, bf16[96,1024]{1,0:T(8,128)(2,1)S(1)}, u32[]{:S(2)}, u32[]{:S(2)}) collective-permute-start(bf16[96,1024]{1,0:T(8,128)(2,1)} %constant_dynamic-slice_fusion.4), channel_id=1, source_target_pairs={{0,4},{4,8},{8,12},{12,16},{16,20},{20,24},{24,28},{1,5},{5,9},{9,... | collective-permute-start | bytes 589832 | tf_op jit(solution)/shard_map/ppermute | solution.py:128
  5.0 3.0 %collective-permute-start.29 = (bf16[96,1024]{1,0:T(8,128)(2,1)}, bf16[96,1024]{1,0:T(8,128)(2,1)S(1)}, u32[]{:S(2)}, u32[]{:S(2)}) collective-permute-start(bf16[96,1024]{1,0:T(8,128)(2,1)} %constant_dynamic-slice_fusion.4), channel_id=1, source_target_pairs={{4,0},{8,4},{12,8},{16,12},{20,16},{24,20},{28,24},{5,1},{9,5},{13... | collective-permute-start | bytes 589832 | tf_op jit(solution)/shard_map/ppermute | solution.py:129
  8.0 0.8 divide_reduce_fusion
  8.8 0.8 fusion.29
  10.9 6.6 %conditional.4 = (bf16[1,96,1024]{2,1,0:T(8,128)(2,1)}) conditional(s32[]{:T(128)} %bitcast.32, bf16[96,1024]{1,0:T(8,128)(2,1)} %constant_dynamic-slice_fusion.4, bf16[96,1024]{1,0:T(8,128)(2,1)} %constant_dynamic-slice_fusion.4, bf16[96,1024]{1,0:T(8,128)(2,1)} %constant_dynamic-slice_fusion.4, ...), branch_computations={%region_0.1_spmd, %region_1.2_spmd, %region_2.3_spmd, %region_3.4_... | conditional | bytes 786480 | solution.py:99
  11.3 6.2 %collective-permute-done.2 = bf16[96,1024]{1,0:T(8,128)(2,1)} collective-permute-done((bf16[96,1024]{1,0:T(8,128)(2,1)}, bf16[96,1024]{1,0:T(8,128)(2,1)}, u32[]{:S(2)}, u32[]{:S(2)}) %collective-permute-start.2) | collective-permute-done | bytes 196640 | tf_op jit(solution)/shard_map/cond/branch_2_fun/ppermute | solution.py:94
  17.5 1.2 collective-permute-start.34
  19.3 5.1 %conditional.5 = (bf16[1,96,1024]{2,1,0:T(8,128)(2,1)}) conditional(s32[]{:T(128)} %bitcast.33, bf16[96,1024]{1,0:T(8,128)(2,1)} %constant_dynamic-slice_fusion.4, bf16[96,1024]{1,0:T(8,128)(2,1)} %constant_dynamic-slice_fusion.4, bf16[96,1024]{1,0:T(8,128)(2,1)} %constant_dynamic-slice_fusion.4, ...), branch_computations={%region_7.8_spmd, %region_8.9_spmd, %region_9.10_spmd, %region_10.... | conditional | bytes 786480 | solution.py:99
  19.4 5.0 %collective-permute-done.8 = bf16[96,1024]{1,0:T(8,128)(2,1)} collective-permute-done((bf16[96,1024]{1,0:T(8,128)(2,1)}, bf16[96,1024]{1,0:T(8,128)(2,1)}, u32[]{:S(2)}, u32[]{:S(2)}) %collective-permute-start.8) | collective-permute-done | bytes 196640 | tf_op jit(solution)/shard_map/cond/branch_1_fun/ppermute | solution.py:94
  25.3 8.5 %conditional.6 = (bf16[1,96,1024]{2,1,0:T(8,128)(2,1)}) conditional(s32[]{:T(128)} %bitcast.34, bf16[96,1024]{1,0:T(8,128)(2,1)} %constant_dynamic-slice_fusion.4, bf16[96,1024]{1,0:T(8,128)(2,1)} %constant_dynamic-slice_fusion.4, bf16[96,1024]{1,0:T(8,128)(2,1)} %constant_dynamic-slice_fusion.4, ...), branch_computations={%region_14.15_spmd, %region_15.16_spmd, %region_16.17_spmd, %regio... | conditional | bytes 786480 | solution.py:99
  25.3 2.9 %collective-permute-start.18 = (bf16[96,1024]{1,0:T(8,128)(2,1)}, bf16[96,1024]{1,0:T(8,128)(2,1)}, u32[]{:S(2)}, u32[]{:S(2)}) collective-permute-start(bf16[96,1024]{1,0:T(8,128)(2,1)} %param.18), channel_id=1, source_target_pairs={{0,20},{4,16},{8,28},{12,24},{16,4},{20,0},{24,12},{28,8},{1,21},{... | collective-permute-start | bytes 589832 | tf_op jit(solution)/shard_map/cond/branch_4_fun/ppermute | solution.py:94
  28.2 5.6 %collective-permute-done.18 = bf16[96,1024]{1,0:T(8,128)(2,1)} collective-permute-done((bf16[96,1024]{1,0:T(8,128)(2,1)}, bf16[96,1024]{1,0:T(8,128)(2,1)}, u32[]{:S(2)}, u32[]{:S(2)}) %collective-permute-start.18) | collective-permute-done | bytes 196640 | tf_op jit(solution)/shard_map/cond/branch_4_fun/ppermute | solution.py:94
  34.4 6.4 %conditional.7 = (bf16[1,96,1024]{2,1,0:T(8,128)(2,1)}) conditional(s32[]{:T(128)} %bitcast.35, bf16[96,1024]{1,0:T(8,128)(2,1)} %constant_dynamic-slice_fusion.4, bf16[96,1024]{1,0:T(8,128)(2,1)} %constant_dynamic-slice_fusion.4, bf16[96,1024]{1,0:T(8,128)(2,1)} %constant_dynamic-slice_fusion.4, ...), branch_computations={%region_21.22_spmd, %region_22.23_spmd, %region_23.24_spmd, %regio... | conditional | bytes 786480 | solution.py:99
  34.4 3.0 %collective-permute-start.27 = (bf16[96,1024]{1,0:T(8,128)(2,1)}, bf16[96,1024]{1,0:T(8,128)(2,1)}, u32[]{:S(2)}, u32[]{:S(2)}) collective-permute-start(bf16[96,1024]{1,0:T(8,128)(2,1)} %param.27), channel_id=1, source_target_pairs={{0,28},{4,24},{8,20},{12,16},{16,12},{20,8},{24,4},{28,0},{1,29},{... | collective-permute-start | bytes 589832 | tf_op jit(solution)/shard_map/cond/branch_6_fun/ppermute | solution.py:94
  37.4 3.4 %collective-permute-done.27 = bf16[96,1024]{1,0:T(8,128)(2,1)} collective-permute-done((bf16[96,1024]{1,0:T(8,128)(2,1)}, bf16[96,1024]{1,0:T(8,128)(2,1)}, u32[]{:S(2)}, u32[]{:S(2)}) %collective-permute-start.27) | collective-permute-done | bytes 196640 | tf_op jit(solution)/shard_map/cond/branch_6_fun/ppermute | solution.py:94
  40.8 1.2 collective-permute-start.38
  42.0 2.2 %convolution_convert_fusion = bf16[384,3,256]{2,0,1:T(8,128)(2,1)S(1)} fusion(bf16[1024,3,256]{2,0,1:T(8,128)(2,1)} %param.36, bf16[384,1024]{1,0:T(8,128)(2,1)S(1)} %copy-done), kind=kOutput, calls=%fused_computation.10 | convolution fusion | flops 604274688 | bytes 2949120 | tf_op jit(solution)/shard_map/nd,dtf->ntf/dot_general | solution.py:236
  46.0 1.0 reshape_reshape.6.own_ref
  47.9 1.2 collective-permute-start.30
  49.4 1.0 pad_maximum_fusion.2
  50.4 10.1 %collective-permute-start.35 = (bf16[2,96,1024]{2,1,0:T(8,128)(2,1)S(1)}, bf16[2,96,1024]{2,1,0:T(8,128)(2,1)S(1)}, u32[]{:S(2)}, u32[]{:S(2)}) collective-permute-start(bf16[2,96,1024]{2,1,0:T(8,128)(2,1)S(1)} %pad_maximum_fusion.2), channel_id=1, source_target_pairs={{0,1},{1,0},{2,3},{3,2},{4,5},{5,4},{6,7},{7,6},{8,9},{9,8},{10,11... | collective-permute-start | bytes 1179656 | tf_op jit(solution)/shard_map/ppermute | solution.py:41
  60.4 1.0 pad_maximum_fusion.3
  61.4 0.9 constant_dynamic-update-slice_fusion.3
  62.4 0.9 constant_dynamic-update-slice_fusion.2
  63.4 1.0 pad_maximum_fusion.4
  65.0 1.0 pad_maximum_fusion.5
  65.9 0.9 constant_dynamic-update-slice_fusion.1
  66.9 0.9 constant_dynamic-update-slice_fusion
  68.7 1.0 collective-permute-done.31
  70.4 1.0 collective-permute-done.41
  71.7 3.9 %fusion.7 = bf16[4,6,96,2,256]{4,2,3,1,0:T(8,128)(2,1)} fusion(bf16[1,6,96,1024]{3,2,1,0:T(8,128)(2,1)S(1)} %bitcast.87, bf16[1,6,96,1024]{3,2,1,0:T(8,128)(2,1)S(1)} %bitcast.85, bf16[1,6,96,1024]{3,2,1,0:T(8,128)(2,1)S(1)} %bitcast.86, bf16[1,6,96,1024]{3,2,1,0:T(8,128)(2,1)S(1)} %bitcast.84, bf16[1024,3,256]{2,0,1:T(8,128)(2,1)S(1)} %copy-done.7), kind=kOutput, calls=%fused_computation.9 | convolution fusion | flops 2435973120 | bytes 8126464 | tf_op jit(solution)/shard_map/kprd,dtf->kprtf/dot_general | solution.py:134
  75.6 2.4 %gather_fusion = bf16[4,6,96,2,256]{4,2,3,1,0:T(8,128)(2,1)S(1)} fusion(bf16[4,6,96,2,256]{4,2,3,1,0:T(8,128)(2,1)} %fusion.7, s32[1024]{0:T(1024)S(1)} %pad_clamp_fusion), kind=kCustom, calls=%fused_computation | custom fusion | bytes 4718608 | tf_op jit(solution)/shard_map/jit(_take)/gather | solution.py:138
  78.0 3.9 %copy.18 = bf16[6,4,96,2,256]{4,3,2,1,0:T(2,128)(2,1)} copy(bf16[6,4,96,2,256]{4,2,3,0,1:T(8,128)(2,1)S(1)} %bitcast.74) | data formatting | bytes 4718592 | tf_op jit(solution)/shard_map/transpose | solution.py:140
  81.9 6.4 %reshape_reshape.7.part_ref = bf16[6,3,128,512]{3,2,1,0:T(8,128)(2,1)} reshape(bf16[6,4,96,2,256]{4,3,2,1,0:T(2,128)(2,1)} %copy.18) | data formatting | bytes 4718592 | tf_op jit(solution)/shard_map/reshape;reshape | solution.py:257
  88.3 18.8 %shard_map.73 = bf16[3,128,256]{2,1,0:T(8,128)(2,1)} custom-call(s32[3,11]{1,0:T(4,128)} %pad_convert_fusion.live_ref, s32[4,3]{1,0:T(4,128)} %add_select_fusion.pick_ref, bf16[3,128,256]{2,1,0:T(8,128)(2,1)} %bitcast.79, bf16[3,128,512]{2,1,0:T(8,128)(2,1)} %reshape_reshape.6.own_ref, bf16[6,3,128,512]{3,2,1,0:T(8,128)(2,1)} %reshape_reshape.7.part_ref), custom_call_target="tpu_custom_call" | custom-call | flops 553648128 | bytes 3145728 | tf_op jit(solution)/shard_map/pallas_call | solution.py:201
  107.1 1.2 collective-permute-start.42
  108.3 5.4 %collective-permute-done.42 = bf16[1,384,256]{2,1,0:T(8,128)(2,1)S(1)} collective-permute-done((bf16[1,384,256]{2,1,0:T(8,128)(2,1)}, bf16[1,384,256]{2,1,0:T(8,128)(2,1)S(1)}, u32[]{:S(2)}, u32[]{:S(2)}) %collective-permute-start.42) | collective-permute-done | bytes 196640 | tf_op jit(solution)/shard_map/ppermute | solution.py:41
  113.7 1.0 pad_maximum_fusion.6
  114.7 1.0 collective-permute-start.43
  116.1 1.3 collective-permute-start.45
  117.5 0.9 collective-permute-start.46
  118.8 2.0 %collective-permute-done.45 = bf16[256,256]{0,1:T(8,128)(2,1)S(1)} collective-permute-done((bf16[256,256]{0,1:T(8,128)(2,1)S(1)}, bf16[256,256]{0,1:T(8,128)(2,1)S(1)}, u32[]{:S(2)}, u32[]{:S(2)}) %collective-permute-start.45) | collective-permute-done | bytes 131104 | tf_op jit(solution)/shard_map/ppermute | solution.py:41
  120.8 3.4 %collective-permute-done.46 = bf16[256,256]{0,1:T(8,128)(2,1)S(1)} collective-permute-done((bf16[256,256]{0,1:T(8,128)(2,1)S(1)}, bf16[256,256]{0,1:T(8,128)(2,1)S(1)}, u32[]{:S(2)}, u32[]{:S(2)}) %collective-permute-start.46) | collective-permute-done | bytes 131104 | tf_op jit(solution)/shard_map/ppermute | solution.py:41
  124.9 1.3 collective-permute-start.48
  126.2 0.8 collective-permute-start.49
  127.4 2.1 %collective-permute-done.49 = f32[384,2]{0,1:T(2,128)S(1)} collective-permute-done((f32[384,2]{0,1:T(2,128)S(1)}, f32[384,2]{0,1:T(2,128)S(1)}, u32[]{:S(2)}, u32[]{:S(2)}) %collective-permute-start.49) | collective-permute-done | bytes 3104 | tf_op jit(solution)/shard_map/ppermute | solution.py:41
  129.7 0.8 copy.23
  (93 shorter events, 9.4 us)
Async XLA Ops:
  0.0 1.1 copy-start
  1.8 45.8 %collective-permute-start.28 = (bf16[96,1024]{1,0:T(8,128)(2,1)}, bf16[96,1024]{1,0:T(8,128)(2,1)S(1)}, u32[]{:S(2)}, u32[]{:S(2)}) collective-permute-start(bf16[96,1024]{1,0:T(8,128)(2,1)} %constant_dynamic-slice_fusion.4), channel_id=1, source_target_pairs={{0,4},{4,8},{8,12},{12,16},{16,20},{20,24},{24,28},{1,5},{5,9},{9,... | collective-permute-start | bytes 589832 | tf_op jit(solution)/shard_map/ppermute | solution.py:128
  5.0 43.0 %collective-permute-start.29 = (bf16[96,1024]{1,0:T(8,128)(2,1)}, bf16[96,1024]{1,0:T(8,128)(2,1)S(1)}, u32[]{:S(2)}, u32[]{:S(2)}) collective-permute-start(bf16[96,1024]{1,0:T(8,128)(2,1)} %constant_dynamic-slice_fusion.4), channel_id=1, source_target_pairs={{4,0},{8,4},{12,8},{16,12},{20,16},{24,20},{28,24},{5,1},{9,5},{13... | collective-permute-start | bytes 589832 | tf_op jit(solution)/shard_map/ppermute | solution.py:129
  11.0 6.5 %collective-permute-start.2 = (bf16[96,1024]{1,0:T(8,128)(2,1)}, bf16[96,1024]{1,0:T(8,128)(2,1)}, u32[]{:S(2)}, u32[]{:S(2)}) collective-permute-start(bf16[96,1024]{1,0:T(8,128)(2,1)} %param.2), channel_id=1, source_target_pairs={{0,12},{4,8},{8,4},{12,0},{16,28},{20,24},{24,20},{28,16},{1,13},{... | collective-permute-start | bytes 589832 | tf_op jit(solution)/shard_map/cond/branch_2_fun/ppermute | solution.py:94
  17.5 31.6 %collective-permute-start.34 = (bf16[1,96,1024]{2,1,0:T(8,128)(2,1)}, bf16[1,96,1024]{2,1,0:T(8,128)(2,1)S(1)}, u32[]{:S(2)}, u32[]{:S(2)}) collective-permute-start(bf16[1,96,1024]{2,1,0:T(8,128)(2,1)} %get-tuple-element.97), channel_id=1, source_target_pairs={{0,2},{1,3},{2,0},{3,1},{4,6},{5,7},{6,4},{7,5},{8,10},{9,11},{10,... | collective-permute-start | bytes 589832 | tf_op jit(solution)/shard_map/ppermute | solution.py:41
  19.3 5.1 %collective-permute-start.8 = (bf16[96,1024]{1,0:T(8,128)(2,1)}, bf16[96,1024]{1,0:T(8,128)(2,1)}, u32[]{:S(2)}, u32[]{:S(2)}) collective-permute-start(bf16[96,1024]{1,0:T(8,128)(2,1)} %param.8), channel_id=1, source_target_pairs={{0,8},{4,12},{8,0},{12,4},{16,24},{20,28},{24,16},{28,20},{1,9},{5... | collective-permute-start | bytes 589832 | tf_op jit(solution)/shard_map/cond/branch_1_fun/ppermute | solution.py:94
  24.4 26.0 %collective-permute-start.36 = (bf16[1,96,1024]{2,1,0:T(8,128)(2,1)}, bf16[1,96,1024]{2,1,0:T(8,128)(2,1)S(1)}, u32[]{:S(2)}, u32[]{:S(2)}) collective-permute-start(bf16[1,96,1024]{2,1,0:T(8,128)(2,1)} %get-tuple-element.98), channel_id=1, source_target_pairs={{0,2},{1,3},{2,0},{3,1},{4,6},{5,7},{6,4},{7,5},{8,10},{9,11},{10,... | collective-permute-start | bytes 589832 | tf_op jit(solution)/shard_map/ppermute | solution.py:41
  25.3 8.5 %collective-permute-start.18 = (bf16[96,1024]{1,0:T(8,128)(2,1)}, bf16[96,1024]{1,0:T(8,128)(2,1)}, u32[]{:S(2)}, u32[]{:S(2)}) collective-permute-start(bf16[96,1024]{1,0:T(8,128)(2,1)} %param.18), channel_id=1, source_target_pairs={{0,20},{4,16},{8,28},{12,24},{16,4},{20,0},{24,12},{28,8},{1,21},{... | collective-permute-start | bytes 589832 | tf_op jit(solution)/shard_map/cond/branch_4_fun/ppermute | solution.py:94
  34.4 6.3 %collective-permute-start.27 = (bf16[96,1024]{1,0:T(8,128)(2,1)}, bf16[96,1024]{1,0:T(8,128)(2,1)}, u32[]{:S(2)}, u32[]{:S(2)}) collective-permute-start(bf16[96,1024]{1,0:T(8,128)(2,1)} %param.27), channel_id=1, source_target_pairs={{0,28},{4,24},{8,20},{12,16},{16,12},{20,8},{24,4},{28,0},{1,29},{... | collective-permute-start | bytes 589832 | tf_op jit(solution)/shard_map/cond/branch_6_fun/ppermute | solution.py:94
  40.8 22.5 %collective-permute-start.38 = (bf16[1,96,1024]{2,1,0:T(8,128)(2,1)}, bf16[1,96,1024]{2,1,0:T(8,128)(2,1)S(1)}, u32[]{:S(2)}, u32[]{:S(2)}) collective-permute-start(bf16[1,96,1024]{2,1,0:T(8,128)(2,1)} %get-tuple-element.99), channel_id=1, source_target_pairs={{0,2},{1,3},{2,0},{3,1},{4,6},{5,7},{6,4},{7,5},{8,10},{9,11},{10,... | collective-permute-start | bytes 589832 | tf_op jit(solution)/shard_map/ppermute | solution.py:41
  44.2 0.8 copy-start.4
  44.2 2.8 %copy-start.3 = (s32[4,3]{1,0:T(4,128)S(1)}, s32[4,3]{1,0:T(4,128)}, u32[]{:S(2)}) copy-start(s32[4,3]{1,0:T(4,128)} %param.41) | copy-start | bytes 148
  47.7 16.7 %collective-permute-start.40 = (bf16[1,96,1024]{2,1,0:T(8,128)(2,1)}, bf16[1,96,1024]{2,1,0:T(8,128)(2,1)S(1)}, u32[]{:S(2)}, u32[]{:S(2)}) collective-permute-start(bf16[1,96,1024]{2,1,0:T(8,128)(2,1)} %get-tuple-element.100), channel_id=1, source_target_pairs={{0,2},{1,3},{2,0},{3,1},{4,6},{5,7},{6,4},{7,5},{8,10},{9,11},{10,... | collective-permute-start | bytes 589832 | tf_op jit(solution)/shard_map/ppermute | solution.py:41
  47.9 19.9 %collective-permute-start.30 = (bf16[1,96,1024]{2,1,0:T(8,128)(2,1)S(1)}, bf16[1,96,1024]{2,1,0:T(8,128)(2,1)S(1)}, u32[]{:S(2)}, u32[]{:S(2)}) collective-permute-start(bf16[1,96,1024]{2,1,0:T(8,128)(2,1)S(1)} %bitcast.77), channel_id=1, source_target_pairs={{0,2},{1,3},{2,0},{3,1},{4,6},{5,7},{6,4},{7,5},{8,10},{9,11},{10,... | collective-permute-start | bytes 589832 | tf_op jit(solution)/shard_map/ppermute | solution.py:41
  49.1 18.8 %collective-permute-start.32 = (bf16[1,96,1024]{2,1,0:T(8,128)(2,1)S(1)}, bf16[1,96,1024]{2,1,0:T(8,128)(2,1)S(1)}, u32[]{:S(2)}, u32[]{:S(2)}) collective-permute-start(bf16[1,96,1024]{2,1,0:T(8,128)(2,1)S(1)} %bitcast.75), channel_id=1, source_target_pairs={{0,2},{1,3},{2,0},{3,1},{4,6},{5,7},{6,4},{7,5},{8,10},{9,11},{10,... | collective-permute-start | bytes 589832 | tf_op jit(solution)/shard_map/ppermute | solution.py:41
  50.4 19.9 %collective-permute-start.35 = (bf16[2,96,1024]{2,1,0:T(8,128)(2,1)S(1)}, bf16[2,96,1024]{2,1,0:T(8,128)(2,1)S(1)}, u32[]{:S(2)}, u32[]{:S(2)}) collective-permute-start(bf16[2,96,1024]{2,1,0:T(8,128)(2,1)S(1)} %pad_maximum_fusion.2), channel_id=1, source_target_pairs={{0,1},{1,0},{2,3},{3,2},{4,5},{5,4},{6,7},{7,6},{8,9},{9,8},{10,11... | collective-permute-start | bytes 1179656 | tf_op jit(solution)/shard_map/ppermute | solution.py:41
  63.3 7.0 %collective-permute-start.37 = (bf16[2,96,1024]{2,1,0:T(8,128)(2,1)S(1)}, bf16[2,96,1024]{2,1,0:T(8,128)(2,1)S(1)}, u32[]{:S(2)}, u32[]{:S(2)}) collective-permute-start(bf16[2,96,1024]{2,1,0:T(8,128)(2,1)S(1)} %pad_maximum_fusion.3), channel_id=1, source_target_pairs={{0,1},{1,0},{2,3},{3,2},{4,5},{5,4},{6,7},{7,6},{8,9},{9,8},{10,11... | collective-permute-start | bytes 1179656 | tf_op jit(solution)/shard_map/ppermute | solution.py:41
  64.4 6.0 %collective-permute-start.39 = (bf16[2,96,1024]{2,1,0:T(8,128)(2,1)S(1)}, bf16[2,96,1024]{2,1,0:T(8,128)(2,1)S(1)}, u32[]{:S(2)}, u32[]{:S(2)}) collective-permute-start(bf16[2,96,1024]{2,1,0:T(8,128)(2,1)S(1)} %pad_maximum_fusion.4), channel_id=1, source_target_pairs={{0,1},{1,0},{2,3},{3,2},{4,5},{5,4},{6,7},{7,6},{8,9},{9,8},{10,11... | collective-permute-start | bytes 1179656 | tf_op jit(solution)/shard_map/ppermute | solution.py:41
  67.9 1.8 %collective-permute-start.31 = (bf16[2,96,1024]{2,1,0:T(8,128)(2,1)S(1)}, bf16[2,96,1024]{2,1,0:T(8,128)(2,1)S(1)}, u32[]{:S(2)}, u32[]{:S(2)}) collective-permute-start(bf16[2,96,1024]{2,1,0:T(8,128)(2,1)S(1)} %pad_maximum_fusion), channel_id=1, source_target_pairs={{0,1},{1,0},{2,3},{3,2},{4,5},{5,4},{6,7},{7,6},{8,9},{9,8},{10,11... | collective-permute-start | bytes 1179656 | tf_op jit(solution)/shard_map/ppermute | solution.py:41
  68.0 2.2 %collective-permute-start.33 = (bf16[2,96,1024]{2,1,0:T(8,128)(2,1)S(1)}, bf16[2,96,1024]{2,1,0:T(8,128)(2,1)S(1)}, u32[]{:S(2)}, u32[]{:S(2)}) collective-permute-start(bf16[2,96,1024]{2,1,0:T(8,128)(2,1)S(1)} %pad_maximum_fusion.1), channel_id=1, source_target_pairs={{0,1},{1,0},{2,3},{3,2},{4,5},{5,4},{6,7},{7,6},{8,9},{9,8},{10,11... | collective-permute-start | bytes 1179656 | tf_op jit(solution)/shard_map/ppermute | solution.py:41
  69.7 1.7 %collective-permute-start.41 = (bf16[2,96,1024]{2,1,0:T(8,128)(2,1)S(1)}, bf16[2,96,1024]{2,1,0:T(8,128)(2,1)S(1)}, u32[]{:S(2)}, u32[]{:S(2)}) collective-permute-start(bf16[2,96,1024]{2,1,0:T(8,128)(2,1)S(1)} %pad_maximum_fusion.5), channel_id=1, source_target_pairs={{0,1},{1,0},{2,3},{3,2},{4,5},{5,4},{6,7},{7,6},{8,9},{9,8},{10,11... | collective-permute-start | bytes 1179656 | tf_op jit(solution)/shard_map/ppermute | solution.py:41
  70.3 1.4 %copy-start.7 = (bf16[1024,3,256]{2,0,1:T(8,128)(2,1)S(1)}, bf16[1024,3,256]{2,0,1:T(8,128)(2,1)}, u32[]{:S(2)}) copy-start(bf16[1024,3,256]{2,0,1:T(8,128)(2,1)} %param.36) | copy-start | bytes 4718596
  107.1 8.6 %copy-start.1 = (bf16[256,1024]{1,0:T(8,128)(2,1)S(1)}, bf16[256,1024]{1,0:T(8,128)(2,1)}, u32[]{:S(2)}) copy-start(bf16[256,1024]{1,0:T(8,128)(2,1)} %param.37) | copy-start | bytes 1572868
  107.1 6.6 %collective-permute-start.42 = (bf16[1,384,256]{2,1,0:T(8,128)(2,1)}, bf16[1,384,256]{2,1,0:T(8,128)(2,1)S(1)}, u32[]{:S(2)}, u32[]{:S(2)}) collective-permute-start(bf16[1,384,256]{2,1,0:T(8,128)(2,1)} %bitcast.80), channel_id=1, source_target_pairs={{0,2},{1,3},{2,0},{3,1},{4,6},{5,7},{6,4},{7,5},{8,10},{9,11},{10,... | collective-permute-start | bytes 589832 | tf_op jit(solution)/shard_map/ppermute | solution.py:41
  114.7 4.1 %collective-permute-start.43 = (bf16[2,384,256]{2,1,0:T(8,128)(2,1)S(1)}, bf16[2,384,256]{2,1,0:T(8,128)(2,1)S(1)}, u32[]{:S(2)}, u32[]{:S(2)}) collective-permute-start(bf16[2,384,256]{2,1,0:T(8,128)(2,1)S(1)} %pad_maximum_fusion.6), channel_id=1, source_target_pairs={{0,1},{1,0},{2,3},{3,2},{4,5},{5,4},{6,7},{7,6},{8,9},{9,8},{10,11... | collective-permute-start | bytes 1179656 | tf_op jit(solution)/shard_map/ppermute | solution.py:41
  115.9 2.9 %collective-permute-start.44 = (bf16[256,256]{0,1:T(8,128)(2,1)S(1)}, bf16[256,256]{0,1:T(8,128)(2,1)S(1)}, u32[]{:S(2)}, u32[]{:S(2)}) collective-permute-start(bf16[256,256]{0,1:T(8,128)(2,1)S(1)} %copy.27), channel_id=1, source_target_pairs={{0,1},{1,0},{2,3},{3,2},{4,5},{5,4},{6,7},{7,6},{8,9},{9,8},{10,11... | collective-permute-start | bytes 393224 | tf_op jit(solution)/shard_map/ppermute | solution.py:41
  116.0 8.2 %copy-start.2 = (bf16[3,128,256]{2,1,0:T(8,128)(2,1)S(1)}, bf16[3,128,256]{2,1,0:T(8,128)(2,1)}, u32[]{:S(2)}) copy-start(bf16[3,128,256]{2,1,0:T(8,128)(2,1)} %shard_map.73) | copy-start | bytes 589828
  116.1 4.7 %collective-permute-start.45 = (bf16[256,256]{0,1:T(8,128)(2,1)S(1)}, bf16[256,256]{0,1:T(8,128)(2,1)S(1)}, u32[]{:S(2)}, u32[]{:S(2)}) collective-permute-start(bf16[256,256]{0,1:T(8,128)(2,1)S(1)} %copy.28), channel_id=1, source_target_pairs={{0,2},{1,3},{2,0},{3,1},{4,6},{5,7},{6,4},{7,5},{8,10},{9,11},{10,... | collective-permute-start | bytes 393224 | tf_op jit(solution)/shard_map/ppermute | solution.py:41
  117.5 6.7 %collective-permute-start.46 = (bf16[256,256]{0,1:T(8,128)(2,1)S(1)}, bf16[256,256]{0,1:T(8,128)(2,1)S(1)}, u32[]{:S(2)}, u32[]{:S(2)}) collective-permute-start(bf16[256,256]{0,1:T(8,128)(2,1)S(1)} %copy.29), channel_id=1, source_target_pairs={{0,3},{1,2},{2,1},{3,0},{4,7},{5,6},{6,5},{7,4},{8,11},{9,10},{10,... | collective-permute-start | bytes 393224 | tf_op jit(solution)/shard_map/ppermute | solution.py:41
  124.2 5.4 %copy-start.5 = (f32[256]{0:T(256)S(1)}, f32[256]{0:T(256)}, u32[]{:S(2)}) copy-start(f32[256]{0:T(256)} %param.39) | copy-start | bytes 3076
  124.2 5.4 %copy-start.6 = (f32[256]{0:T(256)S(1)}, f32[256]{0:T(256)}, u32[]{:S(2)}) copy-start(f32[256]{0:T(256)} %param.38) | copy-start | bytes 3076
  124.8 2.2 %collective-permute-start.47 = (f32[384,2]{0,1:T(2,128)S(1)}, f32[384,2]{0,1:T(2,128)S(1)}, u32[]{:S(2)}, u32[]{:S(2)}) collective-permute-start(f32[384,2]{0,1:T(2,128)S(1)} %get-tuple-element.90), channel_id=1, source_target_pairs={{0,1},{1,0},{2,3},{3,2},{4,5},{5,4},{6,7},{7,6},{8,9},{9,8},{10,11... | collective-permute-start | bytes 9224 | tf_op jit(solution)/shard_map/ppermute | solution.py:41
  124.9 2.5 %collective-permute-start.48 = (f32[384,2]{0,1:T(2,128)S(1)}, f32[384,2]{0,1:T(2,128)S(1)}, u32[]{:S(2)}, u32[]{:S(2)}) collective-permute-start(f32[384,2]{0,1:T(2,128)S(1)} %get-tuple-element.90), channel_id=1, source_target_pairs={{0,2},{1,3},{2,0},{3,1},{4,6},{5,7},{6,4},{7,5},{8,10},{9,11},{10,... | collective-permute-start | bytes 9224 | tf_op jit(solution)/shard_map/ppermute | solution.py:41
  126.2 3.3 %collective-permute-start.49 = (f32[384,2]{0,1:T(2,128)S(1)}, f32[384,2]{0,1:T(2,128)S(1)}, u32[]{:S(2)}, u32[]{:S(2)}) collective-permute-start(f32[384,2]{0,1:T(2,128)S(1)} %get-tuple-element.90), channel_id=1, source_target_pairs={{0,3},{1,2},{2,1},{3,0},{4,7},{5,6},{6,5},{7,4},{8,11},{9,10},{10,... | collective-permute-start | bytes 9224 | tf_op jit(solution)/shard_map/ppermute | solution.py:41
where the time goes:
time: 132 us; the launch traced here: 131 us
  waiting for transfers between devices  35.8 us (27%)
  starting transfers between devices  35 us (27%)
  local copies, waits for them, and re-layouts  23.1 us (18%)
  Pallas kernels  18.8 us (14%)
  other arithmetic  8.09 us (6%)
  matrix products  6.57 us (5%)
  between operations  3.02 us (2%)
    ppermute x20, starting transfers between devices, flip_heads(): return lax.ppermute(array, 'head', [(i, i ^ flip) for i in range(devices)])  22.6 us
    ppermute x4, waiting for transfers between devices, moved(): lax.ppermute(current, 'node', [(i, i ^ shift) for i in range(groups)])  20.2 us
    pallas_call x1, Pallas kernels, attention(): pl.pallas_call(attention_kernel, out_shape=jax.ShapeDtypeStruct(query.sha...  18.8 us
    ppermute x20, waiting for transfers between devices, flip_heads(): return lax.ppermute(array, 'head', [(i, i ^ flip) for i in range(devices)])  15.6 us
    another operation x1, local copies, waits for them, and re-layouts, local(): part.reshape(part.shape[0], blocks_here, ROWS, 2 * head_feats)  6.42 us
    ppermute x4, starting transfers between devices, moved(): lax.ppermute(current, 'node', [(i, i ^ shift) for i in range(groups)])  6.22 us
    unnamed x35, local copies, waits for them, and re-layouts  4.99 us
    another operation x7, other arithmetic, spread_slots(): other = flip_heads(jnp.stack([slots[k] for k in held]), flip, heads_axis)  4.9 us
  transfers between devices with their start and end apart: 26, of which 12 were waited for; matrix products, arithmetic and copies ran while one was open for 13% of the time, Pallas kernels for 0%

commit v1 on v0

--- a/solution.py
+++ b/solution.py
@@ -10,6 +10,7 @@
 HEAD_DIM = 64
 ROWS = 128
 REACH = 3
+LANES = 128
 GATHER_GROUPS = 16
 
 
@@ -18,23 +19,6 @@
 
 def partner(array, axis, bit):
     return lax.ppermute(array, axis, [(i, i ^ 1 << bit) for i in range(lax.axis_size(axis))])
-
-
-def with_halo(array, sides, width):
-    for axis, dim in sides:
-        devices, length = (lax.axis_size(axis), array.shape[dim])
-        up = [(i, (i + 1) % devices) for i in range(devices - 1)]
-        down = [(j, i) for i, j in up]
-        last = lax.slice_in_dim(array, length - width, length, axis=dim)
-        first = lax.slice_in_dim(array, 0, width, axis=dim)
-        before = lax.ppermute(last, axis, up)
-        after = lax.ppermute(first, axis, down)
-        array = jnp.concatenate([before, array, after], axis=dim)
-    return array
-
-
-def shift_heads(array, step, devices):
-    return lax.ppermute(array, "head", [(i, (i + step) % devices) for i in range(devices)])
 
 
 def flip_heads(array, flip, devices):
@@ -65,15 +49,6 @@
         taken = jnp.bitwise_and(jnp.right_shift(shift_val, bit_pos), 1) == 1
         payload = lax.cond(taken, moved, keep_same, payload)
     return payload
-
-
-def select_partner(received, matchings, blocks_here, pair_feats):
-    matches = matchings.shape[0]
-    received = received.reshape(matches, blocks_here, ROWS, pair_feats)
-    sources = matchings % blocks_here
-    selector = (sources[:, :, None] == jnp.arange(blocks_here)[None, None, :]).astype(jnp.bfloat16)
-    picked = jnp.einsum("mjs,msrf->mjrf", selector, received, preferred_element_type=jnp.float32)
-    return picked.astype(jnp.bfloat16)
 
 
 def routed_keys(keyvals, matchings, my_index, groups, blocks_here):
@@ -99,66 +74,50 @@
     return lax.switch(jnp.clip(shift_val - 1, 0, groups - 2), branches, payload)
 
 
-def switched_keys(keyvals, matchings, my_index, groups, blocks_here, window):
-    total_rows, pair_feats = keyvals.shape
-    matches = matchings.shape[0]
-    padded = with_halo(keyvals, (("node", 0),), REACH * ROWS)
-    windows = jnp.stack(
-        [padded[block_pos * ROWS : (block_pos + window) * ROWS] for block_pos in range(blocks_here)]
-    )
-    targets = jnp.bitwise_xor(matchings[:, 0] // blocks_here, my_index)
-    picked = []
-    for match_pos in range(matches):
-        received = switched_send(keyvals, targets[match_pos], groups)
-        received = received.reshape(blocks_here, ROWS, pair_feats)
-        picked.append(jnp.take(received, matchings[match_pos] % blocks_here, axis=0, mode="clip"))
-    partner_rows = jnp.stack(picked, axis=1).reshape(blocks_here, matches * ROWS, pair_feats)
-    return jnp.concatenate([windows, partner_rows], axis=1)
-
-
-def quarter_keys(node_states, w_qkv, matchings, my_index, groups, blocks_here):
-    total_rows = node_states.shape[0]
+def quarter_keys(node_states, w_kv, w_parts, matchings, my_index, groups, blocks_here):
+    total_rows, model_width = node_states.shape
     matches = matchings.shape[0]
     heads_axis = lax.axis_size("head")
-    part_rows = total_rows // heads_axis
+    sub_rows = ROWS // heads_axis
     me = lax.axis_index("head")
-    mine = lax.dynamic_slice_in_dim(node_states, me * part_rows, part_rows, 0)
+    mine = node_states.reshape(blocks_here, heads_axis, sub_rows, model_width)
+    mine = lax.dynamic_index_in_dim(mine, me, axis=1, keepdims=False)
+    mine = mine.reshape(blocks_here * sub_rows, model_width)
     up = [(i, i + 1) for i in range(groups - 1)]
     down = [(i + 1, i) for i in range(groups - 1)]
     before = lax.ppermute(mine, "node", up)
     after = lax.ppermute(mine, "node", down)
     targets = jnp.bitwise_xor(matchings[:, 0] // blocks_here, my_index)
     matched = [switched_send(mine, targets[match_pos], groups) for match_pos in range(matches)]
+    w_parts, matched[0] = lax.optimization_barrier((w_parts, matched[0]))
     spread = [spread_slots(piece, heads_axis) for piece in [before, after] + matched]
-    slots = jnp.stack([jnp.stack([one[k] for one in spread]) for k in range(heads_axis)])
-    slot_kv = jnp.einsum(
-        "kprd,dtf->kprtf", slots, w_qkv[:, 1:], preferred_element_type=jnp.float32
-    ).astype(jnp.bfloat16)
-    order = jnp.bitwise_xor(jnp.arange(heads_axis, dtype=jnp.int32), me.astype(jnp.int32))
-    ordered = jnp.take(slot_kv, order, axis=0, mode="clip")
+    rows = jnp.stack(
+        [
+            jnp.stack(
+                [one[k].reshape(blocks_here, sub_rows, model_width) for k in range(heads_axis)],
+                axis=1,
+            )
+            for one in spread
+        ]
+    )
     count = len(spread)
-    ordered = jnp.transpose(ordered, (1, 0, 2, 3, 4))
-    return ordered.reshape(count, total_rows, -1)
-
-
-def gathered_keys(keyvals, chosen):
-    total_rows, pair_feats = keyvals.shape
-    blocks_here, key_blocks = chosen.shape
-    everyone = lax.all_gather(keyvals, "node", axis=0, tiled=True)
-    everyone = everyone.reshape(-1, ROWS, pair_feats)
-    picked = jnp.take(everyone, chosen.reshape(-1), axis=0, mode="clip")
-    return picked.reshape(blocks_here, key_blocks * ROWS, pair_feats)
+    rows = rows.reshape(count * total_rows, model_width)
+    partner_kv = jnp.dot(rows, w_kv, preferred_element_type=jnp.float32).astype(jnp.bfloat16)
+    return partner_kv.reshape(count, total_rows, w_kv.shape[1]), w_parts
 
 
 def attention_kernel(live_ref, pick_ref, q_ref, own_ref, part_ref, out_ref, score_ref):
     blocks_here = q_ref.shape[0]
-    heads_here = q_ref.shape[2] // HEAD_DIM
     head_feats = q_ref.shape[2]
+    pairs = head_feats // LANES
+    per_pair = LANES // HEAD_DIM
     window = 2 * REACH + 1
     matches = part_ref.shape[0] - 2
     key_blocks = window + matches
     inv_root = 1.0 / math.sqrt(HEAD_DIM)
+    lane = lax.broadcasted_iota(jnp.int32, (ROWS, LANES), 1)
     for j in range(blocks_here):
+
         def key_block(t, cols, j=j):
             if t < window:
                 pos = j + t - REACH
@@ -169,34 +128,46 @@
                 return part_ref[1, pos - blocks_here, :, cols]
             match_pos = t - window
             return part_ref[2 + match_pos, pick_ref[match_pos, j], :, cols]
-        for h in range(heads_here):
-            kcols = pl.ds(h * HEAD_DIM, HEAD_DIM)
-            vcols = pl.ds(head_feats + h * HEAD_DIM, HEAD_DIM)
-            query = q_ref[j, :, kcols]
-            highest = jnp.full((ROWS, 1), -jnp.inf, jnp.float32)
-            for t in range(key_blocks):
-                scores = lax.dot_general(query, key_block(t, kcols), (((1,), (1,)), ((), ())),
-                                         preferred_element_type=jnp.float32) * inv_root
-                scores = jnp.where(live_ref[j, t] != 0, scores, -jnp.inf)
-                score_ref[t] = scores
-                highest = jnp.maximum(highest, jnp.max(scores, axis=1, keepdims=True))
-            total = jnp.zeros((ROWS, 1), jnp.float32)
-            for t in range(key_blocks):
-                weights = jnp.exp(score_ref[t] - highest)
-                score_ref[t] = weights
-                total = total + jnp.sum(weights, axis=1, keepdims=True)
-            context = jnp.zeros((ROWS, HEAD_DIM), jnp.float32)
-            for t in range(key_blocks):
-                probs = (score_ref[t] / total).astype(jnp.bfloat16)
-                context = context + jnp.dot(probs, key_block(t, vcols), preferred_element_type=jnp.float32)
-            out_ref[j, :, kcols] = context.astype(jnp.bfloat16)
+
+        for pair in range(pairs):
+            kcols = pl.ds(pair * LANES, LANES)
+            vcols = pl.ds(head_feats + pair * LANES, LANES)
+            both = q_ref[j, :, kcols]
+            merged = jnp.zeros((ROWS, LANES), jnp.float32)
+            for half in range(per_pair):
+                mine = (lane >= half * HEAD_DIM) & (lane < (half + 1) * HEAD_DIM)
+                query = jnp.where(mine, both, jnp.zeros_like(both))
+                highest = jnp.full((ROWS, ROWS), -jnp.inf, jnp.float32)
+                for t in range(key_blocks):
+                    scores = lax.dot_general(
+                        query, key_block(t, kcols), (((1,), (1,)), ((), ())),
+                        preferred_element_type=jnp.float32,
+                    ) * inv_root
+                    scores = jnp.where(live_ref[j, t] != 0, scores, -jnp.inf)
+                    score_ref[t] = scores
+                    highest = jnp.maximum(highest, scores)
+                highest = jnp.max(highest, axis=1, keepdims=True)
+                total = jnp.zeros((ROWS, ROWS), jnp.float32)
+                for t in range(key_blocks):
+                    weights = jnp.exp(score_ref[t] - highest)
+                    score_ref[t] = weights
+                    total = total + weights
+                total = jnp.sum(total, axis=1, keepdims=True)
+                context = jnp.zeros((ROWS, LANES), jnp.float32)
+                for t in range(key_blocks):
+                    probs = (score_ref[t] / total).astype(jnp.bfloat16)
+                    context = context + jnp.dot(
+                        probs, key_block(t, vcols), preferred_element_type=jnp.float32
+                    )
+                merged = jnp.where(mine, context, merged)
+            out_ref[j, :, kcols] = merged.astype(jnp.bfloat16)
 
 
 def attention(live, pick, query, own, part):
     blocks_here, rows, head_feats = query.shape
     key_blocks = live.shape[1]
     vmem = pltpu.VMEM
-    flops = 4 * blocks_here * rows * key_blocks * rows * head_feats
+    flops = 8 * blocks_here * rows * key_blocks * rows * head_feats
     moved = 2 * (query.size * 2 + own.size + part.size)
     return pl.pallas_call(
         attention_kernel,
@@ -209,7 +180,6 @@
             flops=flops, transcendentals=blocks_here * rows * key_blocks * rows * 4, bytes_accessed=moved
         ),
     )(live, pick, query, own, part)
-
 
 def local(node_states, w_qkv, w_out, ln_gain, ln_bias, local_mask, matchings):
     total_rows, model_width = node_states.shape
@@ -242,7 +212,10 @@
     offsets = jnp.arange(window, dtype=jnp.int32) - REACH
     neighbour = global_blocks[:, None] + offsets[None, :]
     if groups <= GATHER_GROUPS:
-        part = quarter_keys(node_states, w_qkv, matchings, my_index, groups, blocks_here)
+        w_kv = w_qkv[:, 1:].reshape(model_width, 2 * head_feats)
+        part, w_parts = quarter_keys(
+            node_states, w_kv, w_parts, matchings, my_index, groups, blocks_here
+        )
     else:
         part = routed_keys(keyvals, matchings, my_index, groups, blocks_here)
     local_ok = (

time: 132 us -> 130 us (0.985)
  the two profiles are of different devices: /device:TPU:9 before, /device:TPU:0 now
where the time goes in v1:
time: 130 us; the launch traced here: 129 us
  waiting for transfers between devices  54.9 us (42%)
  starting transfers between devices  27.5 us (21%)
  other arithmetic  14.9 us (11%)
  local copies, waits for them, and re-layouts  11 us (8%)
  Pallas kernels  10.8 us (8%)
  matrix products  7 us (5%)
  between operations  2.83 us (2%)
    ppermute x4, waiting for transfers between devices, moved(): lax.ppermute(current, 'node', [(i, i ^ shift) for i in range(groups)])  30.5 us
    ppermute x20, waiting for transfers between devices, flip_heads(): return lax.ppermute(array, 'head', [(i, i ^ flip) for i in range(devices)])  24.4 us
    ppermute x20, starting transfers between devices, flip_heads(): return lax.ppermute(array, 'head', [(i, i ^ flip) for i in range(devices)])  11.1 us
    pallas_call x1, Pallas kernels, attention(): pl.pallas_call(attention_kernel, out_shape=jax.ShapeDtypeStruct(query.sha...  10.8 us
    ppermute x4, starting transfers between devices, moved(): lax.ppermute(current, 'node', [(i, i ^ shift) for i in range(groups)])  9.59 us
    another operation x7, other arithmetic, spread_slots(): other = flip_heads(jnp.stack([slots[k] for k in held]), flip, heads_axis)  6.84 us
    ppermute x1, starting transfers between devices, quarter_keys(): before = lax.ppermute(mine, 'node', up)  5.54 us
    unnamed x5, other arithmetic  5.21 us
  transfers between devices with their start and end apart: 26, of which 14 were waited for; matrix products, arithmetic and copies ran while one was open for 14% of the time, Pallas kernels for 0%

profile of v1, /device:TPU:0, one launch (start us, length us, event | category | flops | bytes accessed | tf_op | source)
XLA Modules:
  0.0 129.1 jit_solution(11004658736684450608)
XLA Ops:
  0.0 1.1 copy-done
  1.8 5.5 %collective-permute-start.28 = (bf16[96,1024]{1,0:T(8,128)(2,1)}, bf16[96,1024]{1,0:T(8,128)(2,1)}, u32[]{:S(2)}, u32[]{:S(2)}) collective-permute-start(bf16[96,1024]{1,0:T(8,128)(2,1)} %bitcast.3), channel_id=1, source_target_pairs={{0,4},{4,8},{8,12},{12,16},{16,20},{20,24},{24,28},{1,5},{5,9},{9,... | collective-permute-start | bytes 589832 | tf_op jit(solution)/shard_map/ppermute | solution.py:88
  7.4 1.3 collective-permute-start.31
  8.7 1.1 constant_dynamic-slice_fusion
  10.8 1.5 %collective-permute-start.35 = (bf16[256,256]{0,1:T(8,128)(2,1)}, bf16[256,256]{0,1:T(8,128)(2,1)}, u32[]{:S(2)}, u32[]{:S(2)}) collective-permute-start(bf16[256,256]{0,1:T(8,128)(2,1)} %copy.29), channel_id=1, source_target_pairs={{0,2},{1,3},{2,0},{3,1},{4,6},{5,7},{6,4},{7,5},{8,10},{9,11},{10,... | collective-permute-start | bytes 393224 | tf_op jit(solution)/shard_map/ppermute | solution.py:25
  14.5 8.3 %conditional.4 = (bf16[96,1024]{1,0:T(8,128)(2,1)}) conditional(s32[]{:T(128)} %bitcast.16, bf16[96,1024]{1,0:T(8,128)(2,1)} %bitcast.3, bf16[96,1024]{1,0:T(8,128)(2,1)} %bitcast.3, bf16[96,1024]{1,0:T(8,128)(2,1)} %bitcast.3, bf16[96,1024]{1,0:T(8,128)(2,1)} %bitcast.3, bf16[96,1024]{1,0:T(8,128)(2,1)} %bitcast.3, ...), branch_computations={%region_0.1_spmd, %region_1.2_spmd, %region_2.3_spmd, %region_3.4_... | conditional | bytes 786480 | solution.py:74
  14.5 2.7 %collective-permute-start = (bf16[96,1024]{1,0:T(8,128)(2,1)}, bf16[96,1024]{1,0:T(8,128)(2,1)}, u32[]{:S(2)}, u32[]{:S(2)}) collective-permute-start(bf16[96,1024]{1,0:T(8,128)(2,1)} %param), channel_id=1, source_target_pairs={{0,4},{4,0},{8,12},{12,8},{16,20},{20,16},{24,28},{28,24},{1,5},{5... | collective-permute-start | bytes 589832 | tf_op jit(solution)/shard_map/cond/branch_0_fun/ppermute | solution.py:69
  17.2 5.6 %collective-permute-done = bf16[96,1024]{1,0:T(8,128)(2,1)} collective-permute-done((bf16[96,1024]{1,0:T(8,128)(2,1)}, bf16[96,1024]{1,0:T(8,128)(2,1)}, u32[]{:S(2)}, u32[]{:S(2)}) %collective-permute-start) | collective-permute-done | bytes 196640 | tf_op jit(solution)/shard_map/cond/branch_0_fun/ppermute | solution.py:69
  23.4 12.9 %conditional.5 = (bf16[96,1024]{1,0:T(8,128)(2,1)}) conditional(s32[]{:T(128)} %bitcast.23, bf16[96,1024]{1,0:T(8,128)(2,1)} %bitcast.3, bf16[96,1024]{1,0:T(8,128)(2,1)} %bitcast.3, bf16[96,1024]{1,0:T(8,128)(2,1)} %bitcast.3, bf16[96,1024]{1,0:T(8,128)(2,1)} %bitcast.3, bf16[96,1024]{1,0:T(8,128)(2,1)} %bitcast.3, ...), branch_computations={%region_7.8_spmd, %region_8.9_spmd, %region_9.10_spmd, %region_10.... | conditional | bytes 786480 | solution.py:74
  23.4 3.2 %collective-permute-start.11 = (bf16[96,1024]{1,0:T(8,128)(2,1)}, bf16[96,1024]{1,0:T(8,128)(2,1)}, u32[]{:S(2)}, u32[]{:S(2)}) collective-permute-start(bf16[96,1024]{1,0:T(8,128)(2,1)} %param.11), channel_id=1, source_target_pairs={{0,20},{4,16},{8,28},{12,24},{16,4},{20,0},{24,12},{28,8},{1,21},{... | collective-permute-start | bytes 589832 | tf_op jit(solution)/shard_map/cond/branch_4_fun/ppermute | solution.py:69
  26.6 9.7 %collective-permute-done.11 = bf16[96,1024]{1,0:T(8,128)(2,1)} collective-permute-done((bf16[96,1024]{1,0:T(8,128)(2,1)}, bf16[96,1024]{1,0:T(8,128)(2,1)}, u32[]{:S(2)}, u32[]{:S(2)}) %collective-permute-start.11) | collective-permute-done | bytes 196640 | tf_op jit(solution)/shard_map/cond/branch_4_fun/ppermute | solution.py:69
  36.9 7.0 %conditional.6 = (bf16[96,1024]{1,0:T(8,128)(2,1)}) conditional(s32[]{:T(128)} %bitcast.30, bf16[96,1024]{1,0:T(8,128)(2,1)} %bitcast.3, bf16[96,1024]{1,0:T(8,128)(2,1)} %bitcast.3, bf16[96,1024]{1,0:T(8,128)(2,1)} %bitcast.3, bf16[96,1024]{1,0:T(8,128)(2,1)} %bitcast.3, bf16[96,1024]{1,0:T(8,128)(2,1)} %bitcast.3, ...), branch_computations={%region_14.15_spmd, %region_15.16_spmd, %region_16.17_spmd, %regio... | conditional | bytes 786480 | solution.py:74
  37.8 6.1 %collective-permute-done.16 = bf16[96,1024]{1,0:T(8,128)(2,1)} collective-permute-done((bf16[96,1024]{1,0:T(8,128)(2,1)}, bf16[96,1024]{1,0:T(8,128)(2,1)}, u32[]{:S(2)}, u32[]{:S(2)}) %collective-permute-start.16) | collective-permute-done | bytes 196640 | tf_op jit(solution)/shard_map/cond/branch_2_fun/ppermute | solution.py:69
  44.6 11.9 %conditional.7 = (bf16[96,1024]{1,0:T(8,128)(2,1)}) conditional(s32[]{:T(128)} %bitcast.37, bf16[96,1024]{1,0:T(8,128)(2,1)} %bitcast.3, bf16[96,1024]{1,0:T(8,128)(2,1)} %bitcast.3, bf16[96,1024]{1,0:T(8,128)(2,1)} %bitcast.3, bf16[96,1024]{1,0:T(8,128)(2,1)} %bitcast.3, bf16[96,1024]{1,0:T(8,128)(2,1)} %bitcast.3, ...), branch_computations={%region_21.22_spmd, %region_22.23_spmd, %region_23.24_spmd, %regio... | conditional | bytes 786480 | solution.py:74
  44.6 2.8 %collective-permute-start.24 = (bf16[96,1024]{1,0:T(8,128)(2,1)}, bf16[96,1024]{1,0:T(8,128)(2,1)}, u32[]{:S(2)}, u32[]{:S(2)}) collective-permute-start(bf16[96,1024]{1,0:T(8,128)(2,1)} %param.24), channel_id=1, source_target_pairs={{0,16},{4,20},{8,24},{12,28},{16,0},{20,4},{24,8},{28,12},{1,17},{... | collective-permute-start | bytes 589832 | tf_op jit(solution)/shard_map/cond/branch_3_fun/ppermute | solution.py:69
  47.4 9.1 %collective-permute-done.24 = bf16[96,1024]{1,0:T(8,128)(2,1)} collective-permute-done((bf16[96,1024]{1,0:T(8,128)(2,1)}, bf16[96,1024]{1,0:T(8,128)(2,1)}, u32[]{:S(2)}, u32[]{:S(2)}) %collective-permute-start.24) | collective-permute-done | bytes 196640 | tf_op jit(solution)/shard_map/cond/branch_3_fun/ppermute | solution.py:69
  57.1 1.6 %convolution_convert_fusion.1 = bf16[384,3,256]{2,0,1:T(8,128)(2,1)} fusion(bf16[1024,3,256]{2,0,1:T(8,128)(2,1)S(1)} %copy-done.1, bf16[384,1024]{1,0:T(8,128)(2,1)S(1)} %copy-done), kind=kOutput, calls=%fused_computation.1 | convolution fusion | flops 604274688 | bytes 2949120 | tf_op jit(solution)/shard_map/nd,dtf->ntf/dot_general | solution.py:206
  61.3 1.3 %copy.31 = bf16[1024,2,256]{0,2,1:T(8,128)(2,1)} copy(bf16[1024,2,256]{2,0,1:T(8,128)(2,1)S(1)} %slice-done) | data formatting | bytes 2097152
  63.0 1.0 reshape_reshape.6.own_ref
  64.0 1.1 collective-permute-start.41
  66.6 1.1 collective-permute-start.37
  68.7 1.1 collective-permute-start.32
  69.8 1.1 pad_maximum_fusion.3
  70.8 1.2 collective-permute-done.41
  72.0 1.0 pad_maximum_fusion.4
  73.0 3.2 %collective-permute-done.43 = bf16[1,96,1024]{2,1,0:T(8,128)(2,1)S(1)} collective-permute-done((bf16[1,96,1024]{2,1,0:T(8,128)(2,1)}, bf16[1,96,1024]{2,1,0:T(8,128)(2,1)S(1)}, u32[]{:S(2)}, u32[]{:S(2)}) %collective-permute-start.43) | collective-permute-done | bytes 196640 | tf_op jit(solution)/shard_map/ppermute | solution.py:25
  76.2 1.0 pad_maximum_fusion.5
  77.2 3.2 %collective-permute-done.37 = bf16[1,96,1024]{2,1,0:T(8,128)(2,1)S(1)} collective-permute-done((bf16[1,96,1024]{2,1,0:T(8,128)(2,1)}, bf16[1,96,1024]{2,1,0:T(8,128)(2,1)S(1)}, u32[]{:S(2)}, u32[]{:S(2)}) %collective-permute-start.37) | collective-permute-done | bytes 196640 | tf_op jit(solution)/shard_map/ppermute | solution.py:25
  80.4 1.0 pad_maximum_fusion.2
  81.4 3.2 %collective-permute-done.29 = bf16[1,96,1024]{2,1,0:T(8,128)(2,1)S(1)} collective-permute-done((bf16[1,96,1024]{2,1,0:T(8,128)(2,1)}, bf16[1,96,1024]{2,1,0:T(8,128)(2,1)S(1)}, u32[]{:S(2)}, u32[]{:S(2)}) %collective-permute-start.29) | collective-permute-done | bytes 196640 | tf_op jit(solution)/shard_map/ppermute | solution.py:25
  84.6 1.0 pad_maximum_fusion
  85.6 3.2 %collective-permute-done.32 = bf16[1,96,1024]{2,1,0:T(8,128)(2,1)S(1)} collective-permute-done((bf16[1,96,1024]{2,1,0:T(8,128)(2,1)}, bf16[1,96,1024]{2,1,0:T(8,128)(2,1)S(1)}, u32[]{:S(2)}, u32[]{:S(2)}) %collective-permute-start.32) | collective-permute-done | bytes 196640 | tf_op jit(solution)/shard_map/ppermute | solution.py:25
  88.9 1.0 pad_maximum_fusion.1
  90.6 1.0 fusion.1
  91.7 1.0 fusion.2
  92.7 1.0 fusion.3
  93.8 1.1 fusion.4
  94.9 1.1 fusion.5
  96.0 1.0 fusion.6
  97.0 3.9 %convolution_convert_fusion = bf16[2304,512]{1,0:T(8,128)(2,1)} fusion(bf16[2304,1024]{1,0:T(8,128)(2,1)S(1)} %bitcast.109, bf16[1024,512]{0,1:T(8,128)(2,1)S(1)} %bitcast.87), kind=kOutput, calls=%fused_computation | convolution fusion | flops 2417098752 | bytes 8126464 | tf_op jit(solution)/shard_map/dot_general | solution.py:105
  100.9 10.8 %shard_map.73 = bf16[3,128,256]{2,1,0:T(8,128)(2,1)} custom-call(s32[3,11]{1,0:T(4,128)} %pad_convert_fusion.live_ref, s32[4,3]{1,0:T(4,128)} %add_select_fusion.pick_ref, bf16[3,128,256]{2,1,0:T(8,128)(2,1)} %bitcast.105, bf16[3,128,512]{2,1,0:T(8,128)(2,1)} %reshape_reshape.6.own_ref, bf16[6,3,128,512]{3,2,1,0:T(8,128)(2,1)} %bitcast.115), custom_call_target="tpu_custom_call" | custom-call | flops 1107296256 | bytes 3145728 | tf_op jit(solution)/shard_map/pallas_call | solution.py:172
  111.8 1.1 collective-permute-start.45
  113.0 6.3 %collective-permute-done.45 = bf16[1,384,256]{2,1,0:T(8,128)(2,1)S(1)} collective-permute-done((bf16[1,384,256]{2,1,0:T(8,128)(2,1)}, bf16[1,384,256]{2,1,0:T(8,128)(2,1)S(1)}, u32[]{:S(2)}, u32[]{:S(2)}) %collective-permute-start.45) | collective-permute-done | bytes 196640 | tf_op jit(solution)/shard_map/ppermute | solution.py:25
  119.3 1.0 pad_maximum_fusion.6
  120.5 1.5 %collective-permute-done.46 = bf16[2,384,256]{2,1,0:T(8,128)(2,1)S(1)} collective-permute-done((bf16[2,384,256]{2,1,0:T(8,128)(2,1)S(1)}, bf16[2,384,256]{2,1,0:T(8,128)(2,1)S(1)}, u32[]{:S(2)}, u32[]{:S(2)}) %collective-permute-start.46) | collective-permute-done | bytes 393248 | tf_op jit(solution)/shard_map/ppermute | solution.py:25
  122.1 1.5 %fusion.37 = (f32[384]{0:T(512)S(1)}, f32[384,256]{0,1:T(8,128)S(1)}) fusion(bf16[1,256,256]{1,2,0:T(8,128)(2,1)} %bitcast.51, bf16[1,256,256]{1,2,0:T(8,128)(2,1)} %bitcast.50, bf16[1,256,256]{1,2,0:T(8,128)(2,1)S(1)} %bitcast.114, bf16[1,256,256]{1,2,0:T(8,128)(2,1)S(1)} %bitcast.110, bf16[1,384,256]{2,1,0:T(8,128)(2,1)S(1)} %get-tuple-element.100, ...), kind=kOutput, calls=%fused_computation.80 | convolution fusion | flops 203587200 | bytes 1902080 | tf_op jit(solution)/shard_map/srf,sfo->ro/dot_general | solution.py:234
  123.9 1.1 collective-permute-start.48
  125.6 1.9 %collective-permute-done.48 = f32[384,2]{0,1:T(2,128)S(1)} collective-permute-done((f32[384,2]{0,1:T(2,128)S(1)}, f32[384,2]{0,1:T(2,128)S(1)}, u32[]{:S(2)}, u32[]{:S(2)}) %collective-permute-start.48) | collective-permute-done | bytes 3104 | tf_op jit(solution)/shard_map/ppermute | solution.py:25
  (94 shorter events, 13.9 us)
Async XLA Ops:
  0.0 1.1 copy-start
  0.0 12.3 %copy-start.6 = (s32[4,3]{1,0:T(4,128)S(1)}, s32[4,3]{1,0:T(4,128)}, u32[]{:S(2)}) copy-start(s32[4,3]{1,0:T(4,128)} %param.41) | copy-start | bytes 148
  0.0 57.1 %copy-start.1 = (bf16[1024,3,256]{2,0,1:T(8,128)(2,1)S(1)}, bf16[1024,3,256]{2,0,1:T(8,128)(2,1)}, u32[]{:S(2)}) copy-start(bf16[1024,3,256]{2,0,1:T(8,128)(2,1)} %param.36) | copy-start | bytes 4718596
  1.8 64.8 %collective-permute-start.28 = (bf16[96,1024]{1,0:T(8,128)(2,1)}, bf16[96,1024]{1,0:T(8,128)(2,1)}, u32[]{:S(2)}, u32[]{:S(2)}) collective-permute-start(bf16[96,1024]{1,0:T(8,128)(2,1)} %bitcast.3), channel_id=1, source_target_pairs={{0,4},{4,8},{8,12},{12,16},{16,20},{20,24},{24,28},{1,5},{5,9},{9,... | collective-permute-start | bytes 589832 | tf_op jit(solution)/shard_map/ppermute | solution.py:88
  7.4 60.4 %collective-permute-start.31 = (bf16[96,1024]{1,0:T(8,128)(2,1)}, bf16[96,1024]{1,0:T(8,128)(2,1)}, u32[]{:S(2)}, u32[]{:S(2)}) collective-permute-start(bf16[96,1024]{1,0:T(8,128)(2,1)} %bitcast.3), channel_id=1, source_target_pairs={{4,0},{8,4},{12,8},{16,12},{20,16},{24,20},{28,24},{5,1},{9,5},{13... | collective-permute-start | bytes 589832 | tf_op jit(solution)/shard_map/ppermute | solution.py:89
  9.9 48.8 %collective-permute-start.34 = (bf16[256,256]{0,1:T(8,128)(2,1)S(1)}, bf16[256,256]{0,1:T(8,128)(2,1)S(1)}, u32[]{:S(2)}, u32[]{:S(2)}) collective-permute-start(bf16[256,256]{0,1:T(8,128)(2,1)S(1)} %copy.28), channel_id=1, source_target_pairs={{0,1},{1,0},{2,3},{3,2},{4,5},{5,4},{6,7},{7,6},{8,9},{9,8},{10,11... | collective-permute-start | bytes 393224 | tf_op jit(solution)/shard_map/ppermute | solution.py:25
  10.8 53.2 %collective-permute-start.35 = (bf16[256,256]{0,1:T(8,128)(2,1)}, bf16[256,256]{0,1:T(8,128)(2,1)}, u32[]{:S(2)}, u32[]{:S(2)}) collective-permute-start(bf16[256,256]{0,1:T(8,128)(2,1)} %copy.29), channel_id=1, source_target_pairs={{0,2},{1,3},{2,0},{3,1},{4,6},{5,7},{6,4},{7,5},{8,10},{9,11},{10,... | collective-permute-start | bytes 393224 | tf_op jit(solution)/shard_map/ppermute | solution.py:25
  14.5 8.3 %collective-permute-start = (bf16[96,1024]{1,0:T(8,128)(2,1)}, bf16[96,1024]{1,0:T(8,128)(2,1)}, u32[]{:S(2)}, u32[]{:S(2)}) collective-permute-start(bf16[96,1024]{1,0:T(8,128)(2,1)} %param), channel_id=1, source_target_pairs={{0,4},{4,0},{8,12},{12,8},{16,20},{20,16},{24,28},{28,24},{1,5},{5... | collective-permute-start | bytes 589832 | tf_op jit(solution)/shard_map/cond/branch_0_fun/ppermute | solution.py:69
  23.4 12.9 %collective-permute-start.11 = (bf16[96,1024]{1,0:T(8,128)(2,1)}, bf16[96,1024]{1,0:T(8,128)(2,1)}, u32[]{:S(2)}, u32[]{:S(2)}) collective-permute-start(bf16[96,1024]{1,0:T(8,128)(2,1)} %param.11), channel_id=1, source_target_pairs={{0,20},{4,16},{8,28},{12,24},{16,4},{20,0},{24,12},{28,8},{1,21},{... | collective-permute-start | bytes 589832 | tf_op jit(solution)/shard_map/cond/branch_4_fun/ppermute | solution.py:69
  37.0 7.0 %collective-permute-start.16 = (bf16[96,1024]{1,0:T(8,128)(2,1)}, bf16[96,1024]{1,0:T(8,128)(2,1)}, u32[]{:S(2)}, u32[]{:S(2)}) collective-permute-start(bf16[96,1024]{1,0:T(8,128)(2,1)} %param.16), channel_id=1, source_target_pairs={{0,12},{4,8},{8,4},{12,0},{16,28},{20,24},{24,20},{28,16},{1,13},{... | collective-permute-start | bytes 589832 | tf_op jit(solution)/shard_map/cond/branch_2_fun/ppermute | solution.py:69
  44.6 11.9 %collective-permute-start.24 = (bf16[96,1024]{1,0:T(8,128)(2,1)}, bf16[96,1024]{1,0:T(8,128)(2,1)}, u32[]{:S(2)}, u32[]{:S(2)}) collective-permute-start(bf16[96,1024]{1,0:T(8,128)(2,1)} %param.24), channel_id=1, source_target_pairs={{0,16},{4,20},{8,24},{12,28},{16,0},{20,4},{24,8},{28,12},{1,17},{... | collective-permute-start | bytes 589832 | tf_op jit(solution)/shard_map/cond/branch_3_fun/ppermute | solution.py:69
  56.5 9.2 %collective-permute-start.36 = (bf16[256,256]{0,1:T(8,128)(2,1)}, bf16[256,256]{0,1:T(8,128)(2,1)}, u32[]{:S(2)}, u32[]{:S(2)}) collective-permute-start(bf16[256,256]{0,1:T(8,128)(2,1)} %copy.30), channel_id=1, source_target_pairs={{0,3},{1,2},{2,1},{3,0},{4,7},{5,6},{6,5},{7,4},{8,11},{9,10},{10,... | collective-permute-start | bytes 393224 | tf_op jit(solution)/shard_map/ppermute | solution.py:25
  57.1 2.2 %copy-start.7 = (s32[3,7]{1,0:T(4,128)S(1)}, s32[3,7]{1,0:T(4,128)}, u32[]{:S(2)}) copy-start(s32[3,7]{1,0:T(4,128)} %param.40) | copy-start | bytes 256
  58.7 1.1 copy-start.2
  58.7 0.6 copy-start.10
  58.7 9.9 %collective-permute-start.39 = (bf16[1,96,1024]{2,1,0:T(8,128)(2,1)}, bf16[1,96,1024]{2,1,0:T(8,128)(2,1)}, u32[]{:S(2)}, u32[]{:S(2)}) collective-permute-start(bf16[1,96,1024]{2,1,0:T(8,128)(2,1)} %bitcast.25), channel_id=1, source_target_pairs={{0,2},{1,3},{2,0},{3,1},{4,6},{5,7},{6,4},{7,5},{8,10},{9,11},{10,... | collective-permute-start | bytes 589832 | tf_op jit(solution)/shard_map/ppermute | solution.py:25
  59.4 1.8 %slice-start = ((bf16[1024,3,256]{2,0,1:T(8,128)(2,1)}), bf16[1024,2,256]{2,0,1:T(8,128)(2,1)S(1)}, s32[]{:S(2)}) async-start(bf16[1024,3,256]{2,0,1:T(8,128)(2,1)} %param.36), calls=%async_computation | async-start | bytes 2097152 | tf_op jit(solution)/shard_map/slice | solution.py:215
  59.8 2.8 %slice-start.1 = ((bf16[384,3,256]{2,0,1:T(8,128)(2,1)}), bf16[384,2,256]{2,0,1:T(8,128)(2,1)S(1)}, s32[]{:S(2)}) async-start(bf16[384,3,256]{2,0,1:T(8,128)(2,1)} %convolution_convert_fusion.1), calls=%async_computation.1 | async-start | bytes 786432 | tf_op jit(solution)/shard_map/slice | solution.py:210
  64.0 8.0 %collective-permute-start.41 = (bf16[1,96,1024]{2,1,0:T(8,128)(2,1)}, bf16[1,96,1024]{2,1,0:T(8,128)(2,1)S(1)}, u32[]{:S(2)}, u32[]{:S(2)}) collective-permute-start(bf16[1,96,1024]{2,1,0:T(8,128)(2,1)} %bitcast.32), channel_id=1, source_target_pairs={{0,2},{1,3},{2,0},{3,1},{4,6},{5,7},{6,4},{7,5},{8,10},{9,11},{10,... | collective-permute-start | bytes 589832 | tf_op jit(solution)/shard_map/ppermute | solution.py:25
  65.7 10.5 %collective-permute-start.43 = (bf16[1,96,1024]{2,1,0:T(8,128)(2,1)}, bf16[1,96,1024]{2,1,0:T(8,128)(2,1)S(1)}, u32[]{:S(2)}, u32[]{:S(2)}) collective-permute-start(bf16[1,96,1024]{2,1,0:T(8,128)(2,1)} %bitcast.39), channel_id=1, source_target_pairs={{0,2},{1,3},{2,0},{3,1},{4,6},{5,7},{6,4},{7,5},{8,10},{9,11},{10,... | collective-permute-start | bytes 589832 | tf_op jit(solution)/shard_map/ppermute | solution.py:25
  66.6 13.8 %collective-permute-start.37 = (bf16[1,96,1024]{2,1,0:T(8,128)(2,1)}, bf16[1,96,1024]{2,1,0:T(8,128)(2,1)S(1)}, u32[]{:S(2)}, u32[]{:S(2)}) collective-permute-start(bf16[1,96,1024]{2,1,0:T(8,128)(2,1)} %bitcast.18), channel_id=1, source_target_pairs={{0,2},{1,3},{2,0},{3,1},{4,6},{5,7},{6,4},{7,5},{8,10},{9,11},{10,... | collective-permute-start | bytes 589832 | tf_op jit(solution)/shard_map/ppermute | solution.py:25
  67.7 16.9 %collective-permute-start.29 = (bf16[1,96,1024]{2,1,0:T(8,128)(2,1)}, bf16[1,96,1024]{2,1,0:T(8,128)(2,1)S(1)}, u32[]{:S(2)}, u32[]{:S(2)}) collective-permute-start(bf16[1,96,1024]{2,1,0:T(8,128)(2,1)} %bitcast.5), channel_id=1, source_target_pairs={{0,2},{1,3},{2,0},{3,1},{4,6},{5,7},{6,4},{7,5},{8,10},{9,11},{10,... | collective-permute-start | bytes 589832 | tf_op jit(solution)/shard_map/ppermute | solution.py:25
  68.7 20.1 %collective-permute-start.32 = (bf16[1,96,1024]{2,1,0:T(8,128)(2,1)}, bf16[1,96,1024]{2,1,0:T(8,128)(2,1)S(1)}, u32[]{:S(2)}, u32[]{:S(2)}) collective-permute-start(bf16[1,96,1024]{2,1,0:T(8,128)(2,1)} %bitcast.11), channel_id=1, source_target_pairs={{0,2},{1,3},{2,0},{3,1},{4,6},{5,7},{6,4},{7,5},{8,10},{9,11},{10,... | collective-permute-start | bytes 589832 | tf_op jit(solution)/shard_map/ppermute | solution.py:25
  72.0 17.8 %collective-permute-start.40 = (bf16[2,96,1024]{2,1,0:T(8,128)(2,1)S(1)}, bf16[2,96,1024]{2,1,0:T(8,128)(2,1)S(1)}, u32[]{:S(2)}, u32[]{:S(2)}) collective-permute-start(bf16[2,96,1024]{2,1,0:T(8,128)(2,1)S(1)} %pad_maximum_fusion.3), channel_id=1, source_target_pairs={{0,1},{1,0},{2,3},{3,2},{4,5},{5,4},{6,7},{7,6},{8,9},{9,8},{10,11... | collective-permute-start | bytes 1179656 | tf_op jit(solution)/shard_map/ppermute | solution.py:25
  76.2 14.2 %collective-permute-start.42 = (bf16[2,96,1024]{2,1,0:T(8,128)(2,1)S(1)}, bf16[2,96,1024]{2,1,0:T(8,128)(2,1)S(1)}, u32[]{:S(2)}, u32[]{:S(2)}) collective-permute-start(bf16[2,96,1024]{2,1,0:T(8,128)(2,1)S(1)} %pad_maximum_fusion.4), channel_id=1, source_target_pairs={{0,1},{1,0},{2,3},{3,2},{4,5},{5,4},{6,7},{7,6},{8,9},{9,8},{10,11... | collective-permute-start | bytes 1179656 | tf_op jit(solution)/shard_map/ppermute | solution.py:25
  80.4 10.0 %collective-permute-start.44 = (bf16[2,96,1024]{2,1,0:T(8,128)(2,1)S(1)}, bf16[2,96,1024]{2,1,0:T(8,128)(2,1)S(1)}, u32[]{:S(2)}, u32[]{:S(2)}) collective-permute-start(bf16[2,96,1024]{2,1,0:T(8,128)(2,1)S(1)} %pad_maximum_fusion.5), channel_id=1, source_target_pairs={{0,1},{1,0},{2,3},{3,2},{4,5},{5,4},{6,7},{7,6},{8,9},{9,8},{10,11... | collective-permute-start | bytes 1179656 | tf_op jit(solution)/shard_map/ppermute | solution.py:25
  84.6 5.8 %collective-permute-start.38 = (bf16[2,96,1024]{2,1,0:T(8,128)(2,1)S(1)}, bf16[2,96,1024]{2,1,0:T(8,128)(2,1)S(1)}, u32[]{:S(2)}, u32[]{:S(2)}) collective-permute-start(bf16[2,96,1024]{2,1,0:T(8,128)(2,1)S(1)} %pad_maximum_fusion.2), channel_id=1, source_target_pairs={{0,1},{1,0},{2,3},{3,2},{4,5},{5,4},{6,7},{7,6},{8,9},{9,8},{10,11... | collective-permute-start | bytes 1179656 | tf_op jit(solution)/shard_map/ppermute | solution.py:25
  88.8 1.7 %collective-permute-start.30 = (bf16[2,96,1024]{2,1,0:T(8,128)(2,1)S(1)}, bf16[2,96,1024]{2,1,0:T(8,128)(2,1)S(1)}, u32[]{:S(2)}, u32[]{:S(2)}) collective-permute-start(bf16[2,96,1024]{2,1,0:T(8,128)(2,1)S(1)} %pad_maximum_fusion), channel_id=1, source_target_pairs={{0,1},{1,0},{2,3},{3,2},{4,5},{5,4},{6,7},{7,6},{8,9},{9,8},{10,11... | collective-permute-start | bytes 1179656 | tf_op jit(solution)/shard_map/ppermute | solution.py:25
  89.8 1.9 %collective-permute-start.33 = (bf16[2,96,1024]{2,1,0:T(8,128)(2,1)S(1)}, bf16[2,96,1024]{2,1,0:T(8,128)(2,1)S(1)}, u32[]{:S(2)}, u32[]{:S(2)}) collective-permute-start(bf16[2,96,1024]{2,1,0:T(8,128)(2,1)S(1)} %pad_maximum_fusion.1), channel_id=1, source_target_pairs={{0,1},{1,0},{2,3},{3,2},{4,5},{5,4},{6,7},{7,6},{8,9},{9,8},{10,11... | collective-permute-start | bytes 1179656 | tf_op jit(solution)/shard_map/ppermute | solution.py:25
  94.9 2.1 %copy-start.3 = (bf16[1024,2,256]{0,2,1:T(8,128)(2,1)S(1)}, bf16[1024,2,256]{0,2,1:T(8,128)(2,1)}, u32[]{:S(2)}) copy-start(bf16[1024,2,256]{0,2,1:T(8,128)(2,1)} %copy.31) | copy-start | bytes 3145732
  111.8 10.3 %copy-start.4 = (bf16[3,128,256]{2,1,0:T(8,128)(2,1)S(1)}, bf16[3,128,256]{2,1,0:T(8,128)(2,1)}, u32[]{:S(2)}) copy-start(bf16[3,128,256]{2,1,0:T(8,128)(2,1)} %shard_map.73) | copy-start | bytes 589828
  111.8 10.3 %copy-start.5 = (bf16[256,256]{0,1:T(8,128)(2,1)S(1)}, bf16[256,256]{0,1:T(8,128)(2,1)}, u32[]{:S(2)}) copy-start(bf16[256,256]{0,1:T(8,128)(2,1)} %copy.27) | copy-start | bytes 393220
  111.8 10.3 %copy-start.11 = (bf16[256,256]{0,1:T(8,128)(2,1)S(1)}, bf16[256,256]{0,1:T(8,128)(2,1)}, u32[]{:S(2)}) copy-start(bf16[256,256]{0,1:T(8,128)(2,1)} %copy-done.10) | copy-start | bytes 393220
  111.8 7.5 %collective-permute-start.45 = (bf16[1,384,256]{2,1,0:T(8,128)(2,1)}, bf16[1,384,256]{2,1,0:T(8,128)(2,1)S(1)}, u32[]{:S(2)}, u32[]{:S(2)}) collective-permute-start(bf16[1,384,256]{2,1,0:T(8,128)(2,1)} %bitcast.106), channel_id=1, source_target_pairs={{0,2},{1,3},{2,0},{3,1},{4,6},{5,7},{6,4},{7,5},{8,10},{9,11},{10,... | collective-permute-start | bytes 589832 | tf_op jit(solution)/shard_map/ppermute | solution.py:25
  120.2 1.8 %collective-permute-start.46 = (bf16[2,384,256]{2,1,0:T(8,128)(2,1)S(1)}, bf16[2,384,256]{2,1,0:T(8,128)(2,1)S(1)}, u32[]{:S(2)}, u32[]{:S(2)}) collective-permute-start(bf16[2,384,256]{2,1,0:T(8,128)(2,1)S(1)} %pad_maximum_fusion.6), channel_id=1, source_target_pairs={{0,1},{1,0},{2,3},{3,2},{4,5},{5,4},{6,7},{7,6},{8,9},{9,8},{10,11... | collective-permute-start | bytes 1179656 | tf_op jit(solution)/shard_map/ppermute | solution.py:25
  122.1 6.0 %copy-start.8 = (f32[256]{0:T(256)S(1)}, f32[256]{0:T(256)}, u32[]{:S(2)}) copy-start(f32[256]{0:T(256)} %param.39) | copy-start | bytes 3076
  122.1 6.0 %copy-start.9 = (f32[256]{0:T(256)S(1)}, f32[256]{0:T(256)}, u32[]{:S(2)}) copy-start(f32[256]{0:T(256)} %param.38) | copy-start | bytes 3076
  123.7 1.9 %collective-permute-start.47 = (f32[384,2]{0,1:T(2,128)S(1)}, f32[384,2]{0,1:T(2,128)S(1)}, u32[]{:S(2)}, u32[]{:S(2)}) collective-permute-start(f32[384,2]{0,1:T(2,128)S(1)} %get-tuple-element.114), channel_id=1, source_target_pairs={{0,1},{1,0},{2,3},{3,2},{4,5},{5,4},{6,7},{7,6},{8,9},{9,8},{10,11... | collective-permute-start | bytes 9224 | tf_op jit(solution)/shard_map/ppermute | solution.py:25
  123.9 3.6 %collective-permute-start.48 = (f32[384,2]{0,1:T(2,128)S(1)}, f32[384,2]{0,1:T(2,128)S(1)}, u32[]{:S(2)}, u32[]{:S(2)}) collective-permute-start(f32[384,2]{0,1:T(2,128)S(1)} %get-tuple-element.114), channel_id=1, source_target_pairs={{0,2},{1,3},{2,0},{3,1},{4,6},{5,7},{6,4},{7,5},{8,10},{9,11},{10,... | collective-permute-start | bytes 9224 | tf_op jit(solution)/shard_map/ppermute | solution.py:25
  125.0 3.0 %collective-permute-start.49 = (f32[384,2]{0,1:T(2,128)S(1)}, f32[384,2]{0,1:T(2,128)S(1)}, u32[]{:S(2)}, u32[]{:S(2)}) collective-permute-start(f32[384,2]{0,1:T(2,128)S(1)} %get-tuple-element.114), channel_id=1, source_target_pairs={{0,3},{1,2},{2,1},{3,0},{4,7},{5,6},{6,5},{7,4},{8,11},{9,10},{10,... | collective-permute-start | bytes 9224 | tf_op jit(solution)/shard_map/ppermute | solution.py:25

commit v2 on v1

--- a/solution.py
+++ b/solution.py
@@ -12,6 +12,7 @@
 REACH = 3
 LANES = 128
 GATHER_GROUPS = 16
+STATIC_GROUPS = 8
 
 
 NORM_EPS = 1e-05
@@ -88,7 +89,21 @@
     before = lax.ppermute(mine, "node", up)
     after = lax.ppermute(mine, "node", down)
     targets = jnp.bitwise_xor(matchings[:, 0] // blocks_here, my_index)
-    matched = [switched_send(mine, targets[match_pos], groups) for match_pos in range(matches)]
+    if groups <= STATIC_GROUPS:
+        every = jnp.stack(
+            [
+                lax.ppermute(mine, "node", [(i, i ^ shift) for i in range(groups)])
+                for shift in range(1, groups)
+            ]
+        )
+        matched = [
+            lax.dynamic_index_in_dim(
+                every, jnp.clip(targets[match_pos] - 1, 0, groups - 2), 0, keepdims=False
+            )
+            for match_pos in range(matches)
+        ]
+    else:
+        matched = [switched_send(mine, targets[match_pos], groups) for match_pos in range(matches)]
     w_parts, matched[0] = lax.optimization_barrier((w_parts, matched[0]))
     spread = [spread_slots(piece, heads_axis) for piece in [before, after] + matched]
     rows = jnp.stack(

time: 130 us -> 117 us (0.900)
  the two profiles are of different devices: /device:TPU:0 before, /device:TPU:17 now
where the time goes in v2:
time: 117 us; the launch traced here: 116 us
  starting transfers between devices  45.5 us (39%)
  waiting for transfers between devices  25.4 us (22%)
  local copies, waits for them, and re-layouts  15.4 us (13%)
  Pallas kernels  10.9 us (9%)
  other arithmetic  10.5 us (9%)
  matrix products  5.18 us (4%)
  between operations  3.09 us (3%)
    ppermute x20, starting transfers between devices, flip_heads(): return lax.ppermute(array, 'head', [(i, i ^ flip) for i in range(devices)])  31.8 us
    ppermute x20, waiting for transfers between devices, flip_heads(): return lax.ppermute(array, 'head', [(i, i ^ flip) for i in range(devices)])  19.4 us
    pallas_call x1, Pallas kernels, attention(): pl.pallas_call(attention_kernel, out_shape=jax.ShapeDtypeStruct(query.sha...  10.9 us
    unnamed x51, local copies, waits for them, and re-layouts  7.5 us
    ppermute x7, starting transfers between devices, quarter_keys(): lax.ppermute(mine, 'node', [(i, i ^ shift) for i in range(groups)])  7.44 us
    ppermute x7, waiting for transfers between devices, quarter_keys(): lax.ppermute(mine, 'node', [(i, i ^ shift) for i in range(groups)])  6.04 us
    another operation x7, other arithmetic, spread_slots(): other = flip_heads(jnp.stack([slots[k] for k in held]), flip, heads_axis)  4.06 us
    dot_general x1, matrix products, quarter_keys(): jnp.dot(rows, w_kv, preferred_element_type=jnp.float32).astype(jnp.bfloat16)  3.92 us
  transfers between devices with their start and end apart: 29, of which 12 were waited for; matrix products, arithmetic and copies ran while one was open for 17% of the time, Pallas kernels for 0%

profile of v2, /device:TPU:17, one launch (start us, length us, event | category | flops | bytes accessed | tf_op | source)
XLA Modules:
  0.0 116.0 jit_solution(384203298471122077)
XLA Ops:
  0.0 1.1 copy-done
  1.8 1.2 %collective-permute-start.9 = (bf16[96,1024]{1,0:T(8,128)(2,1)}, bf16[96,1024]{1,0:T(8,128)(2,1)}, u32[]{:S(2)}, u32[]{:S(2)}) collective-permute-start(bf16[96,1024]{1,0:T(8,128)(2,1)} %bitcast.3), channel_id=1, source_target_pairs={{0,4},{4,0},{8,12},{12,8},{16,20},{20,16},{24,28},{28,24},{1,5},{5... | collective-permute-start | bytes 589832 | tf_op jit(solution)/shard_map/ppermute | solution.py:95
  3.1 1.3 %collective-permute-start.10 = (bf16[96,1024]{1,0:T(8,128)(2,1)}, bf16[96,1024]{1,0:T(8,128)(2,1)}, u32[]{:S(2)}, u32[]{:S(2)}) collective-permute-start(bf16[96,1024]{1,0:T(8,128)(2,1)} %bitcast.3), channel_id=1, source_target_pairs={{0,8},{4,12},{8,0},{12,4},{16,24},{20,28},{24,16},{28,20},{1,9},{5... | collective-permute-start | bytes 589832 | tf_op jit(solution)/shard_map/ppermute | solution.py:95
  4.5 3.3 %collective-permute-start.13 = (bf16[96,1024]{1,0:T(8,128)(2,1)}, bf16[96,1024]{1,0:T(8,128)(2,1)S(1)}, u32[]{:S(2)}, u32[]{:S(2)}) collective-permute-start(bf16[96,1024]{1,0:T(8,128)(2,1)} %bitcast.3), channel_id=1, source_target_pairs={{0,20},{4,16},{8,28},{12,24},{16,4},{20,0},{24,12},{28,8},{1,21},{... | collective-permute-start | bytes 589832 | tf_op jit(solution)/shard_map/ppermute | solution.py:95
  12.6 1.1 constant_dynamic-slice_fusion.3
  17.1 0.9 bitcast_dynamic-update-slice_fusion.6
  18.0 1.3 %collective-permute-start.15 = (bf16[96,1024]{1,0:T(8,128)(2,1)}, bf16[96,1024]{1,0:T(8,128)(2,1)S(1)}, u32[]{:S(2)}, u32[]{:S(2)}) collective-permute-start(bf16[96,1024]{1,0:T(8,128)(2,1)} %bitcast.3), channel_id=1, source_target_pairs={{0,28},{4,24},{8,20},{12,16},{16,12},{20,8},{24,4},{28,0},{1,29},{... | collective-permute-start | bytes 589832 | tf_op jit(solution)/shard_map/ppermute | solution.py:95
  19.3 0.9 bitcast_dynamic-update-slice_fusion.5
  20.3 3.1 %collective-permute-start = (bf16[96,1024]{1,0:T(8,128)(2,1)}, bf16[96,1024]{1,0:T(8,128)(2,1)}, u32[]{:S(2)}, u32[]{:S(2)}) collective-permute-start(bf16[96,1024]{1,0:T(8,128)(2,1)} %bitcast.3), channel_id=1, source_target_pairs={{0,4},{4,8},{8,12},{12,16},{16,20},{20,24},{24,28},{1,5},{5,9},{9,... | collective-permute-start | bytes 589832 | tf_op jit(solution)/shard_map/ppermute | solution.py:89
  23.5 3.0 %collective-permute-start.3 = (bf16[96,1024]{1,0:T(8,128)(2,1)}, bf16[96,1024]{1,0:T(8,128)(2,1)}, u32[]{:S(2)}, u32[]{:S(2)}) collective-permute-start(bf16[96,1024]{1,0:T(8,128)(2,1)} %bitcast.3), channel_id=1, source_target_pairs={{4,0},{8,4},{12,8},{16,12},{20,16},{24,20},{28,24},{5,1},{9,5},{13... | collective-permute-start | bytes 589832 | tf_op jit(solution)/shard_map/ppermute | solution.py:90
  26.6 7.3 %collective-permute-start.6 = (bf16[256,256]{0,1:T(8,128)(2,1)S(1)}, bf16[256,256]{0,1:T(8,128)(2,1)S(1)}, u32[]{:S(2)}, u32[]{:S(2)}) collective-permute-start(bf16[256,256]{0,1:T(8,128)(2,1)S(1)} %copy-done.9), channel_id=1, source_target_pairs={{0,1},{1,0},{2,3},{3,2},{4,5},{5,4},{6,7},{7,6},{8,9},{9,8},{10,11... | collective-permute-start | bytes 393224 | tf_op jit(solution)/shard_map/ppermute | solution.py:26
  33.9 2.0 %collective-permute-done.14 = bf16[96,1024]{1,0:T(8,128)(2,1)S(1)} collective-permute-done((bf16[96,1024]{1,0:T(8,128)(2,1)}, bf16[96,1024]{1,0:T(8,128)(2,1)S(1)}, u32[]{:S(2)}, u32[]{:S(2)}) %collective-permute-start.14) | collective-permute-done | bytes 196640 | tf_op jit(solution)/shard_map/ppermute | solution.py:95
  35.9 1.2 %collective-permute-start.7 = (bf16[256,256]{0,1:T(8,128)(2,1)S(1)}, bf16[256,256]{0,1:T(8,128)(2,1)S(1)}, u32[]{:S(2)}, u32[]{:S(2)}) collective-permute-start(bf16[256,256]{0,1:T(8,128)(2,1)S(1)} %copy.26), channel_id=1, source_target_pairs={{0,2},{1,3},{2,0},{3,1},{4,6},{5,7},{6,4},{7,5},{8,10},{9,11},{10,... | collective-permute-start | bytes 393224 | tf_op jit(solution)/shard_map/ppermute | solution.py:26
  37.2 4.0 %collective-permute-done.15 = bf16[96,1024]{1,0:T(8,128)(2,1)S(1)} collective-permute-done((bf16[96,1024]{1,0:T(8,128)(2,1)}, bf16[96,1024]{1,0:T(8,128)(2,1)S(1)}, u32[]{:S(2)}, u32[]{:S(2)}) %collective-permute-start.15) | collective-permute-done | bytes 196640 | tf_op jit(solution)/shard_map/ppermute | solution.py:95
  41.2 5.5 %collective-permute-start.8 = (bf16[256,256]{0,1:T(8,128)(2,1)S(1)}, bf16[256,256]{0,1:T(8,128)(2,1)S(1)}, u32[]{:S(2)}, u32[]{:S(2)}) collective-permute-start(bf16[256,256]{0,1:T(8,128)(2,1)S(1)} %copy.27), channel_id=1, source_target_pairs={{0,3},{1,2},{2,1},{3,0},{4,7},{5,6},{6,5},{7,4},{8,11},{9,10},{10,... | collective-permute-start | bytes 393224 | tf_op jit(solution)/shard_map/ppermute | solution.py:26
  46.7 0.9 constant_dynamic-slice_fusion
  47.6 3.3 %collective-permute-done.8 = bf16[256,256]{0,1:T(8,128)(2,1)S(1)} collective-permute-done((bf16[256,256]{0,1:T(8,128)(2,1)S(1)}, bf16[256,256]{0,1:T(8,128)(2,1)S(1)}, u32[]{:S(2)}, u32[]{:S(2)}) %collective-permute-start.8) | collective-permute-done | bytes 131104 | tf_op jit(solution)/shard_map/ppermute | solution.py:26
  52.9 1.5 %copy.28 = bf16[1024,2,256]{0,2,1:T(8,128)(2,1)} copy(bf16[1024,2,256]{2,0,1:T(8,128)(2,1)S(1)} %slice-done) | data formatting | bytes 2097152
  54.8 1.0 reshape_reshape.6.own_ref
  55.9 0.8 collective-permute-start.1
  57.9 0.8 collective-permute-start.18
  59.4 0.8 collective-permute-start.22
  60.2 1.1 pad_maximum_fusion.2
  61.3 0.9 collective-permute-done.1
  62.2 2.1 %collective-permute-start.17 = (bf16[2,96,1024]{2,1,0:T(8,128)(2,1)S(1)}, bf16[2,96,1024]{2,1,0:T(8,128)(2,1)S(1)}, u32[]{:S(2)}, u32[]{:S(2)}) collective-permute-start(bf16[2,96,1024]{2,1,0:T(8,128)(2,1)S(1)} %pad_maximum_fusion.2), channel_id=1, source_target_pairs={{0,1},{1,0},{2,3},{3,2},{4,5},{5,4},{6,7},{7,6},{8,9},{9,8},{10,11... | collective-permute-start | bytes 1179656 | tf_op jit(solution)/shard_map/ppermute | solution.py:26
  64.2 1.0 pad_maximum_fusion
  65.2 1.2 %collective-permute-done.4 = bf16[1,96,1024]{2,1,0:T(8,128)(2,1)S(1)} collective-permute-done((bf16[1,96,1024]{2,1,0:T(8,128)(2,1)}, bf16[1,96,1024]{2,1,0:T(8,128)(2,1)S(1)}, u32[]{:S(2)}, u32[]{:S(2)}) %collective-permute-start.4) | collective-permute-done | bytes 196640 | tf_op jit(solution)/shard_map/ppermute | solution.py:26
  66.4 2.1 %collective-permute-start.2 = (bf16[2,96,1024]{2,1,0:T(8,128)(2,1)S(1)}, bf16[2,96,1024]{2,1,0:T(8,128)(2,1)S(1)}, u32[]{:S(2)}, u32[]{:S(2)}) collective-permute-start(bf16[2,96,1024]{2,1,0:T(8,128)(2,1)S(1)} %pad_maximum_fusion), channel_id=1, source_target_pairs={{0,1},{1,0},{2,3},{3,2},{4,5},{5,4},{6,7},{7,6},{8,9},{9,8},{10,11... | collective-permute-start | bytes 1179656 | tf_op jit(solution)/shard_map/ppermute | solution.py:26
  68.4 1.0 pad_maximum_fusion.1
  69.4 1.2 %collective-permute-done.18 = bf16[1,96,1024]{2,1,0:T(8,128)(2,1)S(1)} collective-permute-done((bf16[1,96,1024]{2,1,0:T(8,128)(2,1)S(1)}, bf16[1,96,1024]{2,1,0:T(8,128)(2,1)S(1)}, u32[]{:S(2)}, u32[]{:S(2)}) %collective-permute-start.18) | collective-permute-done | bytes 196640 | tf_op jit(solution)/shard_map/ppermute | solution.py:26
  70.6 2.1 %collective-permute-start.5 = (bf16[2,96,1024]{2,1,0:T(8,128)(2,1)S(1)}, bf16[2,96,1024]{2,1,0:T(8,128)(2,1)S(1)}, u32[]{:S(2)}, u32[]{:S(2)}) collective-permute-start(bf16[2,96,1024]{2,1,0:T(8,128)(2,1)S(1)} %pad_maximum_fusion.1), channel_id=1, source_target_pairs={{0,1},{1,0},{2,3},{3,2},{4,5},{5,4},{6,7},{7,6},{8,9},{9,8},{10,11... | collective-permute-start | bytes 1179656 | tf_op jit(solution)/shard_map/ppermute | solution.py:26
  72.7 2.1 %collective-permute-done.20 = bf16[1,96,1024]{2,1,0:T(8,128)(2,1)S(1)} collective-permute-done((bf16[1,96,1024]{2,1,0:T(8,128)(2,1)S(1)}, bf16[1,96,1024]{2,1,0:T(8,128)(2,1)S(1)}, u32[]{:S(2)}, u32[]{:S(2)}) %collective-permute-start.20) | collective-permute-done | bytes 196640 | tf_op jit(solution)/shard_map/ppermute | solution.py:26
  74.8 2.1 %collective-permute-start.19 = (bf16[2,96,1024]{2,1,0:T(8,128)(2,1)S(1)}, bf16[2,96,1024]{2,1,0:T(8,128)(2,1)S(1)}, u32[]{:S(2)}, u32[]{:S(2)}) collective-permute-start(bf16[2,96,1024]{2,1,0:T(8,128)(2,1)S(1)} %pad_maximum_fusion.3), channel_id=1, source_target_pairs={{0,1},{1,0},{2,3},{3,2},{4,5},{5,4},{6,7},{7,6},{8,9},{9,8},{10,11... | collective-permute-start | bytes 1179656 | tf_op jit(solution)/shard_map/ppermute | solution.py:26
  76.9 2.1 %collective-permute-done.22 = bf16[1,96,1024]{2,1,0:T(8,128)(2,1)S(1)} collective-permute-done((bf16[1,96,1024]{2,1,0:T(8,128)(2,1)S(1)}, bf16[1,96,1024]{2,1,0:T(8,128)(2,1)S(1)}, u32[]{:S(2)}, u32[]{:S(2)}) %collective-permute-start.22) | collective-permute-done | bytes 196640 | tf_op jit(solution)/shard_map/ppermute | solution.py:26
  79.0 1.2 %collective-permute-start.21 = (bf16[2,96,1024]{2,1,0:T(8,128)(2,1)S(1)}, bf16[2,96,1024]{2,1,0:T(8,128)(2,1)S(1)}, u32[]{:S(2)}, u32[]{:S(2)}) collective-permute-start(bf16[2,96,1024]{2,1,0:T(8,128)(2,1)S(1)} %pad_maximum_fusion.4), channel_id=1, source_target_pairs={{0,1},{1,0},{2,3},{3,2},{4,5},{5,4},{6,7},{7,6},{8,9},{9,8},{10,11... | collective-permute-start | bytes 1179656 | tf_op jit(solution)/shard_map/ppermute | solution.py:26
  80.4 1.0 fusion.1
  81.5 1.0 fusion.2
  82.5 1.1 fusion.3
  84.0 1.1 copy-done.6
  85.1 3.9 %convolution_convert_fusion = bf16[2304,512]{1,0:T(8,128)(2,1)} fusion(bf16[2304,1024]{1,0:T(8,128)(2,1)S(1)} %bitcast.123, bf16[1024,512]{0,1:T(8,128)(2,1)S(1)} %bitcast.101), kind=kOutput, calls=%fused_computation | convolution fusion | flops 2417098752 | bytes 8126464 | tf_op jit(solution)/shard_map/dot_general | solution.py:120
  89.0 10.9 %shard_map.73 = bf16[3,128,256]{2,1,0:T(8,128)(2,1)} custom-call(s32[3,11]{1,0:T(4,128)} %pad_convert_fusion.live_ref, s32[4,3]{1,0:T(4,128)} %add_select_fusion.pick_ref, bf16[3,128,256]{2,1,0:T(8,128)(2,1)} %bitcast.119, bf16[3,128,512]{2,1,0:T(8,128)(2,1)} %reshape_reshape.6.own_ref, bf16[6,3,128,512]{3,2,1,0:T(8,128)(2,1)} %bitcast.131), custom_call_target="tpu_custom_call" | custom-call | flops 1107296256 | bytes 3145728 | tf_op jit(solution)/shard_map/pallas_call | solution.py:187
  99.9 0.9 collective-permute-start.24
  100.8 5.4 %collective-permute-done.24 = bf16[1,384,256]{2,1,0:T(8,128)(2,1)S(1)} collective-permute-done((bf16[1,384,256]{2,1,0:T(8,128)(2,1)}, bf16[1,384,256]{2,1,0:T(8,128)(2,1)S(1)}, u32[]{:S(2)}, u32[]{:S(2)}) %collective-permute-start.24) | collective-permute-done | bytes 196640 | tf_op jit(solution)/shard_map/ppermute | solution.py:26
  106.1 1.0 pad_maximum_fusion.6
  107.1 1.4 %collective-permute-start.25 = (bf16[2,384,256]{2,1,0:T(8,128)(2,1)S(1)}, bf16[2,384,256]{2,1,0:T(8,128)(2,1)S(1)}, u32[]{:S(2)}, u32[]{:S(2)}) collective-permute-start(bf16[2,384,256]{2,1,0:T(8,128)(2,1)S(1)} %pad_maximum_fusion.6), channel_id=1, source_target_pairs={{0,1},{1,0},{2,3},{3,2},{4,5},{5,4},{6,7},{7,6},{8,9},{9,8},{10,11... | collective-permute-start | bytes 1179656 | tf_op jit(solution)/shard_map/ppermute | solution.py:26
  108.7 1.2 collective-permute-done.25
  111.9 1.0 collective-permute-start.28
  113.5 1.4 %collective-permute-done.28 = f32[384,2]{0,1:T(2,128)S(1)} collective-permute-done((f32[384,2]{0,1:T(2,128)S(1)}, f32[384,2]{0,1:T(2,128)S(1)}, u32[]{:S(2)}, u32[]{:S(2)}) %collective-permute-start.28) | collective-permute-done | bytes 3104 | tf_op jit(solution)/shard_map/ppermute | solution.py:26
  (120 shorter events, 15.1 us)
Async XLA Ops:
  0.0 15.5 %copy-start.1 = (bf16[1024,3,256]{2,0,1:T(8,128)(2,1)S(1)}, bf16[1024,3,256]{2,0,1:T(8,128)(2,1)}, u32[]{:S(2)}) copy-start(bf16[1024,3,256]{2,0,1:T(8,128)(2,1)} %param.8) | copy-start | bytes 4718596
  1.8 15.1 %collective-permute-start.9 = (bf16[96,1024]{1,0:T(8,128)(2,1)}, bf16[96,1024]{1,0:T(8,128)(2,1)}, u32[]{:S(2)}, u32[]{:S(2)}) collective-permute-start(bf16[96,1024]{1,0:T(8,128)(2,1)} %bitcast.3), channel_id=1, source_target_pairs={{0,4},{4,0},{8,12},{12,8},{16,20},{20,16},{24,28},{28,24},{1,5},{5... | collective-permute-start | bytes 589832 | tf_op jit(solution)/shard_map/ppermute | solution.py:95
  3.1 14.9 %collective-permute-start.10 = (bf16[96,1024]{1,0:T(8,128)(2,1)}, bf16[96,1024]{1,0:T(8,128)(2,1)}, u32[]{:S(2)}, u32[]{:S(2)}) collective-permute-start(bf16[96,1024]{1,0:T(8,128)(2,1)} %bitcast.3), channel_id=1, source_target_pairs={{0,8},{4,12},{8,0},{12,4},{16,24},{20,28},{24,16},{28,20},{1,9},{5... | collective-permute-start | bytes 589832 | tf_op jit(solution)/shard_map/ppermute | solution.py:95
  4.4 15.9 %collective-permute-start.11 = (bf16[96,1024]{1,0:T(8,128)(2,1)}, bf16[96,1024]{1,0:T(8,128)(2,1)S(1)}, u32[]{:S(2)}, u32[]{:S(2)}) collective-permute-start(bf16[96,1024]{1,0:T(8,128)(2,1)} %bitcast.3), channel_id=1, source_target_pairs={{0,12},{4,8},{8,4},{12,0},{16,28},{20,24},{24,20},{28,16},{1,13},{... | collective-permute-start | bytes 589832 | tf_op jit(solution)/shard_map/ppermute | solution.py:95
  4.5 19.0 %collective-permute-start.12 = (bf16[96,1024]{1,0:T(8,128)(2,1)}, bf16[96,1024]{1,0:T(8,128)(2,1)S(1)}, u32[]{:S(2)}, u32[]{:S(2)}) collective-permute-start(bf16[96,1024]{1,0:T(8,128)(2,1)} %bitcast.3), channel_id=1, source_target_pairs={{0,16},{4,20},{8,24},{12,28},{16,0},{20,4},{24,8},{28,12},{1,17},{... | collective-permute-start | bytes 589832 | tf_op jit(solution)/shard_map/ppermute | solution.py:95
  4.5 22.1 %collective-permute-start.13 = (bf16[96,1024]{1,0:T(8,128)(2,1)}, bf16[96,1024]{1,0:T(8,128)(2,1)S(1)}, u32[]{:S(2)}, u32[]{:S(2)}) collective-permute-start(bf16[96,1024]{1,0:T(8,128)(2,1)} %bitcast.3), channel_id=1, source_target_pairs={{0,20},{4,16},{8,28},{12,24},{16,4},{20,0},{24,12},{28,8},{1,21},{... | collective-permute-start | bytes 589832 | tf_op jit(solution)/shard_map/ppermute | solution.py:95
  16.3 35.3 %copy-start.5 = (bf16[384,3,256]{2,0,1:T(8,128)(2,1)}, bf16[384,3,256]{2,0,1:T(8,128)(2,1)S(1)}, u32[]{:S(2)}) copy-start(bf16[384,3,256]{2,0,1:T(8,128)(2,1)S(1)} %convolution_convert_fusion.1) | copy-start | bytes 1769476
  16.3 10.3 %copy-start.9 = (bf16[256,256]{0,1:T(8,128)(2,1)S(1)}, bf16[256,256]{0,1:T(8,128)(2,1)}, u32[]{:S(2)}) copy-start(bf16[256,256]{0,1:T(8,128)(2,1)} %copy.25) | copy-start | bytes 393220
  16.9 19.1 %collective-permute-start.14 = (bf16[96,1024]{1,0:T(8,128)(2,1)}, bf16[96,1024]{1,0:T(8,128)(2,1)S(1)}, u32[]{:S(2)}, u32[]{:S(2)}) collective-permute-start(bf16[96,1024]{1,0:T(8,128)(2,1)} %bitcast.3), channel_id=1, source_target_pairs={{0,24},{4,28},{8,16},{12,20},{16,8},{20,12},{24,0},{28,4},{1,25},{... | collective-permute-start | bytes 589832 | tf_op jit(solution)/shard_map/ppermute | solution.py:95
  18.0 23.1 %collective-permute-start.15 = (bf16[96,1024]{1,0:T(8,128)(2,1)}, bf16[96,1024]{1,0:T(8,128)(2,1)S(1)}, u32[]{:S(2)}, u32[]{:S(2)}) collective-permute-start(bf16[96,1024]{1,0:T(8,128)(2,1)} %bitcast.3), channel_id=1, source_target_pairs={{0,28},{4,24},{8,20},{12,16},{16,12},{20,8},{24,4},{28,0},{1,29},{... | collective-permute-start | bytes 589832 | tf_op jit(solution)/shard_map/ppermute | solution.py:95
  20.3 35.6 %collective-permute-start = (bf16[96,1024]{1,0:T(8,128)(2,1)}, bf16[96,1024]{1,0:T(8,128)(2,1)}, u32[]{:S(2)}, u32[]{:S(2)}) collective-permute-start(bf16[96,1024]{1,0:T(8,128)(2,1)} %bitcast.3), channel_id=1, source_target_pairs={{0,4},{4,8},{8,12},{12,16},{16,20},{20,24},{24,28},{1,5},{5,9},{9,... | collective-permute-start | bytes 589832 | tf_op jit(solution)/shard_map/ppermute | solution.py:89
  23.4 28.1 %copy-start.11 = (s32[3,7]{1,0:T(4,128)S(1)}, s32[3,7]{1,0:T(4,128)}, u32[]{:S(2)}) copy-start(s32[3,7]{1,0:T(4,128)} %param.12) | copy-start | bytes 256
  23.5 33.8 %collective-permute-start.3 = (bf16[96,1024]{1,0:T(8,128)(2,1)}, bf16[96,1024]{1,0:T(8,128)(2,1)}, u32[]{:S(2)}, u32[]{:S(2)}) collective-permute-start(bf16[96,1024]{1,0:T(8,128)(2,1)} %bitcast.3), channel_id=1, source_target_pairs={{4,0},{8,4},{12,8},{16,12},{20,16},{24,20},{28,24},{5,1},{9,5},{13... | collective-permute-start | bytes 589832 | tf_op jit(solution)/shard_map/ppermute | solution.py:90
  26.6 21.0 %collective-permute-start.6 = (bf16[256,256]{0,1:T(8,128)(2,1)S(1)}, bf16[256,256]{0,1:T(8,128)(2,1)S(1)}, u32[]{:S(2)}, u32[]{:S(2)}) collective-permute-start(bf16[256,256]{0,1:T(8,128)(2,1)S(1)} %copy-done.9), channel_id=1, source_target_pairs={{0,1},{1,0},{2,3},{3,2},{4,5},{5,4},{6,7},{7,6},{8,9},{9,8},{10,11... | collective-permute-start | bytes 393224 | tf_op jit(solution)/shard_map/ppermute | solution.py:26
  35.9 11.6 %collective-permute-start.7 = (bf16[256,256]{0,1:T(8,128)(2,1)S(1)}, bf16[256,256]{0,1:T(8,128)(2,1)S(1)}, u32[]{:S(2)}, u32[]{:S(2)}) collective-permute-start(bf16[256,256]{0,1:T(8,128)(2,1)S(1)} %copy.26), channel_id=1, source_target_pairs={{0,2},{1,3},{2,0},{3,1},{4,6},{5,7},{6,4},{7,5},{8,10},{9,11},{10,... | collective-permute-start | bytes 393224 | tf_op jit(solution)/shard_map/ppermute | solution.py:26
  41.2 9.7 %collective-permute-start.8 = (bf16[256,256]{0,1:T(8,128)(2,1)S(1)}, bf16[256,256]{0,1:T(8,128)(2,1)S(1)}, u32[]{:S(2)}, u32[]{:S(2)}) collective-permute-start(bf16[256,256]{0,1:T(8,128)(2,1)S(1)} %copy.27), channel_id=1, source_target_pairs={{0,3},{1,2},{2,1},{3,0},{4,7},{5,6},{6,5},{7,4},{8,11},{9,10},{10,... | collective-permute-start | bytes 393224 | tf_op jit(solution)/shard_map/ppermute | solution.py:26
  47.6 3.3 %copy-start.14 = (bf16[256,256]{0,1:T(8,128)(2,1)}, bf16[256,256]{0,1:T(8,128)(2,1)S(1)}, u32[]{:S(2)}) copy-start(bf16[256,256]{0,1:T(8,128)(2,1)S(1)} %collective-permute-done.6) | copy-start | bytes 393220
  47.6 3.3 %copy-start.16 = (bf16[256,256]{0,1:T(8,128)(2,1)}, bf16[256,256]{0,1:T(8,128)(2,1)S(1)}, u32[]{:S(2)}) copy-start(bf16[256,256]{0,1:T(8,128)(2,1)S(1)} %collective-permute-done.7) | copy-start | bytes 393220
  50.9 8.5 %collective-permute-start.16 = (bf16[1,96,1024]{2,1,0:T(8,128)(2,1)}, bf16[1,96,1024]{2,1,0:T(8,128)(2,1)}, u32[]{:S(2)}, u32[]{:S(2)}) collective-permute-start(bf16[1,96,1024]{2,1,0:T(8,128)(2,1)} %bitcast.26), channel_id=1, source_target_pairs={{0,2},{1,3},{2,0},{3,1},{4,6},{5,7},{6,4},{7,5},{8,10},{9,11},{10,... | collective-permute-start | bytes 589832 | tf_op jit(solution)/shard_map/ppermute | solution.py:26
  51.6 1.3 %slice-start = ((bf16[1024,3,256]{2,0,1:T(8,128)(2,1)}), bf16[1024,2,256]{2,0,1:T(8,128)(2,1)S(1)}, s32[]{:S(2)}) async-start(bf16[1024,3,256]{2,0,1:T(8,128)(2,1)} %param.8), calls=%async_computation | async-start | bytes 2097152 | tf_op jit(solution)/shard_map/slice | solution.py:230
  52.9 1.5 %slice-start.1 = ((bf16[384,3,256]{2,0,1:T(8,128)(2,1)}), bf16[384,2,256]{2,0,1:T(8,128)(2,1)S(1)}, s32[]{:S(2)}) async-start(bf16[384,3,256]{2,0,1:T(8,128)(2,1)} %copy-done.5), calls=%async_computation.1 | async-start | bytes 786432 | tf_op jit(solution)/shard_map/slice | solution.py:225
  52.9 5.0 %copy-start.4 = (bf16[1,96,1024]{2,1,0:T(8,128)(2,1)S(1)}, bf16[1,96,1024]{2,1,0:T(8,128)(2,1)}, u32[]{:S(2)}) copy-start(bf16[1,96,1024]{2,1,0:T(8,128)(2,1)} %get-tuple-element.19) | copy-start | bytes 589828
  52.9 5.8 %copy-start.3 = (bf16[1,96,1024]{2,1,0:T(8,128)(2,1)S(1)}, bf16[1,96,1024]{2,1,0:T(8,128)(2,1)}, u32[]{:S(2)}) copy-start(bf16[1,96,1024]{2,1,0:T(8,128)(2,1)} %get-tuple-element.18) | copy-start | bytes 589828
  52.9 6.5 %copy-start.2 = (bf16[1,96,1024]{2,1,0:T(8,128)(2,1)S(1)}, bf16[1,96,1024]{2,1,0:T(8,128)(2,1)}, u32[]{:S(2)}) copy-start(bf16[1,96,1024]{2,1,0:T(8,128)(2,1)} %get-tuple-element.17) | copy-start | bytes 589828
  55.9 6.3 %collective-permute-start.1 = (bf16[1,96,1024]{2,1,0:T(8,128)(2,1)}, bf16[1,96,1024]{2,1,0:T(8,128)(2,1)S(1)}, u32[]{:S(2)}, u32[]{:S(2)}) collective-permute-start(bf16[1,96,1024]{2,1,0:T(8,128)(2,1)} %bitcast.5), channel_id=1, source_target_pairs={{0,2},{1,3},{2,0},{3,1},{4,6},{5,7},{6,4},{7,5},{8,10},{9,11},{10,... | collective-permute-start | bytes 589832 | tf_op jit(solution)/shard_map/ppermute | solution.py:26
  57.3 9.1 %collective-permute-start.4 = (bf16[1,96,1024]{2,1,0:T(8,128)(2,1)}, bf16[1,96,1024]{2,1,0:T(8,128)(2,1)S(1)}, u32[]{:S(2)}, u32[]{:S(2)}) collective-permute-start(bf16[1,96,1024]{2,1,0:T(8,128)(2,1)} %bitcast.11), channel_id=1, source_target_pairs={{0,2},{1,3},{2,0},{3,1},{4,6},{5,7},{6,4},{7,5},{8,10},{9,11},{10,... | collective-permute-start | bytes 589832 | tf_op jit(solution)/shard_map/ppermute | solution.py:26
  57.9 12.7 %collective-permute-start.18 = (bf16[1,96,1024]{2,1,0:T(8,128)(2,1)S(1)}, bf16[1,96,1024]{2,1,0:T(8,128)(2,1)S(1)}, u32[]{:S(2)}, u32[]{:S(2)}) collective-permute-start(bf16[1,96,1024]{2,1,0:T(8,128)(2,1)S(1)} %copy-done.4), channel_id=1, source_target_pairs={{0,2},{1,3},{2,0},{3,1},{4,6},{5,7},{6,4},{7,5},{8,10},{9,11},{10,... | collective-permute-start | bytes 589832 | tf_op jit(solution)/shard_map/ppermute | solution.py:26
  58.8 16.0 %collective-permute-start.20 = (bf16[1,96,1024]{2,1,0:T(8,128)(2,1)S(1)}, bf16[1,96,1024]{2,1,0:T(8,128)(2,1)S(1)}, u32[]{:S(2)}, u32[]{:S(2)}) collective-permute-start(bf16[1,96,1024]{2,1,0:T(8,128)(2,1)S(1)} %copy-done.3), channel_id=1, source_target_pairs={{0,2},{1,3},{2,0},{3,1},{4,6},{5,7},{6,4},{7,5},{8,10},{9,11},{10,... | collective-permute-start | bytes 589832 | tf_op jit(solution)/shard_map/ppermute | solution.py:26
  59.4 19.6 %collective-permute-start.22 = (bf16[1,96,1024]{2,1,0:T(8,128)(2,1)S(1)}, bf16[1,96,1024]{2,1,0:T(8,128)(2,1)S(1)}, u32[]{:S(2)}, u32[]{:S(2)}) collective-permute-start(bf16[1,96,1024]{2,1,0:T(8,128)(2,1)S(1)} %copy-done.2), channel_id=1, source_target_pairs={{0,2},{1,3},{2,0},{3,1},{4,6},{5,7},{6,4},{7,5},{8,10},{9,11},{10,... | collective-permute-start | bytes 589832 | tf_op jit(solution)/shard_map/ppermute | solution.py:26
  62.2 20.3 %collective-permute-start.17 = (bf16[2,96,1024]{2,1,0:T(8,128)(2,1)S(1)}, bf16[2,96,1024]{2,1,0:T(8,128)(2,1)S(1)}, u32[]{:S(2)}, u32[]{:S(2)}) collective-permute-start(bf16[2,96,1024]{2,1,0:T(8,128)(2,1)S(1)} %pad_maximum_fusion.2), channel_id=1, source_target_pairs={{0,1},{1,0},{2,3},{3,2},{4,5},{5,4},{6,7},{7,6},{8,9},{9,8},{10,11... | collective-permute-start | bytes 1179656 | tf_op jit(solution)/shard_map/ppermute | solution.py:26
  66.4 13.9 %collective-permute-start.2 = (bf16[2,96,1024]{2,1,0:T(8,128)(2,1)S(1)}, bf16[2,96,1024]{2,1,0:T(8,128)(2,1)S(1)}, u32[]{:S(2)}, u32[]{:S(2)}) collective-permute-start(bf16[2,96,1024]{2,1,0:T(8,128)(2,1)S(1)} %pad_maximum_fusion), channel_id=1, source_target_pairs={{0,1},{1,0},{2,3},{3,2},{4,5},{5,4},{6,7},{7,6},{8,9},{9,8},{10,11... | collective-permute-start | bytes 1179656 | tf_op jit(solution)/shard_map/ppermute | solution.py:26
  70.6 10.8 %collective-permute-start.5 = (bf16[2,96,1024]{2,1,0:T(8,128)(2,1)S(1)}, bf16[2,96,1024]{2,1,0:T(8,128)(2,1)S(1)}, u32[]{:S(2)}, u32[]{:S(2)}) collective-permute-start(bf16[2,96,1024]{2,1,0:T(8,128)(2,1)S(1)} %pad_maximum_fusion.1), channel_id=1, source_target_pairs={{0,1},{1,0},{2,3},{3,2},{4,5},{5,4},{6,7},{7,6},{8,9},{9,8},{10,11... | collective-permute-start | bytes 1179656 | tf_op jit(solution)/shard_map/ppermute | solution.py:26
  74.8 8.8 %collective-permute-start.19 = (bf16[2,96,1024]{2,1,0:T(8,128)(2,1)S(1)}, bf16[2,96,1024]{2,1,0:T(8,128)(2,1)S(1)}, u32[]{:S(2)}, u32[]{:S(2)}) collective-permute-start(bf16[2,96,1024]{2,1,0:T(8,128)(2,1)S(1)} %pad_maximum_fusion.3), channel_id=1, source_target_pairs={{0,1},{1,0},{2,3},{3,2},{4,5},{5,4},{6,7},{7,6},{8,9},{9,8},{10,11... | collective-permute-start | bytes 1179656 | tf_op jit(solution)/shard_map/ppermute | solution.py:26
  79.0 4.7 %collective-permute-start.21 = (bf16[2,96,1024]{2,1,0:T(8,128)(2,1)S(1)}, bf16[2,96,1024]{2,1,0:T(8,128)(2,1)S(1)}, u32[]{:S(2)}, u32[]{:S(2)}) collective-permute-start(bf16[2,96,1024]{2,1,0:T(8,128)(2,1)S(1)} %pad_maximum_fusion.4), channel_id=1, source_target_pairs={{0,1},{1,0},{2,3},{3,2},{4,5},{5,4},{6,7},{7,6},{8,9},{9,8},{10,11... | collective-permute-start | bytes 1179656 | tf_op jit(solution)/shard_map/ppermute | solution.py:26
  80.3 3.6 %collective-permute-start.23 = (bf16[2,96,1024]{2,1,0:T(8,128)(2,1)S(1)}, bf16[2,96,1024]{2,1,0:T(8,128)(2,1)S(1)}, u32[]{:S(2)}, u32[]{:S(2)}) collective-permute-start(bf16[2,96,1024]{2,1,0:T(8,128)(2,1)S(1)} %pad_maximum_fusion.5), channel_id=1, source_target_pairs={{0,1},{1,0},{2,3},{3,2},{4,5},{5,4},{6,7},{7,6},{8,9},{9,8},{10,11... | collective-permute-start | bytes 1179656 | tf_op jit(solution)/shard_map/ppermute | solution.py:26
  83.9 1.2 %copy-start.6 = (bf16[1024,2,256]{0,2,1:T(8,128)(2,1)S(1)}, bf16[1024,2,256]{0,2,1:T(8,128)(2,1)}, u32[]{:S(2)}) copy-start(bf16[1024,2,256]{0,2,1:T(8,128)(2,1)} %copy.28) | copy-start | bytes 3145732
  99.9 10.0 %copy-start.7 = (bf16[3,128,256]{2,1,0:T(8,128)(2,1)S(1)}, bf16[3,128,256]{2,1,0:T(8,128)(2,1)}, u32[]{:S(2)}) copy-start(bf16[3,128,256]{2,1,0:T(8,128)(2,1)} %shard_map.73) | copy-start | bytes 589828
  99.9 10.0 %copy-start.8 = (bf16[256,256]{0,1:T(8,128)(2,1)S(1)}, bf16[256,256]{0,1:T(8,128)(2,1)}, u32[]{:S(2)}) copy-start(bf16[256,256]{0,1:T(8,128)(2,1)} %copy.24) | copy-start | bytes 393220
  99.9 10.1 %copy-start.15 = (bf16[256,256]{0,1:T(8,128)(2,1)S(1)}, bf16[256,256]{0,1:T(8,128)(2,1)}, u32[]{:S(2)}) copy-start(bf16[256,256]{0,1:T(8,128)(2,1)} %copy-done.14) | copy-start | bytes 393220
  99.9 10.1 %copy-start.17 = (bf16[256,256]{0,1:T(8,128)(2,1)S(1)}, bf16[256,256]{0,1:T(8,128)(2,1)}, u32[]{:S(2)}) copy-start(bf16[256,256]{0,1:T(8,128)(2,1)} %copy-done.16) | copy-start | bytes 393220
  99.9 10.1 %copy-start.19 = (bf16[256,256]{0,1:T(8,128)(2,1)S(1)}, bf16[256,256]{0,1:T(8,128)(2,1)}, u32[]{:S(2)}) copy-start(bf16[256,256]{0,1:T(8,128)(2,1)} %copy-done.18) | copy-start | bytes 393220
  99.9 6.3 %collective-permute-start.24 = (bf16[1,384,256]{2,1,0:T(8,128)(2,1)}, bf16[1,384,256]{2,1,0:T(8,128)(2,1)S(1)}, u32[]{:S(2)}, u32[]{:S(2)}) collective-permute-start(bf16[1,384,256]{2,1,0:T(8,128)(2,1)} %bitcast.120), channel_id=1, source_target_pairs={{0,2},{1,3},{2,0},{3,1},{4,6},{5,7},{6,4},{7,5},{8,10},{9,11},{10,... | collective-permute-start | bytes 589832 | tf_op jit(solution)/shard_map/ppermute | solution.py:26
  107.1 2.8 %collective-permute-start.25 = (bf16[2,384,256]{2,1,0:T(8,128)(2,1)S(1)}, bf16[2,384,256]{2,1,0:T(8,128)(2,1)S(1)}, u32[]{:S(2)}, u32[]{:S(2)}) collective-permute-start(bf16[2,384,256]{2,1,0:T(8,128)(2,1)S(1)} %pad_maximum_fusion.6), channel_id=1, source_target_pairs={{0,1},{1,0},{2,3},{3,2},{4,5},{5,4},{6,7},{7,6},{8,9},{9,8},{10,11... | collective-permute-start | bytes 1179656 | tf_op jit(solution)/shard_map/ppermute | solution.py:26
  110.0 5.1 %copy-start.12 = (f32[256]{0:T(256)S(1)}, f32[256]{0:T(256)}, u32[]{:S(2)}) copy-start(f32[256]{0:T(256)} %param.11) | copy-start | bytes 3076
  110.0 5.1 %copy-start.13 = (f32[256]{0:T(256)S(1)}, f32[256]{0:T(256)}, u32[]{:S(2)}) copy-start(f32[256]{0:T(256)} %param.10) | copy-start | bytes 3076
  110.6 2.2 %collective-permute-start.26 = (f32[384,2]{0,1:T(2,128)S(1)}, f32[384,2]{0,1:T(2,128)S(1)}, u32[]{:S(2)}, u32[]{:S(2)}) collective-permute-start(f32[384,2]{0,1:T(2,128)S(1)} %get-tuple-element.40), channel_id=1, source_target_pairs={{0,1},{1,0},{2,3},{3,2},{4,5},{5,4},{6,7},{7,6},{8,9},{9,8},{10,11... | collective-permute-start | bytes 9224 | tf_op jit(solution)/shard_map/ppermute | solution.py:26
  111.0 2.4 %collective-permute-start.27 = (f32[384,2]{0,1:T(2,128)S(1)}, f32[384,2]{0,1:T(2,128)S(1)}, u32[]{:S(2)}, u32[]{:S(2)}) collective-permute-start(f32[384,2]{0,1:T(2,128)S(1)} %get-tuple-element.40), channel_id=1, source_target_pairs={{0,2},{1,3},{2,0},{3,1},{4,6},{5,7},{6,4},{7,5},{8,10},{9,11},{10,... | collective-permute-start | bytes 9224 | tf_op jit(solution)/shard_map/ppermute | solution.py:26
  111.9 3.1 %collective-permute-start.28 = (f32[384,2]{0,1:T(2,128)S(1)}, f32[384,2]{0,1:T(2,128)S(1)}, u32[]{:S(2)}, u32[]{:S(2)}) collective-permute-start(f32[384,2]{0,1:T(2,128)S(1)} %get-tuple-element.40), channel_id=1, source_target_pairs={{0,3},{1,2},{2,1},{3,0},{4,7},{5,6},{6,5},{7,4},{8,11},{9,10},{10,... | collective-permute-start | bytes 9224 | tf_op jit(solution)/shard_map/ppermute | solution.py:26
  (3 other events, 2.6 us)

commit v3 on v2

--- a/solution.py
+++ b/solution.py
@@ -35,6 +35,11 @@
         for pos, k in enumerate(held):
             slots[k ^ flip] = other[pos]
     return slots
+
+
+def spread_stack(piece, heads_axis):
+    slots = spread_slots(piece, heads_axis)
+    return jnp.stack([slots[k] for k in range(heads_axis)])
 
 
 def keep_same(current):
@@ -96,29 +101,51 @@
                 for shift in range(1, groups)
             ]
         )
-        matched = [
+        used = [jnp.any(targets == shift) for shift in range(1, groups)]
+        every = jnp.stack(
+            [
+                lax.cond(
+                    used[pos],
+                    lambda piece: spread_stack(piece, heads_axis),
+                    lambda piece: idle_stack(piece, heads_axis),
+                    every[pos],
+                )
+                for pos in range(groups - 1)
+            ]
+        )
+        spread_matched = [
             lax.dynamic_index_in_dim(
                 every, jnp.clip(targets[match_pos] - 1, 0, groups - 2), 0, keepdims=False
             )
             for match_pos in range(matches)
         ]
+        w_parts, spread_matched[0] = lax.optimization_barrier((w_parts, spread_matched[0]))
+        spread = [spread_stack(piece, heads_axis) for piece in [before, after]] + spread_matched
+        return kv_of_spread(spread, w_kv, blocks_here, sub_rows), w_parts
     else:
         matched = [switched_send(mine, targets[match_pos], groups) for match_pos in range(matches)]
     w_parts, matched[0] = lax.optimization_barrier((w_parts, matched[0]))
-    spread = [spread_slots(piece, heads_axis) for piece in [before, after] + matched]
+    spread = [spread_stack(piece, heads_axis) for piece in [before, after] + matched]
+    return kv_of_spread(spread, w_kv, blocks_here, sub_rows), w_parts
+
+
+def idle_stack(piece, heads_axis):
+    return jnp.zeros((heads_axis,) + piece.shape, piece.dtype)
+
+
+def kv_of_spread(spread, w_kv, blocks_here, sub_rows):
+    heads_axis, _, model_width = spread[0].shape
     rows = jnp.stack(
         [
-            jnp.stack(
-                [one[k].reshape(blocks_here, sub_rows, model_width) for k in range(heads_axis)],
-                axis=1,
-            )
+            jnp.transpose(one.reshape(heads_axis, blocks_here, sub_rows, model_width), (1, 0, 2, 3))
             for one in spread
         ]
     )
     count = len(spread)
+    total_rows = blocks_here * heads_axis * sub_rows
     rows = rows.reshape(count * total_rows, model_width)
     partner_kv = jnp.dot(rows, w_kv, preferred_element_type=jnp.float32).astype(jnp.bfloat16)
-    return partner_kv.reshape(count, total_rows, w_kv.shape[1]), w_parts
+    return partner_kv.reshape(count, total_rows, w_kv.shape[1])
 
 
 def attention_kernel(live_ref, pick_ref, q_ref, own_ref, part_ref, out_ref, score_ref):

time: 117 us -> 132 us (1.13)
  the two profiles are of different devices: /device:TPU:17 before, /device:TPU:9 now
where the time goes in v3:
time: 132 us; the launch traced here: 134 us
  waiting for transfers between devices  39.4 us (30%)
  starting transfers between devices  37.1 us (28%)
  local copies, waits for them, and re-layouts  19.9 us (15%)
  other arithmetic  13 us (10%)
  Pallas kernels  10.9 us (8%)
  between operations  7.19 us (5%)
  matrix products  6.46 us (5%)
    ppermute x20, waiting for transfers between devices, flip_heads(): return lax.ppermute(array, 'head', [(i, i ^ flip) for i in range(devices)])  39.4 us
    ppermute x20, starting transfers between devices, flip_heads(): return lax.ppermute(array, 'head', [(i, i ^ flip) for i in range(devices)])  22.8 us
    pallas_call x1, Pallas kernels, attention(): pl.pallas_call(attention_kernel, out_shape=jax.ShapeDtypeStruct(query.sha...  10.9 us
    unnamed x54, local copies, waits for them, and re-layouts  7.55 us
    ppermute x7, starting transfers between devices, quarter_keys(): lax.ppermute(mine, 'node', [(i, i ^ shift) for i in range(groups)])  7.52 us
    dot_general x1, matrix products, kv_of_spread(): jnp.dot(rows, w_kv, preferred_element_type=jnp.float32).astype(jnp.bfloat16)  4.07 us
    another operation x7, other arithmetic, spread_slots(): other = flip_heads(jnp.stack([slots[k] for k in held]), flip, heads_axis)  3.97 us
    ppermute x1, starting transfers between devices, quarter_keys(): after = lax.ppermute(mine, 'node', down)  3.65 us
  transfers between devices with their start and end apart: 29, of which 14 were waited for; matrix products, arithmetic and copies ran while one was open for 20% of the time, Pallas kernels for 0%

profile of v3, /device:TPU:9, one launch (start us, length us, event | category | flops | bytes accessed | tf_op | source)
XLA Modules:
  0.0 134.2 jit_solution(5005923503359545393)
XLA Ops:
  0.0 1.1 copy-done
  1.8 1.2 collective-permute-start.23
  3.2 1.2 collective-permute-start.25
  4.5 2.3 %collective-permute-start.26 = (bf16[96,1024]{1,0:T(8,128)(2,1)}, bf16[96,1024]{1,0:T(8,128)(2,1)}, u32[]{:S(2)}, u32[]{:S(2)}) collective-permute-start(bf16[96,1024]{1,0:T(8,128)(2,1)} %bitcast.17), channel_id=1, source_target_pairs={{0,16},{4,20},{8,24},{12,28},{16,0},{20,4},{24,8},{28,12},{1,17},{... | collective-permute-start | bytes 589832 | tf_op jit(solution)/shard_map/ppermute | solution.py:100
  6.8 1.0 collective-permute-start.27
  10.8 9.4 %conditional.7 = (bf16[1,4,96,1024]{3,2,1,0:T(8,128)(2,1)S(1)}) conditional(s32[]{:T(128)} %convert_element_type.39, () %tuple.62, bf16[96,1024]{1,0:T(8,128)(2,1)S(1)} %collective-permute-done.23), branch_computations={%region_1.2_spmd, %region_2.3_spmd} | conditional | flops 1376256 | bytes 5505112 | solution.py:107
  10.8 1.3 collective-permute-start
  12.1 3.6 %collective-permute-done = bf16[1,96,1024]{2,1,0:T(8,128)(2,1)S(1)} collective-permute-done((bf16[1,96,1024]{2,1,0:T(8,128)(2,1)S(1)}, bf16[1,96,1024]{2,1,0:T(8,128)(2,1)S(1)}, u32[]{:S(2)}, u32[]{:S(2)}) %collective-permute-start) | collective-permute-done | bytes 196640 | tf_op jit(solution)/shard_map/cond/branch_1_fun/ppermute | solution.py:26
  15.8 3.0 %collective-permute-start.1 = (bf16[2,96,1024]{2,1,0:T(8,128)(2,1)S(1)}, bf16[2,96,1024]{2,1,0:T(8,128)(2,1)S(1)}, u32[]{:S(2)}, u32[]{:S(2)}) collective-permute-start(bf16[2,96,1024]{2,1,0:T(8,128)(2,1)S(1)} %pad_maximum_fusion), channel_id=1, source_target_pairs={{0,1},{1,0},{2,3},{3,2},{4,5},{5,4},{6,7},{7,6},{8,9},{9,8},{10,11... | collective-permute-start | bytes 1179656 | tf_op jit(solution)/shard_map/cond/branch_1_fun/ppermute | solution.py:26
  18.8 1.3 %collective-permute-done.1 = bf16[2,96,1024]{2,1,0:T(8,128)(2,1)S(1)} collective-permute-done((bf16[2,96,1024]{2,1,0:T(8,128)(2,1)S(1)}, bf16[2,96,1024]{2,1,0:T(8,128)(2,1)S(1)}, u32[]{:S(2)}, u32[]{:S(2)}) %collective-permute-start.1) | collective-permute-done | bytes 393248 | tf_op jit(solution)/shard_map/cond/branch_1_fun/ppermute | solution.py:26
  20.3 1.4 %collective-permute-start.28 = (bf16[96,1024]{1,0:T(8,128)(2,1)}, bf16[96,1024]{1,0:T(8,128)(2,1)}, u32[]{:S(2)}, u32[]{:S(2)}) collective-permute-start(bf16[96,1024]{1,0:T(8,128)(2,1)} %bitcast.17), channel_id=1, source_target_pairs={{0,24},{4,28},{8,16},{12,20},{16,8},{20,12},{24,0},{28,4},{1,25},{... | collective-permute-start | bytes 589832 | tf_op jit(solution)/shard_map/ppermute | solution.py:100
  23.2 9.9 %conditional.9 = (bf16[1,4,96,1024]{3,2,1,0:T(8,128)(2,1)S(1)}) conditional(s32[]{:T(128)} %convert_element_type.41, () %tuple.64, bf16[96,1024]{1,0:T(8,128)(2,1)S(1)} %collective-permute-done.25), branch_computations={%region_7.8_spmd, %region_8.9_spmd} | conditional | flops 1376256 | bytes 6291572 | solution.py:107
  23.3 1.3 collective-permute-start.4
  24.5 4.3 %collective-permute-done.4 = bf16[1,96,1024]{2,1,0:T(8,128)(2,1)S(1)} collective-permute-done((bf16[1,96,1024]{2,1,0:T(8,128)(2,1)S(1)}, bf16[1,96,1024]{2,1,0:T(8,128)(2,1)S(1)}, u32[]{:S(2)}, u32[]{:S(2)}) %collective-permute-start.4) | collective-permute-done | bytes 196640 | tf_op jit(solution)/shard_map/cond/branch_1_fun/ppermute | solution.py:26
  28.9 1.8 %collective-permute-start.5 = (bf16[2,96,1024]{2,1,0:T(8,128)(2,1)S(1)}, bf16[2,96,1024]{2,1,0:T(8,128)(2,1)S(1)}, u32[]{:S(2)}, u32[]{:S(2)}) collective-permute-start(bf16[2,96,1024]{2,1,0:T(8,128)(2,1)S(1)} %pad_maximum_fusion.2), channel_id=1, source_target_pairs={{0,1},{1,0},{2,3},{3,2},{4,5},{5,4},{6,7},{7,6},{8,9},{9,8},{10,11... | collective-permute-start | bytes 1179656 | tf_op jit(solution)/shard_map/cond/branch_1_fun/ppermute | solution.py:26
  30.8 1.3 %collective-permute-done.5 = bf16[2,96,1024]{2,1,0:T(8,128)(2,1)S(1)} collective-permute-done((bf16[2,96,1024]{2,1,0:T(8,128)(2,1)S(1)}, bf16[2,96,1024]{2,1,0:T(8,128)(2,1)S(1)}, u32[]{:S(2)}, u32[]{:S(2)}) %collective-permute-start.5) | collective-permute-done | bytes 393248 | tf_op jit(solution)/shard_map/cond/branch_1_fun/ppermute | solution.py:26
  32.1 1.0 maximum_bitcast_fusion.2
  33.2 3.1 %collective-permute-start.14 = (bf16[96,1024]{1,0:T(8,128)(2,1)}, bf16[96,1024]{1,0:T(8,128)(2,1)}, u32[]{:S(2)}, u32[]{:S(2)}) collective-permute-start(bf16[96,1024]{1,0:T(8,128)(2,1)} %bitcast.17), channel_id=1, source_target_pairs={{0,4},{4,8},{8,12},{12,16},{16,20},{20,24},{24,28},{1,5},{5,9},{9,... | collective-permute-start | bytes 589832 | tf_op jit(solution)/shard_map/ppermute | solution.py:94
  38.0 3.6 %collective-permute-start.17 = (bf16[96,1024]{1,0:T(8,128)(2,1)}, bf16[96,1024]{1,0:T(8,128)(2,1)}, u32[]{:S(2)}, u32[]{:S(2)}) collective-permute-start(bf16[96,1024]{1,0:T(8,128)(2,1)} %bitcast.17), channel_id=1, source_target_pairs={{4,0},{8,4},{12,8},{16,12},{20,16},{24,20},{28,24},{5,1},{9,5},{13... | collective-permute-start | bytes 589832 | tf_op jit(solution)/shard_map/ppermute | solution.py:95
  42.3 1.9 %constant_dynamic-slice_fusion.3 = (bf16[256,256]{1,0:T(8,128)(2,1)}, bf16[256,256]{1,0:T(8,128)(2,1)}, bf16[256,256]{1,0:T(8,128)(2,1)S(1)}, bf16[256,256]{1,0:T(8,128)(2,1)}) fusion(bf16[256,1024]{1,0:T(8,128)(2,1)} %param.23, s32[]{:T(128)S(6)} %select_n.39, s32[]{:T(128)S(6)} %select_n.38, s32[]{:T(128)S(6)} %select_n.37, s32[]{:T(128)S(6)} %select_n.34), kind=kLoop, calls=%fused_computation.65 | loop fusion | bytes 1048592 | tf_op jit(solution)/shard_map/dynamic_slice | solution.py:242
  46.4 1.7 %copy.39 = bf16[256,256]{0,1:T(8,128)(2,1)} copy(bf16[256,256]{1,0:T(8,128)(2,1)} %get-tuple-element.86) | data formatting | bytes 262144
  48.0 11.1 %conditional.12 = (bf16[1,4,96,1024]{3,2,1,0:T(8,128)(2,1)S(1)}) conditional(s32[]{:T(128)} %convert_element_type.44, () %tuple.67, bf16[96,1024]{1,0:T(8,128)(2,1)} %collective-permute-done.28), branch_computations={%region_16.17_spmd, %region_17.18_spmd} | conditional | flops 1376256 | bytes 5505112 | solution.py:107
  48.0 1.3 collective-permute-start.10
  49.3 5.3 %collective-permute-done.10 = bf16[1,96,1024]{2,1,0:T(8,128)(2,1)S(1)} collective-permute-done((bf16[1,96,1024]{2,1,0:T(8,128)(2,1)}, bf16[1,96,1024]{2,1,0:T(8,128)(2,1)S(1)}, u32[]{:S(2)}, u32[]{:S(2)}) %collective-permute-start.10) | collective-permute-done | bytes 196640 | tf_op jit(solution)/shard_map/cond/branch_1_fun/ppermute | solution.py:26
  55.6 1.1 collective-permute-start.11
  56.7 1.3 %collective-permute-done.11 = bf16[2,96,1024]{2,1,0:T(8,128)(2,1)S(1)} collective-permute-done((bf16[2,96,1024]{2,1,0:T(8,128)(2,1)S(1)}, bf16[2,96,1024]{2,1,0:T(8,128)(2,1)S(1)}, u32[]{:S(2)}, u32[]{:S(2)}) %collective-permute-start.11) | collective-permute-done | bytes 393248 | tf_op jit(solution)/shard_map/cond/branch_1_fun/ppermute | solution.py:26
  58.1 1.0 maximum_bitcast_fusion.5
  59.1 1.3 collective-permute-start.21
  60.9 1.7 %copy.40 = bf16[256,256]{0,1:T(8,128)(2,1)} copy(bf16[256,256]{1,0:T(8,128)(2,1)} %get-tuple-element.85) | data formatting | bytes 262144
  62.6 9.9 %conditional.13 = (bf16[1,4,96,1024]{3,2,1,0:T(8,128)(2,1)}) conditional(s32[]{:T(128)} %convert_element_type.45, () %tuple.68, bf16[96,1024]{1,0:T(8,128)(2,1)S(1)} %collective-permute-done.29), branch_computations={%region_19.20_spmd, %region_20.21_spmd} | conditional | flops 1376256 | bytes 5505112 | solution.py:107
  63.0 5.5 %collective-permute-done.12 = bf16[1,96,1024]{2,1,0:T(8,128)(2,1)S(1)} collective-permute-done((bf16[1,96,1024]{2,1,0:T(8,128)(2,1)S(1)}, bf16[1,96,1024]{2,1,0:T(8,128)(2,1)S(1)}, u32[]{:S(2)}, u32[]{:S(2)}) %collective-permute-start.12) | collective-permute-done | bytes 196640 | tf_op jit(solution)/shard_map/cond/branch_1_fun/ppermute | solution.py:26
  68.5 1.6 %collective-permute-start.13 = (bf16[2,96,1024]{2,1,0:T(8,128)(2,1)S(1)}, bf16[2,96,1024]{2,1,0:T(8,128)(2,1)S(1)}, u32[]{:S(2)}, u32[]{:S(2)}) collective-permute-start(bf16[2,96,1024]{2,1,0:T(8,128)(2,1)S(1)} %pad_maximum_fusion.6), channel_id=1, source_target_pairs={{0,1},{1,0},{2,3},{3,2},{4,5},{5,4},{6,7},{7,6},{8,9},{9,8},{10,11... | collective-permute-start | bytes 1179656 | tf_op jit(solution)/shard_map/cond/branch_1_fun/ppermute | solution.py:26
  70.1 1.3 %collective-permute-done.13 = bf16[2,96,1024]{2,1,0:T(8,128)(2,1)S(1)} collective-permute-done((bf16[2,96,1024]{2,1,0:T(8,128)(2,1)S(1)}, bf16[2,96,1024]{2,1,0:T(8,128)(2,1)S(1)}, u32[]{:S(2)}, u32[]{:S(2)}) %collective-permute-start.13) | collective-permute-done | bytes 393248 | tf_op jit(solution)/shard_map/cond/branch_1_fun/ppermute | solution.py:26
  71.5 1.0 maximum_bitcast_fusion.6
  79.3 1.7 %copy.37 = bf16[256,256]{0,1:T(8,128)(2,1)} copy(bf16[256,256]{1,0:T(8,128)(2,1)} %get-tuple-element.88) | data formatting | bytes 262144 | tf_op jit(solution)/shard_map/optimization_barrier | solution.py:122
  81.0 1.3 copy.41
  82.3 1.5 %copy.26 = bf16[384,2,256]{2,1,0:T(2,128)(2,1)S(1)} copy(bf16[384,2,256]{2,0,1:T(8,128)(2,1)} %slice.122) | data formatting | bytes 786432 | tf_op jit(solution)/shard_map/slice | solution.py:252
  87.3 4.6 %collective-permute-done.15 = bf16[1,96,1024]{2,1,0:T(8,128)(2,1)S(1)} collective-permute-done((bf16[1,96,1024]{2,1,0:T(8,128)(2,1)}, bf16[1,96,1024]{2,1,0:T(8,128)(2,1)S(1)}, u32[]{:S(2)}, u32[]{:S(2)}) %collective-permute-start.15) | collective-permute-done | bytes 196640 | tf_op jit(solution)/shard_map/ppermute | solution.py:26
  92.9 1.6 %collective-permute-start.16 = (bf16[2,96,1024]{2,1,0:T(8,128)(2,1)S(1)}, bf16[2,96,1024]{2,1,0:T(8,128)(2,1)S(1)}, u32[]{:S(2)}, u32[]{:S(2)}) collective-permute-start(bf16[2,96,1024]{2,1,0:T(8,128)(2,1)S(1)} %pad_maximum_fusion.7), channel_id=1, source_target_pairs={{0,1},{1,0},{2,3},{3,2},{4,5},{5,4},{6,7},{7,6},{8,9},{9,8},{10,11... | collective-permute-start | bytes 1179656 | tf_op jit(solution)/shard_map/ppermute | solution.py:26
  94.6 1.6 %collective-permute-done.18 = bf16[1,96,1024]{2,1,0:T(8,128)(2,1)S(1)} collective-permute-done((bf16[1,96,1024]{2,1,0:T(8,128)(2,1)}, bf16[1,96,1024]{2,1,0:T(8,128)(2,1)S(1)}, u32[]{:S(2)}, u32[]{:S(2)}) %collective-permute-start.18) | collective-permute-done | bytes 196640 | tf_op jit(solution)/shard_map/ppermute | solution.py:26
  97.1 1.0 collective-permute-start.19
  102.2 4.1 %convolution_convert_fusion = bf16[2304,512]{1,0:T(8,128)(2,1)} fusion(bf16[2304,1024]{1,0:T(8,128)(2,1)S(1)} %bitcast.98, bf16[1024,512]{0,1:T(8,128)(2,1)S(1)} %bitcast.103), kind=kOutput, calls=%fused_computation.14 | convolution fusion | flops 2417098752 | bytes 8126464 | tf_op jit(solution)/shard_map/dot_general | solution.py:147
  106.2 10.9 %shard_map.73 = bf16[3,128,256]{2,1,0:T(8,128)(2,1)} custom-call(s32[3,11]{1,0:T(4,128)} %pad_convert_fusion.live_ref, s32[4,3]{1,0:T(4,128)} %add_select_fusion.pick_ref, bf16[3,128,256]{2,1,0:T(8,128)(2,1)} %bitcast.125, bf16[3,128,512]{2,1,0:T(8,128)(2,1)} %reshape_reshape.6.own_ref, bf16[6,3,128,512]{3,2,1,0:T(8,128)(2,1)} %bitcast.133), custom_call_target="tpu_custom_call" | custom-call | flops 1107296256 | bytes 3145728 | tf_op jit(solution)/shard_map/pallas_call | solution.py:214
  117.9 5.7 %collective-permute-done.30 = bf16[1,384,256]{2,1,0:T(8,128)(2,1)S(1)} collective-permute-done((bf16[1,384,256]{2,1,0:T(8,128)(2,1)}, bf16[1,384,256]{2,1,0:T(8,128)(2,1)S(1)}, u32[]{:S(2)}, u32[]{:S(2)}) %collective-permute-start.30) | collective-permute-done | bytes 196640 | tf_op jit(solution)/shard_map/ppermute | solution.py:26
  124.6 1.1 collective-permute-start.31
  125.9 1.2 collective-permute-done.31
  127.1 1.6 %fusion.37 = (f32[384]{0:T(512)S(1)}, f32[384,256]{0,1:T(8,128)S(1)}) fusion(bf16[1,256,256]{1,2,0:T(8,128)(2,1)} %bitcast.56, bf16[1,256,256]{1,2,0:T(8,128)(2,1)} %bitcast.55, bf16[1,256,256]{1,2,0:T(8,128)(2,1)} %bitcast.54, bf16[1,256,256]{1,2,0:T(8,128)(2,1)S(1)} %bitcast.129, bf16[1,384,256]{2,1,0:T(8,128)(2,1)S(1)} %get-tuple-element.90, ...), kind=kOutput, calls=%fused_computation.107 | convolution fusion | flops 203587200 | bytes 1902080 | tf_op jit(solution)/shard_map/srf,sfo->ro/dot_general | solution.py:276
  131.7 1.4 %collective-permute-done.34 = f32[384,2]{0,1:T(2,128)S(1)} collective-permute-done((f32[384,2]{0,1:T(2,128)S(1)}, f32[384,2]{0,1:T(2,128)S(1)}, u32[]{:S(2)}, u32[]{:S(2)}) %collective-permute-start.34) | collective-permute-done | bytes 3104 | tf_op jit(solution)/shard_map/ppermute | solution.py:26
  (136 shorter events, 28.7 us)
Async XLA Ops:
  1.8 9.0 %collective-permute-start.23 = (bf16[96,1024]{1,0:T(8,128)(2,1)}, bf16[96,1024]{1,0:T(8,128)(2,1)S(1)}, u32[]{:S(2)}, u32[]{:S(2)}) collective-permute-start(bf16[96,1024]{1,0:T(8,128)(2,1)} %bitcast.17), channel_id=1, source_target_pairs={{0,4},{4,0},{8,12},{12,8},{16,20},{20,16},{24,28},{28,24},{1,5},{5... | collective-permute-start | bytes 589832 | tf_op jit(solution)/shard_map/ppermute | solution.py:100
  3.1 19.2 %collective-permute-start.24 = (bf16[96,1024]{1,0:T(8,128)(2,1)}, bf16[96,1024]{1,0:T(8,128)(2,1)S(1)}, u32[]{:S(2)}, u32[]{:S(2)}) collective-permute-start(bf16[96,1024]{1,0:T(8,128)(2,1)} %bitcast.17), channel_id=1, source_target_pairs={{0,8},{4,12},{8,0},{12,4},{16,24},{20,28},{24,16},{28,20},{1,9},{5... | collective-permute-start | bytes 589832 | tf_op jit(solution)/shard_map/ppermute | solution.py:100
  3.2 20.0 %collective-permute-start.25 = (bf16[96,1024]{1,0:T(8,128)(2,1)}, bf16[96,1024]{1,0:T(8,128)(2,1)S(1)}, u32[]{:S(2)}, u32[]{:S(2)}) collective-permute-start(bf16[96,1024]{1,0:T(8,128)(2,1)} %bitcast.17), channel_id=1, source_target_pairs={{0,12},{4,8},{8,4},{12,0},{16,28},{20,24},{24,20},{28,16},{1,13},{... | collective-permute-start | bytes 589832 | tf_op jit(solution)/shard_map/ppermute | solution.py:100
  4.5 32.5 %collective-permute-start.26 = (bf16[96,1024]{1,0:T(8,128)(2,1)}, bf16[96,1024]{1,0:T(8,128)(2,1)}, u32[]{:S(2)}, u32[]{:S(2)}) collective-permute-start(bf16[96,1024]{1,0:T(8,128)(2,1)} %bitcast.17), channel_id=1, source_target_pairs={{0,16},{4,20},{8,24},{12,28},{16,0},{20,4},{24,8},{28,12},{1,17},{... | collective-permute-start | bytes 589832 | tf_op jit(solution)/shard_map/ppermute | solution.py:100
  6.8 38.1 %collective-permute-start.27 = (bf16[96,1024]{1,0:T(8,128)(2,1)}, bf16[96,1024]{1,0:T(8,128)(2,1)S(1)}, u32[]{:S(2)}, u32[]{:S(2)}) collective-permute-start(bf16[96,1024]{1,0:T(8,128)(2,1)} %bitcast.17), channel_id=1, source_target_pairs={{0,20},{4,16},{8,28},{12,24},{16,4},{20,0},{24,12},{28,8},{1,21},{... | collective-permute-start | bytes 589832 | tf_op jit(solution)/shard_map/ppermute | solution.py:100
  10.8 4.9 %collective-permute-start = (bf16[1,96,1024]{2,1,0:T(8,128)(2,1)S(1)}, bf16[1,96,1024]{2,1,0:T(8,128)(2,1)S(1)}, u32[]{:S(2)}, u32[]{:S(2)}) collective-permute-start(bf16[1,96,1024]{2,1,0:T(8,128)(2,1)S(1)} %bitcast.118), channel_id=1, source_target_pairs={{0,2},{1,3},{2,0},{3,1},{4,6},{5,7},{6,4},{7,5},{8,10},{9,11},{10,... | collective-permute-start | bytes 589832 | tf_op jit(solution)/shard_map/cond/branch_1_fun/ppermute | solution.py:26
  15.8 4.3 %collective-permute-start.1 = (bf16[2,96,1024]{2,1,0:T(8,128)(2,1)S(1)}, bf16[2,96,1024]{2,1,0:T(8,128)(2,1)S(1)}, u32[]{:S(2)}, u32[]{:S(2)}) collective-permute-start(bf16[2,96,1024]{2,1,0:T(8,128)(2,1)S(1)} %pad_maximum_fusion), channel_id=1, source_target_pairs={{0,1},{1,0},{2,3},{3,2},{4,5},{5,4},{6,7},{7,6},{8,9},{9,8},{10,11... | collective-permute-start | bytes 1179656 | tf_op jit(solution)/shard_map/cond/branch_1_fun/ppermute | solution.py:26
  20.2 16.7 %copy-start.2 = (bf16[1,4,96,1024]{3,2,1,0:T(8,128)(2,1)}, bf16[1,4,96,1024]{3,2,1,0:T(8,128)(2,1)S(1)}, u32[]{:S(2)}) copy-start(bf16[1,4,96,1024]{3,2,1,0:T(8,128)(2,1)S(1)} %get-tuple-element.103) | copy-start | bytes 2359300
  20.3 27.8 %collective-permute-start.28 = (bf16[96,1024]{1,0:T(8,128)(2,1)}, bf16[96,1024]{1,0:T(8,128)(2,1)}, u32[]{:S(2)}, u32[]{:S(2)}) collective-permute-start(bf16[96,1024]{1,0:T(8,128)(2,1)} %bitcast.17), channel_id=1, source_target_pairs={{0,24},{4,28},{8,16},{12,20},{16,8},{20,12},{24,0},{28,4},{1,25},{... | collective-permute-start | bytes 589832 | tf_op jit(solution)/shard_map/ppermute | solution.py:100
  22.3 22.5 %copy-start.4 = (bf16[1,4,96,1024]{3,2,1,0:T(8,128)(2,1)}, bf16[1,4,96,1024]{3,2,1,0:T(8,128)(2,1)S(1)}, u32[]{:S(2)}) copy-start(bf16[1,4,96,1024]{3,2,1,0:T(8,128)(2,1)S(1)} %get-tuple-element.104) | copy-start | bytes 2359300
  22.3 40.3 %collective-permute-start.29 = (bf16[96,1024]{1,0:T(8,128)(2,1)}, bf16[96,1024]{1,0:T(8,128)(2,1)S(1)}, u32[]{:S(2)}, u32[]{:S(2)}) collective-permute-start(bf16[96,1024]{1,0:T(8,128)(2,1)} %bitcast.17), channel_id=1, source_target_pairs={{0,28},{4,24},{8,20},{12,16},{16,12},{20,8},{24,4},{28,0},{1,29},{... | collective-permute-start | bytes 589832 | tf_op jit(solution)/shard_map/ppermute | solution.py:100
  23.2 8.9 %copy-start.15 = (bf16[96,1024]{1,0:T(8,128)(2,1)}, bf16[96,1024]{1,0:T(8,128)(2,1)S(1)}, u32[]{:S(2)}) copy-start(bf16[96,1024]{1,0:T(8,128)(2,1)S(1)} %param.5) | copy-start | bytes 589828 | tf_op jit(solution)/shard_map/cond
  23.3 5.6 %collective-permute-start.4 = (bf16[1,96,1024]{2,1,0:T(8,128)(2,1)S(1)}, bf16[1,96,1024]{2,1,0:T(8,128)(2,1)S(1)}, u32[]{:S(2)}, u32[]{:S(2)}) collective-permute-start(bf16[1,96,1024]{2,1,0:T(8,128)(2,1)S(1)} %bitcast.110), channel_id=1, source_target_pairs={{0,2},{1,3},{2,0},{3,1},{4,6},{5,7},{6,4},{7,5},{8,10},{9,11},{10,... | collective-permute-start | bytes 589832 | tf_op jit(solution)/shard_map/cond/branch_1_fun/ppermute | solution.py:26
  28.9 3.2 %collective-permute-start.5 = (bf16[2,96,1024]{2,1,0:T(8,128)(2,1)S(1)}, bf16[2,96,1024]{2,1,0:T(8,128)(2,1)S(1)}, u32[]{:S(2)}, u32[]{:S(2)}) collective-permute-start(bf16[2,96,1024]{2,1,0:T(8,128)(2,1)S(1)} %pad_maximum_fusion.2), channel_id=1, source_target_pairs={{0,1},{1,0},{2,3},{3,2},{4,5},{5,4},{6,7},{7,6},{8,9},{9,8},{10,11... | collective-permute-start | bytes 1179656 | tf_op jit(solution)/shard_map/cond/branch_1_fun/ppermute | solution.py:26
  33.2 14.8 %copy-start.6 = (bf16[1,4,96,1024]{3,2,1,0:T(8,128)(2,1)}, bf16[1,4,96,1024]{3,2,1,0:T(8,128)(2,1)S(1)}, u32[]{:S(2)}) copy-start(bf16[1,4,96,1024]{3,2,1,0:T(8,128)(2,1)S(1)} %get-tuple-element.105) | copy-start | bytes 2359300
  33.2 52.2 %collective-permute-start.14 = (bf16[96,1024]{1,0:T(8,128)(2,1)}, bf16[96,1024]{1,0:T(8,128)(2,1)}, u32[]{:S(2)}, u32[]{:S(2)}) collective-permute-start(bf16[96,1024]{1,0:T(8,128)(2,1)} %bitcast.17), channel_id=1, source_target_pairs={{0,4},{4,8},{8,12},{12,16},{16,20},{20,24},{24,28},{1,5},{5,9},{9,... | collective-permute-start | bytes 589832 | tf_op jit(solution)/shard_map/ppermute | solution.py:94
  38.0 48.3 %collective-permute-start.17 = (bf16[96,1024]{1,0:T(8,128)(2,1)}, bf16[96,1024]{1,0:T(8,128)(2,1)}, u32[]{:S(2)}, u32[]{:S(2)}) collective-permute-start(bf16[96,1024]{1,0:T(8,128)(2,1)} %bitcast.17), channel_id=1, source_target_pairs={{4,0},{8,4},{12,8},{16,12},{20,16},{24,20},{28,24},{5,1},{9,5},{13... | collective-permute-start | bytes 589832 | tf_op jit(solution)/shard_map/ppermute | solution.py:95
  45.0 53.6 %collective-permute-start.20 = (bf16[256,256]{0,1:T(8,128)(2,1)}, bf16[256,256]{0,1:T(8,128)(2,1)}, u32[]{:S(2)}, u32[]{:S(2)}) collective-permute-start(bf16[256,256]{0,1:T(8,128)(2,1)} %copy.38), channel_id=1, source_target_pairs={{0,1},{1,0},{2,3},{3,2},{4,5},{5,4},{6,7},{7,6},{8,9},{9,8},{10,11... | collective-permute-start | bytes 393224 | tf_op jit(solution)/shard_map/ppermute | solution.py:26
  48.0 25.5 %copy-start.1 = (bf16[1024,3,256]{2,0,1:T(8,128)(2,1)S(1)}, bf16[1024,3,256]{2,0,1:T(8,128)(2,1)}, u32[]{:S(2)}) copy-start(bf16[1024,3,256]{2,0,1:T(8,128)(2,1)} %param.22) | copy-start | bytes 4718596
  48.0 6.6 %collective-permute-start.10 = (bf16[1,96,1024]{2,1,0:T(8,128)(2,1)}, bf16[1,96,1024]{2,1,0:T(8,128)(2,1)S(1)}, u32[]{:S(2)}, u32[]{:S(2)}) collective-permute-start(bf16[1,96,1024]{2,1,0:T(8,128)(2,1)} %bitcast.10), channel_id=1, source_target_pairs={{0,2},{1,3},{2,0},{3,1},{4,6},{5,7},{6,4},{7,5},{8,10},{9,11},{10,... | collective-permute-start | bytes 589832 | tf_op jit(solution)/shard_map/cond/branch_1_fun/ppermute | solution.py:26
  55.6 2.4 %collective-permute-start.11 = (bf16[2,96,1024]{2,1,0:T(8,128)(2,1)S(1)}, bf16[2,96,1024]{2,1,0:T(8,128)(2,1)S(1)}, u32[]{:S(2)}, u32[]{:S(2)}) collective-permute-start(bf16[2,96,1024]{2,1,0:T(8,128)(2,1)S(1)} %pad_maximum_fusion.5), channel_id=1, source_target_pairs={{0,1},{1,0},{2,3},{3,2},{4,5},{5,4},{6,7},{7,6},{8,9},{9,8},{10,11... | collective-permute-start | bytes 1179656 | tf_op jit(solution)/shard_map/cond/branch_1_fun/ppermute | solution.py:26
  59.1 3.5 %copy-start.11 = (bf16[1,4,96,1024]{3,2,1,0:T(8,128)(2,1)}, bf16[1,4,96,1024]{3,2,1,0:T(8,128)(2,1)S(1)}, u32[]{:S(2)}) copy-start(bf16[1,4,96,1024]{3,2,1,0:T(8,128)(2,1)S(1)} %get-tuple-element.108) | copy-start | bytes 2359300
  59.1 39.5 %collective-permute-start.21 = (bf16[256,256]{0,1:T(8,128)(2,1)}, bf16[256,256]{0,1:T(8,128)(2,1)}, u32[]{:S(2)}, u32[]{:S(2)}) collective-permute-start(bf16[256,256]{0,1:T(8,128)(2,1)} %copy.39), channel_id=1, source_target_pairs={{0,2},{1,3},{2,0},{3,1},{4,6},{5,7},{6,4},{7,5},{8,10},{9,11},{10,... | collective-permute-start | bytes 393224 | tf_op jit(solution)/shard_map/ppermute | solution.py:26
  62.6 13.1 %copy-start.17 = (s32[4,3]{1,0:T(4,128)S(1)}, s32[4,3]{1,0:T(4,128)}, u32[]{:S(2)}) copy-start(s32[4,3]{1,0:T(4,128)} %param.27) | copy-start | bytes 148
  62.6 13.7 %copy-start.18 = (s32[3,7]{1,0:T(4,128)S(1)}, s32[3,7]{1,0:T(4,128)}, u32[]{:S(2)}) copy-start(s32[3,7]{1,0:T(4,128)} %param.26) | copy-start | bytes 256
  62.6 5.9 %collective-permute-start.12 = (bf16[1,96,1024]{2,1,0:T(8,128)(2,1)S(1)}, bf16[1,96,1024]{2,1,0:T(8,128)(2,1)S(1)}, u32[]{:S(2)}, u32[]{:S(2)}) collective-permute-start(bf16[1,96,1024]{2,1,0:T(8,128)(2,1)S(1)} %bitcast.107), channel_id=1, source_target_pairs={{0,2},{1,3},{2,0},{3,1},{4,6},{5,7},{6,4},{7,5},{8,10},{9,11},{10,... | collective-permute-start | bytes 589832 | tf_op jit(solution)/shard_map/cond/branch_1_fun/ppermute | solution.py:26
  68.5 2.9 %collective-permute-start.13 = (bf16[2,96,1024]{2,1,0:T(8,128)(2,1)S(1)}, bf16[2,96,1024]{2,1,0:T(8,128)(2,1)S(1)}, u32[]{:S(2)}, u32[]{:S(2)}) collective-permute-start(bf16[2,96,1024]{2,1,0:T(8,128)(2,1)S(1)} %pad_maximum_fusion.6), channel_id=1, source_target_pairs={{0,1},{1,0},{2,3},{3,2},{4,5},{5,4},{6,7},{7,6},{8,9},{9,8},{10,11... | collective-permute-start | bytes 1179656 | tf_op jit(solution)/shard_map/cond/branch_1_fun/ppermute | solution.py:26
  72.5 8.5 %slice-start = ((bf16[1024,3,256]{2,0,1:T(8,128)(2,1)}), bf16[1024,2,256]{2,0,1:T(8,128)(2,1)S(1)}, s32[]{:S(2)}) async-start(bf16[1024,3,256]{2,0,1:T(8,128)(2,1)} %param.22), calls=%async_computation | async-start | bytes 2097152 | tf_op jit(solution)/shard_map/slice | solution.py:257
  72.5 26.1 %collective-permute-start.22 = (bf16[256,256]{0,1:T(8,128)(2,1)}, bf16[256,256]{0,1:T(8,128)(2,1)}, u32[]{:S(2)}, u32[]{:S(2)}) collective-permute-start(bf16[256,256]{0,1:T(8,128)(2,1)} %copy.40), channel_id=1, source_target_pairs={{0,3},{1,2},{2,1},{3,0},{4,7},{5,6},{6,5},{7,4},{8,11},{9,10},{10,... | collective-permute-start | bytes 393224 | tf_op jit(solution)/shard_map/ppermute | solution.py:26
  74.3 11.9 %copy-start.3 = (bf16[1,4,96,1024]{3,2,1,0:T(8,128)(2,1)S(1)}, bf16[1,4,96,1024]{3,2,1,0:T(8,128)(2,1)}, u32[]{:S(2)}) copy-start(bf16[1,4,96,1024]{3,2,1,0:T(8,128)(2,1)} %copy-done.2) | copy-start | bytes 2359300
  74.3 12.7 %copy-start.5 = (bf16[1,4,96,1024]{3,2,1,0:T(8,128)(2,1)S(1)}, bf16[1,4,96,1024]{3,2,1,0:T(8,128)(2,1)}, u32[]{:S(2)}) copy-start(bf16[1,4,96,1024]{3,2,1,0:T(8,128)(2,1)} %copy-done.4) | copy-start | bytes 2359300
  82.3 4.7 %copy-start.7 = (bf16[1,4,96,1024]{3,2,1,0:T(8,128)(2,1)S(1)}, bf16[1,4,96,1024]{3,2,1,0:T(8,128)(2,1)}, u32[]{:S(2)}) copy-start(bf16[1,4,96,1024]{3,2,1,0:T(8,128)(2,1)} %copy-done.6) | copy-start | bytes 2359300
  84.8 2.3 %copy-start.8 = (bf16[1,4,96,1024]{3,2,1,0:T(8,128)(2,1)S(1)}, bf16[1,4,96,1024]{3,2,1,0:T(8,128)(2,1)}, u32[]{:S(2)}) copy-start(bf16[1,4,96,1024]{3,2,1,0:T(8,128)(2,1)} %get-tuple-element.106) | copy-start | bytes 2359300
  84.8 2.4 %copy-start.10 = (bf16[1,4,96,1024]{3,2,1,0:T(8,128)(2,1)S(1)}, bf16[1,4,96,1024]{3,2,1,0:T(8,128)(2,1)}, u32[]{:S(2)}) copy-start(bf16[1,4,96,1024]{3,2,1,0:T(8,128)(2,1)} %copy-done.9) | copy-start | bytes 2359300
  84.8 2.5 %copy-start.12 = (bf16[1,4,96,1024]{3,2,1,0:T(8,128)(2,1)S(1)}, bf16[1,4,96,1024]{3,2,1,0:T(8,128)(2,1)}, u32[]{:S(2)}) copy-start(bf16[1,4,96,1024]{3,2,1,0:T(8,128)(2,1)} %copy-done.11) | copy-start | bytes 2359300
  85.4 6.6 %collective-permute-start.15 = (bf16[1,96,1024]{2,1,0:T(8,128)(2,1)}, bf16[1,96,1024]{2,1,0:T(8,128)(2,1)S(1)}, u32[]{:S(2)}, u32[]{:S(2)}) collective-permute-start(bf16[1,96,1024]{2,1,0:T(8,128)(2,1)} %bitcast.19), channel_id=1, source_target_pairs={{0,2},{1,3},{2,0},{3,1},{4,6},{5,7},{6,4},{7,5},{8,10},{9,11},{10,... | collective-permute-start | bytes 589832 | tf_op jit(solution)/shard_map/ppermute | solution.py:26
  86.2 8.3 %copy-start.13 = (bf16[1,4,96,1024]{3,2,1,0:T(8,128)(2,1)S(1)}, bf16[1,4,96,1024]{3,2,1,0:T(8,128)(2,1)}, u32[]{:S(2)}) copy-start(bf16[1,4,96,1024]{3,2,1,0:T(8,128)(2,1)} %get-tuple-element.109) | copy-start | bytes 2359300
  86.2 9.9 %collective-permute-start.18 = (bf16[1,96,1024]{2,1,0:T(8,128)(2,1)}, bf16[1,96,1024]{2,1,0:T(8,128)(2,1)S(1)}, u32[]{:S(2)}, u32[]{:S(2)}) collective-permute-start(bf16[1,96,1024]{2,1,0:T(8,128)(2,1)} %bitcast.26), channel_id=1, source_target_pairs={{0,2},{1,3},{2,0},{3,1},{4,6},{5,7},{6,4},{7,5},{8,10},{9,11},{10,... | collective-permute-start | bytes 589832 | tf_op jit(solution)/shard_map/ppermute | solution.py:26
  92.9 5.7 %collective-permute-start.16 = (bf16[2,96,1024]{2,1,0:T(8,128)(2,1)S(1)}, bf16[2,96,1024]{2,1,0:T(8,128)(2,1)S(1)}, u32[]{:S(2)}, u32[]{:S(2)}) collective-permute-start(bf16[2,96,1024]{2,1,0:T(8,128)(2,1)S(1)} %pad_maximum_fusion.7), channel_id=1, source_target_pairs={{0,1},{1,0},{2,3},{3,2},{4,5},{5,4},{6,7},{7,6},{8,9},{9,8},{10,11... | collective-permute-start | bytes 1179656 | tf_op jit(solution)/shard_map/ppermute | solution.py:26
  97.1 2.5 %collective-permute-start.19 = (bf16[2,96,1024]{2,1,0:T(8,128)(2,1)S(1)}, bf16[2,96,1024]{2,1,0:T(8,128)(2,1)S(1)}, u32[]{:S(2)}, u32[]{:S(2)}) collective-permute-start(bf16[2,96,1024]{2,1,0:T(8,128)(2,1)S(1)} %pad_maximum_fusion.8), channel_id=1, source_target_pairs={{0,1},{1,0},{2,3},{3,2},{4,5},{5,4},{6,7},{7,6},{8,9},{9,8},{10,11... | collective-permute-start | bytes 1179656 | tf_op jit(solution)/shard_map/ppermute | solution.py:26
  106.2 20.9 %copy-start.16 = (bf16[256,256]{0,1:T(8,128)(2,1)S(1)}, bf16[256,256]{0,1:T(8,128)(2,1)}, u32[]{:S(2)}) copy-start(bf16[256,256]{0,1:T(8,128)(2,1)} %copy.37) | copy-start | bytes 393220
  117.1 16.1 %copy-start.19 = (f32[256]{0:T(256)S(1)}, f32[256]{0:T(256)}, u32[]{:S(2)}) copy-start(f32[256]{0:T(256)} %param.25) | copy-start | bytes 3076
  117.1 16.1 %copy-start.20 = (f32[256]{0:T(256)S(1)}, f32[256]{0:T(256)}, u32[]{:S(2)}) copy-start(f32[256]{0:T(256)} %param.24) | copy-start | bytes 3076
  117.1 6.5 %collective-permute-start.30 = (bf16[1,384,256]{2,1,0:T(8,128)(2,1)}, bf16[1,384,256]{2,1,0:T(8,128)(2,1)S(1)}, u32[]{:S(2)}, u32[]{:S(2)}) collective-permute-start(bf16[1,384,256]{2,1,0:T(8,128)(2,1)} %bitcast.126), channel_id=1, source_target_pairs={{0,2},{1,3},{2,0},{3,1},{4,6},{5,7},{6,4},{7,5},{8,10},{9,11},{10,... | collective-permute-start | bytes 589832 | tf_op jit(solution)/shard_map/ppermute | solution.py:26
  124.6 2.4 %collective-permute-start.31 = (bf16[2,384,256]{2,1,0:T(8,128)(2,1)S(1)}, bf16[2,384,256]{2,1,0:T(8,128)(2,1)S(1)}, u32[]{:S(2)}, u32[]{:S(2)}) collective-permute-start(bf16[2,384,256]{2,1,0:T(8,128)(2,1)S(1)} %pad_maximum_fusion.9), channel_id=1, source_target_pairs={{0,1},{1,0},{2,3},{3,2},{4,5},{5,4},{6,7},{7,6},{8,9},{9,8},{10,11... | collective-permute-start | bytes 1179656 | tf_op jit(solution)/shard_map/ppermute | solution.py:26
  128.8 2.2 %collective-permute-start.32 = (f32[384,2]{0,1:T(2,128)S(1)}, f32[384,2]{0,1:T(2,128)S(1)}, u32[]{:S(2)}, u32[]{:S(2)}) collective-permute-start(f32[384,2]{0,1:T(2,128)S(1)} %get-tuple-element.96), channel_id=1, source_target_pairs={{0,1},{1,0},{2,3},{3,2},{4,5},{5,4},{6,7},{7,6},{8,9},{9,8},{10,11... | collective-permute-start | bytes 9224 | tf_op jit(solution)/shard_map/ppermute | solution.py:26
  129.3 2.4 %collective-permute-start.33 = (f32[384,2]{0,1:T(2,128)S(1)}, f32[384,2]{0,1:T(2,128)S(1)}, u32[]{:S(2)}, u32[]{:S(2)}) collective-permute-start(f32[384,2]{0,1:T(2,128)S(1)} %get-tuple-element.96), channel_id=1, source_target_pairs={{0,2},{1,3},{2,0},{3,1},{4,6},{5,7},{6,4},{7,5},{8,10},{9,11},{10,... | collective-permute-start | bytes 9224 | tf_op jit(solution)/shard_map/ppermute | solution.py:26
  130.0 3.1 %collective-permute-start.34 = (f32[384,2]{0,1:T(2,128)S(1)}, f32[384,2]{0,1:T(2,128)S(1)}, u32[]{:S(2)}, u32[]{:S(2)}) collective-permute-start(f32[384,2]{0,1:T(2,128)S(1)} %get-tuple-element.96), channel_id=1, source_target_pairs={{0,3},{1,2},{2,1},{3,0},{4,7},{5,6},{6,5},{7,4},{8,11},{9,10},{10,... | collective-permute-start | bytes 9224 | tf_op jit(solution)/shard_map/ppermute | solution.py:26
  (3 other events, 3.7 us)

commit v4 on v1

--- a/solution.py
+++ b/solution.py
@@ -12,6 +12,7 @@
 REACH = 3
 LANES = 128
 GATHER_GROUPS = 16
+STATIC_GROUPS = 8
 
 
 NORM_EPS = 1e-05
@@ -83,27 +84,63 @@
     mine = node_states.reshape(blocks_here, heads_axis, sub_rows, model_width)
     mine = lax.dynamic_index_in_dim(mine, me, axis=1, keepdims=False)
     mine = mine.reshape(blocks_here * sub_rows, model_width)
+    targets = jnp.bitwise_xor(matchings[:, 0] // blocks_here, my_index)
+    if groups <= STATIC_GROUPS:
+        return static_keys(mine, w_kv, w_parts, targets, my_index, groups, blocks_here, sub_rows)
     up = [(i, i + 1) for i in range(groups - 1)]
     down = [(i + 1, i) for i in range(groups - 1)]
     before = lax.ppermute(mine, "node", up)
     after = lax.ppermute(mine, "node", down)
-    targets = jnp.bitwise_xor(matchings[:, 0] // blocks_here, my_index)
     matched = [switched_send(mine, targets[match_pos], groups) for match_pos in range(matches)]
     w_parts, matched[0] = lax.optimization_barrier((w_parts, matched[0]))
-    spread = [spread_slots(piece, heads_axis) for piece in [before, after] + matched]
+    spread = [spread_stack(piece, heads_axis) for piece in [before, after] + matched]
+    return kv_of_spread(spread, w_kv, blocks_here, sub_rows), w_parts
+
+
+def static_keys(mine, w_kv, w_parts, targets, my_index, groups, blocks_here, sub_rows):
+    heads_axis = lax.axis_size("head")
+    matches = targets.shape[0]
+    far = [(j, j + 1) for j in range(1, groups - 1, 2)] + [(j, j - 1) for j in range(2, groups, 2)]
+    other = spread_stack(lax.ppermute(mine, "node", far), heads_axis)
+    every = jnp.stack(
+        [
+            spread_stack(
+                lax.ppermute(mine, "node", [(i, i ^ shift) for i in range(groups)]), heads_axis
+            )
+            for shift in range(1, groups)
+        ]
+    )
+    odd = (my_index % 2) == 1
+    before = jnp.where(odd, every[0], other)
+    after = jnp.where(odd, other, every[0])
+    matched = [
+        lax.dynamic_index_in_dim(
+            every, jnp.clip(targets[match_pos] - 1, 0, groups - 2), 0, keepdims=False
+        )
+        for match_pos in range(matches)
+    ]
+    w_parts, matched[0] = lax.optimization_barrier((w_parts, matched[0]))
+    return kv_of_spread([before, after] + matched, w_kv, blocks_here, sub_rows), w_parts
+
+
+def spread_stack(piece, heads_axis):
+    slots = spread_slots(piece, heads_axis)
+    return jnp.stack([slots[k] for k in range(heads_axis)])
+
+
+def kv_of_spread(spread, w_kv, blocks_here, sub_rows):
+    heads_axis, _, model_width = spread[0].shape
     rows = jnp.stack(
         [
-            jnp.stack(
-                [one[k].reshape(blocks_here, sub_rows, model_width) for k in range(heads_axis)],
-                axis=1,
-            )
+            jnp.transpose(one.reshape(heads_axis, blocks_here, sub_rows, model_width), (1, 0, 2, 3))
             for one in spread
         ]
     )
     count = len(spread)
+    total_rows = blocks_here * heads_axis * sub_rows
     rows = rows.reshape(count * total_rows, model_width)
     partner_kv = jnp.dot(rows, w_kv, preferred_element_type=jnp.float32).astype(jnp.bfloat16)
-    return partner_kv.reshape(count, total_rows, w_kv.shape[1]), w_parts
+    return partner_kv.reshape(count, total_rows, w_kv.shape[1])
 
 
 def attention_kernel(live_ref, pick_ref, q_ref, own_ref, part_ref, out_ref, score_ref):

time: 130 us -> 108 us (0.83)
  the two profiles are of different devices: /device:TPU:0 before, /device:TPU:9 now
where the time goes in v4:
time: 108 us
  starting transfers between devices  40.7 us (38%)
  waiting for transfers between devices  22.7 us (21%)
  local copies, waits for them, and re-layouts  15.6 us (14%)
  Pallas kernels  10.8 us (10%)
  other arithmetic  8.02 us (7%)
  matrix products  6.75 us (6%)
  between operations  3.1 us (3%)
    ppermute x24, starting transfers between devices, flip_heads(): return lax.ppermute(array, 'head', [(i, i ^ flip) for i in range(devices)])  29.5 us
    ppermute x24, waiting for transfers between devices, flip_heads(): return lax.ppermute(array, 'head', [(i, i ^ flip) for i in range(devices)])  17.3 us
    pallas_call x1, Pallas kernels, attention(): pl.pallas_call(attention_kernel, out_shape=jax.ShapeDtypeStruct(query.sha...  10.8 us
    unnamed x38, local copies, waits for them, and re-layouts  7.75 us
    ppermute x7, starting transfers between devices, static_keys(): lax.ppermute(mine, 'node', [(i, i ^ shift) for i in range(groups)])  7.44 us
    ppermute x7, waiting for transfers between devices, static_keys(): lax.ppermute(mine, 'node', [(i, i ^ shift) for i in range(groups)])  5.38 us
    dot_general x1, matrix products, kv_of_spread(): jnp.dot(rows, w_kv, preferred_element_type=jnp.float32).astype(jnp.bfloat16)  4.06 us
    ppermute x1, starting transfers between devices, static_keys(): other = spread_stack(lax.ppermute(mine, 'node', far), heads_axis)  3.82 us
  transfers between devices with their start and end apart: 32, of which 14 were waited for; matrix products, arithmetic and copies ran while one was open for 18% of the time, Pallas kernels for 0%

profile of v4, /device:TPU:9, one launch (start us, length us, event | category | flops | bytes accessed | tf_op | source)
XLA Modules:
  0.0 107.8 jit_solution(8933731256936626529)
XLA Ops:
  0.0 1.1 %copy-done = bf16[384,1024]{1,0:T(8,128)(2,1)S(1)} copy-done((bf16[384,1024]{1,0:T(8,128)(2,1)S(1)}, bf16[384,1024]{1,0:T(8,128)(2,1)}, u32[]{:S(2)}) %copy-start) | copy-done | bytes 786456
  1.1 0.7 constant_dynamic-slice_fusion.7
  1.8 1.2 %collective-permute-start = (bf16[96,1024]{1,0:T(8,128)(2,1)}, bf16[96,1024]{1,0:T(8,128)(2,1)S(1)}, u32[]{:S(2)}, u32[]{:S(2)}) collective-permute-start(bf16[96,1024]{1,0:T(8,128)(2,1)} %bitcast.3), channel_id=1, source_target_pairs={{0,4},{4,0},{8,12},{12,8},{16,20},{20,16},{24,28},{28,24},{1,5},{5... | collective-permute-start | bytes 589832 | tf_op jit(solution)/shard_map/ppermute | solution.py:108
  3.2 1.2 %collective-permute-start.12 = (bf16[96,1024]{1,0:T(8,128)(2,1)}, bf16[96,1024]{1,0:T(8,128)(2,1)S(1)}, u32[]{:S(2)}, u32[]{:S(2)}) collective-permute-start(bf16[96,1024]{1,0:T(8,128)(2,1)} %bitcast.3), channel_id=1, source_target_pairs={{0,12},{4,8},{8,4},{12,0},{16,28},{20,24},{24,20},{28,16},{1,13},{... | collective-permute-start | bytes 589832 | tf_op jit(solution)/shard_map/ppermute | solution.py:108
  4.5 2.3 %collective-permute-start.15 = (bf16[96,1024]{1,0:T(8,128)(2,1)}, bf16[96,1024]{1,0:T(8,128)(2,1)S(1)}, u32[]{:S(2)}, u32[]{:S(2)}) collective-permute-start(bf16[96,1024]{1,0:T(8,128)(2,1)} %bitcast.3), channel_id=1, source_target_pairs={{0,16},{4,20},{8,24},{12,28},{16,0},{20,4},{24,8},{28,12},{1,17},{... | collective-permute-start | bytes 589832 | tf_op jit(solution)/shard_map/ppermute | solution.py:108
  6.8 1.0 collective-permute-start.18
  7.8 0.8 divide_reduce_fusion
  8.6 0.8 fusion.26
  9.4 1.3 %add_select_fusion.pick_ref = s32[4,3]{1,0:T(4,128)} fusion(s32[4,3]{1,0:T(4,128)} %param.13), kind=kLoop, calls=%fused_computation.58 | loop fusion | flops 72 | bytes 96 | tf_op jit(solution)/shard_map/jit(remainder)/select_n | solution.py:264
  10.7 2.2 %convolution_convert_fusion.1 = bf16[384,3,256]{2,0,1:T(8,128)(2,1)S(1)} fusion(bf16[1024,3,256]{2,0,1:T(8,128)(2,1)} %param.8, bf16[384,1024]{1,0:T(8,128)(2,1)S(1)} %copy-done), kind=kOutput, calls=%fused_computation.1 | convolution fusion | flops 604274688 | bytes 2949120 | tf_op jit(solution)/shard_map/nd,dtf->ntf/dot_general | solution.py:243
  13.0 0.7 slice.113
  17.0 1.3 %collective-permute-start.1 = (bf16[1,96,1024]{2,1,0:T(8,128)(2,1)S(1)}, bf16[1,96,1024]{2,1,0:T(8,128)(2,1)S(1)}, u32[]{:S(2)}, u32[]{:S(2)}) collective-permute-start(bf16[1,96,1024]{2,1,0:T(8,128)(2,1)S(1)} %bitcast.108), channel_id=1, source_target_pairs={{0,2},{1,3},{2,0},{3,1},{4,6},{5,7},{6,4},{7,5},{8,10},{9,11},{10,... | collective-permute-start | bytes 589832 | tf_op jit(solution)/shard_map/ppermute | solution.py:26
  18.3 1.8 %constant_dynamic-slice_fusion.3 = (bf16[256,256]{1,0:T(8,128)(2,1)S(1)}, bf16[256,256]{1,0:T(8,128)(2,1)}, bf16[256,256]{1,0:T(8,128)(2,1)}, bf16[256,256]{1,0:T(8,128)(2,1)S(1)}) fusion(bf16[256,1024]{1,0:T(8,128)(2,1)} %param.9, s32[]{:T(128)S(6)} %select_n.63, s32[]{:T(128)S(6)} %select_n.62, s32[]{:T(128)S(6)} %select_n.61, s32[]{:T(128)S(6)} %select_n.54), kind=kLoop, calls=%fused_computation.64 | loop fusion | bytes 1048592 | tf_op jit(solution)/shard_map/dynamic_slice | solution.py:237
  20.1 1.7 %copy.36 = bf16[256,256]{0,1:T(8,128)(2,1)} copy(bf16[256,256]{1,0:T(8,128)(2,1)} %get-tuple-element.23) | data formatting | bytes 262144
  21.8 1.7 %copy.37 = bf16[256,256]{0,1:T(8,128)(2,1)} copy(bf16[256,256]{1,0:T(8,128)(2,1)} %get-tuple-element.22) | data formatting | bytes 262144
  23.5 0.7 copy.38
  24.4 1.4 %copy.39 = bf16[1024,2,256]{0,2,1:T(8,128)(2,1)} copy(bf16[1024,2,256]{2,0,1:T(8,128)(2,1)S(1)} %slice-done) | data formatting | bytes 2097152
  26.1 1.0 reshape_reshape.6.own_ref
  28.0 1.3 %collective-permute-start.21 = (bf16[96,1024]{1,0:T(8,128)(2,1)}, bf16[96,1024]{1,0:T(8,128)(2,1)S(1)}, u32[]{:S(2)}, u32[]{:S(2)}) collective-permute-start(bf16[96,1024]{1,0:T(8,128)(2,1)} %bitcast.3), channel_id=1, source_target_pairs={{0,24},{4,28},{8,16},{12,20},{16,8},{20,12},{24,0},{28,4},{1,25},{... | collective-permute-start | bytes 589832 | tf_op jit(solution)/shard_map/ppermute | solution.py:108
  29.3 1.2 %collective-permute-start.13 = (bf16[1,96,1024]{2,1,0:T(8,128)(2,1)S(1)}, bf16[1,96,1024]{2,1,0:T(8,128)(2,1)S(1)}, u32[]{:S(2)}, u32[]{:S(2)}) collective-permute-start(bf16[1,96,1024]{2,1,0:T(8,128)(2,1)S(1)} %bitcast.140), channel_id=1, source_target_pairs={{0,2},{1,3},{2,0},{3,1},{4,6},{5,7},{6,4},{7,5},{8,10},{9,11},{10,... | collective-permute-start | bytes 589832 | tf_op jit(solution)/shard_map/ppermute | solution.py:26
  30.8 1.1 %collective-permute-done.10 = bf16[1,96,1024]{2,1,0:T(8,128)(2,1)S(1)} collective-permute-done((bf16[1,96,1024]{2,1,0:T(8,128)(2,1)}, bf16[1,96,1024]{2,1,0:T(8,128)(2,1)S(1)}, u32[]{:S(2)}, u32[]{:S(2)}) %collective-permute-start.10) | collective-permute-done | bytes 196640 | tf_op jit(solution)/shard_map/ppermute | solution.py:26
  32.1 1.0 pad_maximum_fusion.4
  33.1 3.8 %collective-permute-start.3 = (bf16[96,1024]{1,0:T(8,128)(2,1)}, bf16[96,1024]{1,0:T(8,128)(2,1)S(1)}, u32[]{:S(2)}, u32[]{:S(2)}) collective-permute-start(bf16[96,1024]{1,0:T(8,128)(2,1)} %bitcast.3), channel_id=1, source_target_pairs={{4,8},{12,16},{20,24},{8,4},{16,12},{24,20},{5,9},{13,17},{21,25},... | collective-permute-start | bytes 589832 | tf_op jit(solution)/shard_map/ppermute | solution.py:104
  37.0 1.3 %collective-permute-start.19 = (bf16[1,96,1024]{2,1,0:T(8,128)(2,1)S(1)}, bf16[1,96,1024]{2,1,0:T(8,128)(2,1)S(1)}, u32[]{:S(2)}, u32[]{:S(2)}) collective-permute-start(bf16[1,96,1024]{2,1,0:T(8,128)(2,1)S(1)} %bitcast.134), channel_id=1, source_target_pairs={{0,2},{1,3},{2,0},{3,1},{4,6},{5,7},{6,4},{7,5},{8,10},{9,11},{10,... | collective-permute-start | bytes 589832 | tf_op jit(solution)/shard_map/ppermute | solution.py:26
  38.3 2.6 %collective-permute-done.21 = bf16[96,1024]{1,0:T(8,128)(2,1)S(1)} collective-permute-done((bf16[96,1024]{1,0:T(8,128)(2,1)}, bf16[96,1024]{1,0:T(8,128)(2,1)S(1)}, u32[]{:S(2)}, u32[]{:S(2)}) %collective-permute-start.21) | collective-permute-done | bytes 196640 | tf_op jit(solution)/shard_map/ppermute | solution.py:108
  40.9 4.3 %collective-permute-start.6 = (bf16[256,256]{0,1:T(8,128)(2,1)}, bf16[256,256]{0,1:T(8,128)(2,1)S(1)}, u32[]{:S(2)}, u32[]{:S(2)}) collective-permute-start(bf16[256,256]{0,1:T(8,128)(2,1)} %copy.36), channel_id=1, source_target_pairs={{0,1},{1,0},{2,3},{3,2},{4,5},{5,4},{6,7},{7,6},{8,9},{9,8},{10,11... | collective-permute-start | bytes 393224 | tf_op jit(solution)/shard_map/ppermute | solution.py:26
  45.2 2.7 %collective-permute-done.24 = bf16[96,1024]{1,0:T(8,128)(2,1)S(1)} collective-permute-done((bf16[96,1024]{1,0:T(8,128)(2,1)}, bf16[96,1024]{1,0:T(8,128)(2,1)S(1)}, u32[]{:S(2)}, u32[]{:S(2)}) %collective-permute-start.24) | collective-permute-done | bytes 196640 | tf_op jit(solution)/shard_map/ppermute | solution.py:108
  48.0 1.1 collective-permute-start.22
  49.5 2.9 %collective-permute-start.2 = (bf16[2,96,1024]{2,1,0:T(8,128)(2,1)S(1)}, bf16[2,96,1024]{2,1,0:T(8,128)(2,1)S(1)}, u32[]{:S(2)}, u32[]{:S(2)}) collective-permute-start(bf16[2,96,1024]{2,1,0:T(8,128)(2,1)S(1)} %pad_maximum_fusion.2), channel_id=1, source_target_pairs={{0,1},{1,0},{2,3},{3,2},{4,5},{5,4},{6,7},{7,6},{8,9},{9,8},{10,11... | collective-permute-start | bytes 1179656 | tf_op jit(solution)/shard_map/ppermute | solution.py:26
  52.4 1.3 %collective-permute-start.7 = (bf16[256,256]{0,1:T(8,128)(2,1)S(1)}, bf16[256,256]{0,1:T(8,128)(2,1)S(1)}, u32[]{:S(2)}, u32[]{:S(2)}) collective-permute-start(bf16[256,256]{0,1:T(8,128)(2,1)S(1)} %copy-done.5), channel_id=1, source_target_pairs={{0,2},{1,3},{2,0},{3,1},{4,6},{5,7},{6,4},{7,5},{8,10},{9,11},{10,... | collective-permute-start | bytes 393224 | tf_op jit(solution)/shard_map/ppermute | solution.py:26
  54.0 2.3 %collective-permute-done.25 = bf16[1,96,1024]{2,1,0:T(8,128)(2,1)S(1)} collective-permute-done((bf16[1,96,1024]{2,1,0:T(8,128)(2,1)S(1)}, bf16[1,96,1024]{2,1,0:T(8,128)(2,1)S(1)}, u32[]{:S(2)}, u32[]{:S(2)}) %collective-permute-start.25) | collective-permute-done | bytes 196640 | tf_op jit(solution)/shard_map/ppermute | solution.py:26
  56.3 6.0 %collective-permute-start.11 = (bf16[2,96,1024]{2,1,0:T(8,128)(2,1)S(1)}, bf16[2,96,1024]{2,1,0:T(8,128)(2,1)S(1)}, u32[]{:S(2)}, u32[]{:S(2)}) collective-permute-start(bf16[2,96,1024]{2,1,0:T(8,128)(2,1)S(1)} %pad_maximum_fusion.4), channel_id=1, source_target_pairs={{0,1},{1,0},{2,3},{3,2},{4,5},{5,4},{6,7},{7,6},{8,9},{9,8},{10,11... | collective-permute-start | bytes 1179656 | tf_op jit(solution)/shard_map/ppermute | solution.py:26
  62.3 1.0 collective-permute-done.4
  63.3 4.1 %collective-permute-start.8 = (bf16[256,256]{0,1:T(8,128)(2,1)S(1)}, bf16[256,256]{0,1:T(8,128)(2,1)S(1)}, u32[]{:S(2)}, u32[]{:S(2)}) collective-permute-start(bf16[256,256]{0,1:T(8,128)(2,1)S(1)} %copy-done.4), channel_id=1, source_target_pairs={{0,3},{1,2},{2,1},{3,0},{4,7},{5,6},{6,5},{7,4},{8,11},{9,10},{10,... | collective-permute-start | bytes 393224 | tf_op jit(solution)/shard_map/ppermute | solution.py:26
  68.2 1.1 collective-permute-done.14
  70.0 1.0 collective-permute-done.20
  71.7 1.0 collective-permute-done.26
  72.8 1.0 fusion.2
  76.0 0.9 copy.30
  77.2 4.1 %convolution_convert_fusion = bf16[2304,512]{1,0:T(8,128)(2,1)} fusion(bf16[2304,1024]{1,0:T(8,128)(2,1)S(1)} %bitcast.107, bf16[1024,512]{0,1:T(8,128)(2,1)S(1)} %bitcast.133), kind=kOutput, calls=%fused_computation | convolution fusion | flops 2417098752 | bytes 8126464 | tf_op jit(solution)/shard_map/dot_general | solution.py:142
  81.2 10.8 %shard_map.73 = bf16[3,128,256]{2,1,0:T(8,128)(2,1)} custom-call(s32[3,11]{1,0:T(4,128)} %pad_convert_fusion.live_ref, s32[4,3]{1,0:T(4,128)} %add_select_fusion.pick_ref, bf16[3,128,256]{2,1,0:T(8,128)(2,1)} %bitcast.149, bf16[3,128,512]{2,1,0:T(8,128)(2,1)} %reshape_reshape.6.own_ref, bf16[6,3,128,512]{3,2,1,0:T(8,128)(2,1)} %bitcast.160), custom_call_target="tpu_custom_call" | custom-call | flops 1107296256 | bytes 3145728 | tf_op jit(solution)/shard_map/pallas_call | solution.py:209
  92.6 6.2 %collective-permute-done.27 = bf16[1,384,256]{2,1,0:T(8,128)(2,1)S(1)} collective-permute-done((bf16[1,384,256]{2,1,0:T(8,128)(2,1)}, bf16[1,384,256]{2,1,0:T(8,128)(2,1)S(1)}, u32[]{:S(2)}, u32[]{:S(2)}) %collective-permute-start.27) | collective-permute-done | bytes 196640 | tf_op jit(solution)/shard_map/ppermute | solution.py:26
  98.8 1.0 pad_maximum_fusion.10
  99.7 1.0 collective-permute-start.28
  100.9 1.2 %collective-permute-done.28 = bf16[2,384,256]{2,1,0:T(8,128)(2,1)S(1)} collective-permute-done((bf16[2,384,256]{2,1,0:T(8,128)(2,1)S(1)}, bf16[2,384,256]{2,1,0:T(8,128)(2,1)S(1)}, u32[]{:S(2)}, u32[]{:S(2)}) %collective-permute-start.28) | collective-permute-done | bytes 393248 | tf_op jit(solution)/shard_map/ppermute | solution.py:26
  103.6 1.4 %collective-permute-start.31 = (f32[384,2]{0,1:T(2,128)S(1)}, f32[384,2]{0,1:T(2,128)S(1)}, u32[]{:S(2)}, u32[]{:S(2)}) collective-permute-start(f32[384,2]{0,1:T(2,128)S(1)} %get-tuple-element.44), channel_id=1, source_target_pairs={{0,3},{1,2},{2,1},{3,0},{4,7},{5,6},{6,5},{7,4},{8,11},{9,10},{10,... | collective-permute-start | bytes 9224 | tf_op jit(solution)/shard_map/ppermute | solution.py:26
  105.7 1.0 collective-permute-done.31
  107.0 0.8 copy.32
  (121 shorter events, 11.3 us)
Async XLA Ops:
  0.0 1.1 %copy-start = (bf16[384,1024]{1,0:T(8,128)(2,1)S(1)}, bf16[384,1024]{1,0:T(8,128)(2,1)}, u32[]{:S(2)}) copy-start(bf16[384,1024]{1,0:T(8,128)(2,1)} %param.7) | copy-start | bytes 2359300
  1.8 15.2 %collective-permute-start = (bf16[96,1024]{1,0:T(8,128)(2,1)}, bf16[96,1024]{1,0:T(8,128)(2,1)S(1)}, u32[]{:S(2)}, u32[]{:S(2)}) collective-permute-start(bf16[96,1024]{1,0:T(8,128)(2,1)} %bitcast.3), channel_id=1, source_target_pairs={{0,4},{4,0},{8,12},{12,8},{16,20},{20,16},{24,28},{28,24},{1,5},{5... | collective-permute-start | bytes 589832 | tf_op jit(solution)/shard_map/ppermute | solution.py:108
  3.1 24.1 %collective-permute-start.9 = (bf16[96,1024]{1,0:T(8,128)(2,1)}, bf16[96,1024]{1,0:T(8,128)(2,1)}, u32[]{:S(2)}, u32[]{:S(2)}) collective-permute-start(bf16[96,1024]{1,0:T(8,128)(2,1)} %bitcast.3), channel_id=1, source_target_pairs={{0,8},{4,12},{8,0},{12,4},{16,24},{20,28},{24,16},{28,20},{1,9},{5... | collective-permute-start | bytes 589832 | tf_op jit(solution)/shard_map/ppermute | solution.py:108
  3.2 24.8 %collective-permute-start.12 = (bf16[96,1024]{1,0:T(8,128)(2,1)}, bf16[96,1024]{1,0:T(8,128)(2,1)S(1)}, u32[]{:S(2)}, u32[]{:S(2)}) collective-permute-start(bf16[96,1024]{1,0:T(8,128)(2,1)} %bitcast.3), channel_id=1, source_target_pairs={{0,12},{4,8},{8,4},{12,0},{16,28},{20,24},{24,20},{28,16},{1,13},{... | collective-permute-start | bytes 589832 | tf_op jit(solution)/shard_map/ppermute | solution.py:108
  4.5 26.1 %collective-permute-start.15 = (bf16[96,1024]{1,0:T(8,128)(2,1)}, bf16[96,1024]{1,0:T(8,128)(2,1)S(1)}, u32[]{:S(2)}, u32[]{:S(2)}) collective-permute-start(bf16[96,1024]{1,0:T(8,128)(2,1)} %bitcast.3), channel_id=1, source_target_pairs={{0,16},{4,20},{8,24},{12,28},{16,0},{20,4},{24,8},{28,12},{1,17},{... | collective-permute-start | bytes 589832 | tf_op jit(solution)/shard_map/ppermute | solution.py:108
  6.8 26.3 %collective-permute-start.18 = (bf16[96,1024]{1,0:T(8,128)(2,1)}, bf16[96,1024]{1,0:T(8,128)(2,1)S(1)}, u32[]{:S(2)}, u32[]{:S(2)}) collective-permute-start(bf16[96,1024]{1,0:T(8,128)(2,1)} %bitcast.3), channel_id=1, source_target_pairs={{0,20},{4,16},{8,28},{12,24},{16,4},{20,0},{24,12},{28,8},{1,21},{... | collective-permute-start | bytes 589832 | tf_op jit(solution)/shard_map/ppermute | solution.py:108
  10.7 2.2 %copy-start.6 = (s32[3,7]{1,0:T(4,128)S(1)}, s32[3,7]{1,0:T(4,128)}, u32[]{:S(2)}) copy-start(s32[3,7]{1,0:T(4,128)} %param.12) | copy-start | bytes 256
  12.9 0.9 copy-start.1
  13.0 11.4 %slice-start = ((bf16[1024,3,256]{2,0,1:T(8,128)(2,1)}), bf16[1024,2,256]{2,0,1:T(8,128)(2,1)S(1)}, s32[]{:S(2)}) async-start(bf16[1024,3,256]{2,0,1:T(8,128)(2,1)} %param.8), calls=%async_computation | async-start | bytes 2097152 | tf_op jit(solution)/shard_map/slice | solution.py:252
  17.0 12.3 %collective-permute-start.1 = (bf16[1,96,1024]{2,1,0:T(8,128)(2,1)S(1)}, bf16[1,96,1024]{2,1,0:T(8,128)(2,1)S(1)}, u32[]{:S(2)}, u32[]{:S(2)}) collective-permute-start(bf16[1,96,1024]{2,1,0:T(8,128)(2,1)S(1)} %bitcast.108), channel_id=1, source_target_pairs={{0,2},{1,3},{2,0},{3,1},{4,6},{5,7},{6,4},{7,5},{8,10},{9,11},{10,... | collective-permute-start | bytes 589832 | tf_op jit(solution)/shard_map/ppermute | solution.py:26
  20.1 5.6 %slice-start.1 = ((bf16[384,3,256]{2,0,1:T(8,128)(2,1)}), bf16[384,2,256]{2,0,1:T(8,128)(2,1)S(1)}, s32[]{:S(2)}) async-start(bf16[384,3,256]{2,0,1:T(8,128)(2,1)} %copy-done.1), calls=%async_computation.1 | async-start | bytes 786432 | tf_op jit(solution)/shard_map/slice | solution.py:247
  27.2 4.7 %collective-permute-start.10 = (bf16[1,96,1024]{2,1,0:T(8,128)(2,1)}, bf16[1,96,1024]{2,1,0:T(8,128)(2,1)S(1)}, u32[]{:S(2)}, u32[]{:S(2)}) collective-permute-start(bf16[1,96,1024]{2,1,0:T(8,128)(2,1)} %bitcast.19), channel_id=1, source_target_pairs={{0,2},{1,3},{2,0},{3,1},{4,6},{5,7},{6,4},{7,5},{8,10},{9,11},{10,... | collective-permute-start | bytes 589832 | tf_op jit(solution)/shard_map/ppermute | solution.py:26
  28.0 12.9 %collective-permute-start.21 = (bf16[96,1024]{1,0:T(8,128)(2,1)}, bf16[96,1024]{1,0:T(8,128)(2,1)S(1)}, u32[]{:S(2)}, u32[]{:S(2)}) collective-permute-start(bf16[96,1024]{1,0:T(8,128)(2,1)} %bitcast.3), channel_id=1, source_target_pairs={{0,24},{4,28},{8,16},{12,20},{16,8},{20,12},{24,0},{28,4},{1,25},{... | collective-permute-start | bytes 589832 | tf_op jit(solution)/shard_map/ppermute | solution.py:108
  29.3 7.6 %collective-permute-start.13 = (bf16[1,96,1024]{2,1,0:T(8,128)(2,1)S(1)}, bf16[1,96,1024]{2,1,0:T(8,128)(2,1)S(1)}, u32[]{:S(2)}, u32[]{:S(2)}) collective-permute-start(bf16[1,96,1024]{2,1,0:T(8,128)(2,1)S(1)} %bitcast.140), channel_id=1, source_target_pairs={{0,2},{1,3},{2,0},{3,1},{4,6},{5,7},{6,4},{7,5},{8,10},{9,11},{10,... | collective-permute-start | bytes 589832 | tf_op jit(solution)/shard_map/ppermute | solution.py:26
  30.6 17.4 %collective-permute-start.24 = (bf16[96,1024]{1,0:T(8,128)(2,1)}, bf16[96,1024]{1,0:T(8,128)(2,1)S(1)}, u32[]{:S(2)}, u32[]{:S(2)}) collective-permute-start(bf16[96,1024]{1,0:T(8,128)(2,1)} %bitcast.3), channel_id=1, source_target_pairs={{0,28},{4,24},{8,20},{12,16},{16,12},{20,8},{24,4},{28,0},{1,29},{... | collective-permute-start | bytes 589832 | tf_op jit(solution)/shard_map/ppermute | solution.py:108
  31.9 20.5 %copy-start.5 = (bf16[256,256]{0,1:T(8,128)(2,1)S(1)}, bf16[256,256]{0,1:T(8,128)(2,1)}, u32[]{:S(2)}) copy-start(bf16[256,256]{0,1:T(8,128)(2,1)} %copy.37) | copy-start | bytes 393220
  31.9 17.1 %collective-permute-start.16 = (bf16[1,96,1024]{2,1,0:T(8,128)(2,1)S(1)}, bf16[1,96,1024]{2,1,0:T(8,128)(2,1)S(1)}, u32[]{:S(2)}, u32[]{:S(2)}) collective-permute-start(bf16[1,96,1024]{2,1,0:T(8,128)(2,1)S(1)} %bitcast.137), channel_id=1, source_target_pairs={{0,2},{1,3},{2,0},{3,1},{4,6},{5,7},{6,4},{7,5},{8,10},{9,11},{10,... | collective-permute-start | bytes 589832 | tf_op jit(solution)/shard_map/ppermute | solution.py:26
  33.1 19.3 %collective-permute-start.3 = (bf16[96,1024]{1,0:T(8,128)(2,1)}, bf16[96,1024]{1,0:T(8,128)(2,1)S(1)}, u32[]{:S(2)}, u32[]{:S(2)}) collective-permute-start(bf16[96,1024]{1,0:T(8,128)(2,1)} %bitcast.3), channel_id=1, source_target_pairs={{4,8},{12,16},{20,24},{8,4},{16,12},{24,20},{5,9},{13,17},{21,25},... | collective-permute-start | bytes 589832 | tf_op jit(solution)/shard_map/ppermute | solution.py:104
  37.0 12.5 %collective-permute-start.19 = (bf16[1,96,1024]{2,1,0:T(8,128)(2,1)S(1)}, bf16[1,96,1024]{2,1,0:T(8,128)(2,1)S(1)}, u32[]{:S(2)}, u32[]{:S(2)}) collective-permute-start(bf16[1,96,1024]{2,1,0:T(8,128)(2,1)S(1)} %bitcast.134), channel_id=1, source_target_pairs={{0,2},{1,3},{2,0},{3,1},{4,6},{5,7},{6,4},{7,5},{8,10},{9,11},{10,... | collective-permute-start | bytes 589832 | tf_op jit(solution)/shard_map/ppermute | solution.py:26
  40.9 33.7 %collective-permute-start.6 = (bf16[256,256]{0,1:T(8,128)(2,1)}, bf16[256,256]{0,1:T(8,128)(2,1)S(1)}, u32[]{:S(2)}, u32[]{:S(2)}) collective-permute-start(bf16[256,256]{0,1:T(8,128)(2,1)} %copy.36), channel_id=1, source_target_pairs={{0,1},{1,0},{2,3},{3,2},{4,5},{5,4},{6,7},{7,6},{8,9},{9,8},{10,11... | collective-permute-start | bytes 393224 | tf_op jit(solution)/shard_map/ppermute | solution.py:26
  48.0 5.8 %collective-permute-start.22 = (bf16[1,96,1024]{2,1,0:T(8,128)(2,1)S(1)}, bf16[1,96,1024]{2,1,0:T(8,128)(2,1)S(1)}, u32[]{:S(2)}, u32[]{:S(2)}) collective-permute-start(bf16[1,96,1024]{2,1,0:T(8,128)(2,1)S(1)} %bitcast.143), channel_id=1, source_target_pairs={{0,2},{1,3},{2,0},{3,1},{4,6},{5,7},{6,4},{7,5},{8,10},{9,11},{10,... | collective-permute-start | bytes 589832 | tf_op jit(solution)/shard_map/ppermute | solution.py:26
  49.0 14.3 %copy-start.4 = (bf16[256,256]{0,1:T(8,128)(2,1)S(1)}, bf16[256,256]{0,1:T(8,128)(2,1)}, u32[]{:S(2)}) copy-start(bf16[256,256]{0,1:T(8,128)(2,1)} %copy.38) | copy-start | bytes 393220
  49.0 7.3 %collective-permute-start.25 = (bf16[1,96,1024]{2,1,0:T(8,128)(2,1)S(1)}, bf16[1,96,1024]{2,1,0:T(8,128)(2,1)S(1)}, u32[]{:S(2)}, u32[]{:S(2)}) collective-permute-start(bf16[1,96,1024]{2,1,0:T(8,128)(2,1)S(1)} %bitcast.146), channel_id=1, source_target_pairs={{0,2},{1,3},{2,0},{3,1},{4,6},{5,7},{6,4},{7,5},{8,10},{9,11},{10,... | collective-permute-start | bytes 589832 | tf_op jit(solution)/shard_map/ppermute | solution.py:26
  49.5 18.0 %collective-permute-start.2 = (bf16[2,96,1024]{2,1,0:T(8,128)(2,1)S(1)}, bf16[2,96,1024]{2,1,0:T(8,128)(2,1)S(1)}, u32[]{:S(2)}, u32[]{:S(2)}) collective-permute-start(bf16[2,96,1024]{2,1,0:T(8,128)(2,1)S(1)} %pad_maximum_fusion.2), channel_id=1, source_target_pairs={{0,1},{1,0},{2,3},{3,2},{4,5},{5,4},{6,7},{7,6},{8,9},{9,8},{10,11... | collective-permute-start | bytes 1179656 | tf_op jit(solution)/shard_map/ppermute | solution.py:26
  52.4 22.2 %collective-permute-start.7 = (bf16[256,256]{0,1:T(8,128)(2,1)S(1)}, bf16[256,256]{0,1:T(8,128)(2,1)S(1)}, u32[]{:S(2)}, u32[]{:S(2)}) collective-permute-start(bf16[256,256]{0,1:T(8,128)(2,1)S(1)} %copy-done.5), channel_id=1, source_target_pairs={{0,2},{1,3},{2,0},{3,1},{4,6},{5,7},{6,4},{7,5},{8,10},{9,11},{10,... | collective-permute-start | bytes 393224 | tf_op jit(solution)/shard_map/ppermute | solution.py:26
  53.7 9.6 %collective-permute-start.4 = (bf16[1,96,1024]{2,1,0:T(8,128)(2,1)S(1)}, bf16[1,96,1024]{2,1,0:T(8,128)(2,1)S(1)}, u32[]{:S(2)}, u32[]{:S(2)}) collective-permute-start(bf16[1,96,1024]{2,1,0:T(8,128)(2,1)S(1)} %bitcast.123), channel_id=1, source_target_pairs={{0,2},{1,3},{2,0},{3,1},{4,6},{5,7},{6,4},{7,5},{8,10},{9,11},{10,... | collective-permute-start | bytes 589832 | tf_op jit(solution)/shard_map/ppermute | solution.py:26
  56.3 11.3 %collective-permute-start.11 = (bf16[2,96,1024]{2,1,0:T(8,128)(2,1)S(1)}, bf16[2,96,1024]{2,1,0:T(8,128)(2,1)S(1)}, u32[]{:S(2)}, u32[]{:S(2)}) collective-permute-start(bf16[2,96,1024]{2,1,0:T(8,128)(2,1)S(1)} %pad_maximum_fusion.4), channel_id=1, source_target_pairs={{0,1},{1,0},{2,3},{3,2},{4,5},{5,4},{6,7},{7,6},{8,9},{9,8},{10,11... | collective-permute-start | bytes 1179656 | tf_op jit(solution)/shard_map/ppermute | solution.py:26
  63.3 11.3 %collective-permute-start.8 = (bf16[256,256]{0,1:T(8,128)(2,1)S(1)}, bf16[256,256]{0,1:T(8,128)(2,1)S(1)}, u32[]{:S(2)}, u32[]{:S(2)}) collective-permute-start(bf16[256,256]{0,1:T(8,128)(2,1)S(1)} %copy-done.4), channel_id=1, source_target_pairs={{0,3},{1,2},{2,1},{3,0},{4,7},{5,6},{6,5},{7,4},{8,11},{9,10},{10,... | collective-permute-start | bytes 393224 | tf_op jit(solution)/shard_map/ppermute | solution.py:26
  67.5 1.8 %collective-permute-start.14 = (bf16[2,96,1024]{2,1,0:T(8,128)(2,1)S(1)}, bf16[2,96,1024]{2,1,0:T(8,128)(2,1)S(1)}, u32[]{:S(2)}, u32[]{:S(2)}) collective-permute-start(bf16[2,96,1024]{2,1,0:T(8,128)(2,1)S(1)} %pad_maximum_fusion.5), channel_id=1, source_target_pairs={{0,1},{1,0},{2,3},{3,2},{4,5},{5,4},{6,7},{7,6},{8,9},{9,8},{10,11... | collective-permute-start | bytes 1179656 | tf_op jit(solution)/shard_map/ppermute | solution.py:26
  67.6 2.2 %collective-permute-start.17 = (bf16[2,96,1024]{2,1,0:T(8,128)(2,1)S(1)}, bf16[2,96,1024]{2,1,0:T(8,128)(2,1)S(1)}, u32[]{:S(2)}, u32[]{:S(2)}) collective-permute-start(bf16[2,96,1024]{2,1,0:T(8,128)(2,1)S(1)} %pad_maximum_fusion.6), channel_id=1, source_target_pairs={{0,1},{1,0},{2,3},{3,2},{4,5},{5,4},{6,7},{7,6},{8,9},{9,8},{10,11... | collective-permute-start | bytes 1179656 | tf_op jit(solution)/shard_map/ppermute | solution.py:26
  69.3 1.7 %collective-permute-start.20 = (bf16[2,96,1024]{2,1,0:T(8,128)(2,1)S(1)}, bf16[2,96,1024]{2,1,0:T(8,128)(2,1)S(1)}, u32[]{:S(2)}, u32[]{:S(2)}) collective-permute-start(bf16[2,96,1024]{2,1,0:T(8,128)(2,1)S(1)} %pad_maximum_fusion.7), channel_id=1, source_target_pairs={{0,1},{1,0},{2,3},{3,2},{4,5},{5,4},{6,7},{7,6},{8,9},{9,8},{10,11... | collective-permute-start | bytes 1179656 | tf_op jit(solution)/shard_map/ppermute | solution.py:26
  69.9 1.7 %collective-permute-start.23 = (bf16[2,96,1024]{2,1,0:T(8,128)(2,1)S(1)}, bf16[2,96,1024]{2,1,0:T(8,128)(2,1)S(1)}, u32[]{:S(2)}, u32[]{:S(2)}) collective-permute-start(bf16[2,96,1024]{2,1,0:T(8,128)(2,1)S(1)} %pad_maximum_fusion.8), channel_id=1, source_target_pairs={{0,1},{1,0},{2,3},{3,2},{4,5},{5,4},{6,7},{7,6},{8,9},{9,8},{10,11... | collective-permute-start | bytes 1179656 | tf_op jit(solution)/shard_map/ppermute | solution.py:26
  71.0 1.7 %collective-permute-start.26 = (bf16[2,96,1024]{2,1,0:T(8,128)(2,1)S(1)}, bf16[2,96,1024]{2,1,0:T(8,128)(2,1)S(1)}, u32[]{:S(2)}, u32[]{:S(2)}) collective-permute-start(bf16[2,96,1024]{2,1,0:T(8,128)(2,1)S(1)} %pad_maximum_fusion.9), channel_id=1, source_target_pairs={{0,1},{1,0},{2,3},{3,2},{4,5},{5,4},{6,7},{7,6},{8,9},{9,8},{10,11... | collective-permute-start | bytes 1179656 | tf_op jit(solution)/shard_map/ppermute | solution.py:26
  71.6 3.1 %collective-permute-start.5 = (bf16[2,96,1024]{2,1,0:T(8,128)(2,1)S(1)}, bf16[2,96,1024]{2,1,0:T(8,128)(2,1)S(1)}, u32[]{:S(2)}, u32[]{:S(2)}) collective-permute-start(bf16[2,96,1024]{2,1,0:T(8,128)(2,1)S(1)} %pad_maximum_fusion.3), channel_id=1, source_target_pairs={{0,1},{1,0},{2,3},{3,2},{4,5},{5,4},{6,7},{7,6},{8,9},{9,8},{10,11... | collective-permute-start | bytes 1179656 | tf_op jit(solution)/shard_map/ppermute | solution.py:26
  74.6 0.7 copy-start.11
  74.6 0.8 copy-start.13
  76.0 1.2 %copy-start.2 = (bf16[1024,2,256]{0,2,1:T(8,128)(2,1)S(1)}, bf16[1024,2,256]{0,2,1:T(8,128)(2,1)}, u32[]{:S(2)}) copy-start(bf16[1024,2,256]{0,2,1:T(8,128)(2,1)} %copy.39) | copy-start | bytes 3145732
  92.1 10.0 %copy-start.3 = (bf16[3,128,256]{2,1,0:T(8,128)(2,1)S(1)}, bf16[3,128,256]{2,1,0:T(8,128)(2,1)}, u32[]{:S(2)}) copy-start(bf16[3,128,256]{2,1,0:T(8,128)(2,1)} %shard_map.73) | copy-start | bytes 589828
  92.1 10.0 %copy-start.10 = (bf16[256,256]{0,1:T(8,128)(2,1)S(1)}, bf16[256,256]{0,1:T(8,128)(2,1)}, u32[]{:S(2)}) copy-start(bf16[256,256]{0,1:T(8,128)(2,1)} %copy-done.9) | copy-start | bytes 393220
  92.1 10.0 %copy-start.12 = (bf16[256,256]{0,1:T(8,128)(2,1)S(1)}, bf16[256,256]{0,1:T(8,128)(2,1)}, u32[]{:S(2)}) copy-start(bf16[256,256]{0,1:T(8,128)(2,1)} %copy-done.11) | copy-start | bytes 393220
  92.1 10.0 %copy-start.14 = (bf16[256,256]{0,1:T(8,128)(2,1)S(1)}, bf16[256,256]{0,1:T(8,128)(2,1)}, u32[]{:S(2)}) copy-start(bf16[256,256]{0,1:T(8,128)(2,1)} %copy-done.13) | copy-start | bytes 393220
  92.1 6.6 %collective-permute-start.27 = (bf16[1,384,256]{2,1,0:T(8,128)(2,1)}, bf16[1,384,256]{2,1,0:T(8,128)(2,1)S(1)}, u32[]{:S(2)}, u32[]{:S(2)}) collective-permute-start(bf16[1,384,256]{2,1,0:T(8,128)(2,1)} %bitcast.150), channel_id=1, source_target_pairs={{0,2},{1,3},{2,0},{3,1},{4,6},{5,7},{6,4},{7,5},{8,10},{9,11},{10,... | collective-permute-start | bytes 589832 | tf_op jit(solution)/shard_map/ppermute | solution.py:26
  99.7 2.4 %collective-permute-start.28 = (bf16[2,384,256]{2,1,0:T(8,128)(2,1)S(1)}, bf16[2,384,256]{2,1,0:T(8,128)(2,1)S(1)}, u32[]{:S(2)}, u32[]{:S(2)}) collective-permute-start(bf16[2,384,256]{2,1,0:T(8,128)(2,1)S(1)} %pad_maximum_fusion.10), channel_id=1, source_target_pairs={{0,1},{1,0},{2,3},{3,2},{4,5},{5,4},{6,7},{7,6},{8,9},{9,8},{10,11... | collective-permute-start | bytes 1179656 | tf_op jit(solution)/shard_map/ppermute | solution.py:26
  102.2 4.6 %copy-start.7 = (f32[256]{0:T(256)S(1)}, f32[256]{0:T(256)}, u32[]{:S(2)}) copy-start(f32[256]{0:T(256)} %param.11) | copy-start | bytes 3076
  102.2 4.6 %copy-start.8 = (f32[256]{0:T(256)S(1)}, f32[256]{0:T(256)}, u32[]{:S(2)}) copy-start(f32[256]{0:T(256)} %param.10) | copy-start | bytes 3076
  102.8 2.2 %collective-permute-start.29 = (f32[384,2]{0,1:T(2,128)S(1)}, f32[384,2]{0,1:T(2,128)S(1)}, u32[]{:S(2)}, u32[]{:S(2)}) collective-permute-start(f32[384,2]{0,1:T(2,128)S(1)} %get-tuple-element.44), channel_id=1, source_target_pairs={{0,1},{1,0},{2,3},{3,2},{4,5},{5,4},{6,7},{7,6},{8,9},{9,8},{10,11... | collective-permute-start | bytes 9224 | tf_op jit(solution)/shard_map/ppermute | solution.py:26
  103.2 2.4 %collective-permute-start.30 = (f32[384,2]{0,1:T(2,128)S(1)}, f32[384,2]{0,1:T(2,128)S(1)}, u32[]{:S(2)}, u32[]{:S(2)}) collective-permute-start(f32[384,2]{0,1:T(2,128)S(1)} %get-tuple-element.44), channel_id=1, source_target_pairs={{0,2},{1,3},{2,0},{3,1},{4,6},{5,7},{6,4},{7,5},{8,10},{9,11},{10,... | collective-permute-start | bytes 9224 | tf_op jit(solution)/shard_map/ppermute | solution.py:26
  103.6 3.1 %collective-permute-start.31 = (f32[384,2]{0,1:T(2,128)S(1)}, f32[384,2]{0,1:T(2,128)S(1)}, u32[]{:S(2)}, u32[]{:S(2)}) collective-permute-start(f32[384,2]{0,1:T(2,128)S(1)} %get-tuple-element.44), channel_id=1, source_target_pairs={{0,3},{1,2},{2,1},{3,0},{4,7},{5,6},{6,5},{7,4},{8,11},{9,10},{10,... | collective-permute-start | bytes 9224 | tf_op jit(solution)/shard_map/ppermute | solution.py:26
  (1 other events, 0.6 us)

commit v5 on v4

--- a/solution.py
+++ b/solution.py
@@ -101,12 +101,14 @@
     heads_axis = lax.axis_size("head")
     matches = targets.shape[0]
     far = [(j, j + 1) for j in range(1, groups - 1, 2)] + [(j, j - 1) for j in range(2, groups, 2)]
-    other = spread_stack(lax.ppermute(mine, "node", far), heads_axis)
+
+    def arrived(piece):
+        return kv_of_piece(spread_stack(piece, heads_axis), w_kv, blocks_here, sub_rows)
+
+    other = arrived(lax.ppermute(mine, "node", far))
     every = jnp.stack(
         [
-            spread_stack(
-                lax.ppermute(mine, "node", [(i, i ^ shift) for i in range(groups)]), heads_axis
-            )
+            arrived(lax.ppermute(mine, "node", [(i, i ^ shift) for i in range(groups)]))
             for shift in range(1, groups)
         ]
     )
@@ -120,7 +122,15 @@
         for match_pos in range(matches)
     ]
     w_parts, matched[0] = lax.optimization_barrier((w_parts, matched[0]))
-    return kv_of_spread([before, after] + matched, w_kv, blocks_here, sub_rows), w_parts
+    return jnp.stack([before, after] + matched), w_parts
+
+
+def kv_of_piece(full, w_kv, blocks_here, sub_rows):
+    heads_axis, _, model_width = full.shape
+    total_rows = heads_axis * blocks_here * sub_rows
+    kv = jnp.dot(full.reshape(total_rows, model_width), w_kv, preferred_element_type=jnp.float32)
+    kv = kv.astype(jnp.bfloat16).reshape(heads_axis, blocks_here, sub_rows, -1)
+    return jnp.transpose(kv, (1, 0, 2, 3)).reshape(total_rows, -1)
 
 
 def spread_stack(piece, heads_axis):

time: 108 us -> 109 us (level)
  waiting for transfers between devices: 22.7 us -> 15.3 us
  other arithmetic: 8.02 us -> 15.3 us
  local copies, waits for them, and re-layouts: 15.6 us -> 13.4 us
  starting transfers between devices: 40.7 us -> 42.5 us
    another operation x1 -> x8, other arithmetic: 0.05 us -> 5.45 us  [spread_stack(): return jnp.stack([slots[k] for k in range(heads_axis)])]
    ppermute x24, waiting for transfers between devices: 17.3 us -> 12.3 us  [flip_heads(): return lax.ppermute(array, 'head', [(i, i ^ flip) for i in range(devices)])]
    another operation x9, other arithmetic: 2.19 us -> 5.9 us  [spread_slots(): other = flip_heads(jnp.stack([slots[k] for k in held]), flip, heads_axis)]
    ppermute x7, waiting for transfers between devices: 5.38 us -> 3.02 us  [static_keys(): lax.ppermute(mine, 'node', [(i, i ^ shift) for i in range(groups)])]
    unnamed x8 -> x0, other arithmetic: 1.89 us -> none
    unnamed x38 -> x50, local copies, waits for them, and re-layouts: 7.75 us -> 5.88 us
    ppermute x1, starting transfers between devices: 3.82 us -> 4.92 us  [static_keys(): other = arrived(lax.ppermute(mine, 'node', far))]
    dot_general x1 -> x8, matrix products: 4.06 us -> 4.84 us  [kv_of_piece(): jnp.dot(full.reshape(total_rows, model_width), w_kv, preferred_element_ty...]
  transfers between devices with their start and end apart: 32 -> 32, of which waited for: 14 -> 9; matrix products, arithmetic and copies ran while one was open for 18% -> 26% of each run, Pallas kernels for 0% -> 0%
where the time goes in v5:
time: 109 us; the launch traced here: 108 us
  starting transfers between devices  42.5 us (39%)
  other arithmetic  15.3 us (14%)
  waiting for transfers between devices  15.3 us (14%)
  local copies, waits for them, and re-layouts  13.4 us (12%)
  Pallas kernels  11.1 us (10%)
  matrix products  7.5 us (7%)
  between operations  3.35 us (3%)
    ppermute x24, starting transfers between devices, flip_heads(): return lax.ppermute(array, 'head', [(i, i ^ flip) for i in range(devices)])  30.1 us
    ppermute x24, waiting for transfers between devices, flip_heads(): return lax.ppermute(array, 'head', [(i, i ^ flip) for i in range(devices)])  12.3 us
    pallas_call x1, Pallas kernels, attention(): pl.pallas_call(attention_kernel, out_shape=jax.ShapeDtypeStruct(query.sha...  11.1 us
    ppermute x7, starting transfers between devices, static_keys(): lax.ppermute(mine, 'node', [(i, i ^ shift) for i in range(groups)])  7.47 us
    another operation x9, other arithmetic, spread_slots(): other = flip_heads(jnp.stack([slots[k] for k in held]), flip, heads_axis)  5.9 us
    unnamed x50, local copies, waits for them, and re-layouts  5.88 us
    another operation x8, other arithmetic, spread_stack(): return jnp.stack([slots[k] for k in range(heads_axis)])  5.45 us
    ppermute x1, starting transfers between devices, static_keys(): other = arrived(lax.ppermute(mine, 'node', far))  4.92 us
  transfers between devices with their start and end apart: 32, of which 9 were waited for; matrix products, arithmetic and copies ran while one was open for 26% of the time, Pallas kernels for 0%

profile of v5, /device:TPU:9, one launch (start us, length us, event | category | flops | bytes accessed | tf_op | source)
XLA Modules:
  0.0 108.4 jit_solution(7348833825253660078)
XLA Ops:
  0.0 1.1 %copy-done = bf16[384,1024]{1,0:T(8,128)(2,1)S(1)} copy-done((bf16[384,1024]{1,0:T(8,128)(2,1)S(1)}, bf16[384,1024]{1,0:T(8,128)(2,1)}, u32[]{:S(2)}) %copy-start) | copy-done | bytes 786456
  1.8 1.2 %collective-permute-start = (bf16[96,1024]{1,0:T(8,128)(2,1)}, bf16[96,1024]{1,0:T(8,128)(2,1)}, u32[]{:S(2)}, u32[]{:S(2)}) collective-permute-start(bf16[96,1024]{1,0:T(8,128)(2,1)} %bitcast.3), channel_id=1, source_target_pairs={{0,4},{4,0},{8,12},{12,8},{16,20},{20,16},{24,28},{28,24},{1,5},{5... | collective-permute-start | bytes 589832 | tf_op jit(solution)/shard_map/ppermute | solution.py:111
  3.2 1.2 %collective-permute-start.12 = (bf16[96,1024]{1,0:T(8,128)(2,1)}, bf16[96,1024]{1,0:T(8,128)(2,1)}, u32[]{:S(2)}, u32[]{:S(2)}) collective-permute-start(bf16[96,1024]{1,0:T(8,128)(2,1)} %bitcast.3), channel_id=1, source_target_pairs={{0,12},{4,8},{8,4},{12,0},{16,28},{20,24},{24,20},{28,16},{1,13},{... | collective-permute-start | bytes 589832 | tf_op jit(solution)/shard_map/ppermute | solution.py:111
  4.5 2.3 %collective-permute-start.15 = (bf16[96,1024]{1,0:T(8,128)(2,1)}, bf16[96,1024]{1,0:T(8,128)(2,1)}, u32[]{:S(2)}, u32[]{:S(2)}) collective-permute-start(bf16[96,1024]{1,0:T(8,128)(2,1)} %bitcast.3), channel_id=1, source_target_pairs={{0,16},{4,20},{8,24},{12,28},{16,0},{20,4},{24,8},{28,12},{1,17},{... | collective-permute-start | bytes 589832 | tf_op jit(solution)/shard_map/ppermute | solution.py:111
  6.8 1.0 collective-permute-start.18
  7.8 0.8 divide_reduce_fusion
  8.6 0.8 fusion.19
  9.4 1.3 %add_select_fusion.pick_ref = s32[4,3]{1,0:T(4,128)} fusion(s32[4,3]{1,0:T(4,128)} %param.13), kind=kLoop, calls=%fused_computation.66 | loop fusion | flops 72 | bytes 96 | tf_op jit(solution)/shard_map/jit(remainder)/select_n | solution.py:274
  10.7 2.2 %convolution_convert_fusion = bf16[384,3,256]{2,0,1:T(8,128)(2,1)S(1)} fusion(bf16[1024,3,256]{2,0,1:T(8,128)(2,1)} %param.8, bf16[384,1024]{1,0:T(8,128)(2,1)S(1)} %copy-done), kind=kOutput, calls=%fused_computation | convolution fusion | flops 604274688 | bytes 2949120 | tf_op jit(solution)/shard_map/nd,dtf->ntf/dot_general | solution.py:253
  18.2 1.3 %collective-permute-start.1 = (bf16[1,96,1024]{2,1,0:T(8,128)(2,1)}, bf16[1,96,1024]{2,1,0:T(8,128)(2,1)S(1)}, u32[]{:S(2)}, u32[]{:S(2)}) collective-permute-start(bf16[1,96,1024]{2,1,0:T(8,128)(2,1)} %bitcast.4), channel_id=1, source_target_pairs={{0,2},{1,3},{2,0},{3,1},{4,6},{5,7},{6,4},{7,5},{8,10},{9,11},{10,... | collective-permute-start | bytes 589832 | tf_op jit(solution)/shard_map/ppermute | solution.py:26
  19.5 1.1 %constant_dynamic-slice_fusion.3 = (bf16[256,256]{1,0:T(8,128)(2,1)S(1)}, bf16[256,256]{1,0:T(8,128)(2,1)S(1)}, bf16[256,256]{1,0:T(8,128)(2,1)S(1)}, bf16[256,256]{1,0:T(8,128)(2,1)S(1)}) fusion(bf16[256,1024]{1,0:T(8,128)(2,1)} %param.9, s32[]{:T(128)S(6)} %select_n.85, s32[]{:T(128)S(6)} %select_n.84, s32[]{:T(128)S(6)} %select_n.83, s32[]{:T(128)S(6)} %select_n.74), kind=kLoop, calls=%fused_computation.72 | loop fusion | bytes 1048592 | tf_op jit(solution)/shard_map/dynamic_slice | solution.py:247
  21.4 0.8 copy.43
  22.1 0.8 copy.44
  22.9 0.8 copy.41
  24.1 1.0 reshape_reshape.3.own_ref
  25.9 1.3 %collective-permute-start.21 = (bf16[96,1024]{1,0:T(8,128)(2,1)}, bf16[96,1024]{1,0:T(8,128)(2,1)S(1)}, u32[]{:S(2)}, u32[]{:S(2)}) collective-permute-start(bf16[96,1024]{1,0:T(8,128)(2,1)} %bitcast.3), channel_id=1, source_target_pairs={{0,24},{4,28},{8,16},{12,20},{16,8},{20,12},{24,0},{28,4},{1,25},{... | collective-permute-start | bytes 589832 | tf_op jit(solution)/shard_map/ppermute | solution.py:111
  27.2 1.2 %collective-permute-start.13 = (bf16[1,96,1024]{2,1,0:T(8,128)(2,1)}, bf16[1,96,1024]{2,1,0:T(8,128)(2,1)S(1)}, u32[]{:S(2)}, u32[]{:S(2)}) collective-permute-start(bf16[1,96,1024]{2,1,0:T(8,128)(2,1)} %bitcast.21), channel_id=1, source_target_pairs={{0,2},{1,3},{2,0},{3,1},{4,6},{5,7},{6,4},{7,5},{8,10},{9,11},{10,... | collective-permute-start | bytes 589832 | tf_op jit(solution)/shard_map/ppermute | solution.py:26
  28.4 1.0 pad_maximum_fusion.8
  30.1 1.0 pad_maximum_fusion.10
  31.0 4.9 %collective-permute-start.3 = (bf16[96,1024]{1,0:T(8,128)(2,1)}, bf16[96,1024]{1,0:T(8,128)(2,1)S(1)}, u32[]{:S(2)}, u32[]{:S(2)}) collective-permute-start(bf16[96,1024]{1,0:T(8,128)(2,1)} %bitcast.3), channel_id=1, source_target_pairs={{4,8},{12,16},{20,24},{8,4},{16,12},{24,20},{5,9},{13,17},{21,25},... | collective-permute-start | bytes 589832 | tf_op jit(solution)/shard_map/ppermute | solution.py:108
  36.0 1.3 %collective-permute-start.19 = (bf16[1,96,1024]{2,1,0:T(8,128)(2,1)}, bf16[1,96,1024]{2,1,0:T(8,128)(2,1)S(1)}, u32[]{:S(2)}, u32[]{:S(2)}) collective-permute-start(bf16[1,96,1024]{2,1,0:T(8,128)(2,1)} %bitcast.31), channel_id=1, source_target_pairs={{0,2},{1,3},{2,0},{3,1},{4,6},{5,7},{6,4},{7,5},{8,10},{9,11},{10,... | collective-permute-start | bytes 589832 | tf_op jit(solution)/shard_map/ppermute | solution.py:26
  37.2 1.0 pad_maximum_fusion.11
  38.3 4.8 %collective-permute-start.6 = (bf16[256,256]{0,1:T(8,128)(2,1)}, bf16[256,256]{0,1:T(8,128)(2,1)S(1)}, u32[]{:S(2)}, u32[]{:S(2)}) collective-permute-start(bf16[256,256]{0,1:T(8,128)(2,1)} %copy.42), channel_id=1, source_target_pairs={{0,1},{1,0},{2,3},{3,2},{4,5},{5,4},{6,7},{7,6},{8,9},{9,8},{10,11... | collective-permute-start | bytes 393224 | tf_op jit(solution)/shard_map/ppermute | solution.py:26
  43.1 2.9 %collective-permute-done.24 = bf16[96,1024]{1,0:T(8,128)(2,1)S(1)} collective-permute-done((bf16[96,1024]{1,0:T(8,128)(2,1)}, bf16[96,1024]{1,0:T(8,128)(2,1)S(1)}, u32[]{:S(2)}, u32[]{:S(2)}) %collective-permute-start.24) | collective-permute-done | bytes 196640 | tf_op jit(solution)/shard_map/ppermute | solution.py:111
  46.1 0.9 collective-permute-start.22
  47.5 1.0 pad_maximum_fusion.12
  48.5 2.7 %collective-permute-start.2 = (bf16[2,96,1024]{2,1,0:T(8,128)(2,1)S(1)}, bf16[2,96,1024]{2,1,0:T(8,128)(2,1)S(1)}, u32[]{:S(2)}, u32[]{:S(2)}) collective-permute-start(bf16[2,96,1024]{2,1,0:T(8,128)(2,1)S(1)} %pad_maximum_fusion.8), channel_id=1, source_target_pairs={{0,1},{1,0},{2,3},{3,2},{4,5},{5,4},{6,7},{7,6},{8,9},{9,8},{10,11... | collective-permute-start | bytes 1179656 | tf_op jit(solution)/shard_map/ppermute | solution.py:26
  51.2 1.0 pad_maximum_fusion.13
  52.2 1.2 %collective-permute-start.7 = (bf16[256,256]{0,1:T(8,128)(2,1)}, bf16[256,256]{0,1:T(8,128)(2,1)S(1)}, u32[]{:S(2)}, u32[]{:S(2)}) collective-permute-start(bf16[256,256]{0,1:T(8,128)(2,1)} %copy.43), channel_id=1, source_target_pairs={{0,2},{1,3},{2,0},{3,1},{4,6},{5,7},{6,4},{7,5},{8,10},{9,11},{10,... | collective-permute-start | bytes 393224 | tf_op jit(solution)/shard_map/ppermute | solution.py:26
  54.6 5.5 %collective-permute-start.8 = (bf16[256,256]{0,1:T(8,128)(2,1)S(1)}, bf16[256,256]{0,1:T(8,128)(2,1)S(1)}, u32[]{:S(2)}, u32[]{:S(2)}) collective-permute-start(bf16[256,256]{0,1:T(8,128)(2,1)S(1)} %copy-done.6), channel_id=1, source_target_pairs={{0,3},{1,2},{2,1},{3,0},{4,7},{5,6},{6,5},{7,4},{8,11},{9,10},{10,... | collective-permute-start | bytes 393224 | tf_op jit(solution)/shard_map/ppermute | solution.py:26
  60.1 2.2 %collective-permute-done.4 = bf16[1,96,1024]{2,1,0:T(8,128)(2,1)S(1)} collective-permute-done((bf16[1,96,1024]{2,1,0:T(8,128)(2,1)S(1)}, bf16[1,96,1024]{2,1,0:T(8,128)(2,1)S(1)}, u32[]{:S(2)}, u32[]{:S(2)}) %collective-permute-start.4) | collective-permute-done | bytes 196640 | tf_op jit(solution)/shard_map/ppermute | solution.py:26
  62.3 3.7 %collective-permute-start.11 = (bf16[2,96,1024]{2,1,0:T(8,128)(2,1)S(1)}, bf16[2,96,1024]{2,1,0:T(8,128)(2,1)S(1)}, u32[]{:S(2)}, u32[]{:S(2)}) collective-permute-start(bf16[2,96,1024]{2,1,0:T(8,128)(2,1)S(1)} %pad_maximum_fusion.10), channel_id=1, source_target_pairs={{0,1},{1,0},{2,3},{3,2},{4,5},{5,4},{6,7},{7,6},{8,9},{9,8},{10,11... | collective-permute-start | bytes 1179656 | tf_op jit(solution)/shard_map/ppermute | solution.py:26
  66.2 1.0 pad_maximum_fusion
  68.5 1.0 pad_maximum_fusion.2
  70.3 1.0 pad_maximum_fusion.3
  72.5 1.0 pad_maximum_fusion.4
  74.4 1.0 pad_maximum_fusion.5
  79.7 1.4 %copy-done.7 = bf16[6,3,128,512]{3,2,1,0:T(8,128)(2,1)} copy-done((bf16[6,3,128,512]{3,2,1,0:T(8,128)(2,1)}, bf16[6,3,128,512]{3,2,1,0:T(8,128)(2,1)S(1)}, u32[]{:S(2)}) %copy-start.7) | copy-done | bytes 2359320
  81.1 11.1 %shard_map.73 = bf16[3,128,256]{2,1,0:T(8,128)(2,1)} custom-call(s32[3,11]{1,0:T(4,128)} %pad_convert_fusion.live_ref, s32[4,3]{1,0:T(4,128)} %add_select_fusion.pick_ref, bf16[3,128,256]{2,1,0:T(8,128)(2,1)} %bitcast.148, bf16[3,128,512]{2,1,0:T(8,128)(2,1)} %reshape_reshape.3.own_ref, bf16[6,3,128,512]{3,2,1,0:T(8,128)(2,1)} %copy-done.7), custom_call_target="tpu_custom_call" | custom-call | flops 1107296256 | bytes 3145728 | tf_op jit(solution)/shard_map/pallas_call | solution.py:219
  92.3 0.9 collective-permute-start.27
  93.2 5.8 %collective-permute-done.27 = bf16[1,384,256]{2,1,0:T(8,128)(2,1)S(1)} collective-permute-done((bf16[1,384,256]{2,1,0:T(8,128)(2,1)}, bf16[1,384,256]{2,1,0:T(8,128)(2,1)S(1)}, u32[]{:S(2)}, u32[]{:S(2)}) %collective-permute-start.27) | collective-permute-done | bytes 196640 | tf_op jit(solution)/shard_map/ppermute | solution.py:26
  99.0 1.0 pad_maximum_fusion.16
  99.9 0.9 collective-permute-start.28
  101.0 1.2 %collective-permute-done.28 = bf16[2,384,256]{2,1,0:T(8,128)(2,1)S(1)} collective-permute-done((bf16[2,384,256]{2,1,0:T(8,128)(2,1)S(1)}, bf16[2,384,256]{2,1,0:T(8,128)(2,1)S(1)}, u32[]{:S(2)}, u32[]{:S(2)}) %collective-permute-start.28) | collective-permute-done | bytes 393248 | tf_op jit(solution)/shard_map/ppermute | solution.py:26
  103.3 0.9 collective-permute-start.30
  104.3 0.8 collective-permute-start.31
  105.8 1.5 %collective-permute-done.31 = f32[384,2]{0,1:T(2,128)S(1)} collective-permute-done((f32[384,2]{0,1:T(2,128)S(1)}, f32[384,2]{0,1:T(2,128)S(1)}, u32[]{:S(2)}, u32[]{:S(2)}) %collective-permute-start.31) | collective-permute-done | bytes 3104 | tf_op jit(solution)/shard_map/ppermute | solution.py:26
  107.6 0.8 copy.38
  (147 shorter events, 18.2 us)
Async XLA Ops:
  0.0 1.1 %copy-start = (bf16[384,1024]{1,0:T(8,128)(2,1)S(1)}, bf16[384,1024]{1,0:T(8,128)(2,1)}, u32[]{:S(2)}) copy-start(bf16[384,1024]{1,0:T(8,128)(2,1)} %param.7) | copy-start | bytes 2359300
  0.0 12.9 %copy-start.8 = (s32[3,7]{1,0:T(4,128)S(1)}, s32[3,7]{1,0:T(4,128)}, u32[]{:S(2)}) copy-start(s32[3,7]{1,0:T(4,128)} %param.12) | copy-start | bytes 256
  1.8 16.4 %collective-permute-start = (bf16[96,1024]{1,0:T(8,128)(2,1)}, bf16[96,1024]{1,0:T(8,128)(2,1)}, u32[]{:S(2)}, u32[]{:S(2)}) collective-permute-start(bf16[96,1024]{1,0:T(8,128)(2,1)} %bitcast.3), channel_id=1, source_target_pairs={{0,4},{4,0},{8,12},{12,8},{16,20},{20,16},{24,28},{28,24},{1,5},{5... | collective-permute-start | bytes 589832 | tf_op jit(solution)/shard_map/ppermute | solution.py:111
  3.1 22.0 %collective-permute-start.9 = (bf16[96,1024]{1,0:T(8,128)(2,1)}, bf16[96,1024]{1,0:T(8,128)(2,1)}, u32[]{:S(2)}, u32[]{:S(2)}) collective-permute-start(bf16[96,1024]{1,0:T(8,128)(2,1)} %bitcast.3), channel_id=1, source_target_pairs={{0,8},{4,12},{8,0},{12,4},{16,24},{20,28},{24,16},{28,20},{1,9},{5... | collective-permute-start | bytes 589832 | tf_op jit(solution)/shard_map/ppermute | solution.py:111
  3.2 22.7 %collective-permute-start.12 = (bf16[96,1024]{1,0:T(8,128)(2,1)}, bf16[96,1024]{1,0:T(8,128)(2,1)}, u32[]{:S(2)}, u32[]{:S(2)}) collective-permute-start(bf16[96,1024]{1,0:T(8,128)(2,1)} %bitcast.3), channel_id=1, source_target_pairs={{0,12},{4,8},{8,4},{12,0},{16,28},{20,24},{24,20},{28,16},{1,13},{... | collective-permute-start | bytes 589832 | tf_op jit(solution)/shard_map/ppermute | solution.py:111
  4.5 24.9 %collective-permute-start.15 = (bf16[96,1024]{1,0:T(8,128)(2,1)}, bf16[96,1024]{1,0:T(8,128)(2,1)}, u32[]{:S(2)}, u32[]{:S(2)}) collective-permute-start(bf16[96,1024]{1,0:T(8,128)(2,1)} %bitcast.3), channel_id=1, source_target_pairs={{0,16},{4,20},{8,24},{12,28},{16,0},{20,4},{24,8},{28,12},{1,17},{... | collective-permute-start | bytes 589832 | tf_op jit(solution)/shard_map/ppermute | solution.py:111
  6.8 24.2 %collective-permute-start.18 = (bf16[96,1024]{1,0:T(8,128)(2,1)}, bf16[96,1024]{1,0:T(8,128)(2,1)}, u32[]{:S(2)}, u32[]{:S(2)}) collective-permute-start(bf16[96,1024]{1,0:T(8,128)(2,1)} %bitcast.3), channel_id=1, source_target_pairs={{0,20},{4,16},{8,28},{12,24},{16,4},{20,0},{24,12},{28,8},{1,21},{... | collective-permute-start | bytes 589832 | tf_op jit(solution)/shard_map/ppermute | solution.py:111
  12.9 2.1 %copy-start.1 = (bf16[384,3,256]{2,0,1:T(8,128)(2,1)}, bf16[384,3,256]{2,0,1:T(8,128)(2,1)S(1)}, u32[]{:S(2)}) copy-start(bf16[384,3,256]{2,0,1:T(8,128)(2,1)S(1)} %convolution_convert_fusion) | copy-start | bytes 1769476
  12.9 1.5 %slice-start = ((bf16[1024,3,256]{2,0,1:T(8,128)(2,1)}), bf16[1024,2,256]{2,0,1:T(8,128)(2,1)S(1)}, s32[]{:S(2)}) async-start(bf16[1024,3,256]{2,0,1:T(8,128)(2,1)} %param.8), calls=%async_computation | async-start | bytes 2097152 | tf_op jit(solution)/shard_map/slice | solution.py:262
  15.6 8.0 %slice-start.1 = ((bf16[384,3,256]{2,0,1:T(8,128)(2,1)}), bf16[384,2,256]{2,0,1:T(8,128)(2,1)S(1)}, s32[]{:S(2)}) async-start(bf16[384,3,256]{2,0,1:T(8,128)(2,1)} %copy-done.1), calls=%async_computation.1 | async-start | bytes 786432 | tf_op jit(solution)/shard_map/slice | solution.py:257
  18.2 9.0 %collective-permute-start.1 = (bf16[1,96,1024]{2,1,0:T(8,128)(2,1)}, bf16[1,96,1024]{2,1,0:T(8,128)(2,1)S(1)}, u32[]{:S(2)}, u32[]{:S(2)}) collective-permute-start(bf16[1,96,1024]{2,1,0:T(8,128)(2,1)} %bitcast.4), channel_id=1, source_target_pairs={{0,2},{1,3},{2,0},{3,1},{4,6},{5,7},{6,4},{7,5},{8,10},{9,11},{10,... | collective-permute-start | bytes 589832 | tf_op jit(solution)/shard_map/ppermute | solution.py:26
  25.1 4.7 %collective-permute-start.10 = (bf16[1,96,1024]{2,1,0:T(8,128)(2,1)}, bf16[1,96,1024]{2,1,0:T(8,128)(2,1)S(1)}, u32[]{:S(2)}, u32[]{:S(2)}) collective-permute-start(bf16[1,96,1024]{2,1,0:T(8,128)(2,1)} %bitcast.16), channel_id=1, source_target_pairs={{0,2},{1,3},{2,0},{3,1},{4,6},{5,7},{6,4},{7,5},{8,10},{9,11},{10,... | collective-permute-start | bytes 589832 | tf_op jit(solution)/shard_map/ppermute | solution.py:26
  25.9 12.4 %collective-permute-start.21 = (bf16[96,1024]{1,0:T(8,128)(2,1)}, bf16[96,1024]{1,0:T(8,128)(2,1)S(1)}, u32[]{:S(2)}, u32[]{:S(2)}) collective-permute-start(bf16[96,1024]{1,0:T(8,128)(2,1)} %bitcast.3), channel_id=1, source_target_pairs={{0,24},{4,28},{8,16},{12,20},{16,8},{20,12},{24,0},{28,4},{1,25},{... | collective-permute-start | bytes 589832 | tf_op jit(solution)/shard_map/ppermute | solution.py:111
  27.2 26.3 %copy-start.2 = (bf16[1,96,1024]{2,1,0:T(8,128)(2,1)}, bf16[1,96,1024]{2,1,0:T(8,128)(2,1)S(1)}, u32[]{:S(2)}) copy-start(bf16[1,96,1024]{2,1,0:T(8,128)(2,1)S(1)} %collective-permute-done.1) | copy-start | bytes 589828
  27.2 27.4 %copy-start.6 = (bf16[256,256]{0,1:T(8,128)(2,1)S(1)}, bf16[256,256]{0,1:T(8,128)(2,1)}, u32[]{:S(2)}) copy-start(bf16[256,256]{0,1:T(8,128)(2,1)} %copy.44) | copy-start | bytes 393220
  27.2 8.8 %collective-permute-start.13 = (bf16[1,96,1024]{2,1,0:T(8,128)(2,1)}, bf16[1,96,1024]{2,1,0:T(8,128)(2,1)S(1)}, u32[]{:S(2)}, u32[]{:S(2)}) collective-permute-start(bf16[1,96,1024]{2,1,0:T(8,128)(2,1)} %bitcast.21), channel_id=1, source_target_pairs={{0,2},{1,3},{2,0},{3,1},{4,6},{5,7},{6,4},{7,5},{8,10},{9,11},{10,... | collective-permute-start | bytes 589832 | tf_op jit(solution)/shard_map/ppermute | solution.py:26
  29.4 16.7 %collective-permute-start.24 = (bf16[96,1024]{1,0:T(8,128)(2,1)}, bf16[96,1024]{1,0:T(8,128)(2,1)S(1)}, u32[]{:S(2)}, u32[]{:S(2)}) collective-permute-start(bf16[96,1024]{1,0:T(8,128)(2,1)} %bitcast.3), channel_id=1, source_target_pairs={{0,28},{4,24},{8,20},{12,16},{16,12},{20,8},{24,4},{28,0},{1,29},{... | collective-permute-start | bytes 589832 | tf_op jit(solution)/shard_map/ppermute | solution.py:111
  29.8 17.2 %collective-permute-start.16 = (bf16[1,96,1024]{2,1,0:T(8,128)(2,1)}, bf16[1,96,1024]{2,1,0:T(8,128)(2,1)S(1)}, u32[]{:S(2)}, u32[]{:S(2)}) collective-permute-start(bf16[1,96,1024]{2,1,0:T(8,128)(2,1)} %bitcast.26), channel_id=1, source_target_pairs={{0,2},{1,3},{2,0},{3,1},{4,6},{5,7},{6,4},{7,5},{8,10},{9,11},{10,... | collective-permute-start | bytes 589832 | tf_op jit(solution)/shard_map/ppermute | solution.py:26
  31.0 21.2 %collective-permute-start.3 = (bf16[96,1024]{1,0:T(8,128)(2,1)}, bf16[96,1024]{1,0:T(8,128)(2,1)S(1)}, u32[]{:S(2)}, u32[]{:S(2)}) collective-permute-start(bf16[96,1024]{1,0:T(8,128)(2,1)} %bitcast.3), channel_id=1, source_target_pairs={{4,8},{12,16},{20,24},{8,4},{16,12},{24,20},{5,9},{13,17},{21,25},... | collective-permute-start | bytes 589832 | tf_op jit(solution)/shard_map/ppermute | solution.py:108
  36.0 12.5 %collective-permute-start.19 = (bf16[1,96,1024]{2,1,0:T(8,128)(2,1)}, bf16[1,96,1024]{2,1,0:T(8,128)(2,1)S(1)}, u32[]{:S(2)}, u32[]{:S(2)}) collective-permute-start(bf16[1,96,1024]{2,1,0:T(8,128)(2,1)} %bitcast.31), channel_id=1, source_target_pairs={{0,2},{1,3},{2,0},{3,1},{4,6},{5,7},{6,4},{7,5},{8,10},{9,11},{10,... | collective-permute-start | bytes 589832 | tf_op jit(solution)/shard_map/ppermute | solution.py:26
  38.3 40.3 %collective-permute-start.6 = (bf16[256,256]{0,1:T(8,128)(2,1)}, bf16[256,256]{0,1:T(8,128)(2,1)S(1)}, u32[]{:S(2)}, u32[]{:S(2)}) collective-permute-start(bf16[256,256]{0,1:T(8,128)(2,1)} %copy.42), channel_id=1, source_target_pairs={{0,1},{1,0},{2,3},{3,2},{4,5},{5,4},{6,7},{7,6},{8,9},{9,8},{10,11... | collective-permute-start | bytes 393224 | tf_op jit(solution)/shard_map/ppermute | solution.py:26
  46.1 7.4 %collective-permute-start.22 = (bf16[1,96,1024]{2,1,0:T(8,128)(2,1)S(1)}, bf16[1,96,1024]{2,1,0:T(8,128)(2,1)S(1)}, u32[]{:S(2)}, u32[]{:S(2)}) collective-permute-start(bf16[1,96,1024]{2,1,0:T(8,128)(2,1)S(1)} %bitcast.138), channel_id=1, source_target_pairs={{0,2},{1,3},{2,0},{3,1},{4,6},{5,7},{6,4},{7,5},{8,10},{9,11},{10,... | collective-permute-start | bytes 589832 | tf_op jit(solution)/shard_map/ppermute | solution.py:26
  47.0 7.6 %collective-permute-start.25 = (bf16[1,96,1024]{2,1,0:T(8,128)(2,1)S(1)}, bf16[1,96,1024]{2,1,0:T(8,128)(2,1)S(1)}, u32[]{:S(2)}, u32[]{:S(2)}) collective-permute-start(bf16[1,96,1024]{2,1,0:T(8,128)(2,1)S(1)} %bitcast.135), channel_id=1, source_target_pairs={{0,2},{1,3},{2,0},{3,1},{4,6},{5,7},{6,4},{7,5},{8,10},{9,11},{10,... | collective-permute-start | bytes 589832 | tf_op jit(solution)/shard_map/ppermute | solution.py:26
  48.5 17.6 %collective-permute-start.2 = (bf16[2,96,1024]{2,1,0:T(8,128)(2,1)S(1)}, bf16[2,96,1024]{2,1,0:T(8,128)(2,1)S(1)}, u32[]{:S(2)}, u32[]{:S(2)}) collective-permute-start(bf16[2,96,1024]{2,1,0:T(8,128)(2,1)S(1)} %pad_maximum_fusion.8), channel_id=1, source_target_pairs={{0,1},{1,0},{2,3},{3,2},{4,5},{5,4},{6,7},{7,6},{8,9},{9,8},{10,11... | collective-permute-start | bytes 1179656 | tf_op jit(solution)/shard_map/ppermute | solution.py:26
  52.2 26.4 %collective-permute-start.7 = (bf16[256,256]{0,1:T(8,128)(2,1)}, bf16[256,256]{0,1:T(8,128)(2,1)S(1)}, u32[]{:S(2)}, u32[]{:S(2)}) collective-permute-start(bf16[256,256]{0,1:T(8,128)(2,1)} %copy.43), channel_id=1, source_target_pairs={{0,2},{1,3},{2,0},{3,1},{4,6},{5,7},{6,4},{7,5},{8,10},{9,11},{10,... | collective-permute-start | bytes 393224 | tf_op jit(solution)/shard_map/ppermute | solution.py:26
  53.4 12.7 %copy-start.3 = (bf16[1,96,1024]{2,1,0:T(8,128)(2,1)S(1)}, bf16[1,96,1024]{2,1,0:T(8,128)(2,1)}, u32[]{:S(2)}) copy-start(bf16[1,96,1024]{2,1,0:T(8,128)(2,1)} %copy-done.2) | copy-start | bytes 589828
  53.4 8.8 %collective-permute-start.4 = (bf16[1,96,1024]{2,1,0:T(8,128)(2,1)S(1)}, bf16[1,96,1024]{2,1,0:T(8,128)(2,1)S(1)}, u32[]{:S(2)}, u32[]{:S(2)}) collective-permute-start(bf16[1,96,1024]{2,1,0:T(8,128)(2,1)S(1)} %bitcast.132), channel_id=1, source_target_pairs={{0,2},{1,3},{2,0},{3,1},{4,6},{5,7},{6,4},{7,5},{8,10},{9,11},{10,... | collective-permute-start | bytes 589832 | tf_op jit(solution)/shard_map/ppermute | solution.py:26
  54.6 24.0 %collective-permute-start.8 = (bf16[256,256]{0,1:T(8,128)(2,1)S(1)}, bf16[256,256]{0,1:T(8,128)(2,1)S(1)}, u32[]{:S(2)}, u32[]{:S(2)}) collective-permute-start(bf16[256,256]{0,1:T(8,128)(2,1)S(1)} %copy-done.6), channel_id=1, source_target_pairs={{0,3},{1,2},{2,1},{3,0},{4,7},{5,6},{6,5},{7,4},{8,11},{9,10},{10,... | collective-permute-start | bytes 393224 | tf_op jit(solution)/shard_map/ppermute | solution.py:26
  62.3 5.6 %collective-permute-start.11 = (bf16[2,96,1024]{2,1,0:T(8,128)(2,1)S(1)}, bf16[2,96,1024]{2,1,0:T(8,128)(2,1)S(1)}, u32[]{:S(2)}, u32[]{:S(2)}) collective-permute-start(bf16[2,96,1024]{2,1,0:T(8,128)(2,1)S(1)} %pad_maximum_fusion.10), channel_id=1, source_target_pairs={{0,1},{1,0},{2,3},{3,2},{4,5},{5,4},{6,7},{7,6},{8,9},{9,8},{10,11... | collective-permute-start | bytes 1179656 | tf_op jit(solution)/shard_map/ppermute | solution.py:26
  66.1 4.1 %collective-permute-start.14 = (bf16[2,96,1024]{2,1,0:T(8,128)(2,1)S(1)}, bf16[2,96,1024]{2,1,0:T(8,128)(2,1)S(1)}, u32[]{:S(2)}, u32[]{:S(2)}) collective-permute-start(bf16[2,96,1024]{2,1,0:T(8,128)(2,1)S(1)} %pad_maximum_fusion.11), channel_id=1, source_target_pairs={{0,1},{1,0},{2,3},{3,2},{4,5},{5,4},{6,7},{7,6},{8,9},{9,8},{10,11... | collective-permute-start | bytes 1179656 | tf_op jit(solution)/shard_map/ppermute | solution.py:26
  67.9 4.1 %collective-permute-start.17 = (bf16[2,96,1024]{2,1,0:T(8,128)(2,1)S(1)}, bf16[2,96,1024]{2,1,0:T(8,128)(2,1)S(1)}, u32[]{:S(2)}, u32[]{:S(2)}) collective-permute-start(bf16[2,96,1024]{2,1,0:T(8,128)(2,1)S(1)} %pad_maximum_fusion.12), channel_id=1, source_target_pairs={{0,1},{1,0},{2,3},{3,2},{4,5},{5,4},{6,7},{7,6},{8,9},{9,8},{10,11... | collective-permute-start | bytes 1179656 | tf_op jit(solution)/shard_map/ppermute | solution.py:26
  70.2 4.1 %collective-permute-start.20 = (bf16[2,96,1024]{2,1,0:T(8,128)(2,1)S(1)}, bf16[2,96,1024]{2,1,0:T(8,128)(2,1)S(1)}, u32[]{:S(2)}, u32[]{:S(2)}) collective-permute-start(bf16[2,96,1024]{2,1,0:T(8,128)(2,1)S(1)} %pad_maximum_fusion.13), channel_id=1, source_target_pairs={{0,1},{1,0},{2,3},{3,2},{4,5},{5,4},{6,7},{7,6},{8,9},{9,8},{10,11... | collective-permute-start | bytes 1179656 | tf_op jit(solution)/shard_map/ppermute | solution.py:26
  72.0 4.1 %collective-permute-start.23 = (bf16[2,96,1024]{2,1,0:T(8,128)(2,1)S(1)}, bf16[2,96,1024]{2,1,0:T(8,128)(2,1)S(1)}, u32[]{:S(2)}, u32[]{:S(2)}) collective-permute-start(bf16[2,96,1024]{2,1,0:T(8,128)(2,1)S(1)} %pad_maximum_fusion.14), channel_id=1, source_target_pairs={{0,1},{1,0},{2,3},{3,2},{4,5},{5,4},{6,7},{7,6},{8,9},{9,8},{10,11... | collective-permute-start | bytes 1179656 | tf_op jit(solution)/shard_map/ppermute | solution.py:26
  74.2 3.1 %collective-permute-start.26 = (bf16[2,96,1024]{2,1,0:T(8,128)(2,1)S(1)}, bf16[2,96,1024]{2,1,0:T(8,128)(2,1)S(1)}, u32[]{:S(2)}, u32[]{:S(2)}) collective-permute-start(bf16[2,96,1024]{2,1,0:T(8,128)(2,1)S(1)} %pad_maximum_fusion.15), channel_id=1, source_target_pairs={{0,1},{1,0},{2,3},{3,2},{4,5},{5,4},{6,7},{7,6},{8,9},{9,8},{10,11... | collective-permute-start | bytes 1179656 | tf_op jit(solution)/shard_map/ppermute | solution.py:26
  76.0 2.6 %collective-permute-start.5 = (bf16[2,96,1024]{2,1,0:T(8,128)(2,1)S(1)}, bf16[2,96,1024]{2,1,0:T(8,128)(2,1)S(1)}, u32[]{:S(2)}, u32[]{:S(2)}) collective-permute-start(bf16[2,96,1024]{2,1,0:T(8,128)(2,1)S(1)} %pad_maximum_fusion.9), channel_id=1, source_target_pairs={{0,1},{1,0},{2,3},{3,2},{4,5},{5,4},{6,7},{7,6},{8,9},{9,8},{10,11... | collective-permute-start | bytes 1179656 | tf_op jit(solution)/shard_map/ppermute | solution.py:26
  79.7 1.4 %copy-start.7 = (bf16[6,3,128,512]{3,2,1,0:T(8,128)(2,1)}, bf16[6,3,128,512]{3,2,1,0:T(8,128)(2,1)S(1)}, u32[]{:S(2)}) copy-start(bf16[6,3,128,512]{3,2,1,0:T(8,128)(2,1)S(1)} %constant_dynamic-update-slice_fusion.7.part_ref) | copy-start | bytes 7077892
  81.1 21.1 %copy-start.5 = (bf16[256,256]{0,1:T(8,128)(2,1)S(1)}, bf16[256,256]{0,1:T(8,128)(2,1)}, u32[]{:S(2)}) copy-start(bf16[256,256]{0,1:T(8,128)(2,1)} %copy.41) | copy-start | bytes 393220
  81.1 21.1 %copy-start.12 = (bf16[256,256]{0,1:T(8,128)(2,1)S(1)}, bf16[256,256]{0,1:T(8,128)(2,1)}, u32[]{:S(2)}) copy-start(bf16[256,256]{0,1:T(8,128)(2,1)} %copy-done.11) | copy-start | bytes 393220
  81.1 21.1 %copy-start.14 = (bf16[256,256]{0,1:T(8,128)(2,1)S(1)}, bf16[256,256]{0,1:T(8,128)(2,1)}, u32[]{:S(2)}) copy-start(bf16[256,256]{0,1:T(8,128)(2,1)} %copy-done.13) | copy-start | bytes 393220
  81.1 21.1 %copy-start.16 = (bf16[256,256]{0,1:T(8,128)(2,1)S(1)}, bf16[256,256]{0,1:T(8,128)(2,1)}, u32[]{:S(2)}) copy-start(bf16[256,256]{0,1:T(8,128)(2,1)} %copy-done.15) | copy-start | bytes 393220
  92.3 10.0 %copy-start.4 = (bf16[3,128,256]{2,1,0:T(8,128)(2,1)S(1)}, bf16[3,128,256]{2,1,0:T(8,128)(2,1)}, u32[]{:S(2)}) copy-start(bf16[3,128,256]{2,1,0:T(8,128)(2,1)} %shard_map.73) | copy-start | bytes 589828
  92.3 6.7 %collective-permute-start.27 = (bf16[1,384,256]{2,1,0:T(8,128)(2,1)}, bf16[1,384,256]{2,1,0:T(8,128)(2,1)S(1)}, u32[]{:S(2)}, u32[]{:S(2)}) collective-permute-start(bf16[1,384,256]{2,1,0:T(8,128)(2,1)} %bitcast.149), channel_id=1, source_target_pairs={{0,2},{1,3},{2,0},{3,1},{4,6},{5,7},{6,4},{7,5},{8,10},{9,11},{10,... | collective-permute-start | bytes 589832 | tf_op jit(solution)/shard_map/ppermute | solution.py:26
  99.9 2.2 %collective-permute-start.28 = (bf16[2,384,256]{2,1,0:T(8,128)(2,1)S(1)}, bf16[2,384,256]{2,1,0:T(8,128)(2,1)S(1)}, u32[]{:S(2)}, u32[]{:S(2)}) collective-permute-start(bf16[2,384,256]{2,1,0:T(8,128)(2,1)S(1)} %pad_maximum_fusion.16), channel_id=1, source_target_pairs={{0,1},{1,0},{2,3},{3,2},{4,5},{5,4},{6,7},{7,6},{8,9},{9,8},{10,11... | collective-permute-start | bytes 1179656 | tf_op jit(solution)/shard_map/ppermute | solution.py:26
  102.2 5.2 %copy-start.9 = (f32[256]{0:T(256)S(1)}, f32[256]{0:T(256)}, u32[]{:S(2)}) copy-start(f32[256]{0:T(256)} %param.11) | copy-start | bytes 3076
  102.3 5.2 %copy-start.10 = (f32[256]{0:T(256)S(1)}, f32[256]{0:T(256)}, u32[]{:S(2)}) copy-start(f32[256]{0:T(256)} %param.10) | copy-start | bytes 3076
  102.9 2.2 %collective-permute-start.29 = (f32[384,2]{0,1:T(2,128)S(1)}, f32[384,2]{0,1:T(2,128)S(1)}, u32[]{:S(2)}, u32[]{:S(2)}) collective-permute-start(f32[384,2]{0,1:T(2,128)S(1)} %get-tuple-element.46), channel_id=1, source_target_pairs={{0,1},{1,0},{2,3},{3,2},{4,5},{5,4},{6,7},{7,6},{8,9},{9,8},{10,11... | collective-permute-start | bytes 9224 | tf_op jit(solution)/shard_map/ppermute | solution.py:26
  103.3 2.4 %collective-permute-start.30 = (f32[384,2]{0,1:T(2,128)S(1)}, f32[384,2]{0,1:T(2,128)S(1)}, u32[]{:S(2)}, u32[]{:S(2)}) collective-permute-start(f32[384,2]{0,1:T(2,128)S(1)} %get-tuple-element.46), channel_id=1, source_target_pairs={{0,2},{1,3},{2,0},{3,1},{4,6},{5,7},{6,4},{7,5},{8,10},{9,11},{10,... | collective-permute-start | bytes 9224 | tf_op jit(solution)/shard_map/ppermute | solution.py:26
  104.3 3.1 %collective-permute-start.31 = (f32[384,2]{0,1:T(2,128)S(1)}, f32[384,2]{0,1:T(2,128)S(1)}, u32[]{:S(2)}, u32[]{:S(2)}) collective-permute-start(f32[384,2]{0,1:T(2,128)S(1)} %get-tuple-element.46), channel_id=1, source_target_pairs={{0,3},{1,2},{2,1},{3,0},{4,7},{5,6},{6,5},{7,4},{8,11},{9,10},{10,... | collective-permute-start | bytes 9224 | tf_op jit(solution)/shard_map/ppermute | solution.py:26
  (3 other events, 2.4 us)

commit v6 on v4

--- a/solution.py
+++ b/solution.py
@@ -1,3 +1,4 @@
+import functools
 import math
 
 import jax
@@ -143,10 +144,9 @@
     return partner_kv.reshape(count, total_rows, w_kv.shape[1])
 
 
-def attention_kernel(live_ref, pick_ref, q_ref, own_ref, part_ref, out_ref, score_ref):
+def attention_kernel(pair, live_ref, pick_ref, q_ref, own_ref, part_ref, out_ref, score_ref):
     blocks_here = q_ref.shape[0]
     head_feats = q_ref.shape[2]
-    pairs = head_feats // LANES
     per_pair = LANES // HEAD_DIM
     window = 2 * REACH + 1
     matches = part_ref.shape[0] - 2
@@ -166,7 +166,7 @@
             match_pos = t - window
             return part_ref[2 + match_pos, pick_ref[match_pos, j], :, cols]
 
-        for pair in range(pairs):
+        for pair in [pair]:
             kcols = pl.ds(pair * LANES, LANES)
             vcols = pl.ds(head_feats + pair * LANES, LANES)
             both = q_ref[j, :, kcols]
@@ -197,18 +197,18 @@
                         probs, key_block(t, vcols), preferred_element_type=jnp.float32
                     )
                 merged = jnp.where(mine, context, merged)
-            out_ref[j, :, kcols] = merged.astype(jnp.bfloat16)
-
-
-def attention(live, pick, query, own, part):
+            out_ref[j] = merged.astype(jnp.bfloat16)
+
+
+def attention(live, pick, query, own, part, pair):
     blocks_here, rows, head_feats = query.shape
     key_blocks = live.shape[1]
     vmem = pltpu.VMEM
-    flops = 8 * blocks_here * rows * key_blocks * rows * head_feats
-    moved = 2 * (query.size * 2 + own.size + part.size)
+    flops = 8 * blocks_here * rows * key_blocks * rows * LANES
+    moved = 2 * (query.size + own.size + part.size) // 2
     return pl.pallas_call(
-        attention_kernel,
-        out_shape=jax.ShapeDtypeStruct(query.shape, jnp.bfloat16),
+        functools.partial(attention_kernel, pair),
+        out_shape=jax.ShapeDtypeStruct((blocks_here, rows, LANES), jnp.bfloat16),
         in_specs=[pl.BlockSpec(memory_space=pltpu.SMEM), pl.BlockSpec(memory_space=pltpu.SMEM),
                   pl.BlockSpec(memory_space=vmem), pl.BlockSpec(memory_space=vmem), pl.BlockSpec(memory_space=vmem)],
         out_specs=pl.BlockSpec(memory_space=vmem),
@@ -259,14 +259,21 @@
         (neighbour >= 0) & (neighbour < all_blocks) & ((offsets[None, :] == 0) | (local_mask == 1))
     )
     block_ok = jnp.concatenate([local_ok, jnp.ones((blocks_here, matches), dtype=bool)], axis=1)
-    context = attention(
-        block_ok.astype(jnp.int32),
-        (matchings % blocks_here).astype(jnp.int32),
-        queries.reshape(blocks_here, ROWS, head_feats),
-        keyvals.reshape(blocks_here, ROWS, 2 * head_feats),
-        part.reshape(part.shape[0], blocks_here, ROWS, 2 * head_feats),
-    ).reshape(total_rows, head_feats)
-    context_slots = spread_slots(context, heads_axis)
+    per_pair = []
+    for pair in range(head_feats // LANES):
+        pair_context = attention(
+            block_ok.astype(jnp.int32),
+            (matchings % blocks_here).astype(jnp.int32),
+            queries.reshape(blocks_here, ROWS, head_feats),
+            keyvals.reshape(blocks_here, ROWS, 2 * head_feats),
+            part.reshape(part.shape[0], blocks_here, ROWS, 2 * head_feats),
+            pair,
+        ).reshape(total_rows, LANES)
+        per_pair.append(spread_slots(pair_context, heads_axis))
+    context_slots = {
+        flip: jnp.concatenate([slots[flip] for slots in per_pair], axis=1)
+        for flip in range(heads_axis)
+    }
     own_cols = lax.dynamic_slice_in_dim(node_states, head_index * out_cols, out_cols, 1)
     mixed_rows = own_cols.astype(jnp.float32) + jnp.einsum(
         "srf,sfo->ro",

time: 108 us -> 108 us (level)
  waiting for transfers between devices: 22.7 us -> 18.4 us
  Pallas kernels: 10.8 us -> 13.7 us
  other arithmetic: 8.02 us -> 10.2 us
  starting transfers between devices: 40.7 us -> 42.3 us
  local copies, waits for them, and re-layouts: 15.6 us -> 14.1 us
  matrix products: 6.75 us -> 5.34 us
    ppermute x7, waiting for transfers between devices: 5.38 us -> 0.02 us  [static_keys(): lax.ppermute(mine, 'node', [(i, i ^ shift) for i in range(groups)])]
    pallas_call x1 -> x2, Pallas kernels: 10.8 us -> 13.7 us  [attention(): pl.pallas_call(functools.partial(attention_kernel, pair), out_shape=jax.S...]
    ppermute x24 -> x26, starting transfers between devices: 29.5 us -> 31.1 us  [flip_heads(): return lax.ppermute(array, 'head', [(i, i ^ flip) for i in range(devices)])]
    dot_general x1, matrix products: 2.2 us -> 0.77 us  [local(): jnp.einsum('nd,dtf->ntf', node_states, w_qkv, preferred_element_type=jnp....]
    unnamed x38 -> x46, local copies, waits for them, and re-layouts: 7.75 us -> 6.35 us
    ppermute x1, starting transfers between devices: 3.82 us -> 2.67 us  [static_keys(): other = spread_stack(lax.ppermute(mine, 'node', far), heads_axis)]
    ppermute x7, starting transfers between devices: 7.44 us -> 8.58 us  [static_keys(): lax.ppermute(mine, 'node', [(i, i ^ shift) for i in range(groups)])]
    ppermute x24 -> x26, waiting for transfers between devices: 17.3 us -> 18.4 us  [flip_heads(): return lax.ppermute(array, 'head', [(i, i ^ flip) for i in range(devices)])]
  transfers between devices with their start and end apart: 32 -> 34, of which waited for: 14 -> 15; matrix products, arithmetic and copies ran while one was open for 18% -> 18% of each run, Pallas kernels for 0% -> 0%
where the time goes in v6:
time: 108 us; the launch traced here: 107 us
  starting transfers between devices  42.3 us (39%)
  waiting for transfers between devices  18.4 us (17%)
  local copies, waits for them, and re-layouts  14.1 us (13%)
  Pallas kernels  13.7 us (13%)
  other arithmetic  10.2 us (9%)
  matrix products  5.34 us (5%)
  between operations  3.13 us (3%)
    ppermute x26, starting transfers between devices, flip_heads(): return lax.ppermute(array, 'head', [(i, i ^ flip) for i in range(devices)])  31.1 us
    ppermute x26, waiting for transfers between devices, flip_heads(): return lax.ppermute(array, 'head', [(i, i ^ flip) for i in range(devices)])  18.4 us
    pallas_call x2, Pallas kernels, attention(): pl.pallas_call(functools.partial(attention_kernel, pair), out_shape=jax.S...  13.7 us
    ppermute x7, starting transfers between devices, static_keys(): lax.ppermute(mine, 'node', [(i, i ^ shift) for i in range(groups)])  8.58 us
    unnamed x46, local copies, waits for them, and re-layouts  6.35 us
    dot_general x1, matrix products, kv_of_spread(): jnp.dot(rows, w_kv, preferred_element_type=jnp.float32).astype(jnp.bfloat16)  4.08 us
    another operation x10, other arithmetic, spread_slots(): other = flip_heads(jnp.stack([slots[k] for k in held]), flip, heads_axis)  3.09 us
    unnamed x8, other arithmetic  2.81 us
  transfers between devices with their start and end apart: 34, of which 15 were waited for; matrix products, arithmetic and copies ran while one was open for 18% of the time, Pallas kernels for 0%

profile of v6, /device:TPU:9, one launch (start us, length us, event | category | flops | bytes accessed | tf_op | source)
XLA Modules:
  0.0 107.2 jit_solution(15457560242455881516)
XLA Ops:
  0.0 1.1 %copy-done = bf16[384,1024]{1,0:T(8,128)(2,1)S(1)} copy-done((bf16[384,1024]{1,0:T(8,128)(2,1)S(1)}, bf16[384,1024]{1,0:T(8,128)(2,1)}, u32[]{:S(2)}) %copy-start) | copy-done | bytes 786456
  1.8 1.2 %collective-permute-start = (bf16[96,1024]{1,0:T(8,128)(2,1)}, bf16[96,1024]{1,0:T(8,128)(2,1)S(1)}, u32[]{:S(2)}, u32[]{:S(2)}) collective-permute-start(bf16[96,1024]{1,0:T(8,128)(2,1)} %bitcast.3), channel_id=1, source_target_pairs={{0,4},{4,0},{8,12},{12,8},{16,20},{20,16},{24,28},{28,24},{1,5},{5... | collective-permute-start | bytes 589832 | tf_op jit(solution)/shard_map/ppermute | solution.py:109
  3.2 1.2 %collective-permute-start.12 = (bf16[96,1024]{1,0:T(8,128)(2,1)}, bf16[96,1024]{1,0:T(8,128)(2,1)}, u32[]{:S(2)}, u32[]{:S(2)}) collective-permute-start(bf16[96,1024]{1,0:T(8,128)(2,1)} %bitcast.3), channel_id=1, source_target_pairs={{0,12},{4,8},{8,4},{12,0},{16,28},{20,24},{24,20},{28,16},{1,13},{... | collective-permute-start | bytes 589832 | tf_op jit(solution)/shard_map/ppermute | solution.py:109
  4.5 2.3 %collective-permute-start.15 = (bf16[96,1024]{1,0:T(8,128)(2,1)}, bf16[96,1024]{1,0:T(8,128)(2,1)S(1)}, u32[]{:S(2)}, u32[]{:S(2)}) collective-permute-start(bf16[96,1024]{1,0:T(8,128)(2,1)} %bitcast.3), channel_id=1, source_target_pairs={{0,16},{4,20},{8,24},{12,28},{16,0},{20,4},{24,8},{28,12},{1,17},{... | collective-permute-start | bytes 589832 | tf_op jit(solution)/shard_map/ppermute | solution.py:109
  6.8 1.0 collective-permute-start.18
  7.8 0.8 divide_reduce_fusion
  8.6 0.8 fusion.26
  14.8 1.1 %constant_dynamic-slice_fusion.3 = (bf16[256,256]{1,0:T(8,128)(2,1)S(1)}, bf16[256,256]{1,0:T(8,128)(2,1)S(1)}, bf16[256,256]{1,0:T(8,128)(2,1)S(1)}, bf16[256,256]{1,0:T(8,128)(2,1)S(1)}) fusion(bf16[256,1024]{1,0:T(8,128)(2,1)} %param.9, s32[]{:T(128)S(6)} %select_n.65, s32[]{:T(128)S(6)} %select_n.64, s32[]{:T(128)S(6)} %select_n.63, s32[]{:T(128)S(6)} %select_n.56), kind=kLoop, calls=%fused_computation.73 | loop fusion | bytes 1048592 | tf_op jit(solution)/shard_map/dynamic_slice | solution.py:237
  19.0 1.3 %copy.39 = bf16[1024,2,256]{0,2,1:T(8,128)(2,1)} copy(bf16[1024,2,256]{2,0,1:T(8,128)(2,1)S(1)} %slice-done) | data formatting | bytes 2097152
  20.7 1.0 reshape_reshape.8.own_ref
  21.7 1.2 %collective-permute-start.1 = (bf16[1,96,1024]{2,1,0:T(8,128)(2,1)S(1)}, bf16[1,96,1024]{2,1,0:T(8,128)(2,1)S(1)}, u32[]{:S(2)}, u32[]{:S(2)}) collective-permute-start(bf16[1,96,1024]{2,1,0:T(8,128)(2,1)S(1)} %bitcast.129), channel_id=1, source_target_pairs={{0,2},{1,3},{2,0},{3,1},{4,6},{5,7},{6,4},{7,5},{8,10},{9,11},{10,... | collective-permute-start | bytes 589832 | tf_op jit(solution)/shard_map/ppermute | solution.py:27
  22.9 0.8 copy.33
  24.6 1.3 %collective-permute-start.21 = (bf16[96,1024]{1,0:T(8,128)(2,1)}, bf16[96,1024]{1,0:T(8,128)(2,1)S(1)}, u32[]{:S(2)}, u32[]{:S(2)}) collective-permute-start(bf16[96,1024]{1,0:T(8,128)(2,1)} %bitcast.3), channel_id=1, source_target_pairs={{0,24},{4,28},{8,16},{12,20},{16,8},{20,12},{24,0},{28,4},{1,25},{... | collective-permute-start | bytes 589832 | tf_op jit(solution)/shard_map/ppermute | solution.py:109
  26.2 1.2 %collective-permute-start.13 = (bf16[1,96,1024]{2,1,0:T(8,128)(2,1)}, bf16[1,96,1024]{2,1,0:T(8,128)(2,1)S(1)}, u32[]{:S(2)}, u32[]{:S(2)}) collective-permute-start(bf16[1,96,1024]{2,1,0:T(8,128)(2,1)} %bitcast.21), channel_id=1, source_target_pairs={{0,2},{1,3},{2,0},{3,1},{4,6},{5,7},{6,4},{7,5},{8,10},{9,11},{10,... | collective-permute-start | bytes 589832 | tf_op jit(solution)/shard_map/ppermute | solution.py:27
  27.5 1.3 %collective-permute-start.24 = (bf16[96,1024]{1,0:T(8,128)(2,1)}, bf16[96,1024]{1,0:T(8,128)(2,1)S(1)}, u32[]{:S(2)}, u32[]{:S(2)}) collective-permute-start(bf16[96,1024]{1,0:T(8,128)(2,1)} %bitcast.3), channel_id=1, source_target_pairs={{0,28},{4,24},{8,20},{12,16},{16,12},{20,8},{24,4},{28,0},{1,29},{... | collective-permute-start | bytes 589832 | tf_op jit(solution)/shard_map/ppermute | solution.py:109
  28.8 1.8 %collective-permute-done.10 = bf16[1,96,1024]{2,1,0:T(8,128)(2,1)S(1)} collective-permute-done((bf16[1,96,1024]{2,1,0:T(8,128)(2,1)}, bf16[1,96,1024]{2,1,0:T(8,128)(2,1)S(1)}, u32[]{:S(2)}, u32[]{:S(2)}) %collective-permute-start.10) | collective-permute-done | bytes 196640 | tf_op jit(solution)/shard_map/ppermute | solution.py:27
  30.6 0.8 collective-permute-start.16
  31.5 1.0 pad_maximum_fusion.4
  32.4 2.7 %collective-permute-start.3 = (bf16[96,1024]{1,0:T(8,128)(2,1)}, bf16[96,1024]{1,0:T(8,128)(2,1)S(1)}, u32[]{:S(2)}, u32[]{:S(2)}) collective-permute-start(bf16[96,1024]{1,0:T(8,128)(2,1)} %bitcast.3), channel_id=1, source_target_pairs={{4,8},{12,16},{20,24},{8,4},{16,12},{24,20},{5,9},{13,17},{21,25},... | collective-permute-start | bytes 589832 | tf_op jit(solution)/shard_map/ppermute | solution.py:105
  35.1 1.3 %collective-permute-start.19 = (bf16[1,96,1024]{2,1,0:T(8,128)(2,1)S(1)}, bf16[1,96,1024]{2,1,0:T(8,128)(2,1)S(1)}, u32[]{:S(2)}, u32[]{:S(2)}) collective-permute-start(bf16[1,96,1024]{2,1,0:T(8,128)(2,1)S(1)} %bitcast.155), channel_id=1, source_target_pairs={{0,2},{1,3},{2,0},{3,1},{4,6},{5,7},{6,4},{7,5},{8,10},{9,11},{10,... | collective-permute-start | bytes 589832 | tf_op jit(solution)/shard_map/ppermute | solution.py:27
  36.4 1.0 pad_maximum_fusion.5
  37.4 6.9 %collective-permute-start.6 = (bf16[256,256]{0,1:T(8,128)(2,1)}, bf16[256,256]{0,1:T(8,128)(2,1)S(1)}, u32[]{:S(2)}, u32[]{:S(2)}) collective-permute-start(bf16[256,256]{0,1:T(8,128)(2,1)} %copy.36), channel_id=1, source_target_pairs={{0,1},{1,0},{2,3},{3,2},{4,5},{5,4},{6,7},{7,6},{8,9},{9,8},{10,11... | collective-permute-start | bytes 393224 | tf_op jit(solution)/shard_map/ppermute | solution.py:27
  44.5 1.2 %collective-permute-start.25 = (bf16[1,96,1024]{2,1,0:T(8,128)(2,1)S(1)}, bf16[1,96,1024]{2,1,0:T(8,128)(2,1)S(1)}, u32[]{:S(2)}, u32[]{:S(2)}) collective-permute-start(bf16[1,96,1024]{2,1,0:T(8,128)(2,1)S(1)} %bitcast.164), channel_id=1, source_target_pairs={{0,2},{1,3},{2,0},{3,1},{4,6},{5,7},{6,4},{7,5},{8,10},{9,11},{10,... | collective-permute-start | bytes 589832 | tf_op jit(solution)/shard_map/ppermute | solution.py:27
  45.8 1.6 %collective-permute-start.2 = (bf16[2,96,1024]{2,1,0:T(8,128)(2,1)S(1)}, bf16[2,96,1024]{2,1,0:T(8,128)(2,1)S(1)}, u32[]{:S(2)}, u32[]{:S(2)}) collective-permute-start(bf16[2,96,1024]{2,1,0:T(8,128)(2,1)S(1)} %pad_maximum_fusion.2), channel_id=1, source_target_pairs={{0,1},{1,0},{2,3},{3,2},{4,5},{5,4},{6,7},{7,6},{8,9},{9,8},{10,11... | collective-permute-start | bytes 1179656 | tf_op jit(solution)/shard_map/ppermute | solution.py:27
  47.4 2.3 %collective-permute-start.7 = (bf16[256,256]{0,1:T(8,128)(2,1)S(1)}, bf16[256,256]{0,1:T(8,128)(2,1)S(1)}, u32[]{:S(2)}, u32[]{:S(2)}) collective-permute-start(bf16[256,256]{0,1:T(8,128)(2,1)S(1)} %copy-done.8), channel_id=1, source_target_pairs={{0,2},{1,3},{2,0},{3,1},{4,6},{5,7},{6,4},{7,5},{8,10},{9,11},{10,... | collective-permute-start | bytes 393224 | tf_op jit(solution)/shard_map/ppermute | solution.py:27
  50.6 3.5 %collective-permute-done.25 = bf16[1,96,1024]{2,1,0:T(8,128)(2,1)S(1)} collective-permute-done((bf16[1,96,1024]{2,1,0:T(8,128)(2,1)S(1)}, bf16[1,96,1024]{2,1,0:T(8,128)(2,1)S(1)}, u32[]{:S(2)}, u32[]{:S(2)}) %collective-permute-start.25) | collective-permute-done | bytes 196640 | tf_op jit(solution)/shard_map/ppermute | solution.py:27
  54.0 3.1 %collective-permute-start.11 = (bf16[2,96,1024]{2,1,0:T(8,128)(2,1)S(1)}, bf16[2,96,1024]{2,1,0:T(8,128)(2,1)S(1)}, u32[]{:S(2)}, u32[]{:S(2)}) collective-permute-start(bf16[2,96,1024]{2,1,0:T(8,128)(2,1)S(1)} %pad_maximum_fusion.4), channel_id=1, source_target_pairs={{0,1},{1,0},{2,3},{3,2},{4,5},{5,4},{6,7},{7,6},{8,9},{9,8},{10,11... | collective-permute-start | bytes 1179656 | tf_op jit(solution)/shard_map/ppermute | solution.py:27
  57.1 3.9 %collective-permute-done.4 = bf16[1,96,1024]{2,1,0:T(8,128)(2,1)S(1)} collective-permute-done((bf16[1,96,1024]{2,1,0:T(8,128)(2,1)S(1)}, bf16[1,96,1024]{2,1,0:T(8,128)(2,1)S(1)}, u32[]{:S(2)}, u32[]{:S(2)}) %collective-permute-start.4) | collective-permute-done | bytes 196640 | tf_op jit(solution)/shard_map/ppermute | solution.py:27
  61.0 2.9 %collective-permute-start.8 = (bf16[256,256]{0,1:T(8,128)(2,1)S(1)}, bf16[256,256]{0,1:T(8,128)(2,1)S(1)}, u32[]{:S(2)}, u32[]{:S(2)}) collective-permute-start(bf16[256,256]{0,1:T(8,128)(2,1)S(1)} %copy-done.7), channel_id=1, source_target_pairs={{0,3},{1,2},{2,1},{3,0},{4,7},{5,6},{6,5},{7,4},{8,11},{9,10},{10,... | collective-permute-start | bytes 393224 | tf_op jit(solution)/shard_map/ppermute | solution.py:27
  64.7 1.1 %collective-permute-done.14 = bf16[2,96,1024]{2,1,0:T(8,128)(2,1)S(1)} collective-permute-done((bf16[2,96,1024]{2,1,0:T(8,128)(2,1)S(1)}, bf16[2,96,1024]{2,1,0:T(8,128)(2,1)S(1)}, u32[]{:S(2)}, u32[]{:S(2)}) %collective-permute-start.14) | collective-permute-done | bytes 393248 | tf_op jit(solution)/shard_map/ppermute | solution.py:27
  66.5 1.0 collective-permute-done.20
  68.2 1.0 collective-permute-done.26
  69.3 1.0 fusion.2
  70.3 1.0 fusion.3
  73.2 0.9 copy.30
  74.4 4.1 %convolution_convert_fusion = bf16[2304,512]{1,0:T(8,128)(2,1)} fusion(bf16[2304,1024]{1,0:T(8,128)(2,1)S(1)} %bitcast.128, bf16[1024,512]{0,1:T(8,128)(2,1)S(1)} %bitcast.154), kind=kOutput, calls=%fused_computation | convolution fusion | flops 2417098752 | bytes 8126464 | tf_op jit(solution)/shard_map/dot_general | solution.py:143
  78.5 6.8 %shard_map.73 = bf16[3,128,128]{2,1,0:T(8,128)(2,1)} custom-call(s32[3,11]{1,0:T(4,128)} %pad_convert_fusion.live_ref, s32[4,3]{1,0:T(4,128)} %add_select_fusion.pick_ref, bf16[3,128,256]{2,1,0:T(8,128)(2,1)} %bitcast.175, bf16[3,128,512]{2,1,0:T(8,128)(2,1)} %reshape_reshape.8.own_ref, bf16[6,3,128,512]{3,2,1,0:T(8,128)(2,1)} %bitcast.184), custom_call_target="tpu_custom_call" | custom-call | flops 553648128 | bytes 1474560 | tf_op jit(solution)/shard_map/pallas_call | solution.py:209
  85.3 6.8 %shard_map.74 = bf16[3,128,128]{2,1,0:T(8,128)(2,1)} custom-call(s32[3,11]{1,0:T(4,128)} %pad_convert_fusion.live_ref, s32[4,3]{1,0:T(4,128)} %add_select_fusion.pick_ref, bf16[3,128,256]{2,1,0:T(8,128)(2,1)} %bitcast.176, bf16[3,128,512]{2,1,0:T(8,128)(2,1)} %reshape_reshape.8.own_ref, bf16[6,3,128,512]{3,2,1,0:T(8,128)(2,1)} %bitcast.185), custom_call_target="tpu_custom_call" | custom-call | flops 553648128 | bytes 1474560 | tf_op jit(solution)/shard_map/pallas_call | solution.py:209
  92.4 1.2 %collective-permute-start.29 = (bf16[1,384,128]{2,1,0:T(8,128)(2,1)}, bf16[1,384,128]{2,1,0:T(8,128)(2,1)S(1)}, u32[]{:S(2)}, u32[]{:S(2)}) collective-permute-start(bf16[1,384,128]{2,1,0:T(8,128)(2,1)} %bitcast.167), channel_id=1, source_target_pairs={{0,2},{1,3},{2,0},{3,1},{4,6},{5,7},{6,4},{7,5},{8,10},{9,11},{10,... | collective-permute-start | bytes 294920 | tf_op jit(solution)/shard_map/ppermute | solution.py:27
  93.7 1.0 maximum_bitcast_fusion.7
  94.7 1.8 %collective-permute-done.27 = bf16[1,384,128]{2,1,0:T(8,128)(2,1)S(1)} collective-permute-done((bf16[1,384,128]{2,1,0:T(8,128)(2,1)S(1)}, bf16[1,384,128]{2,1,0:T(8,128)(2,1)S(1)}, u32[]{:S(2)}, u32[]{:S(2)}) %collective-permute-start.27) | collective-permute-done | bytes 98336 | tf_op jit(solution)/shard_map/ppermute | solution.py:27
  96.5 1.6 %collective-permute-start.28 = (bf16[2,384,128]{2,1,0:T(8,128)(2,1)S(1)}, bf16[2,384,128]{2,1,0:T(8,128)(2,1)S(1)}, u32[]{:S(2)}, u32[]{:S(2)}) collective-permute-start(bf16[2,384,128]{2,1,0:T(8,128)(2,1)S(1)} %pad_maximum_fusion.10), channel_id=1, source_target_pairs={{0,1},{1,0},{2,3},{3,2},{4,5},{5,4},{6,7},{7,6},{8,9},{9,8},{10,11... | collective-permute-start | bytes 589832 | tf_op jit(solution)/shard_map/ppermute | solution.py:27
  98.5 0.9 pad_maximum_fusion.11
  99.5 1.0 collective-permute-start.30
  100.5 1.0 collective-permute-done.30
  103.0 1.6 %collective-permute-start.33 = (f32[384,2]{0,1:T(2,128)S(1)}, f32[384,2]{0,1:T(2,128)S(1)}, u32[]{:S(2)}, u32[]{:S(2)}) collective-permute-start(f32[384,2]{0,1:T(2,128)S(1)} %get-tuple-element.46), channel_id=1, source_target_pairs={{0,3},{1,2},{2,1},{3,0},{4,7},{5,6},{6,5},{7,4},{8,11},{9,10},{10,... | collective-permute-start | bytes 9224 | tf_op jit(solution)/shard_map/ppermute | solution.py:27
  105.2 0.9 collective-permute-done.33
  106.4 0.8 copy.32
  (139 shorter events, 17.0 us)
Async XLA Ops:
  0.0 9.5 %copy-start.1 = (bf16[1024,3,256]{2,0,1:T(8,128)(2,1)S(1)}, bf16[1024,3,256]{2,0,1:T(8,128)(2,1)}, u32[]{:S(2)}) copy-start(bf16[1024,3,256]{2,0,1:T(8,128)(2,1)} %param.8) | copy-start | bytes 4718596
  1.8 19.9 %collective-permute-start = (bf16[96,1024]{1,0:T(8,128)(2,1)}, bf16[96,1024]{1,0:T(8,128)(2,1)S(1)}, u32[]{:S(2)}, u32[]{:S(2)}) collective-permute-start(bf16[96,1024]{1,0:T(8,128)(2,1)} %bitcast.3), channel_id=1, source_target_pairs={{0,4},{4,0},{8,12},{12,8},{16,20},{20,16},{24,28},{28,24},{1,5},{5... | collective-permute-start | bytes 589832 | tf_op jit(solution)/shard_map/ppermute | solution.py:109
  3.1 20.7 %collective-permute-start.9 = (bf16[96,1024]{1,0:T(8,128)(2,1)}, bf16[96,1024]{1,0:T(8,128)(2,1)}, u32[]{:S(2)}, u32[]{:S(2)}) collective-permute-start(bf16[96,1024]{1,0:T(8,128)(2,1)} %bitcast.3), channel_id=1, source_target_pairs={{0,8},{4,12},{8,0},{12,4},{16,24},{20,28},{24,16},{28,20},{1,9},{5... | collective-permute-start | bytes 589832 | tf_op jit(solution)/shard_map/ppermute | solution.py:109
  3.2 21.4 %collective-permute-start.12 = (bf16[96,1024]{1,0:T(8,128)(2,1)}, bf16[96,1024]{1,0:T(8,128)(2,1)}, u32[]{:S(2)}, u32[]{:S(2)}) collective-permute-start(bf16[96,1024]{1,0:T(8,128)(2,1)} %bitcast.3), channel_id=1, source_target_pairs={{0,12},{4,8},{8,4},{12,0},{16,28},{20,24},{24,20},{28,16},{1,13},{... | collective-permute-start | bytes 589832 | tf_op jit(solution)/shard_map/ppermute | solution.py:109
  4.5 23.0 %collective-permute-start.15 = (bf16[96,1024]{1,0:T(8,128)(2,1)}, bf16[96,1024]{1,0:T(8,128)(2,1)S(1)}, u32[]{:S(2)}, u32[]{:S(2)}) collective-permute-start(bf16[96,1024]{1,0:T(8,128)(2,1)} %bitcast.3), channel_id=1, source_target_pairs={{0,16},{4,20},{8,24},{12,28},{16,0},{20,4},{24,8},{28,12},{1,17},{... | collective-permute-start | bytes 589832 | tf_op jit(solution)/shard_map/ppermute | solution.py:109
  6.8 25.6 %collective-permute-start.18 = (bf16[96,1024]{1,0:T(8,128)(2,1)}, bf16[96,1024]{1,0:T(8,128)(2,1)S(1)}, u32[]{:S(2)}, u32[]{:S(2)}) collective-permute-start(bf16[96,1024]{1,0:T(8,128)(2,1)} %bitcast.3), channel_id=1, source_target_pairs={{0,20},{4,16},{8,28},{12,24},{16,4},{20,0},{24,12},{28,8},{1,21},{... | collective-permute-start | bytes 589832 | tf_op jit(solution)/shard_map/ppermute | solution.py:109
  9.5 2.1 %copy-start.10 = (s32[3,7]{1,0:T(4,128)S(1)}, s32[3,7]{1,0:T(4,128)}, u32[]{:S(2)}) copy-start(s32[3,7]{1,0:T(4,128)} %param.12) | copy-start | bytes 256
  10.3 8.7 %copy-start.2 = (bf16[384,3,256]{2,0,1:T(8,128)(2,1)}, bf16[384,3,256]{2,0,1:T(8,128)(2,1)S(1)}, u32[]{:S(2)}) copy-start(bf16[384,3,256]{2,0,1:T(8,128)(2,1)S(1)} %convolution_convert_fusion.1) | copy-start | bytes 1769476
  10.3 8.7 %slice-start = ((bf16[1024,3,256]{2,0,1:T(8,128)(2,1)}), bf16[1024,2,256]{2,0,1:T(8,128)(2,1)S(1)}, s32[]{:S(2)}) async-start(bf16[1024,3,256]{2,0,1:T(8,128)(2,1)} %param.8), calls=%async_computation | async-start | bytes 2097152 | tf_op jit(solution)/shard_map/slice | solution.py:252
  21.7 4.5 %collective-permute-start.1 = (bf16[1,96,1024]{2,1,0:T(8,128)(2,1)S(1)}, bf16[1,96,1024]{2,1,0:T(8,128)(2,1)S(1)}, u32[]{:S(2)}, u32[]{:S(2)}) collective-permute-start(bf16[1,96,1024]{2,1,0:T(8,128)(2,1)S(1)} %bitcast.129), channel_id=1, source_target_pairs={{0,2},{1,3},{2,0},{3,1},{4,6},{5,7},{6,4},{7,5},{8,10},{9,11},{10,... | collective-permute-start | bytes 589832 | tf_op jit(solution)/shard_map/ppermute | solution.py:27
  23.8 6.9 %collective-permute-start.10 = (bf16[1,96,1024]{2,1,0:T(8,128)(2,1)}, bf16[1,96,1024]{2,1,0:T(8,128)(2,1)S(1)}, u32[]{:S(2)}, u32[]{:S(2)}) collective-permute-start(bf16[1,96,1024]{2,1,0:T(8,128)(2,1)} %bitcast.19), channel_id=1, source_target_pairs={{0,2},{1,3},{2,0},{3,1},{4,6},{5,7},{6,4},{7,5},{8,10},{9,11},{10,... | collective-permute-start | bytes 589832 | tf_op jit(solution)/shard_map/ppermute | solution.py:27
  24.6 12.7 %collective-permute-start.21 = (bf16[96,1024]{1,0:T(8,128)(2,1)}, bf16[96,1024]{1,0:T(8,128)(2,1)S(1)}, u32[]{:S(2)}, u32[]{:S(2)}) collective-permute-start(bf16[96,1024]{1,0:T(8,128)(2,1)} %bitcast.3), channel_id=1, source_target_pairs={{0,24},{4,28},{8,16},{12,20},{16,8},{20,12},{24,0},{28,4},{1,25},{... | collective-permute-start | bytes 589832 | tf_op jit(solution)/shard_map/ppermute | solution.py:109
  26.2 8.9 %collective-permute-start.13 = (bf16[1,96,1024]{2,1,0:T(8,128)(2,1)}, bf16[1,96,1024]{2,1,0:T(8,128)(2,1)S(1)}, u32[]{:S(2)}, u32[]{:S(2)}) collective-permute-start(bf16[1,96,1024]{2,1,0:T(8,128)(2,1)} %bitcast.21), channel_id=1, source_target_pairs={{0,2},{1,3},{2,0},{3,1},{4,6},{5,7},{6,4},{7,5},{8,10},{9,11},{10,... | collective-permute-start | bytes 589832 | tf_op jit(solution)/shard_map/ppermute | solution.py:27
  27.5 16.7 %collective-permute-start.24 = (bf16[96,1024]{1,0:T(8,128)(2,1)}, bf16[96,1024]{1,0:T(8,128)(2,1)S(1)}, u32[]{:S(2)}, u32[]{:S(2)}) collective-permute-start(bf16[96,1024]{1,0:T(8,128)(2,1)} %bitcast.3), channel_id=1, source_target_pairs={{0,28},{4,24},{8,20},{12,16},{16,12},{20,8},{24,4},{28,0},{1,29},{... | collective-permute-start | bytes 589832 | tf_op jit(solution)/shard_map/ppermute | solution.py:109
  30.6 16.8 %copy-start.8 = (bf16[256,256]{0,1:T(8,128)(2,1)S(1)}, bf16[256,256]{0,1:T(8,128)(2,1)}, u32[]{:S(2)}) copy-start(bf16[256,256]{0,1:T(8,128)(2,1)} %copy.37) | copy-start | bytes 393220
  30.6 13.9 %collective-permute-start.16 = (bf16[1,96,1024]{2,1,0:T(8,128)(2,1)S(1)}, bf16[1,96,1024]{2,1,0:T(8,128)(2,1)S(1)}, u32[]{:S(2)}, u32[]{:S(2)}) collective-permute-start(bf16[1,96,1024]{2,1,0:T(8,128)(2,1)S(1)} %bitcast.158), channel_id=1, source_target_pairs={{0,2},{1,3},{2,0},{3,1},{4,6},{5,7},{6,4},{7,5},{8,10},{9,11},{10,... | collective-permute-start | bytes 589832 | tf_op jit(solution)/shard_map/ppermute | solution.py:27
  32.4 14.9 %collective-permute-start.3 = (bf16[96,1024]{1,0:T(8,128)(2,1)}, bf16[96,1024]{1,0:T(8,128)(2,1)S(1)}, u32[]{:S(2)}, u32[]{:S(2)}) collective-permute-start(bf16[96,1024]{1,0:T(8,128)(2,1)} %bitcast.3), channel_id=1, source_target_pairs={{4,8},{12,16},{20,24},{8,4},{16,12},{24,20},{5,9},{13,17},{21,25},... | collective-permute-start | bytes 589832 | tf_op jit(solution)/shard_map/ppermute | solution.py:105
  35.1 10.6 %collective-permute-start.19 = (bf16[1,96,1024]{2,1,0:T(8,128)(2,1)S(1)}, bf16[1,96,1024]{2,1,0:T(8,128)(2,1)S(1)}, u32[]{:S(2)}, u32[]{:S(2)}) collective-permute-start(bf16[1,96,1024]{2,1,0:T(8,128)(2,1)S(1)} %bitcast.155), channel_id=1, source_target_pairs={{0,2},{1,3},{2,0},{3,1},{4,6},{5,7},{6,4},{7,5},{8,10},{9,11},{10,... | collective-permute-start | bytes 589832 | tf_op jit(solution)/shard_map/ppermute | solution.py:27
  37.4 34.5 %collective-permute-start.6 = (bf16[256,256]{0,1:T(8,128)(2,1)}, bf16[256,256]{0,1:T(8,128)(2,1)S(1)}, u32[]{:S(2)}, u32[]{:S(2)}) collective-permute-start(bf16[256,256]{0,1:T(8,128)(2,1)} %copy.36), channel_id=1, source_target_pairs={{0,1},{1,0},{2,3},{3,2},{4,5},{5,4},{6,7},{7,6},{8,9},{9,8},{10,11... | collective-permute-start | bytes 393224 | tf_op jit(solution)/shard_map/ppermute | solution.py:27
  44.2 5.6 %collective-permute-start.22 = (bf16[1,96,1024]{2,1,0:T(8,128)(2,1)S(1)}, bf16[1,96,1024]{2,1,0:T(8,128)(2,1)S(1)}, u32[]{:S(2)}, u32[]{:S(2)}) collective-permute-start(bf16[1,96,1024]{2,1,0:T(8,128)(2,1)S(1)} %bitcast.161), channel_id=1, source_target_pairs={{0,2},{1,3},{2,0},{3,1},{4,6},{5,7},{6,4},{7,5},{8,10},{9,11},{10,... | collective-permute-start | bytes 589832 | tf_op jit(solution)/shard_map/ppermute | solution.py:27
  44.5 16.5 %copy-start.7 = (bf16[256,256]{0,1:T(8,128)(2,1)S(1)}, bf16[256,256]{0,1:T(8,128)(2,1)}, u32[]{:S(2)}) copy-start(bf16[256,256]{0,1:T(8,128)(2,1)} %copy.38) | copy-start | bytes 393220
  44.5 9.5 %collective-permute-start.25 = (bf16[1,96,1024]{2,1,0:T(8,128)(2,1)S(1)}, bf16[1,96,1024]{2,1,0:T(8,128)(2,1)S(1)}, u32[]{:S(2)}, u32[]{:S(2)}) collective-permute-start(bf16[1,96,1024]{2,1,0:T(8,128)(2,1)S(1)} %bitcast.164), channel_id=1, source_target_pairs={{0,2},{1,3},{2,0},{3,1},{4,6},{5,7},{6,4},{7,5},{8,10},{9,11},{10,... | collective-permute-start | bytes 589832 | tf_op jit(solution)/shard_map/ppermute | solution.py:27
  45.8 18.2 %collective-permute-start.2 = (bf16[2,96,1024]{2,1,0:T(8,128)(2,1)S(1)}, bf16[2,96,1024]{2,1,0:T(8,128)(2,1)S(1)}, u32[]{:S(2)}, u32[]{:S(2)}) collective-permute-start(bf16[2,96,1024]{2,1,0:T(8,128)(2,1)S(1)} %pad_maximum_fusion.2), channel_id=1, source_target_pairs={{0,1},{1,0},{2,3},{3,2},{4,5},{5,4},{6,7},{7,6},{8,9},{9,8},{10,11... | collective-permute-start | bytes 1179656 | tf_op jit(solution)/shard_map/ppermute | solution.py:27
  47.4 24.5 %collective-permute-start.7 = (bf16[256,256]{0,1:T(8,128)(2,1)S(1)}, bf16[256,256]{0,1:T(8,128)(2,1)S(1)}, u32[]{:S(2)}, u32[]{:S(2)}) collective-permute-start(bf16[256,256]{0,1:T(8,128)(2,1)S(1)} %copy-done.8), channel_id=1, source_target_pairs={{0,2},{1,3},{2,0},{3,1},{4,6},{5,7},{6,4},{7,5},{8,10},{9,11},{10,... | collective-permute-start | bytes 393224 | tf_op jit(solution)/shard_map/ppermute | solution.py:27
  49.8 11.2 %collective-permute-start.4 = (bf16[1,96,1024]{2,1,0:T(8,128)(2,1)S(1)}, bf16[1,96,1024]{2,1,0:T(8,128)(2,1)S(1)}, u32[]{:S(2)}, u32[]{:S(2)}) collective-permute-start(bf16[1,96,1024]{2,1,0:T(8,128)(2,1)S(1)} %bitcast.144), channel_id=1, source_target_pairs={{0,2},{1,3},{2,0},{3,1},{4,6},{5,7},{6,4},{7,5},{8,10},{9,11},{10,... | collective-permute-start | bytes 589832 | tf_op jit(solution)/shard_map/ppermute | solution.py:27
  54.0 10.1 %collective-permute-start.11 = (bf16[2,96,1024]{2,1,0:T(8,128)(2,1)S(1)}, bf16[2,96,1024]{2,1,0:T(8,128)(2,1)S(1)}, u32[]{:S(2)}, u32[]{:S(2)}) collective-permute-start(bf16[2,96,1024]{2,1,0:T(8,128)(2,1)S(1)} %pad_maximum_fusion.4), channel_id=1, source_target_pairs={{0,1},{1,0},{2,3},{3,2},{4,5},{5,4},{6,7},{7,6},{8,9},{9,8},{10,11... | collective-permute-start | bytes 1179656 | tf_op jit(solution)/shard_map/ppermute | solution.py:27
  61.0 10.9 %collective-permute-start.8 = (bf16[256,256]{0,1:T(8,128)(2,1)S(1)}, bf16[256,256]{0,1:T(8,128)(2,1)S(1)}, u32[]{:S(2)}, u32[]{:S(2)}) collective-permute-start(bf16[256,256]{0,1:T(8,128)(2,1)S(1)} %copy-done.7), channel_id=1, source_target_pairs={{0,3},{1,2},{2,1},{3,0},{4,7},{5,6},{6,5},{7,4},{8,11},{9,10},{10,... | collective-permute-start | bytes 393224 | tf_op jit(solution)/shard_map/ppermute | solution.py:27
  64.0 1.8 %collective-permute-start.14 = (bf16[2,96,1024]{2,1,0:T(8,128)(2,1)S(1)}, bf16[2,96,1024]{2,1,0:T(8,128)(2,1)S(1)}, u32[]{:S(2)}, u32[]{:S(2)}) collective-permute-start(bf16[2,96,1024]{2,1,0:T(8,128)(2,1)S(1)} %pad_maximum_fusion.5), channel_id=1, source_target_pairs={{0,1},{1,0},{2,3},{3,2},{4,5},{5,4},{6,7},{7,6},{8,9},{9,8},{10,11... | collective-permute-start | bytes 1179656 | tf_op jit(solution)/shard_map/ppermute | solution.py:27
  64.1 2.2 %collective-permute-start.17 = (bf16[2,96,1024]{2,1,0:T(8,128)(2,1)S(1)}, bf16[2,96,1024]{2,1,0:T(8,128)(2,1)S(1)}, u32[]{:S(2)}, u32[]{:S(2)}) collective-permute-start(bf16[2,96,1024]{2,1,0:T(8,128)(2,1)S(1)} %pad_maximum_fusion.6), channel_id=1, source_target_pairs={{0,1},{1,0},{2,3},{3,2},{4,5},{5,4},{6,7},{7,6},{8,9},{9,8},{10,11... | collective-permute-start | bytes 1179656 | tf_op jit(solution)/shard_map/ppermute | solution.py:27
  65.8 1.7 %collective-permute-start.20 = (bf16[2,96,1024]{2,1,0:T(8,128)(2,1)S(1)}, bf16[2,96,1024]{2,1,0:T(8,128)(2,1)S(1)}, u32[]{:S(2)}, u32[]{:S(2)}) collective-permute-start(bf16[2,96,1024]{2,1,0:T(8,128)(2,1)S(1)} %pad_maximum_fusion.7), channel_id=1, source_target_pairs={{0,1},{1,0},{2,3},{3,2},{4,5},{5,4},{6,7},{7,6},{8,9},{9,8},{10,11... | collective-permute-start | bytes 1179656 | tf_op jit(solution)/shard_map/ppermute | solution.py:27
  66.3 1.7 %collective-permute-start.23 = (bf16[2,96,1024]{2,1,0:T(8,128)(2,1)S(1)}, bf16[2,96,1024]{2,1,0:T(8,128)(2,1)S(1)}, u32[]{:S(2)}, u32[]{:S(2)}) collective-permute-start(bf16[2,96,1024]{2,1,0:T(8,128)(2,1)S(1)} %pad_maximum_fusion.8), channel_id=1, source_target_pairs={{0,1},{1,0},{2,3},{3,2},{4,5},{5,4},{6,7},{7,6},{8,9},{9,8},{10,11... | collective-permute-start | bytes 1179656 | tf_op jit(solution)/shard_map/ppermute | solution.py:27
  67.5 1.7 %collective-permute-start.26 = (bf16[2,96,1024]{2,1,0:T(8,128)(2,1)S(1)}, bf16[2,96,1024]{2,1,0:T(8,128)(2,1)S(1)}, u32[]{:S(2)}, u32[]{:S(2)}) collective-permute-start(bf16[2,96,1024]{2,1,0:T(8,128)(2,1)S(1)} %pad_maximum_fusion.9), channel_id=1, source_target_pairs={{0,1},{1,0},{2,3},{3,2},{4,5},{5,4},{6,7},{7,6},{8,9},{9,8},{10,11... | collective-permute-start | bytes 1179656 | tf_op jit(solution)/shard_map/ppermute | solution.py:27
  68.0 3.9 %collective-permute-start.5 = (bf16[2,96,1024]{2,1,0:T(8,128)(2,1)S(1)}, bf16[2,96,1024]{2,1,0:T(8,128)(2,1)S(1)}, u32[]{:S(2)}, u32[]{:S(2)}) collective-permute-start(bf16[2,96,1024]{2,1,0:T(8,128)(2,1)S(1)} %pad_maximum_fusion.3), channel_id=1, source_target_pairs={{0,1},{1,0},{2,3},{3,2},{4,5},{5,4},{6,7},{7,6},{8,9},{9,8},{10,11... | collective-permute-start | bytes 1179656 | tf_op jit(solution)/shard_map/ppermute | solution.py:27
  85.3 6.8 %copy-start.4 = (bf16[3,128,128]{2,1,0:T(8,128)(2,1)S(1)}, bf16[3,128,128]{2,1,0:T(8,128)(2,1)}, u32[]{:S(2)}) copy-start(bf16[3,128,128]{2,1,0:T(8,128)(2,1)} %shard_map.73) | copy-start | bytes 294916
  92.2 4.3 %collective-permute-start.27 = (bf16[1,384,128]{2,1,0:T(8,128)(2,1)S(1)}, bf16[1,384,128]{2,1,0:T(8,128)(2,1)S(1)}, u32[]{:S(2)}, u32[]{:S(2)}) collective-permute-start(bf16[1,384,128]{2,1,0:T(8,128)(2,1)S(1)} %bitcast.172), channel_id=1, source_target_pairs={{0,2},{1,3},{2,0},{3,1},{4,6},{5,7},{6,4},{7,5},{8,10},{9,11},{10,... | collective-permute-start | bytes 294920 | tf_op jit(solution)/shard_map/ppermute | solution.py:27
  92.4 6.1 %collective-permute-start.29 = (bf16[1,384,128]{2,1,0:T(8,128)(2,1)}, bf16[1,384,128]{2,1,0:T(8,128)(2,1)S(1)}, u32[]{:S(2)}, u32[]{:S(2)}) collective-permute-start(bf16[1,384,128]{2,1,0:T(8,128)(2,1)} %bitcast.167), channel_id=1, source_target_pairs={{0,2},{1,3},{2,0},{3,1},{4,6},{5,7},{6,4},{7,5},{8,10},{9,11},{10,... | collective-permute-start | bytes 294920 | tf_op jit(solution)/shard_map/ppermute | solution.py:27
  93.7 8.0 %copy-start.5 = (bf16[384,256]{0,1:T(8,128)(2,1)S(1)}, bf16[384,256]{0,1:T(8,128)(2,1)}, u32[]{:S(2)}) copy-start(bf16[384,256]{0,1:T(8,128)(2,1)} %copy.33) | copy-start | bytes 589828
  93.7 8.0 %copy-start.6 = (bf16[256,256]{0,1:T(8,128)(2,1)S(1)}, bf16[256,256]{0,1:T(8,128)(2,1)}, u32[]{:S(2)}) copy-start(bf16[256,256]{0,1:T(8,128)(2,1)} %copy.35) | copy-start | bytes 393220
  93.7 8.0 %copy-start.14 = (bf16[256,256]{0,1:T(8,128)(2,1)S(1)}, bf16[256,256]{0,1:T(8,128)(2,1)}, u32[]{:S(2)}) copy-start(bf16[256,256]{0,1:T(8,128)(2,1)} %copy-done.13) | copy-start | bytes 393220
  93.7 8.0 %copy-start.16 = (bf16[256,256]{0,1:T(8,128)(2,1)S(1)}, bf16[256,256]{0,1:T(8,128)(2,1)}, u32[]{:S(2)}) copy-start(bf16[256,256]{0,1:T(8,128)(2,1)} %copy-done.15) | copy-start | bytes 393220
  93.7 8.0 %copy-start.18 = (bf16[256,256]{0,1:T(8,128)(2,1)S(1)}, bf16[256,256]{0,1:T(8,128)(2,1)}, u32[]{:S(2)}) copy-start(bf16[256,256]{0,1:T(8,128)(2,1)} %copy-done.17) | copy-start | bytes 393220
  96.5 4.0 %collective-permute-start.28 = (bf16[2,384,128]{2,1,0:T(8,128)(2,1)S(1)}, bf16[2,384,128]{2,1,0:T(8,128)(2,1)S(1)}, u32[]{:S(2)}, u32[]{:S(2)}) collective-permute-start(bf16[2,384,128]{2,1,0:T(8,128)(2,1)S(1)} %pad_maximum_fusion.10), channel_id=1, source_target_pairs={{0,1},{1,0},{2,3},{3,2},{4,5},{5,4},{6,7},{7,6},{8,9},{9,8},{10,11... | collective-permute-start | bytes 589832 | tf_op jit(solution)/shard_map/ppermute | solution.py:27
  99.5 2.1 %collective-permute-start.30 = (bf16[2,384,128]{2,1,0:T(8,128)(2,1)S(1)}, bf16[2,384,128]{2,1,0:T(8,128)(2,1)S(1)}, u32[]{:S(2)}, u32[]{:S(2)}) collective-permute-start(bf16[2,384,128]{2,1,0:T(8,128)(2,1)S(1)} %pad_maximum_fusion.11), channel_id=1, source_target_pairs={{0,1},{1,0},{2,3},{3,2},{4,5},{5,4},{6,7},{7,6},{8,9},{9,8},{10,11... | collective-permute-start | bytes 589832 | tf_op jit(solution)/shard_map/ppermute | solution.py:27
  101.7 4.5 %copy-start.11 = (f32[256]{0:T(256)S(1)}, f32[256]{0:T(256)}, u32[]{:S(2)}) copy-start(f32[256]{0:T(256)} %param.11) | copy-start | bytes 3076
  101.7 4.5 %copy-start.12 = (f32[256]{0:T(256)S(1)}, f32[256]{0:T(256)}, u32[]{:S(2)}) copy-start(f32[256]{0:T(256)} %param.10) | copy-start | bytes 3076
  102.3 2.2 %collective-permute-start.31 = (f32[384,2]{0,1:T(2,128)S(1)}, f32[384,2]{0,1:T(2,128)S(1)}, u32[]{:S(2)}, u32[]{:S(2)}) collective-permute-start(f32[384,2]{0,1:T(2,128)S(1)} %get-tuple-element.46), channel_id=1, source_target_pairs={{0,1},{1,0},{2,3},{3,2},{4,5},{5,4},{6,7},{7,6},{8,9},{9,8},{10,11... | collective-permute-start | bytes 9224 | tf_op jit(solution)/shard_map/ppermute | solution.py:27
  102.7 2.4 %collective-permute-start.32 = (f32[384,2]{0,1:T(2,128)S(1)}, f32[384,2]{0,1:T(2,128)S(1)}, u32[]{:S(2)}, u32[]{:S(2)}) collective-permute-start(f32[384,2]{0,1:T(2,128)S(1)} %get-tuple-element.46), channel_id=1, source_target_pairs={{0,2},{1,3},{2,0},{3,1},{4,6},{5,7},{6,4},{7,5},{8,10},{9,11},{10,... | collective-permute-start | bytes 9224 | tf_op jit(solution)/shard_map/ppermute | solution.py:27
  103.0 3.1 %collective-permute-start.33 = (f32[384,2]{0,1:T(2,128)S(1)}, f32[384,2]{0,1:T(2,128)S(1)}, u32[]{:S(2)}, u32[]{:S(2)}) collective-permute-start(f32[384,2]{0,1:T(2,128)S(1)} %get-tuple-element.46), channel_id=1, source_target_pairs={{0,3},{1,2},{2,1},{3,0},{4,7},{5,6},{6,5},{7,4},{8,11},{9,10},{10,... | collective-permute-start | bytes 9224 | tf_op jit(solution)/shard_map/ppermute | solution.py:27
  (7 other events, 7.2 us)

commit v7 on v4

--- a/solution.py
+++ b/solution.py
@@ -13,6 +13,7 @@
 LANES = 128
 GATHER_GROUPS = 16
 STATIC_GROUPS = 8
+NEAR_SHIFTS = 4
 
 
 NORM_EPS = 1e-05
@@ -86,7 +87,9 @@
     mine = mine.reshape(blocks_here * sub_rows, model_width)
     targets = jnp.bitwise_xor(matchings[:, 0] // blocks_here, my_index)
     if groups <= STATIC_GROUPS:
-        return static_keys(mine, w_kv, w_parts, targets, my_index, groups, blocks_here, sub_rows)
+        return static_keys(
+            node_states, mine, w_kv, w_parts, targets, my_index, groups, blocks_here, sub_rows
+        )
     up = [(i, i + 1) for i in range(groups - 1)]
     down = [(i + 1, i) for i in range(groups - 1)]
     before = lax.ppermute(mine, "node", up)
@@ -97,14 +100,21 @@
     return kv_of_spread(spread, w_kv, blocks_here, sub_rows), w_parts
 
 
-def static_keys(mine, w_kv, w_parts, targets, my_index, groups, blocks_here, sub_rows):
+def static_keys(
+    node_states, mine, w_kv, w_parts, targets, my_index, groups, blocks_here, sub_rows
+):
     heads_axis = lax.axis_size("head")
     matches = targets.shape[0]
     far = [(j, j + 1) for j in range(1, groups - 1, 2)] + [(j, j - 1) for j in range(2, groups, 2)]
     other = spread_stack(lax.ppermute(mine, "node", far), heads_axis)
+    near = near_rows(node_states, blocks_here, sub_rows)
     every = jnp.stack(
         [
-            spread_stack(
+            pair_stack(
+                lax.ppermute(near, "node", [(i, i ^ shift) for i in range(groups)]), heads_axis
+            )
+            if shift < NEAR_SHIFTS and heads_axis == 4
+            else spread_stack(
                 lax.ppermute(mine, "node", [(i, i ^ shift) for i in range(groups)]), heads_axis
             )
             for shift in range(1, groups)
@@ -121,6 +131,25 @@
     ]
     w_parts, matched[0] = lax.optimization_barrier((w_parts, matched[0]))
     return kv_of_spread([before, after] + matched, w_kv, blocks_here, sub_rows), w_parts
+
+
+def near_rows(node_states, blocks_here, sub_rows):
+    model_width = node_states.shape[1]
+    me = lax.axis_index("head")
+    parts = node_states.reshape(blocks_here, 4, sub_rows, model_width)
+    return jnp.stack(
+        [
+            lax.dynamic_index_in_dim(parts, me ^ flip, axis=1, keepdims=False).reshape(
+                blocks_here * sub_rows, model_width
+            )
+            for flip in (0, 2)
+        ]
+    )
+
+
+def pair_stack(received, heads_axis):
+    beside = flip_heads(received, 1, heads_axis)
+    return jnp.stack([received[0], beside[0], received[1], beside[1]])
 
 
 def spread_stack(piece, heads_axis):

time: 108 us -> 106 us (0.981)
  waiting for transfers between devices: 22.7 us -> 31.5 us
  starting transfers between devices: 40.7 us -> 34.7 us
  other arithmetic: 8.02 us -> 4.71 us
  local copies, waits for them, and re-layouts: 15.6 us -> 14 us
    ppermute x7 -> x4, waiting for transfers between devices: 5.38 us -> 15.1 us  [static_keys(): lax.ppermute(mine, 'node', [(i, i ^ shift) for i in range(groups)])]
    unnamed x38 -> x32, local copies, waits for them, and re-layouts: 7.75 us -> 2.18 us
    ppermute x24 -> x21, starting transfers between devices: 29.5 us -> 25.1 us  [flip_heads(): return lax.ppermute(array, 'head', [(i, i ^ flip) for i in range(devices)])]
    slice x0 -> x6, local copies, waits for them, and re-layouts: none -> 3.22 us  [pair_stack(): return jnp.stack([received[0], beside[0], received[1], beside[1]])]
    ppermute x0 -> x3, starting transfers between devices: none -> 2.65 us  [static_keys(): lax.ppermute(near, 'node', [(i, i ^ shift) for i in range(groups)])]
    ppermute x7 -> x4, starting transfers between devices: 7.44 us -> 4.8 us  [static_keys(): lax.ppermute(mine, 'node', [(i, i ^ shift) for i in range(groups)])]
    ppermute x1, starting transfers between devices: 3.82 us -> 2.19 us  [static_keys(): other = spread_stack(lax.ppermute(mine, 'node', far), heads_axis)]
    another operation x9 -> x6, other arithmetic: 2.19 us -> 1.15 us  [spread_slots(): other = flip_heads(jnp.stack([slots[k] for k in held]), flip, heads_axis)]
  transfers between devices with their start and end apart: 32 -> 29, of which waited for: 14 -> 15; matrix products, arithmetic and copies ran while one was open for 18% -> 14% of each run, Pallas kernels for 0% -> 0%
where the time goes in v7:
time: 106 us
  starting transfers between devices  34.7 us (33%)
  waiting for transfers between devices  31.5 us (30%)
  local copies, waits for them, and re-layouts  14 us (13%)
  Pallas kernels  10.8 us (10%)
  matrix products  6.69 us (6%)
  other arithmetic  4.71 us (4%)
  between operations  3.06 us (3%)
    ppermute x21, starting transfers between devices, flip_heads(): return lax.ppermute(array, 'head', [(i, i ^ flip) for i in range(devices)])  25.1 us
    ppermute x21, waiting for transfers between devices, flip_heads(): return lax.ppermute(array, 'head', [(i, i ^ flip) for i in range(devices)])  16.4 us
    ppermute x4, waiting for transfers between devices, static_keys(): lax.ppermute(mine, 'node', [(i, i ^ shift) for i in range(groups)])  15.1 us
    pallas_call x1, Pallas kernels, attention(): pl.pallas_call(attention_kernel, out_shape=jax.ShapeDtypeStruct(query.sha...  10.8 us
    ppermute x4, starting transfers between devices, static_keys(): lax.ppermute(mine, 'node', [(i, i ^ shift) for i in range(groups)])  4.8 us
    dot_general x1, matrix products, kv_of_spread(): jnp.dot(rows, w_kv, preferred_element_type=jnp.float32).astype(jnp.bfloat16)  4.28 us
    slice x6, local copies, waits for them, and re-layouts, pair_stack(): return jnp.stack([received[0], beside[0], received[1], beside[1]])  3.22 us
    ppermute x3, starting transfers between devices, static_keys(): lax.ppermute(near, 'node', [(i, i ^ shift) for i in range(groups)])  2.65 us
  transfers between devices with their start and end apart: 29, of which 15 were waited for; matrix products, arithmetic and copies ran while one was open for 14% of the time, Pallas kernels for 0%

profile of v7, /device:TPU:9, one launch (start us, length us, event | category | flops | bytes accessed | tf_op | source)
XLA Modules:
  0.0 105.5 jit_solution(10313602927026111866)
XLA Ops:
  0.0 1.2 %constant_dynamic-slice_fusion.7 = (bf16[3,1,32,1024]{3,2,1,0:T(8,128)(2,1)S(1)}, bf16[3,1,32,1024]{3,2,1,0:T(8,128)(2,1)S(1)}) fusion(bf16[3,4,32,1024]{3,2,1,0:T(8,128)(2,1)} %bitcast.151, s32[]{:T(128)S(6)} %select_n.63, s32[]{:T(128)S(6)} %select_n.62), kind=kLoop, calls=%fused_computation.66 | loop fusion | bytes 786440 | tf_op jit(solution)/shard_map/jit(dynamic_index_in_dim)/dynamic_slice | solution.py:142
  1.2 0.8 pad_maximum_fusion.2
  2.0 1.2 %collective-permute-start = (bf16[2,96,1024]{2,1,0:T(8,128)(2,1)}, bf16[2,96,1024]{2,1,0:T(8,128)(2,1)}, u32[]{:S(2)}, u32[]{:S(2)}) collective-permute-start(bf16[2,96,1024]{2,1,0:T(8,128)(2,1)} %pad_maximum_fusion.2), channel_id=1, source_target_pairs={{0,4},{4,0},{8,12},{12,8},{16,20},{20,16},{24,28},{28,24},{1,5},{5... | collective-permute-start | bytes 1179656 | tf_op jit(solution)/shard_map/ppermute | solution.py:114
  3.4 1.2 %collective-permute-start.10 = (bf16[2,96,1024]{2,1,0:T(8,128)(2,1)}, bf16[2,96,1024]{2,1,0:T(8,128)(2,1)}, u32[]{:S(2)}, u32[]{:S(2)}) collective-permute-start(bf16[2,96,1024]{2,1,0:T(8,128)(2,1)} %pad_maximum_fusion.2), channel_id=1, source_target_pairs={{0,12},{4,8},{8,4},{12,0},{16,28},{20,24},{24,20},{28,16},{1,13},{... | collective-permute-start | bytes 1179656 | tf_op jit(solution)/shard_map/ppermute | solution.py:114
  4.6 2.3 %collective-permute-start.12 = (bf16[96,1024]{1,0:T(8,128)(2,1)S(1)}, bf16[96,1024]{1,0:T(8,128)(2,1)S(1)}, u32[]{:S(2)}, u32[]{:S(2)}) collective-permute-start(bf16[96,1024]{1,0:T(8,128)(2,1)S(1)} %bitcast.145), channel_id=1, source_target_pairs={{0,16},{4,20},{8,24},{12,28},{16,0},{20,4},{24,8},{28,12},{1,17},{... | collective-permute-start | bytes 589832 | tf_op jit(solution)/shard_map/ppermute | solution.py:118
  6.9 1.0 collective-permute-start.15
  8.2 0.6 add_select_fusion.pick_ref
  8.8 1.9 %convolution_convert_fusion.1 = bf16[384,3,256]{2,0,1:T(8,128)(2,1)S(1)} fusion(bf16[1024,3,256]{2,0,1:T(8,128)(2,1)S(1)} %copy-done, bf16[384,1024]{1,0:T(8,128)(2,1)} %param.7), kind=kOutput, calls=%fused_computation.1 | convolution fusion | flops 604274688 | bytes 2949120 | tf_op jit(solution)/shard_map/nd,dtf->ntf/dot_general | solution.py:272
  10.8 1.3 %constant_dynamic-slice_fusion.3 = (bf16[256,256]{1,0:T(8,128)(2,1)S(1)}, bf16[256,256]{1,0:T(8,128)(2,1)S(1)}, bf16[256,256]{1,0:T(8,128)(2,1)S(1)}, bf16[256,256]{1,0:T(8,128)(2,1)S(1)}) fusion(bf16[256,1024]{1,0:T(8,128)(2,1)} %param.9, s32[]{:T(128)S(6)} %select_n.68, s32[]{:T(128)S(6)} %select_n.67, s32[]{:T(128)S(6)} %select_n.66, s32[]{:T(128)S(6)} %select_n.58), kind=kLoop, calls=%fused_computation.62 | loop fusion | bytes 1048592 | tf_op jit(solution)/shard_map/dynamic_slice | solution.py:266
  12.1 0.7 fusion.42
  12.7 0.7 slice.137
  15.9 0.8 copy.38
  17.0 0.5 copy.41
  18.0 1.0 reshape_reshape.6.own_ref
  19.0 0.5 pad_convert_fusion.live_ref
  19.6 1.3 %collective-permute-start.18 = (bf16[96,1024]{1,0:T(8,128)(2,1)S(1)}, bf16[96,1024]{1,0:T(8,128)(2,1)S(1)}, u32[]{:S(2)}, u32[]{:S(2)}) collective-permute-start(bf16[96,1024]{1,0:T(8,128)(2,1)S(1)} %bitcast.147), channel_id=1, source_target_pairs={{0,24},{4,28},{8,16},{12,20},{16,8},{20,12},{24,0},{28,4},{1,25},{... | collective-permute-start | bytes 589832 | tf_op jit(solution)/shard_map/ppermute | solution.py:118
  20.9 1.0 fusion.39
  22.1 1.0 fusion.37
  23.2 3.6 %collective-permute-done.12 = bf16[96,1024]{1,0:T(8,128)(2,1)S(1)} collective-permute-done((bf16[96,1024]{1,0:T(8,128)(2,1)S(1)}, bf16[96,1024]{1,0:T(8,128)(2,1)S(1)}, u32[]{:S(2)}, u32[]{:S(2)}) %collective-permute-start.12) | collective-permute-done | bytes 196640 | tf_op jit(solution)/shard_map/ppermute | solution.py:118
  26.8 2.2 %collective-permute-start.2 = (bf16[96,1024]{1,0:T(8,128)(2,1)S(1)}, bf16[96,1024]{1,0:T(8,128)(2,1)S(1)}, u32[]{:S(2)}, u32[]{:S(2)}) collective-permute-start(bf16[96,1024]{1,0:T(8,128)(2,1)S(1)} %bitcast.149), channel_id=1, source_target_pairs={{4,8},{12,16},{20,24},{8,4},{16,12},{24,20},{5,9},{13,17},{21,25},... | collective-permute-start | bytes 589832 | tf_op jit(solution)/shard_map/ppermute | solution.py:109
  29.0 2.0 %collective-permute-done.15 = bf16[96,1024]{1,0:T(8,128)(2,1)S(1)} collective-permute-done((bf16[96,1024]{1,0:T(8,128)(2,1)S(1)}, bf16[96,1024]{1,0:T(8,128)(2,1)S(1)}, u32[]{:S(2)}, u32[]{:S(2)}) %collective-permute-start.15) | collective-permute-done | bytes 196640 | tf_op jit(solution)/shard_map/ppermute | solution.py:118
  30.9 1.2 %collective-permute-start.13 = (bf16[1,96,1024]{2,1,0:T(8,128)(2,1)S(1)}, bf16[1,96,1024]{2,1,0:T(8,128)(2,1)S(1)}, u32[]{:S(2)}, u32[]{:S(2)}) collective-permute-start(bf16[1,96,1024]{2,1,0:T(8,128)(2,1)S(1)} %bitcast.135), channel_id=1, source_target_pairs={{0,2},{1,3},{2,0},{3,1},{4,6},{5,7},{6,4},{7,5},{8,10},{9,11},{10,... | collective-permute-start | bytes 589832 | tf_op jit(solution)/shard_map/ppermute | solution.py:27
  32.4 1.0 fusion.35
  33.4 7.9 %collective-permute-done.18 = bf16[96,1024]{1,0:T(8,128)(2,1)S(1)} collective-permute-done((bf16[96,1024]{1,0:T(8,128)(2,1)S(1)}, bf16[96,1024]{1,0:T(8,128)(2,1)S(1)}, u32[]{:S(2)}, u32[]{:S(2)}) %collective-permute-start.18) | collective-permute-done | bytes 196640 | tf_op jit(solution)/shard_map/ppermute | solution.py:118
  41.4 3.8 %collective-permute-start.5 = (bf16[256,256]{0,1:T(8,128)(2,1)S(1)}, bf16[256,256]{0,1:T(8,128)(2,1)S(1)}, u32[]{:S(2)}, u32[]{:S(2)}) collective-permute-start(bf16[256,256]{0,1:T(8,128)(2,1)S(1)} %copy-done.3), channel_id=1, source_target_pairs={{0,1},{1,0},{2,3},{3,2},{4,5},{5,4},{6,7},{7,6},{8,9},{9,8},{10,11... | collective-permute-start | bytes 393224 | tf_op jit(solution)/shard_map/ppermute | solution.py:27
  45.2 1.6 %collective-permute-done.21 = bf16[96,1024]{1,0:T(8,128)(2,1)S(1)} collective-permute-done((bf16[96,1024]{1,0:T(8,128)(2,1)S(1)}, bf16[96,1024]{1,0:T(8,128)(2,1)S(1)}, u32[]{:S(2)}, u32[]{:S(2)}) %collective-permute-start.21) | collective-permute-done | bytes 196640 | tf_op jit(solution)/shard_map/ppermute | solution.py:118
  46.8 1.2 %collective-permute-start.19 = (bf16[1,96,1024]{2,1,0:T(8,128)(2,1)S(1)}, bf16[1,96,1024]{2,1,0:T(8,128)(2,1)S(1)}, u32[]{:S(2)}, u32[]{:S(2)}) collective-permute-start(bf16[1,96,1024]{2,1,0:T(8,128)(2,1)S(1)} %bitcast.138), channel_id=1, source_target_pairs={{0,2},{1,3},{2,0},{3,1},{4,6},{5,7},{6,4},{7,5},{8,10},{9,11},{10,... | collective-permute-start | bytes 589832 | tf_op jit(solution)/shard_map/ppermute | solution.py:27
  48.3 2.5 %collective-permute-start.1 = (bf16[2,96,1024]{2,1,0:T(8,128)(2,1)}, bf16[2,96,1024]{2,1,0:T(8,128)(2,1)S(1)}, u32[]{:S(2)}, u32[]{:S(2)}) collective-permute-start(bf16[2,96,1024]{2,1,0:T(8,128)(2,1)} %collective-permute-done), channel_id=1, source_target_pairs={{0,1},{1,0},{2,3},{3,2},{4,5},{5,4},{6,7},{7,6},{8,9},{9,8},{10,11... | collective-permute-start | bytes 1179656 | tf_op jit(solution)/shard_map/ppermute | solution.py:27
  50.9 1.3 %collective-permute-start.6 = (bf16[256,256]{0,1:T(8,128)(2,1)S(1)}, bf16[256,256]{0,1:T(8,128)(2,1)S(1)}, u32[]{:S(2)}, u32[]{:S(2)}) collective-permute-start(bf16[256,256]{0,1:T(8,128)(2,1)S(1)} %copy.39), channel_id=1, source_target_pairs={{0,2},{1,3},{2,0},{3,1},{4,6},{5,7},{6,4},{7,5},{8,10},{9,11},{10,... | collective-permute-start | bytes 393224 | tf_op jit(solution)/shard_map/ppermute | solution.py:27
  52.5 2.9 %collective-permute-done.22 = bf16[1,96,1024]{2,1,0:T(8,128)(2,1)S(1)} collective-permute-done((bf16[1,96,1024]{2,1,0:T(8,128)(2,1)S(1)}, bf16[1,96,1024]{2,1,0:T(8,128)(2,1)S(1)}, u32[]{:S(2)}, u32[]{:S(2)}) %collective-permute-start.22) | collective-permute-done | bytes 196640 | tf_op jit(solution)/shard_map/ppermute | solution.py:27
  55.5 5.2 %collective-permute-start.9 = (bf16[2,96,1024]{2,1,0:T(8,128)(2,1)}, bf16[2,96,1024]{2,1,0:T(8,128)(2,1)S(1)}, u32[]{:S(2)}, u32[]{:S(2)}) collective-permute-start(bf16[2,96,1024]{2,1,0:T(8,128)(2,1)} %collective-permute-done.8), channel_id=1, source_target_pairs={{0,1},{1,0},{2,3},{3,2},{4,5},{5,4},{6,7},{7,6},{8,9},{9,8},{10,11... | collective-permute-start | bytes 1179656 | tf_op jit(solution)/shard_map/ppermute | solution.py:27
  60.8 1.7 %collective-permute-done.3 = bf16[1,96,1024]{2,1,0:T(8,128)(2,1)S(1)} collective-permute-done((bf16[1,96,1024]{2,1,0:T(8,128)(2,1)S(1)}, bf16[1,96,1024]{2,1,0:T(8,128)(2,1)S(1)}, u32[]{:S(2)}, u32[]{:S(2)}) %collective-permute-start.3) | collective-permute-done | bytes 196640 | tf_op jit(solution)/shard_map/ppermute | solution.py:27
  62.5 3.9 %collective-permute-start.7 = (bf16[256,256]{0,1:T(8,128)(2,1)S(1)}, bf16[256,256]{0,1:T(8,128)(2,1)S(1)}, u32[]{:S(2)}, u32[]{:S(2)}) collective-permute-start(bf16[256,256]{0,1:T(8,128)(2,1)S(1)} %copy.40), channel_id=1, source_target_pairs={{0,3},{1,2},{2,1},{3,0},{4,7},{5,6},{6,5},{7,4},{8,11},{9,10},{10,... | collective-permute-start | bytes 393224 | tf_op jit(solution)/shard_map/ppermute | solution.py:27
  66.6 0.6 collective-permute-start.14
  67.2 1.3 %collective-permute-done.11 = bf16[2,96,1024]{2,1,0:T(8,128)(2,1)S(1)} collective-permute-done((bf16[2,96,1024]{2,1,0:T(8,128)(2,1)}, bf16[2,96,1024]{2,1,0:T(8,128)(2,1)S(1)}, u32[]{:S(2)}, u32[]{:S(2)}) %collective-permute-start.11) | collective-permute-done | bytes 393248 | tf_op jit(solution)/shard_map/ppermute | solution.py:27
  69.1 1.1 %collective-permute-done.17 = bf16[2,96,1024]{2,1,0:T(8,128)(2,1)S(1)} collective-permute-done((bf16[2,96,1024]{2,1,0:T(8,128)(2,1)S(1)}, bf16[2,96,1024]{2,1,0:T(8,128)(2,1)S(1)}, u32[]{:S(2)}, u32[]{:S(2)}) %collective-permute-start.17) | collective-permute-done | bytes 393248 | tf_op jit(solution)/shard_map/ppermute | solution.py:27
  71.0 0.9 collective-permute-done.23
  73.9 0.9 copy.31
  74.9 4.3 %convolution_convert_fusion = bf16[2304,512]{1,0:T(8,128)(2,1)} fusion(bf16[2304,1024]{1,0:T(8,128)(2,1)S(1)} %bitcast.108, bf16[1024,512]{0,1:T(8,128)(2,1)S(1)} %bitcast.131), kind=kOutput, calls=%fused_computation | convolution fusion | flops 2417098752 | bytes 8126464 | tf_op jit(solution)/shard_map/dot_general | solution.py:171
  79.2 10.8 %shard_map.73 = bf16[3,128,256]{2,1,0:T(8,128)(2,1)} custom-call(s32[3,11]{1,0:T(4,128)} %pad_convert_fusion.live_ref, s32[4,3]{1,0:T(4,128)} %add_select_fusion.pick_ref, bf16[3,128,256]{2,1,0:T(8,128)(2,1)} %bitcast.152, bf16[3,128,512]{2,1,0:T(8,128)(2,1)} %reshape_reshape.6.own_ref, bf16[6,3,128,512]{3,2,1,0:T(8,128)(2,1)} %bitcast.163), custom_call_target="tpu_custom_call" | custom-call | flops 1107296256 | bytes 3145728 | tf_op jit(solution)/shard_map/pallas_call | solution.py:238
  90.3 6.3 %collective-permute-done.24 = bf16[1,384,256]{2,1,0:T(8,128)(2,1)S(1)} collective-permute-done((bf16[1,384,256]{2,1,0:T(8,128)(2,1)}, bf16[1,384,256]{2,1,0:T(8,128)(2,1)S(1)}, u32[]{:S(2)}, u32[]{:S(2)}) %collective-permute-start.24) | collective-permute-done | bytes 196640 | tf_op jit(solution)/shard_map/ppermute | solution.py:27
  96.6 1.0 pad_maximum_fusion.8
  97.6 1.0 collective-permute-start.25
  98.6 0.9 constant_dynamic-slice_fusion.9
  101.4 1.5 %collective-permute-start.28 = (f32[384,2]{0,1:T(2,128)S(1)}, f32[384,2]{0,1:T(2,128)S(1)}, u32[]{:S(2)}, u32[]{:S(2)}) collective-permute-start(f32[384,2]{0,1:T(2,128)S(1)} %get-tuple-element.52), channel_id=1, source_target_pairs={{0,3},{1,2},{2,1},{3,0},{4,7},{5,6},{6,5},{7,4},{8,11},{9,10},{10,... | collective-permute-start | bytes 9224 | tf_op jit(solution)/shard_map/ppermute | solution.py:27
  102.9 0.7 collective-permute-done.27
  103.6 0.9 collective-permute-done.28
  104.7 0.8 copy.33
  (110 shorter events, 8.2 us)
Async XLA Ops:
  0.0 7.9 %copy-start.4 = (s32[4,3]{1,0:T(4,128)S(1)}, s32[4,3]{1,0:T(4,128)}, u32[]{:S(2)}) copy-start(s32[4,3]{1,0:T(4,128)} %param.13) | copy-start | bytes 148
  0.0 8.8 %copy-start = (bf16[1024,3,256]{2,0,1:T(8,128)(2,1)S(1)}, bf16[1024,3,256]{2,0,1:T(8,128)(2,1)}, u32[]{:S(2)}) copy-start(bf16[1024,3,256]{2,0,1:T(8,128)(2,1)} %param.8) | copy-start | bytes 4718596
  2.0 17.6 %collective-permute-start = (bf16[2,96,1024]{2,1,0:T(8,128)(2,1)}, bf16[2,96,1024]{2,1,0:T(8,128)(2,1)}, u32[]{:S(2)}, u32[]{:S(2)}) collective-permute-start(bf16[2,96,1024]{2,1,0:T(8,128)(2,1)} %pad_maximum_fusion.2), channel_id=1, source_target_pairs={{0,4},{4,0},{8,12},{12,8},{16,20},{20,16},{24,28},{28,24},{1,5},{5... | collective-permute-start | bytes 1179656 | tf_op jit(solution)/shard_map/ppermute | solution.py:114
  3.2 18.7 %collective-permute-start.8 = (bf16[2,96,1024]{2,1,0:T(8,128)(2,1)}, bf16[2,96,1024]{2,1,0:T(8,128)(2,1)}, u32[]{:S(2)}, u32[]{:S(2)}) collective-permute-start(bf16[2,96,1024]{2,1,0:T(8,128)(2,1)} %pad_maximum_fusion.2), channel_id=1, source_target_pairs={{0,8},{4,12},{8,0},{12,4},{16,24},{20,28},{24,16},{28,20},{1,9},{5... | collective-permute-start | bytes 1179656 | tf_op jit(solution)/shard_map/ppermute | solution.py:114
  3.4 28.8 %collective-permute-start.10 = (bf16[2,96,1024]{2,1,0:T(8,128)(2,1)}, bf16[2,96,1024]{2,1,0:T(8,128)(2,1)}, u32[]{:S(2)}, u32[]{:S(2)}) collective-permute-start(bf16[2,96,1024]{2,1,0:T(8,128)(2,1)} %pad_maximum_fusion.2), channel_id=1, source_target_pairs={{0,12},{4,8},{8,4},{12,0},{16,28},{20,24},{24,20},{28,16},{1,13},{... | collective-permute-start | bytes 1179656 | tf_op jit(solution)/shard_map/ppermute | solution.py:114
  4.6 22.2 %collective-permute-start.12 = (bf16[96,1024]{1,0:T(8,128)(2,1)S(1)}, bf16[96,1024]{1,0:T(8,128)(2,1)S(1)}, u32[]{:S(2)}, u32[]{:S(2)}) collective-permute-start(bf16[96,1024]{1,0:T(8,128)(2,1)S(1)} %bitcast.145), channel_id=1, source_target_pairs={{0,16},{4,20},{8,24},{12,28},{16,0},{20,4},{24,8},{28,12},{1,17},{... | collective-permute-start | bytes 589832 | tf_op jit(solution)/shard_map/ppermute | solution.py:118
  6.9 24.0 %collective-permute-start.15 = (bf16[96,1024]{1,0:T(8,128)(2,1)S(1)}, bf16[96,1024]{1,0:T(8,128)(2,1)S(1)}, u32[]{:S(2)}, u32[]{:S(2)}) collective-permute-start(bf16[96,1024]{1,0:T(8,128)(2,1)S(1)} %bitcast.146), channel_id=1, source_target_pairs={{0,20},{4,16},{8,28},{12,24},{16,4},{20,0},{24,12},{28,8},{1,21},{... | collective-permute-start | bytes 589832 | tf_op jit(solution)/shard_map/ppermute | solution.py:118
  8.8 1.9 %copy-start.5 = (s32[3,7]{1,0:T(4,128)S(1)}, s32[3,7]{1,0:T(4,128)}, u32[]{:S(2)}) copy-start(s32[3,7]{1,0:T(4,128)} %param.12) | copy-start | bytes 256
  10.7 2.0 %copy-start.1 = (bf16[384,3,256]{2,0,1:T(8,128)(2,1)}, bf16[384,3,256]{2,0,1:T(8,128)(2,1)S(1)}, u32[]{:S(2)}) copy-start(bf16[384,3,256]{2,0,1:T(8,128)(2,1)S(1)} %convolution_convert_fusion.1) | copy-start | bytes 1769476
  12.7 4.3 %slice-start = ((bf16[1024,3,256]{2,0,1:T(8,128)(2,1)}), bf16[1024,2,256]{2,0,1:T(8,128)(2,1)S(1)}, s32[]{:S(2)}) async-start(bf16[1024,3,256]{2,0,1:T(8,128)(2,1)} %param.8), calls=%async_computation | async-start | bytes 2097152 | tf_op jit(solution)/shard_map/slice | solution.py:281
  15.9 1.6 %slice-start.1 = ((bf16[384,3,256]{2,0,1:T(8,128)(2,1)}), bf16[384,2,256]{2,0,1:T(8,128)(2,1)S(1)}, s32[]{:S(2)}) async-start(bf16[384,3,256]{2,0,1:T(8,128)(2,1)} %copy-done.1), calls=%async_computation.1 | async-start | bytes 786432 | tf_op jit(solution)/shard_map/slice | solution.py:276
  18.0 23.4 %copy-start.3 = (bf16[256,256]{0,1:T(8,128)(2,1)S(1)}, bf16[256,256]{0,1:T(8,128)(2,1)}, u32[]{:S(2)}) copy-start(bf16[256,256]{0,1:T(8,128)(2,1)} %copy.38) | copy-start | bytes 393220
  19.6 21.8 %collective-permute-start.18 = (bf16[96,1024]{1,0:T(8,128)(2,1)S(1)}, bf16[96,1024]{1,0:T(8,128)(2,1)S(1)}, u32[]{:S(2)}, u32[]{:S(2)}) collective-permute-start(bf16[96,1024]{1,0:T(8,128)(2,1)S(1)} %bitcast.147), channel_id=1, source_target_pairs={{0,24},{4,28},{8,16},{12,20},{16,8},{20,12},{24,0},{28,4},{1,25},{... | collective-permute-start | bytes 589832 | tf_op jit(solution)/shard_map/ppermute | solution.py:118
  21.9 24.9 %collective-permute-start.21 = (bf16[96,1024]{1,0:T(8,128)(2,1)S(1)}, bf16[96,1024]{1,0:T(8,128)(2,1)S(1)}, u32[]{:S(2)}, u32[]{:S(2)}) collective-permute-start(bf16[96,1024]{1,0:T(8,128)(2,1)S(1)} %bitcast.148), channel_id=1, source_target_pairs={{0,28},{4,24},{8,20},{12,16},{16,12},{20,8},{24,4},{28,0},{1,29},{... | collective-permute-start | bytes 589832 | tf_op jit(solution)/shard_map/ppermute | solution.py:118
  26.8 24.1 %collective-permute-start.2 = (bf16[96,1024]{1,0:T(8,128)(2,1)S(1)}, bf16[96,1024]{1,0:T(8,128)(2,1)S(1)}, u32[]{:S(2)}, u32[]{:S(2)}) collective-permute-start(bf16[96,1024]{1,0:T(8,128)(2,1)S(1)} %bitcast.149), channel_id=1, source_target_pairs={{4,8},{12,16},{20,24},{8,4},{16,12},{24,20},{5,9},{13,17},{21,25},... | collective-permute-start | bytes 589832 | tf_op jit(solution)/shard_map/ppermute | solution.py:109
  30.9 17.1 %collective-permute-start.13 = (bf16[1,96,1024]{2,1,0:T(8,128)(2,1)S(1)}, bf16[1,96,1024]{2,1,0:T(8,128)(2,1)S(1)}, u32[]{:S(2)}, u32[]{:S(2)}) collective-permute-start(bf16[1,96,1024]{2,1,0:T(8,128)(2,1)S(1)} %bitcast.135), channel_id=1, source_target_pairs={{0,2},{1,3},{2,0},{3,1},{4,6},{5,7},{6,4},{7,5},{8,10},{9,11},{10,... | collective-permute-start | bytes 589832 | tf_op jit(solution)/shard_map/ppermute | solution.py:27
  32.1 16.1 %collective-permute-start.16 = (bf16[1,96,1024]{2,1,0:T(8,128)(2,1)S(1)}, bf16[1,96,1024]{2,1,0:T(8,128)(2,1)S(1)}, u32[]{:S(2)}, u32[]{:S(2)}) collective-permute-start(bf16[1,96,1024]{2,1,0:T(8,128)(2,1)S(1)} %bitcast.132), channel_id=1, source_target_pairs={{0,2},{1,3},{2,0},{3,1},{4,6},{5,7},{6,4},{7,5},{8,10},{9,11},{10,... | collective-permute-start | bytes 589832 | tf_op jit(solution)/shard_map/ppermute | solution.py:27
  41.4 31.3 %collective-permute-start.5 = (bf16[256,256]{0,1:T(8,128)(2,1)S(1)}, bf16[256,256]{0,1:T(8,128)(2,1)S(1)}, u32[]{:S(2)}, u32[]{:S(2)}) collective-permute-start(bf16[256,256]{0,1:T(8,128)(2,1)S(1)} %copy-done.3), channel_id=1, source_target_pairs={{0,1},{1,0},{2,3},{3,2},{4,5},{5,4},{6,7},{7,6},{8,9},{9,8},{10,11... | collective-permute-start | bytes 393224 | tf_op jit(solution)/shard_map/ppermute | solution.py:27
  46.8 5.4 %collective-permute-start.19 = (bf16[1,96,1024]{2,1,0:T(8,128)(2,1)S(1)}, bf16[1,96,1024]{2,1,0:T(8,128)(2,1)S(1)}, u32[]{:S(2)}, u32[]{:S(2)}) collective-permute-start(bf16[1,96,1024]{2,1,0:T(8,128)(2,1)S(1)} %bitcast.138), channel_id=1, source_target_pairs={{0,2},{1,3},{2,0},{3,1},{4,6},{5,7},{6,4},{7,5},{8,10},{9,11},{10,... | collective-permute-start | bytes 589832 | tf_op jit(solution)/shard_map/ppermute | solution.py:27
  48.0 7.5 %collective-permute-start.22 = (bf16[1,96,1024]{2,1,0:T(8,128)(2,1)S(1)}, bf16[1,96,1024]{2,1,0:T(8,128)(2,1)S(1)}, u32[]{:S(2)}, u32[]{:S(2)}) collective-permute-start(bf16[1,96,1024]{2,1,0:T(8,128)(2,1)S(1)} %bitcast.141), channel_id=1, source_target_pairs={{0,2},{1,3},{2,0},{3,1},{4,6},{5,7},{6,4},{7,5},{8,10},{9,11},{10,... | collective-permute-start | bytes 589832 | tf_op jit(solution)/shard_map/ppermute | solution.py:27
  48.3 18.2 %collective-permute-start.1 = (bf16[2,96,1024]{2,1,0:T(8,128)(2,1)}, bf16[2,96,1024]{2,1,0:T(8,128)(2,1)S(1)}, u32[]{:S(2)}, u32[]{:S(2)}) collective-permute-start(bf16[2,96,1024]{2,1,0:T(8,128)(2,1)} %collective-permute-done), channel_id=1, source_target_pairs={{0,1},{1,0},{2,3},{3,2},{4,5},{5,4},{6,7},{7,6},{8,9},{9,8},{10,11... | collective-permute-start | bytes 1179656 | tf_op jit(solution)/shard_map/ppermute | solution.py:27
  50.9 21.8 %collective-permute-start.6 = (bf16[256,256]{0,1:T(8,128)(2,1)S(1)}, bf16[256,256]{0,1:T(8,128)(2,1)S(1)}, u32[]{:S(2)}, u32[]{:S(2)}) collective-permute-start(bf16[256,256]{0,1:T(8,128)(2,1)S(1)} %copy.39), channel_id=1, source_target_pairs={{0,2},{1,3},{2,0},{3,1},{4,6},{5,7},{6,4},{7,5},{8,10},{9,11},{10,... | collective-permute-start | bytes 393224 | tf_op jit(solution)/shard_map/ppermute | solution.py:27
  52.2 10.3 %collective-permute-start.3 = (bf16[1,96,1024]{2,1,0:T(8,128)(2,1)S(1)}, bf16[1,96,1024]{2,1,0:T(8,128)(2,1)S(1)}, u32[]{:S(2)}, u32[]{:S(2)}) collective-permute-start(bf16[1,96,1024]{2,1,0:T(8,128)(2,1)S(1)} %bitcast.121), channel_id=1, source_target_pairs={{0,2},{1,3},{2,0},{3,1},{4,6},{5,7},{6,4},{7,5},{8,10},{9,11},{10,... | collective-permute-start | bytes 589832 | tf_op jit(solution)/shard_map/ppermute | solution.py:27
  55.5 11.1 %collective-permute-start.9 = (bf16[2,96,1024]{2,1,0:T(8,128)(2,1)}, bf16[2,96,1024]{2,1,0:T(8,128)(2,1)S(1)}, u32[]{:S(2)}, u32[]{:S(2)}) collective-permute-start(bf16[2,96,1024]{2,1,0:T(8,128)(2,1)} %collective-permute-done.8), channel_id=1, source_target_pairs={{0,1},{1,0},{2,3},{3,2},{4,5},{5,4},{6,7},{7,6},{8,9},{9,8},{10,11... | collective-permute-start | bytes 1179656 | tf_op jit(solution)/shard_map/ppermute | solution.py:27
  62.5 10.2 %collective-permute-start.7 = (bf16[256,256]{0,1:T(8,128)(2,1)S(1)}, bf16[256,256]{0,1:T(8,128)(2,1)S(1)}, u32[]{:S(2)}, u32[]{:S(2)}) collective-permute-start(bf16[256,256]{0,1:T(8,128)(2,1)S(1)} %copy.40), channel_id=1, source_target_pairs={{0,3},{1,2},{2,1},{3,0},{4,7},{5,6},{6,5},{7,4},{8,11},{9,10},{10,... | collective-permute-start | bytes 393224 | tf_op jit(solution)/shard_map/ppermute | solution.py:27
  66.5 2.0 %collective-permute-start.11 = (bf16[2,96,1024]{2,1,0:T(8,128)(2,1)}, bf16[2,96,1024]{2,1,0:T(8,128)(2,1)S(1)}, u32[]{:S(2)}, u32[]{:S(2)}) collective-permute-start(bf16[2,96,1024]{2,1,0:T(8,128)(2,1)} %collective-permute-done.10), channel_id=1, source_target_pairs={{0,1},{1,0},{2,3},{3,2},{4,5},{5,4},{6,7},{7,6},{8,9},{9,8},{10,11... | collective-permute-start | bytes 1179656 | tf_op jit(solution)/shard_map/ppermute | solution.py:27
  66.6 2.2 %collective-permute-start.14 = (bf16[2,96,1024]{2,1,0:T(8,128)(2,1)S(1)}, bf16[2,96,1024]{2,1,0:T(8,128)(2,1)S(1)}, u32[]{:S(2)}, u32[]{:S(2)}) collective-permute-start(bf16[2,96,1024]{2,1,0:T(8,128)(2,1)S(1)} %pad_maximum_fusion.4), channel_id=1, source_target_pairs={{0,1},{1,0},{2,3},{3,2},{4,5},{5,4},{6,7},{7,6},{8,9},{9,8},{10,11... | collective-permute-start | bytes 1179656 | tf_op jit(solution)/shard_map/ppermute | solution.py:27
  68.5 1.7 %collective-permute-start.17 = (bf16[2,96,1024]{2,1,0:T(8,128)(2,1)S(1)}, bf16[2,96,1024]{2,1,0:T(8,128)(2,1)S(1)}, u32[]{:S(2)}, u32[]{:S(2)}) collective-permute-start(bf16[2,96,1024]{2,1,0:T(8,128)(2,1)S(1)} %pad_maximum_fusion.5), channel_id=1, source_target_pairs={{0,1},{1,0},{2,3},{3,2},{4,5},{5,4},{6,7},{7,6},{8,9},{9,8},{10,11... | collective-permute-start | bytes 1179656 | tf_op jit(solution)/shard_map/ppermute | solution.py:27
  68.8 1.9 %collective-permute-start.20 = (bf16[2,96,1024]{2,1,0:T(8,128)(2,1)S(1)}, bf16[2,96,1024]{2,1,0:T(8,128)(2,1)S(1)}, u32[]{:S(2)}, u32[]{:S(2)}) collective-permute-start(bf16[2,96,1024]{2,1,0:T(8,128)(2,1)S(1)} %pad_maximum_fusion.6), channel_id=1, source_target_pairs={{0,1},{1,0},{2,3},{3,2},{4,5},{5,4},{6,7},{7,6},{8,9},{9,8},{10,11... | collective-permute-start | bytes 1179656 | tf_op jit(solution)/shard_map/ppermute | solution.py:27
  70.2 1.7 %collective-permute-start.23 = (bf16[2,96,1024]{2,1,0:T(8,128)(2,1)S(1)}, bf16[2,96,1024]{2,1,0:T(8,128)(2,1)S(1)}, u32[]{:S(2)}, u32[]{:S(2)}) collective-permute-start(bf16[2,96,1024]{2,1,0:T(8,128)(2,1)S(1)} %pad_maximum_fusion.7), channel_id=1, source_target_pairs={{0,1},{1,0},{2,3},{3,2},{4,5},{5,4},{6,7},{7,6},{8,9},{9,8},{10,11... | collective-permute-start | bytes 1179656 | tf_op jit(solution)/shard_map/ppermute | solution.py:27
  70.8 1.9 %collective-permute-start.4 = (bf16[2,96,1024]{2,1,0:T(8,128)(2,1)S(1)}, bf16[2,96,1024]{2,1,0:T(8,128)(2,1)S(1)}, u32[]{:S(2)}, u32[]{:S(2)}) collective-permute-start(bf16[2,96,1024]{2,1,0:T(8,128)(2,1)S(1)} %pad_maximum_fusion.3), channel_id=1, source_target_pairs={{0,1},{1,0},{2,3},{3,2},{4,5},{5,4},{6,7},{7,6},{8,9},{9,8},{10,11... | collective-permute-start | bytes 1179656 | tf_op jit(solution)/shard_map/ppermute | solution.py:27
  72.6 0.6 copy-start.8
  72.7 0.7 copy-start.10
  90.0 10.0 %copy-start.2 = (bf16[3,128,256]{2,1,0:T(8,128)(2,1)S(1)}, bf16[3,128,256]{2,1,0:T(8,128)(2,1)}, u32[]{:S(2)}) copy-start(bf16[3,128,256]{2,1,0:T(8,128)(2,1)} %shard_map.73) | copy-start | bytes 589828
  90.0 10.0 %copy-start.9 = (bf16[256,256]{0,1:T(8,128)(2,1)S(1)}, bf16[256,256]{0,1:T(8,128)(2,1)}, u32[]{:S(2)}) copy-start(bf16[256,256]{0,1:T(8,128)(2,1)} %copy-done.8) | copy-start | bytes 393220
  90.0 10.0 %copy-start.11 = (bf16[256,256]{0,1:T(8,128)(2,1)S(1)}, bf16[256,256]{0,1:T(8,128)(2,1)}, u32[]{:S(2)}) copy-start(bf16[256,256]{0,1:T(8,128)(2,1)} %copy-done.10) | copy-start | bytes 393220
  90.0 6.6 %collective-permute-start.24 = (bf16[1,384,256]{2,1,0:T(8,128)(2,1)}, bf16[1,384,256]{2,1,0:T(8,128)(2,1)S(1)}, u32[]{:S(2)}, u32[]{:S(2)}) collective-permute-start(bf16[1,384,256]{2,1,0:T(8,128)(2,1)} %bitcast.153), channel_id=1, source_target_pairs={{0,2},{1,3},{2,0},{3,1},{4,6},{5,7},{6,4},{7,5},{8,10},{9,11},{10,... | collective-permute-start | bytes 589832 | tf_op jit(solution)/shard_map/ppermute | solution.py:27
  97.6 2.4 %collective-permute-start.25 = (bf16[2,384,256]{2,1,0:T(8,128)(2,1)S(1)}, bf16[2,384,256]{2,1,0:T(8,128)(2,1)S(1)}, u32[]{:S(2)}, u32[]{:S(2)}) collective-permute-start(bf16[2,384,256]{2,1,0:T(8,128)(2,1)S(1)} %pad_maximum_fusion.8), channel_id=1, source_target_pairs={{0,1},{1,0},{2,3},{3,2},{4,5},{5,4},{6,7},{7,6},{8,9},{9,8},{10,11... | collective-permute-start | bytes 1179656 | tf_op jit(solution)/shard_map/ppermute | solution.py:27
  100.0 4.5 %copy-start.6 = (f32[256]{0:T(256)S(1)}, f32[256]{0:T(256)}, u32[]{:S(2)}) copy-start(f32[256]{0:T(256)} %param.11) | copy-start | bytes 3076
  100.1 4.5 %copy-start.7 = (f32[256]{0:T(256)S(1)}, f32[256]{0:T(256)}, u32[]{:S(2)}) copy-start(f32[256]{0:T(256)} %param.10) | copy-start | bytes 3076
  100.7 2.2 %collective-permute-start.26 = (f32[384,2]{0,1:T(2,128)S(1)}, f32[384,2]{0,1:T(2,128)S(1)}, u32[]{:S(2)}, u32[]{:S(2)}) collective-permute-start(f32[384,2]{0,1:T(2,128)S(1)} %get-tuple-element.52), channel_id=1, source_target_pairs={{0,1},{1,0},{2,3},{3,2},{4,5},{5,4},{6,7},{7,6},{8,9},{9,8},{10,11... | collective-permute-start | bytes 9224 | tf_op jit(solution)/shard_map/ppermute | solution.py:27
  101.1 2.4 %collective-permute-start.27 = (f32[384,2]{0,1:T(2,128)S(1)}, f32[384,2]{0,1:T(2,128)S(1)}, u32[]{:S(2)}, u32[]{:S(2)}) collective-permute-start(f32[384,2]{0,1:T(2,128)S(1)} %get-tuple-element.52), channel_id=1, source_target_pairs={{0,2},{1,3},{2,0},{3,1},{4,6},{5,7},{6,4},{7,5},{8,10},{9,11},{10,... | collective-permute-start | bytes 9224 | tf_op jit(solution)/shard_map/ppermute | solution.py:27
  101.4 3.1 %collective-permute-start.28 = (f32[384,2]{0,1:T(2,128)S(1)}, f32[384,2]{0,1:T(2,128)S(1)}, u32[]{:S(2)}, u32[]{:S(2)}) collective-permute-start(f32[384,2]{0,1:T(2,128)S(1)} %get-tuple-element.52), channel_id=1, source_target_pairs={{0,3},{1,2},{2,1},{3,0},{4,7},{5,6},{6,5},{7,4},{8,11},{9,10},{10,... | collective-permute-start | bytes 9224 | tf_op jit(solution)/shard_map/ppermute | solution.py:27

commit v8 on v7

--- a/solution.py
+++ b/solution.py
@@ -106,8 +106,11 @@
     heads_axis = lax.axis_size("head")
     matches = targets.shape[0]
     far = [(j, j + 1) for j in range(1, groups - 1, 2)] + [(j, j - 1) for j in range(2, groups, 2)]
-    other = spread_stack(lax.ppermute(mine, "node", far), heads_axis)
     near = near_rows(node_states, blocks_here, sub_rows)
+    if heads_axis == 4:
+        other = pair_stack(lax.ppermute(near, "node", far), heads_axis)
+    else:
+        other = spread_stack(lax.ppermute(mine, "node", far), heads_axis)
     every = jnp.stack(
         [
             pair_stack(

time: 106 us -> 107 us (level)
  the two profiles are of different devices: /device:TPU:9 before, /device:TPU:13 now
where the time goes in v8:
time: 107 us; the launch traced here: 106 us
  starting transfers between devices  37.4 us (35%)
  waiting for transfers between devices  29.7 us (28%)
  local copies, waits for them, and re-layouts  14.1 us (13%)
  Pallas kernels  10.8 us (10%)
  matrix products  6.69 us (6%)
  other arithmetic  4.68 us (4%)
  between operations  3.08 us (3%)
    ppermute x20, starting transfers between devices, flip_heads(): return lax.ppermute(array, 'head', [(i, i ^ flip) for i in range(devices)])  24.9 us
    ppermute x20, waiting for transfers between devices, flip_heads(): return lax.ppermute(array, 'head', [(i, i ^ flip) for i in range(devices)])  16.7 us
    pallas_call x1, Pallas kernels, attention(): pl.pallas_call(attention_kernel, out_shape=jax.ShapeDtypeStruct(query.sha...  10.8 us
    ppermute x1, waiting for transfers between devices, static_keys(): other = pair_stack(lax.ppermute(near, 'node', far), heads_axis)  8.34 us
    ppermute x4, starting transfers between devices, static_keys(): lax.ppermute(mine, 'node', [(i, i ^ shift) for i in range(groups)])  6.89 us
    dot_general x1, matrix products, kv_of_spread(): jnp.dot(rows, w_kv, preferred_element_type=jnp.float32).astype(jnp.bfloat16)  4.28 us
    slice x8, local copies, waits for them, and re-layouts, pair_stack(): return jnp.stack([received[0], beside[0], received[1], beside[1]])  3.28 us
    ppermute x1, starting transfers between devices, static_keys(): other = pair_stack(lax.ppermute(near, 'node', far), heads_axis)  3.04 us
  transfers between devices with their start and end apart: 28, of which 13 were waited for; matrix products, arithmetic and copies ran while one was open for 14% of the time, Pallas kernels for 0%

profile of v8, /device:TPU:13, one launch (start us, length us, event | category | flops | bytes accessed | tf_op | source)
XLA Modules:
  0.0 106.5 jit_solution(6529705193462133565)
XLA Ops:
  0.0 1.2 %constant_dynamic-slice_fusion.8 = (bf16[3,1,32,1024]{3,2,1,0:T(8,128)(2,1)S(1)}, bf16[3,1,32,1024]{3,2,1,0:T(8,128)(2,1)S(1)}) fusion(bf16[3,4,32,1024]{3,2,1,0:T(8,128)(2,1)} %bitcast.147, s32[]{:T(128)S(6)} %select_n.62, s32[]{:T(128)S(6)} %select_n.63), kind=kLoop, calls=%fused_computation.66 | loop fusion | bytes 786440 | tf_op jit(solution)/shard_map/jit(dynamic_index_in_dim)/dynamic_slice | solution.py:145
  1.2 0.8 pad_maximum_fusion.2
  2.2 2.4 %collective-permute-start.9 = (bf16[2,96,1024]{2,1,0:T(8,128)(2,1)}, bf16[2,96,1024]{2,1,0:T(8,128)(2,1)}, u32[]{:S(2)}, u32[]{:S(2)}) collective-permute-start(bf16[2,96,1024]{2,1,0:T(8,128)(2,1)} %pad_maximum_fusion.2), channel_id=1, source_target_pairs={{0,12},{4,8},{8,4},{12,0},{16,28},{20,24},{24,20},{28,16},{1,13},{... | collective-permute-start | bytes 1179656 | tf_op jit(solution)/shard_map/ppermute | solution.py:117
  4.6 2.3 %collective-permute-start.11 = (bf16[96,1024]{1,0:T(8,128)(2,1)S(1)}, bf16[96,1024]{1,0:T(8,128)(2,1)S(1)}, u32[]{:S(2)}, u32[]{:S(2)}) collective-permute-start(bf16[96,1024]{1,0:T(8,128)(2,1)S(1)} %bitcast.142), channel_id=1, source_target_pairs={{0,16},{4,20},{8,24},{12,28},{16,0},{20,4},{24,8},{28,12},{1,17},{... | collective-permute-start | bytes 589832 | tf_op jit(solution)/shard_map/ppermute | solution.py:121
  7.2 0.6 add_select_fusion.pick_ref
  7.8 1.9 %convolution_convert_fusion.1 = bf16[384,3,256]{2,0,1:T(8,128)(2,1)S(1)} fusion(bf16[1024,3,256]{2,0,1:T(8,128)(2,1)S(1)} %copy-done, bf16[384,1024]{1,0:T(8,128)(2,1)} %param.7), kind=kOutput, calls=%fused_computation.1 | convolution fusion | flops 604274688 | bytes 2949120 | tf_op jit(solution)/shard_map/nd,dtf->ntf/dot_general | solution.py:275
  9.8 1.3 %constant_dynamic-slice_fusion.3 = (bf16[256,256]{1,0:T(8,128)(2,1)S(1)}, bf16[256,256]{1,0:T(8,128)(2,1)S(1)}, bf16[256,256]{1,0:T(8,128)(2,1)S(1)}, bf16[256,256]{1,0:T(8,128)(2,1)S(1)}) fusion(bf16[256,1024]{1,0:T(8,128)(2,1)} %param.9, s32[]{:T(128)S(6)} %select_n.68, s32[]{:T(128)S(6)} %select_n.67, s32[]{:T(128)S(6)} %select_n.66, s32[]{:T(128)S(6)} %select_n.58), kind=kLoop, calls=%fused_computation.61 | loop fusion | bytes 1048592 | tf_op jit(solution)/shard_map/dynamic_slice | solution.py:269
  11.1 0.7 fusion.43
  11.7 0.7 slice.145
  14.9 0.8 copy.38
  16.0 0.5 copy.41
  17.0 1.0 reshape_reshape.6.own_ref
  18.0 0.5 pad_convert_fusion.live_ref
  18.6 1.3 %collective-permute-start.17 = (bf16[96,1024]{1,0:T(8,128)(2,1)S(1)}, bf16[96,1024]{1,0:T(8,128)(2,1)S(1)}, u32[]{:S(2)}, u32[]{:S(2)}) collective-permute-start(bf16[96,1024]{1,0:T(8,128)(2,1)S(1)} %bitcast.144), channel_id=1, source_target_pairs={{0,24},{4,28},{8,16},{12,20},{16,8},{20,12},{24,0},{28,4},{1,25},{... | collective-permute-start | bytes 589832 | tf_op jit(solution)/shard_map/ppermute | solution.py:121
  19.9 1.0 fusion.39
  20.9 3.0 %collective-permute-start.2 = (bf16[2,96,1024]{2,1,0:T(8,128)(2,1)}, bf16[2,96,1024]{2,1,0:T(8,128)(2,1)S(1)}, u32[]{:S(2)}, u32[]{:S(2)}) collective-permute-start(bf16[2,96,1024]{2,1,0:T(8,128)(2,1)} %pad_maximum_fusion.2), channel_id=1, source_target_pairs={{4,8},{12,16},{20,24},{8,4},{16,12},{24,20},{5,9},{13,17},{21,25},... | collective-permute-start | bytes 1179656 | tf_op jit(solution)/shard_map/ppermute | solution.py:111
  24.0 1.0 fusion.37
  25.0 2.2 %collective-permute-done.9 = bf16[2,96,1024]{2,1,0:T(8,128)(2,1)} collective-permute-done((bf16[2,96,1024]{2,1,0:T(8,128)(2,1)}, bf16[2,96,1024]{2,1,0:T(8,128)(2,1)}, u32[]{:S(2)}, u32[]{:S(2)}) %collective-permute-start.9) | collective-permute-done | bytes 393248 | tf_op jit(solution)/shard_map/ppermute | solution.py:117
  27.2 3.3 %collective-permute-start.20 = (bf16[96,1024]{1,0:T(8,128)(2,1)S(1)}, bf16[96,1024]{1,0:T(8,128)(2,1)S(1)}, u32[]{:S(2)}, u32[]{:S(2)}) collective-permute-start(bf16[96,1024]{1,0:T(8,128)(2,1)S(1)} %bitcast.145), channel_id=1, source_target_pairs={{0,28},{4,24},{8,20},{12,16},{16,12},{20,8},{24,4},{28,0},{1,29},{... | collective-permute-start | bytes 589832 | tf_op jit(solution)/shard_map/ppermute | solution.py:121
  30.5 1.0 fusion.35
  31.5 3.6 %collective-permute-start.4 = (bf16[256,256]{0,1:T(8,128)(2,1)S(1)}, bf16[256,256]{0,1:T(8,128)(2,1)S(1)}, u32[]{:S(2)}, u32[]{:S(2)}) collective-permute-start(bf16[256,256]{0,1:T(8,128)(2,1)S(1)} %copy-done.3), channel_id=1, source_target_pairs={{0,1},{1,0},{2,3},{3,2},{4,5},{5,4},{6,7},{7,6},{8,9},{9,8},{10,11... | collective-permute-start | bytes 393224 | tf_op jit(solution)/shard_map/ppermute | solution.py:27
  35.1 1.2 %collective-permute-start.12 = (bf16[1,96,1024]{2,1,0:T(8,128)(2,1)S(1)}, bf16[1,96,1024]{2,1,0:T(8,128)(2,1)S(1)}, u32[]{:S(2)}, u32[]{:S(2)}) collective-permute-start(bf16[1,96,1024]{2,1,0:T(8,128)(2,1)S(1)} %bitcast.132), channel_id=1, source_target_pairs={{0,2},{1,3},{2,0},{3,1},{4,6},{5,7},{6,4},{7,5},{8,10},{9,11},{10,... | collective-permute-start | bytes 589832 | tf_op jit(solution)/shard_map/ppermute | solution.py:27
  36.3 2.4 %collective-permute-done.17 = bf16[96,1024]{1,0:T(8,128)(2,1)S(1)} collective-permute-done((bf16[96,1024]{1,0:T(8,128)(2,1)S(1)}, bf16[96,1024]{1,0:T(8,128)(2,1)S(1)}, u32[]{:S(2)}, u32[]{:S(2)}) %collective-permute-start.17) | collective-permute-done | bytes 196640 | tf_op jit(solution)/shard_map/ppermute | solution.py:121
  38.8 1.2 %collective-permute-start.15 = (bf16[1,96,1024]{2,1,0:T(8,128)(2,1)S(1)}, bf16[1,96,1024]{2,1,0:T(8,128)(2,1)S(1)}, u32[]{:S(2)}, u32[]{:S(2)}) collective-permute-start(bf16[1,96,1024]{2,1,0:T(8,128)(2,1)S(1)} %bitcast.129), channel_id=1, source_target_pairs={{0,2},{1,3},{2,0},{3,1},{4,6},{5,7},{6,4},{7,5},{8,10},{9,11},{10,... | collective-permute-start | bytes 589832 | tf_op jit(solution)/shard_map/ppermute | solution.py:27
  40.0 8.3 %collective-permute-done.2 = bf16[2,96,1024]{2,1,0:T(8,128)(2,1)S(1)} collective-permute-done((bf16[2,96,1024]{2,1,0:T(8,128)(2,1)}, bf16[2,96,1024]{2,1,0:T(8,128)(2,1)S(1)}, u32[]{:S(2)}, u32[]{:S(2)}) %collective-permute-start.2) | collective-permute-done | bytes 393248 | tf_op jit(solution)/shard_map/ppermute | solution.py:111
  48.3 1.2 %collective-permute-start.18 = (bf16[1,96,1024]{2,1,0:T(8,128)(2,1)S(1)}, bf16[1,96,1024]{2,1,0:T(8,128)(2,1)S(1)}, u32[]{:S(2)}, u32[]{:S(2)}) collective-permute-start(bf16[1,96,1024]{2,1,0:T(8,128)(2,1)S(1)} %bitcast.135), channel_id=1, source_target_pairs={{0,2},{1,3},{2,0},{3,1},{4,6},{5,7},{6,4},{7,5},{8,10},{9,11},{10,... | collective-permute-start | bytes 589832 | tf_op jit(solution)/shard_map/ppermute | solution.py:27
  49.6 5.6 %collective-permute-start.1 = (bf16[2,96,1024]{2,1,0:T(8,128)(2,1)}, bf16[2,96,1024]{2,1,0:T(8,128)(2,1)S(1)}, u32[]{:S(2)}, u32[]{:S(2)}) collective-permute-start(bf16[2,96,1024]{2,1,0:T(8,128)(2,1)} %collective-permute-done), channel_id=1, source_target_pairs={{0,1},{1,0},{2,3},{3,2},{4,5},{5,4},{6,7},{7,6},{8,9},{9,8},{10,11... | collective-permute-start | bytes 1179656 | tf_op jit(solution)/shard_map/ppermute | solution.py:27
  55.2 0.5 collective-permute-start.5
  55.7 1.1 collective-permute-start.21
  56.8 3.2 %collective-permute-start.8 = (bf16[2,96,1024]{2,1,0:T(8,128)(2,1)}, bf16[2,96,1024]{2,1,0:T(8,128)(2,1)S(1)}, u32[]{:S(2)}, u32[]{:S(2)}) collective-permute-start(bf16[2,96,1024]{2,1,0:T(8,128)(2,1)} %collective-permute-done.7), channel_id=1, source_target_pairs={{0,1},{1,0},{2,3},{3,2},{4,5},{5,4},{6,7},{7,6},{8,9},{9,8},{10,11... | collective-permute-start | bytes 1179656 | tf_op jit(solution)/shard_map/ppermute | solution.py:27
  60.1 4.9 %collective-permute-done.21 = bf16[1,96,1024]{2,1,0:T(8,128)(2,1)S(1)} collective-permute-done((bf16[1,96,1024]{2,1,0:T(8,128)(2,1)S(1)}, bf16[1,96,1024]{2,1,0:T(8,128)(2,1)S(1)}, u32[]{:S(2)}, u32[]{:S(2)}) %collective-permute-start.21) | collective-permute-done | bytes 196640 | tf_op jit(solution)/shard_map/ppermute | solution.py:27
  65.0 2.3 %collective-permute-start.6 = (bf16[256,256]{0,1:T(8,128)(2,1)S(1)}, bf16[256,256]{0,1:T(8,128)(2,1)S(1)}, u32[]{:S(2)}, u32[]{:S(2)}) collective-permute-start(bf16[256,256]{0,1:T(8,128)(2,1)S(1)} %copy.40), channel_id=1, source_target_pairs={{0,3},{1,2},{2,1},{3,0},{4,7},{5,6},{6,5},{7,4},{8,11},{9,10},{10,... | collective-permute-start | bytes 393224 | tf_op jit(solution)/shard_map/ppermute | solution.py:27
  67.5 0.6 collective-permute-start.13
  68.1 1.3 %collective-permute-done.10 = bf16[2,96,1024]{2,1,0:T(8,128)(2,1)S(1)} collective-permute-done((bf16[2,96,1024]{2,1,0:T(8,128)(2,1)}, bf16[2,96,1024]{2,1,0:T(8,128)(2,1)S(1)}, u32[]{:S(2)}, u32[]{:S(2)}) %collective-permute-start.10) | collective-permute-done | bytes 393248 | tf_op jit(solution)/shard_map/ppermute | solution.py:27
  70.1 1.1 %collective-permute-done.16 = bf16[2,96,1024]{2,1,0:T(8,128)(2,1)S(1)} collective-permute-done((bf16[2,96,1024]{2,1,0:T(8,128)(2,1)S(1)}, bf16[2,96,1024]{2,1,0:T(8,128)(2,1)S(1)}, u32[]{:S(2)}, u32[]{:S(2)}) %collective-permute-start.16) | collective-permute-done | bytes 393248 | tf_op jit(solution)/shard_map/ppermute | solution.py:27
  72.0 0.9 collective-permute-done.22
  74.9 0.9 copy.31
  75.8 4.3 %convolution_convert_fusion = bf16[2304,512]{1,0:T(8,128)(2,1)} fusion(bf16[2304,1024]{1,0:T(8,128)(2,1)S(1)} %bitcast.107, bf16[1024,512]{0,1:T(8,128)(2,1)S(1)} %bitcast.128), kind=kOutput, calls=%fused_computation | convolution fusion | flops 2417098752 | bytes 8126464 | tf_op jit(solution)/shard_map/dot_general | solution.py:174
  80.1 10.8 %shard_map.73 = bf16[3,128,256]{2,1,0:T(8,128)(2,1)} custom-call(s32[3,11]{1,0:T(4,128)} %pad_convert_fusion.live_ref, s32[4,3]{1,0:T(4,128)} %add_select_fusion.pick_ref, bf16[3,128,256]{2,1,0:T(8,128)(2,1)} %bitcast.148, bf16[3,128,512]{2,1,0:T(8,128)(2,1)} %reshape_reshape.6.own_ref, bf16[6,3,128,512]{3,2,1,0:T(8,128)(2,1)} %bitcast.159), custom_call_target="tpu_custom_call" | custom-call | flops 1107296256 | bytes 3145728 | tf_op jit(solution)/shard_map/pallas_call | solution.py:241
  91.3 6.3 %collective-permute-done.23 = bf16[1,384,256]{2,1,0:T(8,128)(2,1)S(1)} collective-permute-done((bf16[1,384,256]{2,1,0:T(8,128)(2,1)}, bf16[1,384,256]{2,1,0:T(8,128)(2,1)S(1)}, u32[]{:S(2)}, u32[]{:S(2)}) %collective-permute-start.23) | collective-permute-done | bytes 196640 | tf_op jit(solution)/shard_map/ppermute | solution.py:27
  97.6 1.0 pad_maximum_fusion.7
  98.5 1.0 collective-permute-start.24
  99.6 0.9 constant_dynamic-slice_fusion.9
  101.0 0.5 fusion.44
  102.3 1.5 %collective-permute-start.27 = (f32[384,2]{0,1:T(2,128)S(1)}, f32[384,2]{0,1:T(2,128)S(1)}, u32[]{:S(2)}, u32[]{:S(2)}) collective-permute-start(f32[384,2]{0,1:T(2,128)S(1)} %get-tuple-element.54), channel_id=1, source_target_pairs={{0,3},{1,2},{2,1},{3,0},{4,7},{5,6},{6,5},{7,4},{8,11},{9,10},{10,... | collective-permute-start | bytes 9224 | tf_op jit(solution)/shard_map/ppermute | solution.py:27
  103.8 0.7 collective-permute-done.26
  104.5 0.9 collective-permute-done.27
  105.7 0.8 copy.33
  (108 shorter events, 6.7 us)
Async XLA Ops:
  0.0 6.9 %copy-start.4 = (s32[4,3]{1,0:T(4,128)S(1)}, s32[4,3]{1,0:T(4,128)}, u32[]{:S(2)}) copy-start(s32[4,3]{1,0:T(4,128)} %param.13) | copy-start | bytes 148
  0.0 7.8 %copy-start = (bf16[1024,3,256]{2,0,1:T(8,128)(2,1)S(1)}, bf16[1024,3,256]{2,0,1:T(8,128)(2,1)}, u32[]{:S(2)}) copy-start(bf16[1024,3,256]{2,0,1:T(8,128)(2,1)} %param.8) | copy-start | bytes 4718596
  2.0 16.6 %collective-permute-start = (bf16[2,96,1024]{2,1,0:T(8,128)(2,1)}, bf16[2,96,1024]{2,1,0:T(8,128)(2,1)}, u32[]{:S(2)}, u32[]{:S(2)}) collective-permute-start(bf16[2,96,1024]{2,1,0:T(8,128)(2,1)} %pad_maximum_fusion.2), channel_id=1, source_target_pairs={{0,4},{4,0},{8,12},{12,8},{16,20},{20,16},{24,28},{28,24},{1,5},{5... | collective-permute-start | bytes 1179656 | tf_op jit(solution)/shard_map/ppermute | solution.py:117
  2.2 18.7 %collective-permute-start.7 = (bf16[2,96,1024]{2,1,0:T(8,128)(2,1)}, bf16[2,96,1024]{2,1,0:T(8,128)(2,1)}, u32[]{:S(2)}, u32[]{:S(2)}) collective-permute-start(bf16[2,96,1024]{2,1,0:T(8,128)(2,1)} %pad_maximum_fusion.2), channel_id=1, source_target_pairs={{0,8},{4,12},{8,0},{12,4},{16,24},{20,28},{24,16},{28,20},{1,9},{5... | collective-permute-start | bytes 1179656 | tf_op jit(solution)/shard_map/ppermute | solution.py:117
  2.2 25.0 %collective-permute-start.9 = (bf16[2,96,1024]{2,1,0:T(8,128)(2,1)}, bf16[2,96,1024]{2,1,0:T(8,128)(2,1)}, u32[]{:S(2)}, u32[]{:S(2)}) collective-permute-start(bf16[2,96,1024]{2,1,0:T(8,128)(2,1)} %pad_maximum_fusion.2), channel_id=1, source_target_pairs={{0,12},{4,8},{8,4},{12,0},{16,28},{20,24},{24,20},{28,16},{1,13},{... | collective-permute-start | bytes 1179656 | tf_op jit(solution)/shard_map/ppermute | solution.py:117
  4.6 26.9 %collective-permute-start.11 = (bf16[96,1024]{1,0:T(8,128)(2,1)S(1)}, bf16[96,1024]{1,0:T(8,128)(2,1)S(1)}, u32[]{:S(2)}, u32[]{:S(2)}) collective-permute-start(bf16[96,1024]{1,0:T(8,128)(2,1)S(1)} %bitcast.142), channel_id=1, source_target_pairs={{0,16},{4,20},{8,24},{12,28},{16,0},{20,4},{24,8},{28,12},{1,17},{... | collective-permute-start | bytes 589832 | tf_op jit(solution)/shard_map/ppermute | solution.py:121
  6.9 28.2 %collective-permute-start.14 = (bf16[96,1024]{1,0:T(8,128)(2,1)S(1)}, bf16[96,1024]{1,0:T(8,128)(2,1)S(1)}, u32[]{:S(2)}, u32[]{:S(2)}) collective-permute-start(bf16[96,1024]{1,0:T(8,128)(2,1)S(1)} %bitcast.143), channel_id=1, source_target_pairs={{0,20},{4,16},{8,28},{12,24},{16,4},{20,0},{24,12},{28,8},{1,21},{... | collective-permute-start | bytes 589832 | tf_op jit(solution)/shard_map/ppermute | solution.py:121
  7.8 1.9 %copy-start.5 = (s32[3,7]{1,0:T(4,128)S(1)}, s32[3,7]{1,0:T(4,128)}, u32[]{:S(2)}) copy-start(s32[3,7]{1,0:T(4,128)} %param.12) | copy-start | bytes 256
  9.7 2.0 %copy-start.1 = (bf16[384,3,256]{2,0,1:T(8,128)(2,1)}, bf16[384,3,256]{2,0,1:T(8,128)(2,1)S(1)}, u32[]{:S(2)}) copy-start(bf16[384,3,256]{2,0,1:T(8,128)(2,1)S(1)} %convolution_convert_fusion.1) | copy-start | bytes 1769476
  11.7 4.3 %slice-start = ((bf16[1024,3,256]{2,0,1:T(8,128)(2,1)}), bf16[1024,2,256]{2,0,1:T(8,128)(2,1)S(1)}, s32[]{:S(2)}) async-start(bf16[1024,3,256]{2,0,1:T(8,128)(2,1)} %param.8), calls=%async_computation | async-start | bytes 2097152 | tf_op jit(solution)/shard_map/slice | solution.py:284
  14.9 1.6 %slice-start.1 = ((bf16[384,3,256]{2,0,1:T(8,128)(2,1)}), bf16[384,2,256]{2,0,1:T(8,128)(2,1)S(1)}, s32[]{:S(2)}) async-start(bf16[384,3,256]{2,0,1:T(8,128)(2,1)} %copy-done.1), calls=%async_computation.1 | async-start | bytes 786432 | tf_op jit(solution)/shard_map/slice | solution.py:279
  17.0 14.5 %copy-start.3 = (bf16[256,256]{0,1:T(8,128)(2,1)S(1)}, bf16[256,256]{0,1:T(8,128)(2,1)}, u32[]{:S(2)}) copy-start(bf16[256,256]{0,1:T(8,128)(2,1)} %copy.38) | copy-start | bytes 393220
  18.6 20.2 %collective-permute-start.17 = (bf16[96,1024]{1,0:T(8,128)(2,1)S(1)}, bf16[96,1024]{1,0:T(8,128)(2,1)S(1)}, u32[]{:S(2)}, u32[]{:S(2)}) collective-permute-start(bf16[96,1024]{1,0:T(8,128)(2,1)S(1)} %bitcast.144), channel_id=1, source_target_pairs={{0,24},{4,28},{8,16},{12,20},{16,8},{20,12},{24,0},{28,4},{1,25},{... | collective-permute-start | bytes 589832 | tf_op jit(solution)/shard_map/ppermute | solution.py:121
  20.9 27.4 %collective-permute-start.2 = (bf16[2,96,1024]{2,1,0:T(8,128)(2,1)}, bf16[2,96,1024]{2,1,0:T(8,128)(2,1)S(1)}, u32[]{:S(2)}, u32[]{:S(2)}) collective-permute-start(bf16[2,96,1024]{2,1,0:T(8,128)(2,1)} %pad_maximum_fusion.2), channel_id=1, source_target_pairs={{4,8},{12,16},{20,24},{8,4},{16,12},{24,20},{5,9},{13,17},{21,25},... | collective-permute-start | bytes 1179656 | tf_op jit(solution)/shard_map/ppermute | solution.py:111
  27.2 28.0 %collective-permute-start.20 = (bf16[96,1024]{1,0:T(8,128)(2,1)S(1)}, bf16[96,1024]{1,0:T(8,128)(2,1)S(1)}, u32[]{:S(2)}, u32[]{:S(2)}) collective-permute-start(bf16[96,1024]{1,0:T(8,128)(2,1)S(1)} %bitcast.145), channel_id=1, source_target_pairs={{0,28},{4,24},{8,20},{12,16},{16,12},{20,8},{24,4},{28,0},{1,29},{... | collective-permute-start | bytes 589832 | tf_op jit(solution)/shard_map/ppermute | solution.py:121
  31.5 42.0 %collective-permute-start.4 = (bf16[256,256]{0,1:T(8,128)(2,1)S(1)}, bf16[256,256]{0,1:T(8,128)(2,1)S(1)}, u32[]{:S(2)}, u32[]{:S(2)}) collective-permute-start(bf16[256,256]{0,1:T(8,128)(2,1)S(1)} %copy-done.3), channel_id=1, source_target_pairs={{0,1},{1,0},{2,3},{3,2},{4,5},{5,4},{6,7},{7,6},{8,9},{9,8},{10,11... | collective-permute-start | bytes 393224 | tf_op jit(solution)/shard_map/ppermute | solution.py:27
  35.1 14.5 %collective-permute-start.12 = (bf16[1,96,1024]{2,1,0:T(8,128)(2,1)S(1)}, bf16[1,96,1024]{2,1,0:T(8,128)(2,1)S(1)}, u32[]{:S(2)}, u32[]{:S(2)}) collective-permute-start(bf16[1,96,1024]{2,1,0:T(8,128)(2,1)S(1)} %bitcast.132), channel_id=1, source_target_pairs={{0,2},{1,3},{2,0},{3,1},{4,6},{5,7},{6,4},{7,5},{8,10},{9,11},{10,... | collective-permute-start | bytes 589832 | tf_op jit(solution)/shard_map/ppermute | solution.py:27
  38.8 16.9 %collective-permute-start.15 = (bf16[1,96,1024]{2,1,0:T(8,128)(2,1)S(1)}, bf16[1,96,1024]{2,1,0:T(8,128)(2,1)S(1)}, u32[]{:S(2)}, u32[]{:S(2)}) collective-permute-start(bf16[1,96,1024]{2,1,0:T(8,128)(2,1)S(1)} %bitcast.129), channel_id=1, source_target_pairs={{0,2},{1,3},{2,0},{3,1},{4,6},{5,7},{6,4},{7,5},{8,10},{9,11},{10,... | collective-permute-start | bytes 589832 | tf_op jit(solution)/shard_map/ppermute | solution.py:27
  48.3 8.5 %collective-permute-start.18 = (bf16[1,96,1024]{2,1,0:T(8,128)(2,1)S(1)}, bf16[1,96,1024]{2,1,0:T(8,128)(2,1)S(1)}, u32[]{:S(2)}, u32[]{:S(2)}) collective-permute-start(bf16[1,96,1024]{2,1,0:T(8,128)(2,1)S(1)} %bitcast.135), channel_id=1, source_target_pairs={{0,2},{1,3},{2,0},{3,1},{4,6},{5,7},{6,4},{7,5},{8,10},{9,11},{10,... | collective-permute-start | bytes 589832 | tf_op jit(solution)/shard_map/ppermute | solution.py:27
  49.6 17.8 %collective-permute-start.1 = (bf16[2,96,1024]{2,1,0:T(8,128)(2,1)}, bf16[2,96,1024]{2,1,0:T(8,128)(2,1)S(1)}, u32[]{:S(2)}, u32[]{:S(2)}) collective-permute-start(bf16[2,96,1024]{2,1,0:T(8,128)(2,1)} %collective-permute-done), channel_id=1, source_target_pairs={{0,1},{1,0},{2,3},{3,2},{4,5},{5,4},{6,7},{7,6},{8,9},{9,8},{10,11... | collective-permute-start | bytes 1179656 | tf_op jit(solution)/shard_map/ppermute | solution.py:27
  55.2 18.4 %collective-permute-start.5 = (bf16[256,256]{0,1:T(8,128)(2,1)S(1)}, bf16[256,256]{0,1:T(8,128)(2,1)S(1)}, u32[]{:S(2)}, u32[]{:S(2)}) collective-permute-start(bf16[256,256]{0,1:T(8,128)(2,1)S(1)} %copy.39), channel_id=1, source_target_pairs={{0,2},{1,3},{2,0},{3,1},{4,6},{5,7},{6,4},{7,5},{8,10},{9,11},{10,... | collective-permute-start | bytes 393224 | tf_op jit(solution)/shard_map/ppermute | solution.py:27
  55.7 9.4 %collective-permute-start.21 = (bf16[1,96,1024]{2,1,0:T(8,128)(2,1)S(1)}, bf16[1,96,1024]{2,1,0:T(8,128)(2,1)S(1)}, u32[]{:S(2)}, u32[]{:S(2)}) collective-permute-start(bf16[1,96,1024]{2,1,0:T(8,128)(2,1)S(1)} %bitcast.138), channel_id=1, source_target_pairs={{0,2},{1,3},{2,0},{3,1},{4,6},{5,7},{6,4},{7,5},{8,10},{9,11},{10,... | collective-permute-start | bytes 589832 | tf_op jit(solution)/shard_map/ppermute | solution.py:27
  56.8 10.7 %collective-permute-start.8 = (bf16[2,96,1024]{2,1,0:T(8,128)(2,1)}, bf16[2,96,1024]{2,1,0:T(8,128)(2,1)S(1)}, u32[]{:S(2)}, u32[]{:S(2)}) collective-permute-start(bf16[2,96,1024]{2,1,0:T(8,128)(2,1)} %collective-permute-done.7), channel_id=1, source_target_pairs={{0,1},{1,0},{2,3},{3,2},{4,5},{5,4},{6,7},{7,6},{8,9},{9,8},{10,11... | collective-permute-start | bytes 1179656 | tf_op jit(solution)/shard_map/ppermute | solution.py:27
  65.0 8.6 %collective-permute-start.6 = (bf16[256,256]{0,1:T(8,128)(2,1)S(1)}, bf16[256,256]{0,1:T(8,128)(2,1)S(1)}, u32[]{:S(2)}, u32[]{:S(2)}) collective-permute-start(bf16[256,256]{0,1:T(8,128)(2,1)S(1)} %copy.40), channel_id=1, source_target_pairs={{0,3},{1,2},{2,1},{3,0},{4,7},{5,6},{6,5},{7,4},{8,11},{9,10},{10,... | collective-permute-start | bytes 393224 | tf_op jit(solution)/shard_map/ppermute | solution.py:27
  67.4 2.0 %collective-permute-start.10 = (bf16[2,96,1024]{2,1,0:T(8,128)(2,1)}, bf16[2,96,1024]{2,1,0:T(8,128)(2,1)S(1)}, u32[]{:S(2)}, u32[]{:S(2)}) collective-permute-start(bf16[2,96,1024]{2,1,0:T(8,128)(2,1)} %collective-permute-done.9), channel_id=1, source_target_pairs={{0,1},{1,0},{2,3},{3,2},{4,5},{5,4},{6,7},{7,6},{8,9},{9,8},{10,11... | collective-permute-start | bytes 1179656 | tf_op jit(solution)/shard_map/ppermute | solution.py:27
  67.5 2.2 %collective-permute-start.13 = (bf16[2,96,1024]{2,1,0:T(8,128)(2,1)S(1)}, bf16[2,96,1024]{2,1,0:T(8,128)(2,1)S(1)}, u32[]{:S(2)}, u32[]{:S(2)}) collective-permute-start(bf16[2,96,1024]{2,1,0:T(8,128)(2,1)S(1)} %pad_maximum_fusion.3), channel_id=1, source_target_pairs={{0,1},{1,0},{2,3},{3,2},{4,5},{5,4},{6,7},{7,6},{8,9},{9,8},{10,11... | collective-permute-start | bytes 1179656 | tf_op jit(solution)/shard_map/ppermute | solution.py:27
  69.4 1.7 %collective-permute-start.16 = (bf16[2,96,1024]{2,1,0:T(8,128)(2,1)S(1)}, bf16[2,96,1024]{2,1,0:T(8,128)(2,1)S(1)}, u32[]{:S(2)}, u32[]{:S(2)}) collective-permute-start(bf16[2,96,1024]{2,1,0:T(8,128)(2,1)S(1)} %pad_maximum_fusion.4), channel_id=1, source_target_pairs={{0,1},{1,0},{2,3},{3,2},{4,5},{5,4},{6,7},{7,6},{8,9},{9,8},{10,11... | collective-permute-start | bytes 1179656 | tf_op jit(solution)/shard_map/ppermute | solution.py:27
  69.8 1.9 %collective-permute-start.19 = (bf16[2,96,1024]{2,1,0:T(8,128)(2,1)S(1)}, bf16[2,96,1024]{2,1,0:T(8,128)(2,1)S(1)}, u32[]{:S(2)}, u32[]{:S(2)}) collective-permute-start(bf16[2,96,1024]{2,1,0:T(8,128)(2,1)S(1)} %pad_maximum_fusion.5), channel_id=1, source_target_pairs={{0,1},{1,0},{2,3},{3,2},{4,5},{5,4},{6,7},{7,6},{8,9},{9,8},{10,11... | collective-permute-start | bytes 1179656 | tf_op jit(solution)/shard_map/ppermute | solution.py:27
  71.1 1.7 %collective-permute-start.22 = (bf16[2,96,1024]{2,1,0:T(8,128)(2,1)S(1)}, bf16[2,96,1024]{2,1,0:T(8,128)(2,1)S(1)}, u32[]{:S(2)}, u32[]{:S(2)}) collective-permute-start(bf16[2,96,1024]{2,1,0:T(8,128)(2,1)S(1)} %pad_maximum_fusion.6), channel_id=1, source_target_pairs={{0,1},{1,0},{2,3},{3,2},{4,5},{5,4},{6,7},{7,6},{8,9},{9,8},{10,11... | collective-permute-start | bytes 1179656 | tf_op jit(solution)/shard_map/ppermute | solution.py:27
  71.7 1.9 %collective-permute-start.3 = (bf16[2,96,1024]{2,1,0:T(8,128)(2,1)S(1)}, bf16[2,96,1024]{2,1,0:T(8,128)(2,1)S(1)}, u32[]{:S(2)}, u32[]{:S(2)}) collective-permute-start(bf16[2,96,1024]{2,1,0:T(8,128)(2,1)S(1)} %collective-permute-done.2), channel_id=1, source_target_pairs={{0,1},{1,0},{2,3},{3,2},{4,5},{5,4},{6,7},{7,6},{8,9},{9,8},{10,11... | collective-permute-start | bytes 1179656 | tf_op jit(solution)/shard_map/ppermute | solution.py:27
  73.6 0.6 copy-start.8
  73.6 0.7 copy-start.10
  90.9 10.0 %copy-start.2 = (bf16[3,128,256]{2,1,0:T(8,128)(2,1)S(1)}, bf16[3,128,256]{2,1,0:T(8,128)(2,1)}, u32[]{:S(2)}) copy-start(bf16[3,128,256]{2,1,0:T(8,128)(2,1)} %shard_map.73) | copy-start | bytes 589828
  90.9 10.0 %copy-start.9 = (bf16[256,256]{0,1:T(8,128)(2,1)S(1)}, bf16[256,256]{0,1:T(8,128)(2,1)}, u32[]{:S(2)}) copy-start(bf16[256,256]{0,1:T(8,128)(2,1)} %copy-done.8) | copy-start | bytes 393220
  90.9 10.0 %copy-start.11 = (bf16[256,256]{0,1:T(8,128)(2,1)S(1)}, bf16[256,256]{0,1:T(8,128)(2,1)}, u32[]{:S(2)}) copy-start(bf16[256,256]{0,1:T(8,128)(2,1)} %copy-done.10) | copy-start | bytes 393220
  90.9 6.6 %collective-permute-start.23 = (bf16[1,384,256]{2,1,0:T(8,128)(2,1)}, bf16[1,384,256]{2,1,0:T(8,128)(2,1)S(1)}, u32[]{:S(2)}, u32[]{:S(2)}) collective-permute-start(bf16[1,384,256]{2,1,0:T(8,128)(2,1)} %bitcast.149), channel_id=1, source_target_pairs={{0,2},{1,3},{2,0},{3,1},{4,6},{5,7},{6,4},{7,5},{8,10},{9,11},{10,... | collective-permute-start | bytes 589832 | tf_op jit(solution)/shard_map/ppermute | solution.py:27
  98.5 2.4 %collective-permute-start.24 = (bf16[2,384,256]{2,1,0:T(8,128)(2,1)S(1)}, bf16[2,384,256]{2,1,0:T(8,128)(2,1)S(1)}, u32[]{:S(2)}, u32[]{:S(2)}) collective-permute-start(bf16[2,384,256]{2,1,0:T(8,128)(2,1)S(1)} %pad_maximum_fusion.7), channel_id=1, source_target_pairs={{0,1},{1,0},{2,3},{3,2},{4,5},{5,4},{6,7},{7,6},{8,9},{9,8},{10,11... | collective-permute-start | bytes 1179656 | tf_op jit(solution)/shard_map/ppermute | solution.py:27
  101.0 4.5 %copy-start.6 = (f32[256]{0:T(256)S(1)}, f32[256]{0:T(256)}, u32[]{:S(2)}) copy-start(f32[256]{0:T(256)} %param.11) | copy-start | bytes 3076
  101.0 4.5 %copy-start.7 = (f32[256]{0:T(256)S(1)}, f32[256]{0:T(256)}, u32[]{:S(2)}) copy-start(f32[256]{0:T(256)} %param.10) | copy-start | bytes 3076
  101.6 2.2 %collective-permute-start.25 = (f32[384,2]{0,1:T(2,128)S(1)}, f32[384,2]{0,1:T(2,128)S(1)}, u32[]{:S(2)}, u32[]{:S(2)}) collective-permute-start(f32[384,2]{0,1:T(2,128)S(1)} %get-tuple-element.54), channel_id=1, source_target_pairs={{0,1},{1,0},{2,3},{3,2},{4,5},{5,4},{6,7},{7,6},{8,9},{9,8},{10,11... | collective-permute-start | bytes 9224 | tf_op jit(solution)/shard_map/ppermute | solution.py:27
  102.1 2.4 %collective-permute-start.26 = (f32[384,2]{0,1:T(2,128)S(1)}, f32[384,2]{0,1:T(2,128)S(1)}, u32[]{:S(2)}, u32[]{:S(2)}) collective-permute-start(f32[384,2]{0,1:T(2,128)S(1)} %get-tuple-element.54), channel_id=1, source_target_pairs={{0,2},{1,3},{2,0},{3,1},{4,6},{5,7},{6,4},{7,5},{8,10},{9,11},{10,... | collective-permute-start | bytes 9224 | tf_op jit(solution)/shard_map/ppermute | solution.py:27
  102.3 3.1 %collective-permute-start.27 = (f32[384,2]{0,1:T(2,128)S(1)}, f32[384,2]{0,1:T(2,128)S(1)}, u32[]{:S(2)}, u32[]{:S(2)}) collective-permute-start(f32[384,2]{0,1:T(2,128)S(1)} %get-tuple-element.54), channel_id=1, source_target_pairs={{0,3},{1,2},{2,1},{3,0},{4,7},{5,6},{6,5},{7,4},{8,11},{9,10},{10,... | collective-permute-start | bytes 9224 | tf_op jit(solution)/shard_map/ppermute | solution.py:27

commit v9 on v7

--- a/solution.py
+++ b/solution.py
@@ -28,6 +28,14 @@
 
 
 def spread_slots(piece, heads_axis):
+    if heads_axis == 4:
+        across = flip_heads(piece, 2, heads_axis)
+        return {
+            0: piece,
+            1: flip_heads(piece, 1, heads_axis),
+            2: across,
+            3: flip_heads(across, 1, heads_axis),
+        }
     slots = {0: piece}
     for bit in reversed(range(heads_axis.bit_length() - 1)):
         flip = 1 << bit

time: 106 us -> 108 us (1.019)
  starting transfers between devices: 34.7 us -> 50.7 us
  waiting for transfers between devices: 31.5 us -> 18.5 us
  local copies, waits for them, and re-layouts: 14 us -> 11.7 us
    ppermute x4, waiting for transfers between devices: 15.1 us -> 0.01 us  [static_keys(): lax.ppermute(mine, 'node', [(i, i ^ shift) for i in range(groups)])]
    ppermute x1, starting transfers between devices: 2.19 us -> 8.68 us  [static_keys(): other = spread_stack(lax.ppermute(mine, 'node', far), heads_axis)]
    ppermute x21 -> x27, starting transfers between devices: 25.1 us -> 31 us  [flip_heads(): return lax.ppermute(array, 'head', [(i, i ^ flip) for i in range(devices)])]
    ppermute x3, waiting for transfers between devices: 0.01 us -> 4.05 us  [static_keys(): lax.ppermute(near, 'node', [(i, i ^ shift) for i in range(groups)])]
    ppermute x4, starting transfers between devices: 4.8 us -> 8.43 us  [static_keys(): lax.ppermute(mine, 'node', [(i, i ^ shift) for i in range(groups)])]
    ppermute x21 -> x27, waiting for transfers between devices: 16.4 us -> 14.4 us  [flip_heads(): return lax.ppermute(array, 'head', [(i, i ^ flip) for i in range(devices)])]
    unnamed x8, other arithmetic: 0.96 us -> 2.8 us
    dynamic_slice x1, local copies, waits for them, and re-layouts: 1.27 us -> 0.08 us  [local(): lax.dynamic_slice_in_dim(w_out, (head_index ^ flip) * out_cols, out_cols, 1)]
  transfers between devices with their start and end apart: 29 -> 35, of which waited for: 15 -> 9; matrix products, arithmetic and copies ran while one was open for 14% -> 13% of each run, Pallas kernels for 0% -> 0%
where the time goes in v9:
time: 108 us
  starting transfers between devices  50.7 us (47%)
  waiting for transfers between devices  18.5 us (17%)
  local copies, waits for them, and re-layouts  11.7 us (11%)
  Pallas kernels  10.9 us (10%)
  matrix products  7.68 us (7%)
  other arithmetic  5.46 us (5%)
  between operations  3.04 us (3%)
    ppermute x27, starting transfers between devices, flip_heads(): return lax.ppermute(array, 'head', [(i, i ^ flip) for i in range(devices)])  31 us
    ppermute x27, waiting for transfers between devices, flip_heads(): return lax.ppermute(array, 'head', [(i, i ^ flip) for i in range(devices)])  14.4 us
    pallas_call x1, Pallas kernels, attention(): pl.pallas_call(attention_kernel, out_shape=jax.ShapeDtypeStruct(query.sha...  10.9 us
    ppermute x1, starting transfers between devices, static_keys(): other = spread_stack(lax.ppermute(mine, 'node', far), heads_axis)  8.68 us
    ppermute x4, starting transfers between devices, static_keys(): lax.ppermute(mine, 'node', [(i, i ^ shift) for i in range(groups)])  8.43 us
    dot_general x1, matrix products, kv_of_spread(): jnp.dot(rows, w_kv, preferred_element_type=jnp.float32).astype(jnp.bfloat16)  4.3 us
    ppermute x3, waiting for transfers between devices, static_keys(): lax.ppermute(near, 'node', [(i, i ^ shift) for i in range(groups)])  4.05 us
    slice x6, local copies, waits for them, and re-layouts, pair_stack(): return jnp.stack([received[0], beside[0], received[1], beside[1]])  3.22 us
  transfers between devices with their start and end apart: 35, of which 9 were waited for; matrix products, arithmetic and copies ran while one was open for 13% of the time, Pallas kernels for 0%

profile of v9, /device:TPU:9, one launch (start us, length us, event | category | flops | bytes accessed | tf_op | source)
XLA Modules:
  0.0 107.9 jit_solution(5557490104140728835)
XLA Ops:
  0.0 1.2 %constant_dynamic-slice_fusion.7 = (bf16[3,1,32,1024]{3,2,1,0:T(8,128)(2,1)S(1)}, bf16[3,1,32,1024]{3,2,1,0:T(8,128)(2,1)S(1)}) fusion(bf16[3,4,32,1024]{3,2,1,0:T(8,128)(2,1)} %bitcast.152, s32[]{:T(128)S(6)} %select_n.63, s32[]{:T(128)S(6)} %select_n.62), kind=kLoop, calls=%fused_computation.60 | loop fusion | bytes 786440 | tf_op jit(solution)/shard_map/jit(dynamic_index_in_dim)/dynamic_slice | solution.py:150
  1.2 0.8 pad_maximum_fusion.2
  2.0 1.2 %collective-permute-start = (bf16[2,96,1024]{2,1,0:T(8,128)(2,1)}, bf16[2,96,1024]{2,1,0:T(8,128)(2,1)}, u32[]{:S(2)}, u32[]{:S(2)}) collective-permute-start(bf16[2,96,1024]{2,1,0:T(8,128)(2,1)} %pad_maximum_fusion.2), channel_id=1, source_target_pairs={{0,4},{4,0},{8,12},{12,8},{16,20},{20,16},{24,28},{28,24},{1,5},{5... | collective-permute-start | bytes 1179656 | tf_op jit(solution)/shard_map/ppermute | solution.py:122
  3.4 1.2 %collective-permute-start.11 = (bf16[2,96,1024]{2,1,0:T(8,128)(2,1)}, bf16[2,96,1024]{2,1,0:T(8,128)(2,1)}, u32[]{:S(2)}, u32[]{:S(2)}) collective-permute-start(bf16[2,96,1024]{2,1,0:T(8,128)(2,1)} %pad_maximum_fusion.2), channel_id=1, source_target_pairs={{0,12},{4,8},{8,4},{12,0},{16,28},{20,24},{24,20},{28,16},{1,13},{... | collective-permute-start | bytes 1179656 | tf_op jit(solution)/shard_map/ppermute | solution.py:122
  4.6 2.3 %collective-permute-start.13 = (bf16[96,1024]{1,0:T(8,128)(2,1)S(1)}, bf16[96,1024]{1,0:T(8,128)(2,1)}, u32[]{:S(2)}, u32[]{:S(2)}) collective-permute-start(bf16[96,1024]{1,0:T(8,128)(2,1)S(1)} %bitcast.146), channel_id=1, source_target_pairs={{0,16},{4,20},{8,24},{12,28},{16,0},{20,4},{24,8},{28,12},{1,17},{... | collective-permute-start | bytes 589832 | tf_op jit(solution)/shard_map/ppermute | solution.py:126
  6.9 1.0 collective-permute-start.17
  8.8 2.0 %convolution_convert_fusion.1 = bf16[384,3,256]{2,0,1:T(8,128)(2,1)S(1)} fusion(bf16[1024,3,256]{2,0,1:T(8,128)(2,1)S(1)} %copy-done, bf16[384,1024]{1,0:T(8,128)(2,1)} %param.7), kind=kOutput, calls=%fused_computation.1 | convolution fusion | flops 604274688 | bytes 2949120 | tf_op jit(solution)/shard_map/nd,dtf->ntf/dot_general | solution.py:280
  11.0 0.6 fusion.36
  11.7 0.7 slice.89
  16.3 1.0 reshape_reshape.6.own_ref
  17.9 1.3 %collective-permute-start.21 = (bf16[96,1024]{1,0:T(8,128)(2,1)S(1)}, bf16[96,1024]{1,0:T(8,128)(2,1)S(1)}, u32[]{:S(2)}, u32[]{:S(2)}) collective-permute-start(bf16[96,1024]{1,0:T(8,128)(2,1)S(1)} %bitcast.148), channel_id=1, source_target_pairs={{0,24},{4,28},{8,16},{12,20},{16,8},{20,12},{24,0},{28,4},{1,25},{... | collective-permute-start | bytes 589832 | tf_op jit(solution)/shard_map/ppermute | solution.py:126
  19.2 1.0 fusion.34
  20.2 2.7 %collective-permute-start.1 = (bf16[2,96,1024]{2,1,0:T(8,128)(2,1)}, bf16[2,96,1024]{2,1,0:T(8,128)(2,1)S(1)}, u32[]{:S(2)}, u32[]{:S(2)}) collective-permute-start(bf16[2,96,1024]{2,1,0:T(8,128)(2,1)} %collective-permute-done), channel_id=1, source_target_pairs={{0,1},{1,0},{2,3},{3,2},{4,5},{5,4},{6,7},{7,6},{8,9},{9,8},{10,11... | collective-permute-start | bytes 1179656 | tf_op jit(solution)/shard_map/ppermute | solution.py:27
  22.9 1.0 fusion.32
  24.0 4.0 %collective-permute-done.11 = bf16[2,96,1024]{2,1,0:T(8,128)(2,1)} collective-permute-done((bf16[2,96,1024]{2,1,0:T(8,128)(2,1)}, bf16[2,96,1024]{2,1,0:T(8,128)(2,1)}, u32[]{:S(2)}, u32[]{:S(2)}) %collective-permute-start.11) | collective-permute-done | bytes 393248 | tf_op jit(solution)/shard_map/ppermute | solution.py:122
  28.0 1.9 %collective-permute-start.10 = (bf16[2,96,1024]{2,1,0:T(8,128)(2,1)}, bf16[2,96,1024]{2,1,0:T(8,128)(2,1)S(1)}, u32[]{:S(2)}, u32[]{:S(2)}) collective-permute-start(bf16[2,96,1024]{2,1,0:T(8,128)(2,1)} %collective-permute-done.9), channel_id=1, source_target_pairs={{0,1},{1,0},{2,3},{3,2},{4,5},{5,4},{6,7},{7,6},{8,9},{9,8},{10,11... | collective-permute-start | bytes 1179656 | tf_op jit(solution)/shard_map/ppermute | solution.py:27
  29.9 1.0 fusion.30
  31.4 3.8 %collective-permute-start.25 = (bf16[96,1024]{1,0:T(8,128)(2,1)S(1)}, bf16[96,1024]{1,0:T(8,128)(2,1)S(1)}, u32[]{:S(2)}, u32[]{:S(2)}) collective-permute-start(bf16[96,1024]{1,0:T(8,128)(2,1)S(1)} %bitcast.149), channel_id=1, source_target_pairs={{0,28},{4,24},{8,20},{12,16},{16,12},{20,8},{24,4},{28,0},{1,29},{... | collective-permute-start | bytes 589832 | tf_op jit(solution)/shard_map/ppermute | solution.py:126
  35.3 8.7 %collective-permute-start.2 = (bf16[96,1024]{1,0:T(8,128)(2,1)S(1)}, bf16[96,1024]{1,0:T(8,128)(2,1)S(1)}, u32[]{:S(2)}, u32[]{:S(2)}) collective-permute-start(bf16[96,1024]{1,0:T(8,128)(2,1)S(1)} %bitcast.150), channel_id=1, source_target_pairs={{4,8},{12,16},{20,24},{8,4},{16,12},{24,20},{5,9},{13,17},{21,25},... | collective-permute-start | bytes 589832 | tf_op jit(solution)/shard_map/ppermute | solution.py:117
  44.0 1.3 %collective-permute-start.15 = (bf16[96,1024]{1,0:T(8,128)(2,1)}, bf16[96,1024]{1,0:T(8,128)(2,1)S(1)}, u32[]{:S(2)}, u32[]{:S(2)}) collective-permute-start(bf16[96,1024]{1,0:T(8,128)(2,1)} %collective-permute-done.13), channel_id=1, source_target_pairs={{0,2},{1,3},{2,0},{3,1},{4,6},{5,7},{6,4},{7,5},{8,10},{9,11},{10,... | collective-permute-start | bytes 589832 | tf_op jit(solution)/shard_map/ppermute | solution.py:27
  45.3 1.3 %collective-permute-start.14 = (bf16[96,1024]{1,0:T(8,128)(2,1)}, bf16[96,1024]{1,0:T(8,128)(2,1)S(1)}, u32[]{:S(2)}, u32[]{:S(2)}) collective-permute-start(bf16[96,1024]{1,0:T(8,128)(2,1)} %collective-permute-done.13), channel_id=1, source_target_pairs={{0,1},{1,0},{2,3},{3,2},{4,5},{5,4},{6,7},{7,6},{8,9},{9,8},{10,11... | collective-permute-start | bytes 589832 | tf_op jit(solution)/shard_map/ppermute | solution.py:27
  46.9 1.3 %collective-permute-start.23 = (bf16[96,1024]{1,0:T(8,128)(2,1)S(1)}, bf16[96,1024]{1,0:T(8,128)(2,1)S(1)}, u32[]{:S(2)}, u32[]{:S(2)}) collective-permute-start(bf16[96,1024]{1,0:T(8,128)(2,1)S(1)} %collective-permute-done.21), channel_id=1, source_target_pairs={{0,2},{1,3},{2,0},{3,1},{4,6},{5,7},{6,4},{7,5},{8,10},{9,11},{10,... | collective-permute-start | bytes 589832 | tf_op jit(solution)/shard_map/ppermute | solution.py:27
  48.2 1.5 %collective-permute-done.15 = bf16[96,1024]{1,0:T(8,128)(2,1)S(1)} collective-permute-done((bf16[96,1024]{1,0:T(8,128)(2,1)}, bf16[96,1024]{1,0:T(8,128)(2,1)S(1)}, u32[]{:S(2)}, u32[]{:S(2)}) %collective-permute-start.15) | collective-permute-done | bytes 196640 | tf_op jit(solution)/shard_map/ppermute | solution.py:27
  49.7 3.3 %collective-permute-start.16 = (bf16[96,1024]{1,0:T(8,128)(2,1)S(1)}, bf16[96,1024]{1,0:T(8,128)(2,1)S(1)}, u32[]{:S(2)}, u32[]{:S(2)}) collective-permute-start(bf16[96,1024]{1,0:T(8,128)(2,1)S(1)} %collective-permute-done.15), channel_id=1, source_target_pairs={{0,1},{1,0},{2,3},{3,2},{4,5},{5,4},{6,7},{7,6},{8,9},{9,8},{10,11... | collective-permute-start | bytes 589832 | tf_op jit(solution)/shard_map/ppermute | solution.py:27
  53.2 1.3 %collective-permute-start.27 = (bf16[96,1024]{1,0:T(8,128)(2,1)S(1)}, bf16[96,1024]{1,0:T(8,128)(2,1)S(1)}, u32[]{:S(2)}, u32[]{:S(2)}) collective-permute-start(bf16[96,1024]{1,0:T(8,128)(2,1)S(1)} %collective-permute-done.25), channel_id=1, source_target_pairs={{0,2},{1,3},{2,0},{3,1},{4,6},{5,7},{6,4},{7,5},{8,10},{9,11},{10,... | collective-permute-start | bytes 589832 | tf_op jit(solution)/shard_map/ppermute | solution.py:27
  54.5 2.8 %collective-permute-start.20 = (bf16[96,1024]{1,0:T(8,128)(2,1)S(1)}, bf16[96,1024]{1,0:T(8,128)(2,1)S(1)}, u32[]{:S(2)}, u32[]{:S(2)}) collective-permute-start(bf16[96,1024]{1,0:T(8,128)(2,1)S(1)} %collective-permute-done.19), channel_id=1, source_target_pairs={{0,1},{1,0},{2,3},{3,2},{4,5},{5,4},{6,7},{7,6},{8,9},{9,8},{10,11... | collective-permute-start | bytes 589832 | tf_op jit(solution)/shard_map/ppermute | solution.py:27
  57.3 0.9 collective-permute-done.23
  58.2 3.3 %collective-permute-start.22 = (bf16[96,1024]{1,0:T(8,128)(2,1)S(1)}, bf16[96,1024]{1,0:T(8,128)(2,1)S(1)}, u32[]{:S(2)}, u32[]{:S(2)}) collective-permute-start(bf16[96,1024]{1,0:T(8,128)(2,1)S(1)} %collective-permute-done.21), channel_id=1, source_target_pairs={{0,1},{1,0},{2,3},{3,2},{4,5},{5,4},{6,7},{7,6},{8,9},{9,8},{10,11... | collective-permute-start | bytes 589832 | tf_op jit(solution)/shard_map/ppermute | solution.py:27
  61.5 1.0 fusion.4
  63.0 1.2 %collective-permute-start.4 = (bf16[96,1024]{1,0:T(8,128)(2,1)S(1)}, bf16[96,1024]{1,0:T(8,128)(2,1)S(1)}, u32[]{:S(2)}, u32[]{:S(2)}) collective-permute-start(bf16[96,1024]{1,0:T(8,128)(2,1)S(1)} %collective-permute-done.2), channel_id=1, source_target_pairs={{0,2},{1,3},{2,0},{3,1},{4,6},{5,7},{6,4},{7,5},{8,10},{9,11},{10,... | collective-permute-start | bytes 589832 | tf_op jit(solution)/shard_map/ppermute | solution.py:27
  64.2 1.5 %collective-permute-start.28 = (bf16[96,1024]{1,0:T(8,128)(2,1)S(1)}, bf16[96,1024]{1,0:T(8,128)(2,1)S(1)}, u32[]{:S(2)}, u32[]{:S(2)}) collective-permute-start(bf16[96,1024]{1,0:T(8,128)(2,1)S(1)} %collective-permute-done.27), channel_id=1, source_target_pairs={{0,1},{1,0},{2,3},{3,2},{4,5},{5,4},{6,7},{7,6},{8,9},{9,8},{10,11... | collective-permute-start | bytes 589832 | tf_op jit(solution)/shard_map/ppermute | solution.py:27
  65.7 1.0 fusion.5
  67.2 1.9 %collective-permute-start.8 = (bf16[256,256]{0,1:T(8,128)(2,1)S(1)}, bf16[256,256]{0,1:T(8,128)(2,1)S(1)}, u32[]{:S(2)}, u32[]{:S(2)}) collective-permute-start(bf16[256,256]{0,1:T(8,128)(2,1)S(1)} %copy.40), channel_id=1, source_target_pairs={{0,3},{1,2},{2,1},{3,0},{4,7},{5,6},{6,5},{7,4},{8,11},{9,10},{10,... | collective-permute-start | bytes 393224 | tf_op jit(solution)/shard_map/ppermute | solution.py:27
  69.1 1.6 %collective-permute-start.3 = (bf16[96,1024]{1,0:T(8,128)(2,1)S(1)}, bf16[96,1024]{1,0:T(8,128)(2,1)S(1)}, u32[]{:S(2)}, u32[]{:S(2)}) collective-permute-start(bf16[96,1024]{1,0:T(8,128)(2,1)S(1)} %collective-permute-done.2), channel_id=1, source_target_pairs={{0,1},{1,0},{2,3},{3,2},{4,5},{5,4},{6,7},{7,6},{8,9},{9,8},{10,11... | collective-permute-start | bytes 589832 | tf_op jit(solution)/shard_map/ppermute | solution.py:27
  71.2 1.1 %collective-permute-done.7 = bf16[256,256]{0,1:T(8,128)(2,1)S(1)} collective-permute-done((bf16[256,256]{0,1:T(8,128)(2,1)S(1)}, bf16[256,256]{0,1:T(8,128)(2,1)S(1)}, u32[]{:S(2)}, u32[]{:S(2)}) %collective-permute-start.7) | collective-permute-done | bytes 131104 | tf_op jit(solution)/shard_map/ppermute | solution.py:27
  72.3 3.0 %collective-permute-done.8 = bf16[256,256]{0,1:T(8,128)(2,1)S(1)} collective-permute-done((bf16[256,256]{0,1:T(8,128)(2,1)S(1)}, bf16[256,256]{0,1:T(8,128)(2,1)S(1)}, u32[]{:S(2)}, u32[]{:S(2)}) %collective-permute-start.8) | collective-permute-done | bytes 131104 | tf_op jit(solution)/shard_map/ppermute | solution.py:27
  76.2 0.9 copy.31
  77.1 4.3 %convolution_convert_fusion = bf16[2304,512]{1,0:T(8,128)(2,1)} fusion(bf16[2304,1024]{1,0:T(8,128)(2,1)S(1)} %bitcast.123, bf16[1024,512]{0,1:T(8,128)(2,1)S(1)} %bitcast.136), kind=kOutput, calls=%fused_computation | convolution fusion | flops 2417098752 | bytes 8126464 | tf_op jit(solution)/shard_map/dot_general | solution.py:179
  81.4 10.9 %shard_map.73 = bf16[3,128,256]{2,1,0:T(8,128)(2,1)} custom-call(s32[3,11]{1,0:T(4,128)} %pad_convert_fusion.live_ref, s32[4,3]{1,0:T(4,128)} %add_select_fusion.pick_ref, bf16[3,128,256]{2,1,0:T(8,128)(2,1)} %bitcast.167, bf16[3,128,512]{2,1,0:T(8,128)(2,1)} %reshape_reshape.6.own_ref, bf16[6,3,128,512]{3,2,1,0:T(8,128)(2,1)} %bitcast.181), custom_call_target="tpu_custom_call" | custom-call | flops 1107296256 | bytes 3145728 | tf_op jit(solution)/shard_map/pallas_call | solution.py:246
  92.3 1.2 %collective-permute-start.30 = (bf16[384,256]{1,0:T(8,128)(2,1)}, bf16[384,256]{1,0:T(8,128)(2,1)S(1)}, u32[]{:S(2)}, u32[]{:S(2)}) collective-permute-start(bf16[384,256]{1,0:T(8,128)(2,1)} %bitcast.172), channel_id=1, source_target_pairs={{0,2},{1,3},{2,0},{3,1},{4,6},{5,7},{6,4},{7,5},{8,10},{9,11},{10,... | collective-permute-start | bytes 589832 | tf_op jit(solution)/shard_map/ppermute | solution.py:27
  93.5 5.3 %collective-permute-done.30 = bf16[384,256]{1,0:T(8,128)(2,1)S(1)} collective-permute-done((bf16[384,256]{1,0:T(8,128)(2,1)}, bf16[384,256]{1,0:T(8,128)(2,1)S(1)}, u32[]{:S(2)}, u32[]{:S(2)}) %collective-permute-start.30) | collective-permute-done | bytes 196640 | tf_op jit(solution)/shard_map/ppermute | solution.py:27
  98.8 1.0 collective-permute-start.31
  99.8 0.9 constant_dynamic-slice_fusion.9
  100.9 1.4 %fusion.37 = (f32[384]{0:T(512)S(1)}, f32[384,256]{0,1:T(8,128)S(1)}) fusion(bf16[1,256,256]{1,2,0:T(8,128)(2,1)S(1)} %bitcast.180, bf16[1,256,256]{1,2,0:T(8,128)(2,1)S(1)} %bitcast.179, bf16[1,256,256]{1,2,0:T(8,128)(2,1)S(1)} %bitcast.178, bf16[1,256,256]{1,2,0:T(8,128)(2,1)S(1)} %bitcast.168, bf16[1,384,256]{2,1,0:T(8,128)(2,1)S(1)} %bitcast.177, ...), kind=kOutput, calls=%fused_computation.88 | convolution fusion | flops 203587200 | bytes 1902080 | tf_op jit(solution)/shard_map/srf,sfo->ro/dot_general | solution.py:308
  102.9 0.9 collective-permute-start.33
  103.8 0.9 collective-permute-start.34
  105.3 1.6 %collective-permute-done.34 = f32[384,2]{0,1:T(2,128)S(1)} collective-permute-done((f32[384,2]{0,1:T(2,128)S(1)}, f32[384,2]{0,1:T(2,128)S(1)}, u32[]{:S(2)}, u32[]{:S(2)}) %collective-permute-start.34) | collective-permute-done | bytes 3104 | tf_op jit(solution)/shard_map/ppermute | solution.py:27
  107.1 0.8 copy.33
  (100 shorter events, 8.0 us)
Async XLA Ops:
  0.0 7.9 %copy-start.3 = (s32[4,3]{1,0:T(4,128)S(1)}, s32[4,3]{1,0:T(4,128)}, u32[]{:S(2)}) copy-start(s32[4,3]{1,0:T(4,128)} %param.13) | copy-start | bytes 148
  0.0 8.8 %copy-start = (bf16[1024,3,256]{2,0,1:T(8,128)(2,1)S(1)}, bf16[1024,3,256]{2,0,1:T(8,128)(2,1)}, u32[]{:S(2)}) copy-start(bf16[1024,3,256]{2,0,1:T(8,128)(2,1)} %param.8) | copy-start | bytes 4718596
  2.0 15.9 %collective-permute-start = (bf16[2,96,1024]{2,1,0:T(8,128)(2,1)}, bf16[2,96,1024]{2,1,0:T(8,128)(2,1)}, u32[]{:S(2)}, u32[]{:S(2)}) collective-permute-start(bf16[2,96,1024]{2,1,0:T(8,128)(2,1)} %pad_maximum_fusion.2), channel_id=1, source_target_pairs={{0,4},{4,0},{8,12},{12,8},{16,20},{20,16},{24,28},{28,24},{1,5},{5... | collective-permute-start | bytes 1179656 | tf_op jit(solution)/shard_map/ppermute | solution.py:122
  3.2 17.0 %collective-permute-start.9 = (bf16[2,96,1024]{2,1,0:T(8,128)(2,1)}, bf16[2,96,1024]{2,1,0:T(8,128)(2,1)}, u32[]{:S(2)}, u32[]{:S(2)}) collective-permute-start(bf16[2,96,1024]{2,1,0:T(8,128)(2,1)} %pad_maximum_fusion.2), channel_id=1, source_target_pairs={{0,8},{4,12},{8,0},{12,4},{16,24},{20,28},{24,16},{28,20},{1,9},{5... | collective-permute-start | bytes 1179656 | tf_op jit(solution)/shard_map/ppermute | solution.py:122
  3.4 24.6 %collective-permute-start.11 = (bf16[2,96,1024]{2,1,0:T(8,128)(2,1)}, bf16[2,96,1024]{2,1,0:T(8,128)(2,1)}, u32[]{:S(2)}, u32[]{:S(2)}) collective-permute-start(bf16[2,96,1024]{2,1,0:T(8,128)(2,1)} %pad_maximum_fusion.2), channel_id=1, source_target_pairs={{0,12},{4,8},{8,4},{12,0},{16,28},{20,24},{24,20},{28,16},{1,13},{... | collective-permute-start | bytes 1179656 | tf_op jit(solution)/shard_map/ppermute | solution.py:122
  4.6 30.7 %collective-permute-start.13 = (bf16[96,1024]{1,0:T(8,128)(2,1)S(1)}, bf16[96,1024]{1,0:T(8,128)(2,1)}, u32[]{:S(2)}, u32[]{:S(2)}) collective-permute-start(bf16[96,1024]{1,0:T(8,128)(2,1)S(1)} %bitcast.146), channel_id=1, source_target_pairs={{0,16},{4,20},{8,24},{12,28},{16,0},{20,4},{24,8},{28,12},{1,17},{... | collective-permute-start | bytes 589832 | tf_op jit(solution)/shard_map/ppermute | solution.py:126
  6.9 38.4 %collective-permute-start.17 = (bf16[96,1024]{1,0:T(8,128)(2,1)S(1)}, bf16[96,1024]{1,0:T(8,128)(2,1)}, u32[]{:S(2)}, u32[]{:S(2)}) collective-permute-start(bf16[96,1024]{1,0:T(8,128)(2,1)S(1)} %bitcast.147), channel_id=1, source_target_pairs={{0,20},{4,16},{8,28},{12,24},{16,4},{20,0},{24,12},{28,8},{1,21},{... | collective-permute-start | bytes 589832 | tf_op jit(solution)/shard_map/ppermute | solution.py:126
  8.8 2.0 %copy-start.4 = (s32[3,7]{1,0:T(4,128)S(1)}, s32[3,7]{1,0:T(4,128)}, u32[]{:S(2)}) copy-start(s32[3,7]{1,0:T(4,128)} %param.12) | copy-start | bytes 256
  8.8 2.1 %copy-start.2 = (bf16[256,1024]{1,0:T(8,128)(2,1)S(1)}, bf16[256,1024]{1,0:T(8,128)(2,1)}, u32[]{:S(2)}) copy-start(bf16[256,1024]{1,0:T(8,128)(2,1)} %param.9) | copy-start | bytes 1572868
  10.8 0.8 copy-start.1
  11.6 3.7 %slice-start = ((bf16[1024,3,256]{2,0,1:T(8,128)(2,1)}), bf16[1024,2,256]{2,0,1:T(8,128)(2,1)S(1)}, s32[]{:S(2)}) async-start(bf16[1024,3,256]{2,0,1:T(8,128)(2,1)} %param.8), calls=%async_computation | async-start | bytes 2097152 | tf_op jit(solution)/shard_map/slice | solution.py:289
  14.9 1.0 slice-start.1
  17.9 28.7 %collective-permute-start.21 = (bf16[96,1024]{1,0:T(8,128)(2,1)S(1)}, bf16[96,1024]{1,0:T(8,128)(2,1)S(1)}, u32[]{:S(2)}, u32[]{:S(2)}) collective-permute-start(bf16[96,1024]{1,0:T(8,128)(2,1)S(1)} %bitcast.148), channel_id=1, source_target_pairs={{0,24},{4,28},{8,16},{12,20},{16,8},{20,12},{24,0},{28,4},{1,25},{... | collective-permute-start | bytes 589832 | tf_op jit(solution)/shard_map/ppermute | solution.py:126
  20.2 10.7 %collective-permute-start.1 = (bf16[2,96,1024]{2,1,0:T(8,128)(2,1)}, bf16[2,96,1024]{2,1,0:T(8,128)(2,1)S(1)}, u32[]{:S(2)}, u32[]{:S(2)}) collective-permute-start(bf16[2,96,1024]{2,1,0:T(8,128)(2,1)} %collective-permute-done), channel_id=1, source_target_pairs={{0,1},{1,0},{2,3},{3,2},{4,5},{5,4},{6,7},{7,6},{8,9},{9,8},{10,11... | collective-permute-start | bytes 1179656 | tf_op jit(solution)/shard_map/ppermute | solution.py:27
  28.0 3.4 %collective-permute-start.10 = (bf16[2,96,1024]{2,1,0:T(8,128)(2,1)}, bf16[2,96,1024]{2,1,0:T(8,128)(2,1)S(1)}, u32[]{:S(2)}, u32[]{:S(2)}) collective-permute-start(bf16[2,96,1024]{2,1,0:T(8,128)(2,1)} %collective-permute-done.9), channel_id=1, source_target_pairs={{0,1},{1,0},{2,3},{3,2},{4,5},{5,4},{6,7},{7,6},{8,9},{9,8},{10,11... | collective-permute-start | bytes 1179656 | tf_op jit(solution)/shard_map/ppermute | solution.py:27
  30.9 13.0 %collective-permute-start.12 = (bf16[2,96,1024]{2,1,0:T(8,128)(2,1)}, bf16[2,96,1024]{2,1,0:T(8,128)(2,1)S(1)}, u32[]{:S(2)}, u32[]{:S(2)}) collective-permute-start(bf16[2,96,1024]{2,1,0:T(8,128)(2,1)} %collective-permute-done.11), channel_id=1, source_target_pairs={{0,1},{1,0},{2,3},{3,2},{4,5},{5,4},{6,7},{7,6},{8,9},{9,8},{10,11... | collective-permute-start | bytes 1179656 | tf_op jit(solution)/shard_map/ppermute | solution.py:27
  31.4 15.5 %collective-permute-start.25 = (bf16[96,1024]{1,0:T(8,128)(2,1)S(1)}, bf16[96,1024]{1,0:T(8,128)(2,1)S(1)}, u32[]{:S(2)}, u32[]{:S(2)}) collective-permute-start(bf16[96,1024]{1,0:T(8,128)(2,1)S(1)} %bitcast.149), channel_id=1, source_target_pairs={{0,28},{4,24},{8,20},{12,16},{16,12},{20,8},{24,4},{28,0},{1,29},{... | collective-permute-start | bytes 589832 | tf_op jit(solution)/shard_map/ppermute | solution.py:126
  35.3 17.8 %collective-permute-start.2 = (bf16[96,1024]{1,0:T(8,128)(2,1)S(1)}, bf16[96,1024]{1,0:T(8,128)(2,1)S(1)}, u32[]{:S(2)}, u32[]{:S(2)}) collective-permute-start(bf16[96,1024]{1,0:T(8,128)(2,1)S(1)} %bitcast.150), channel_id=1, source_target_pairs={{4,8},{12,16},{20,24},{8,4},{16,12},{24,20},{5,9},{13,17},{21,25},... | collective-permute-start | bytes 589832 | tf_op jit(solution)/shard_map/ppermute | solution.py:117
  44.0 5.7 %collective-permute-start.15 = (bf16[96,1024]{1,0:T(8,128)(2,1)}, bf16[96,1024]{1,0:T(8,128)(2,1)S(1)}, u32[]{:S(2)}, u32[]{:S(2)}) collective-permute-start(bf16[96,1024]{1,0:T(8,128)(2,1)} %collective-permute-done.13), channel_id=1, source_target_pairs={{0,2},{1,3},{2,0},{3,1},{4,6},{5,7},{6,4},{7,5},{8,10},{9,11},{10,... | collective-permute-start | bytes 589832 | tf_op jit(solution)/shard_map/ppermute | solution.py:27
  45.3 7.9 %collective-permute-start.14 = (bf16[96,1024]{1,0:T(8,128)(2,1)}, bf16[96,1024]{1,0:T(8,128)(2,1)S(1)}, u32[]{:S(2)}, u32[]{:S(2)}) collective-permute-start(bf16[96,1024]{1,0:T(8,128)(2,1)} %collective-permute-done.13), channel_id=1, source_target_pairs={{0,1},{1,0},{2,3},{3,2},{4,5},{5,4},{6,7},{7,6},{8,9},{9,8},{10,11... | collective-permute-start | bytes 589832 | tf_op jit(solution)/shard_map/ppermute | solution.py:27
  46.6 7.9 %collective-permute-start.19 = (bf16[96,1024]{1,0:T(8,128)(2,1)}, bf16[96,1024]{1,0:T(8,128)(2,1)S(1)}, u32[]{:S(2)}, u32[]{:S(2)}) collective-permute-start(bf16[96,1024]{1,0:T(8,128)(2,1)} %collective-permute-done.17), channel_id=1, source_target_pairs={{0,2},{1,3},{2,0},{3,1},{4,6},{5,7},{6,4},{7,5},{8,10},{9,11},{10,... | collective-permute-start | bytes 589832 | tf_op jit(solution)/shard_map/ppermute | solution.py:27
  46.9 11.2 %collective-permute-start.23 = (bf16[96,1024]{1,0:T(8,128)(2,1)S(1)}, bf16[96,1024]{1,0:T(8,128)(2,1)S(1)}, u32[]{:S(2)}, u32[]{:S(2)}) collective-permute-start(bf16[96,1024]{1,0:T(8,128)(2,1)S(1)} %collective-permute-done.21), channel_id=1, source_target_pairs={{0,2},{1,3},{2,0},{3,1},{4,6},{5,7},{6,4},{7,5},{8,10},{9,11},{10,... | collective-permute-start | bytes 589832 | tf_op jit(solution)/shard_map/ppermute | solution.py:27
  49.7 11.7 %collective-permute-start.16 = (bf16[96,1024]{1,0:T(8,128)(2,1)S(1)}, bf16[96,1024]{1,0:T(8,128)(2,1)S(1)}, u32[]{:S(2)}, u32[]{:S(2)}) collective-permute-start(bf16[96,1024]{1,0:T(8,128)(2,1)S(1)} %collective-permute-done.15), channel_id=1, source_target_pairs={{0,1},{1,0},{2,3},{3,2},{4,5},{5,4},{6,7},{7,6},{8,9},{9,8},{10,11... | collective-permute-start | bytes 589832 | tf_op jit(solution)/shard_map/ppermute | solution.py:27
  53.1 9.4 %collective-permute-start.18 = (bf16[96,1024]{1,0:T(8,128)(2,1)}, bf16[96,1024]{1,0:T(8,128)(2,1)S(1)}, u32[]{:S(2)}, u32[]{:S(2)}) collective-permute-start(bf16[96,1024]{1,0:T(8,128)(2,1)} %collective-permute-done.17), channel_id=1, source_target_pairs={{0,1},{1,0},{2,3},{3,2},{4,5},{5,4},{6,7},{7,6},{8,9},{9,8},{10,11... | collective-permute-start | bytes 589832 | tf_op jit(solution)/shard_map/ppermute | solution.py:27
  53.2 9.9 %collective-permute-start.27 = (bf16[96,1024]{1,0:T(8,128)(2,1)S(1)}, bf16[96,1024]{1,0:T(8,128)(2,1)S(1)}, u32[]{:S(2)}, u32[]{:S(2)}) collective-permute-start(bf16[96,1024]{1,0:T(8,128)(2,1)S(1)} %collective-permute-done.25), channel_id=1, source_target_pairs={{0,2},{1,3},{2,0},{3,1},{4,6},{5,7},{6,4},{7,5},{8,10},{9,11},{10,... | collective-permute-start | bytes 589832 | tf_op jit(solution)/shard_map/ppermute | solution.py:27
  54.5 9.8 %collective-permute-start.20 = (bf16[96,1024]{1,0:T(8,128)(2,1)S(1)}, bf16[96,1024]{1,0:T(8,128)(2,1)S(1)}, u32[]{:S(2)}, u32[]{:S(2)}) collective-permute-start(bf16[96,1024]{1,0:T(8,128)(2,1)S(1)} %collective-permute-done.19), channel_id=1, source_target_pairs={{0,1},{1,0},{2,3},{3,2},{4,5},{5,4},{6,7},{7,6},{8,9},{9,8},{10,11... | collective-permute-start | bytes 589832 | tf_op jit(solution)/shard_map/ppermute | solution.py:27
  58.2 8.5 %collective-permute-start.22 = (bf16[96,1024]{1,0:T(8,128)(2,1)S(1)}, bf16[96,1024]{1,0:T(8,128)(2,1)S(1)}, u32[]{:S(2)}, u32[]{:S(2)}) collective-permute-start(bf16[96,1024]{1,0:T(8,128)(2,1)S(1)} %collective-permute-done.21), channel_id=1, source_target_pairs={{0,1},{1,0},{2,3},{3,2},{4,5},{5,4},{6,7},{7,6},{8,9},{9,8},{10,11... | collective-permute-start | bytes 589832 | tf_op jit(solution)/shard_map/ppermute | solution.py:27
  61.5 5.3 %collective-permute-start.24 = (bf16[96,1024]{1,0:T(8,128)(2,1)S(1)}, bf16[96,1024]{1,0:T(8,128)(2,1)S(1)}, u32[]{:S(2)}, u32[]{:S(2)}) collective-permute-start(bf16[96,1024]{1,0:T(8,128)(2,1)S(1)} %collective-permute-done.23), channel_id=1, source_target_pairs={{0,1},{1,0},{2,3},{3,2},{4,5},{5,4},{6,7},{7,6},{8,9},{9,8},{10,11... | collective-permute-start | bytes 589832 | tf_op jit(solution)/shard_map/ppermute | solution.py:27
  62.5 4.7 %collective-permute-start.26 = (bf16[96,1024]{1,0:T(8,128)(2,1)S(1)}, bf16[96,1024]{1,0:T(8,128)(2,1)S(1)}, u32[]{:S(2)}, u32[]{:S(2)}) collective-permute-start(bf16[96,1024]{1,0:T(8,128)(2,1)S(1)} %collective-permute-done.25), channel_id=1, source_target_pairs={{0,1},{1,0},{2,3},{3,2},{4,5},{5,4},{6,7},{7,6},{8,9},{9,8},{10,11... | collective-permute-start | bytes 589832 | tf_op jit(solution)/shard_map/ppermute | solution.py:27
  63.0 6.0 %collective-permute-start.4 = (bf16[96,1024]{1,0:T(8,128)(2,1)S(1)}, bf16[96,1024]{1,0:T(8,128)(2,1)S(1)}, u32[]{:S(2)}, u32[]{:S(2)}) collective-permute-start(bf16[96,1024]{1,0:T(8,128)(2,1)S(1)} %collective-permute-done.2), channel_id=1, source_target_pairs={{0,2},{1,3},{2,0},{3,1},{4,6},{5,7},{6,4},{7,5},{8,10},{9,11},{10,... | collective-permute-start | bytes 589832 | tf_op jit(solution)/shard_map/ppermute | solution.py:27
  64.2 6.4 %collective-permute-start.28 = (bf16[96,1024]{1,0:T(8,128)(2,1)S(1)}, bf16[96,1024]{1,0:T(8,128)(2,1)S(1)}, u32[]{:S(2)}, u32[]{:S(2)}) collective-permute-start(bf16[96,1024]{1,0:T(8,128)(2,1)S(1)} %collective-permute-done.27), channel_id=1, source_target_pairs={{0,1},{1,0},{2,3},{3,2},{4,5},{5,4},{6,7},{7,6},{8,9},{9,8},{10,11... | collective-permute-start | bytes 589832 | tf_op jit(solution)/shard_map/ppermute | solution.py:27
  66.7 4.4 %collective-permute-start.6 = (bf16[256,256]{0,1:T(8,128)(2,1)S(1)}, bf16[256,256]{0,1:T(8,128)(2,1)S(1)}, u32[]{:S(2)}, u32[]{:S(2)}) collective-permute-start(bf16[256,256]{0,1:T(8,128)(2,1)S(1)} %copy.38), channel_id=1, source_target_pairs={{0,1},{1,0},{2,3},{3,2},{4,5},{5,4},{6,7},{7,6},{8,9},{9,8},{10,11... | collective-permute-start | bytes 393224 | tf_op jit(solution)/shard_map/ppermute | solution.py:27
  66.8 5.5 %collective-permute-start.7 = (bf16[256,256]{0,1:T(8,128)(2,1)S(1)}, bf16[256,256]{0,1:T(8,128)(2,1)S(1)}, u32[]{:S(2)}, u32[]{:S(2)}) collective-permute-start(bf16[256,256]{0,1:T(8,128)(2,1)S(1)} %copy.39), channel_id=1, source_target_pairs={{0,2},{1,3},{2,0},{3,1},{4,6},{5,7},{6,4},{7,5},{8,10},{9,11},{10,... | collective-permute-start | bytes 393224 | tf_op jit(solution)/shard_map/ppermute | solution.py:27
  67.2 8.1 %collective-permute-start.8 = (bf16[256,256]{0,1:T(8,128)(2,1)S(1)}, bf16[256,256]{0,1:T(8,128)(2,1)S(1)}, u32[]{:S(2)}, u32[]{:S(2)}) collective-permute-start(bf16[256,256]{0,1:T(8,128)(2,1)S(1)} %copy.40), channel_id=1, source_target_pairs={{0,3},{1,2},{2,1},{3,0},{4,7},{5,6},{6,5},{7,4},{8,11},{9,10},{10,... | collective-permute-start | bytes 393224 | tf_op jit(solution)/shard_map/ppermute | solution.py:27
  69.1 6.2 %collective-permute-start.3 = (bf16[96,1024]{1,0:T(8,128)(2,1)S(1)}, bf16[96,1024]{1,0:T(8,128)(2,1)S(1)}, u32[]{:S(2)}, u32[]{:S(2)}) collective-permute-start(bf16[96,1024]{1,0:T(8,128)(2,1)S(1)} %collective-permute-done.2), channel_id=1, source_target_pairs={{0,1},{1,0},{2,3},{3,2},{4,5},{5,4},{6,7},{7,6},{8,9},{9,8},{10,11... | collective-permute-start | bytes 589832 | tf_op jit(solution)/shard_map/ppermute | solution.py:27
  70.7 4.6 %collective-permute-start.5 = (bf16[96,1024]{1,0:T(8,128)(2,1)S(1)}, bf16[96,1024]{1,0:T(8,128)(2,1)S(1)}, u32[]{:S(2)}, u32[]{:S(2)}) collective-permute-start(bf16[96,1024]{1,0:T(8,128)(2,1)S(1)} %collective-permute-done.4), channel_id=1, source_target_pairs={{0,1},{1,0},{2,3},{3,2},{4,5},{5,4},{6,7},{7,6},{8,9},{9,8},{10,11... | collective-permute-start | bytes 589832 | tf_op jit(solution)/shard_map/ppermute | solution.py:27
  92.3 6.5 %collective-permute-start.30 = (bf16[384,256]{1,0:T(8,128)(2,1)}, bf16[384,256]{1,0:T(8,128)(2,1)S(1)}, u32[]{:S(2)}, u32[]{:S(2)}) collective-permute-start(bf16[384,256]{1,0:T(8,128)(2,1)} %bitcast.172), channel_id=1, source_target_pairs={{0,2},{1,3},{2,0},{3,1},{4,6},{5,7},{6,4},{7,5},{8,10},{9,11},{10,... | collective-permute-start | bytes 589832 | tf_op jit(solution)/shard_map/ppermute | solution.py:27
  93.5 7.4 %collective-permute-start.29 = (bf16[384,256]{1,0:T(8,128)(2,1)}, bf16[384,256]{1,0:T(8,128)(2,1)S(1)}, u32[]{:S(2)}, u32[]{:S(2)}) collective-permute-start(bf16[384,256]{1,0:T(8,128)(2,1)} %bitcast.173), channel_id=1, source_target_pairs={{0,1},{1,0},{2,3},{3,2},{4,5},{5,4},{6,7},{7,6},{8,9},{9,8},{10,11... | collective-permute-start | bytes 589832 | tf_op jit(solution)/shard_map/ppermute | solution.py:27
  98.8 2.1 %collective-permute-start.31 = (bf16[384,256]{1,0:T(8,128)(2,1)S(1)}, bf16[384,256]{1,0:T(8,128)(2,1)S(1)}, u32[]{:S(2)}, u32[]{:S(2)}) collective-permute-start(bf16[384,256]{1,0:T(8,128)(2,1)S(1)} %collective-permute-done.30), channel_id=1, source_target_pairs={{0,1},{1,0},{2,3},{3,2},{4,5},{5,4},{6,7},{7,6},{8,9},{9,8},{10,11... | collective-permute-start | bytes 589832 | tf_op jit(solution)/shard_map/ppermute | solution.py:27
  100.9 6.0 %copy-start.5 = (f32[256]{0:T(256)S(1)}, f32[256]{0:T(256)}, u32[]{:S(2)}) copy-start(f32[256]{0:T(256)} %param.11) | copy-start | bytes 3076
  100.9 6.0 %copy-start.6 = (f32[256]{0:T(256)S(1)}, f32[256]{0:T(256)}, u32[]{:S(2)}) copy-start(f32[256]{0:T(256)} %param.10) | copy-start | bytes 3076
  102.5 2.2 %collective-permute-start.32 = (f32[384,2]{0,1:T(2,128)S(1)}, f32[384,2]{0,1:T(2,128)S(1)}, u32[]{:S(2)}, u32[]{:S(2)}) collective-permute-start(f32[384,2]{0,1:T(2,128)S(1)} %get-tuple-element.40), channel_id=1, source_target_pairs={{0,1},{1,0},{2,3},{3,2},{4,5},{5,4},{6,7},{7,6},{8,9},{9,8},{10,11... | collective-permute-start | bytes 9224 | tf_op jit(solution)/shard_map/ppermute | solution.py:27
  102.9 2.4 %collective-permute-start.33 = (f32[384,2]{0,1:T(2,128)S(1)}, f32[384,2]{0,1:T(2,128)S(1)}, u32[]{:S(2)}, u32[]{:S(2)}) collective-permute-start(f32[384,2]{0,1:T(2,128)S(1)} %get-tuple-element.40), channel_id=1, source_target_pairs={{0,2},{1,3},{2,0},{3,1},{4,6},{5,7},{6,4},{7,5},{8,10},{9,11},{10,... | collective-permute-start | bytes 9224 | tf_op jit(solution)/shard_map/ppermute | solution.py:27
  103.8 3.1 %collective-permute-start.34 = (f32[384,2]{0,1:T(2,128)S(1)}, f32[384,2]{0,1:T(2,128)S(1)}, u32[]{:S(2)}, u32[]{:S(2)}) collective-permute-start(f32[384,2]{0,1:T(2,128)S(1)} %get-tuple-element.40), channel_id=1, source_target_pairs={{0,3},{1,2},{2,1},{3,0},{4,7},{5,6},{6,5},{7,4},{8,11},{9,10},{10,... | collective-permute-start | bytes 9224 | tf_op jit(solution)/shard_map/ppermute | solution.py:27

commit v10 on v7

--- a/solution.py
+++ b/solution.py
@@ -13,7 +13,7 @@
 LANES = 128
 GATHER_GROUPS = 16
 STATIC_GROUPS = 8
-NEAR_SHIFTS = 4
+NEAR_SHIFTS = 2
 
 
 NORM_EPS = 1e-05

time: 106 us -> 105 us (level); the launches traced: 106 us -> 103 us
  waiting for transfers between devices: 31.5 us -> 21.1 us
  starting transfers between devices: 34.7 us -> 39.8 us
  local copies, waits for them, and re-layouts: 14 us -> 16.4 us
    ppermute x4 -> x6, waiting for transfers between devices: 15.1 us -> 0.82 us  [static_keys(): lax.ppermute(mine, 'node', [(i, i ^ shift) for i in range(groups)])]
    ppermute x21 -> x23, waiting for transfers between devices: 16.4 us -> 20.3 us  [flip_heads(): return lax.ppermute(array, 'head', [(i, i ^ flip) for i in range(devices)])]
    unnamed x32 -> x34, local copies, waits for them, and re-layouts: 2.18 us -> 5.27 us
    ppermute x4 -> x6, starting transfers between devices: 4.8 us -> 7.17 us  [static_keys(): lax.ppermute(mine, 'node', [(i, i ^ shift) for i in range(groups)])]
    ppermute x21 -> x23, starting transfers between devices: 25.1 us -> 27.4 us  [flip_heads(): return lax.ppermute(array, 'head', [(i, i ^ flip) for i in range(devices)])]
    slice x6 -> x2, local copies, waits for them, and re-layouts: 3.22 us -> 1.07 us  [pair_stack(): return jnp.stack([received[0], beside[0], received[1], beside[1]])]
    ppermute x1, starting transfers between devices: 2.19 us -> 4.05 us  [static_keys(): other = spread_stack(lax.ppermute(mine, 'node', far), heads_axis)]
    ppermute x3 -> x1, starting transfers between devices: 2.65 us -> 1.24 us  [static_keys(): lax.ppermute(near, 'node', [(i, i ^ shift) for i in range(groups)])]
  transfers between devices with their start and end apart: 29 -> 31, of which waited for: 15 -> 15; matrix products, arithmetic and copies ran while one was open for 14% -> 17% of each run, Pallas kernels for 0% -> 0%
where the time goes in v10:
time: 105 us; the launch traced here: 103 us
  starting transfers between devices  39.8 us (38%)
  waiting for transfers between devices  21.1 us (20%)
  local copies, waits for them, and re-layouts  16.4 us (16%)
  Pallas kernels  10.9 us (10%)
  matrix products  6.68 us (6%)
  other arithmetic  4.82 us (5%)
  between operations  3.17 us (3%)
    ppermute x23, starting transfers between devices, flip_heads(): return lax.ppermute(array, 'head', [(i, i ^ flip) for i in range(devices)])  27.4 us
    ppermute x23, waiting for transfers between devices, flip_heads(): return lax.ppermute(array, 'head', [(i, i ^ flip) for i in range(devices)])  20.3 us
    pallas_call x1, Pallas kernels, attention(): pl.pallas_call(attention_kernel, out_shape=jax.ShapeDtypeStruct(query.sha...  10.9 us
    ppermute x6, starting transfers between devices, static_keys(): lax.ppermute(mine, 'node', [(i, i ^ shift) for i in range(groups)])  7.17 us
    unnamed x34, local copies, waits for them, and re-layouts  5.27 us
    dot_general x1, matrix products, kv_of_spread(): jnp.dot(rows, w_kv, preferred_element_type=jnp.float32).astype(jnp.bfloat16)  4.28 us
    ppermute x1, starting transfers between devices, static_keys(): other = spread_stack(lax.ppermute(mine, 'node', far), heads_axis)  4.05 us
  transfers between devices with their start and end apart: 31, of which 15 were waited for; matrix products, arithmetic and copies ran while one was open for 17% of the time, Pallas kernels for 0%

profile of v10, /device:TPU:9, one launch (start us, length us, event | category | flops | bytes accessed | tf_op | source)
XLA Modules:
  0.0 102.9 jit_solution(1943636808907221487)
XLA Ops:
  0.0 1.2 %constant_dynamic-slice_fusion.7 = (bf16[3,1,32,1024]{3,2,1,0:T(8,128)(2,1)S(1)}, bf16[3,1,32,1024]{3,2,1,0:T(8,128)(2,1)S(1)}) fusion(bf16[3,4,32,1024]{3,2,1,0:T(8,128)(2,1)} %bitcast.161, s32[]{:T(128)S(6)} %select_n.63, s32[]{:T(128)S(6)} %select_n.62), kind=kLoop, calls=%fused_computation.68 | loop fusion | bytes 786440 | tf_op jit(solution)/shard_map/jit(dynamic_index_in_dim)/dynamic_slice | solution.py:142
  1.3 2.4 %collective-permute-start.11 = (bf16[96,1024]{1,0:T(8,128)(2,1)S(1)}, bf16[96,1024]{1,0:T(8,128)(2,1)S(1)}, u32[]{:S(2)}, u32[]{:S(2)}) collective-permute-start(bf16[96,1024]{1,0:T(8,128)(2,1)S(1)} %bitcast.153), channel_id=1, source_target_pairs={{0,12},{4,8},{8,4},{12,0},{16,28},{20,24},{24,20},{28,16},{1,13},{... | collective-permute-start | bytes 589832 | tf_op jit(solution)/shard_map/ppermute | solution.py:118
  3.7 2.3 %collective-permute-start.14 = (bf16[96,1024]{1,0:T(8,128)(2,1)S(1)}, bf16[96,1024]{1,0:T(8,128)(2,1)S(1)}, u32[]{:S(2)}, u32[]{:S(2)}) collective-permute-start(bf16[96,1024]{1,0:T(8,128)(2,1)S(1)} %bitcast.154), channel_id=1, source_target_pairs={{0,16},{4,20},{8,24},{12,28},{16,0},{20,4},{24,8},{28,12},{1,17},{... | collective-permute-start | bytes 589832 | tf_op jit(solution)/shard_map/ppermute | solution.py:118
  6.0 0.8 pad_maximum_fusion.2
  6.8 1.2 %collective-permute-start = (bf16[2,96,1024]{2,1,0:T(8,128)(2,1)}, bf16[2,96,1024]{2,1,0:T(8,128)(2,1)}, u32[]{:S(2)}, u32[]{:S(2)}) collective-permute-start(bf16[2,96,1024]{2,1,0:T(8,128)(2,1)} %pad_maximum_fusion.2), channel_id=1, source_target_pairs={{0,4},{4,0},{8,12},{12,8},{16,20},{20,16},{24,28},{28,24},{1,5},{5... | collective-permute-start | bytes 1179656 | tf_op jit(solution)/shard_map/ppermute | solution.py:114
  8.3 1.9 %convolution_convert_fusion.1 = bf16[384,3,256]{2,0,1:T(8,128)(2,1)S(1)} fusion(bf16[1024,3,256]{2,0,1:T(8,128)(2,1)S(1)} %copy-done, bf16[384,1024]{1,0:T(8,128)(2,1)} %param.7), kind=kOutput, calls=%fused_computation.1 | convolution fusion | flops 604274688 | bytes 2949120 | tf_op jit(solution)/shard_map/nd,dtf->ntf/dot_general | solution.py:272
  10.4 2.0 %constant_dynamic-slice_fusion.3 = (bf16[256,256]{1,0:T(8,128)(2,1)S(1)}, bf16[256,256]{1,0:T(8,128)(2,1)}, bf16[256,256]{1,0:T(8,128)(2,1)}, bf16[256,256]{1,0:T(8,128)(2,1)S(1)}) fusion(bf16[256,1024]{1,0:T(8,128)(2,1)} %param.9, s32[]{:T(128)S(6)} %select_n.68, s32[]{:T(128)S(6)} %select_n.67, s32[]{:T(128)S(6)} %select_n.66, s32[]{:T(128)S(6)} %select_n.58), kind=kLoop, calls=%fused_computation.64 | loop fusion | bytes 1048592 | tf_op jit(solution)/shard_map/dynamic_slice | solution.py:266
  12.3 0.7 fusion.40
  13.0 0.7 slice.121
  16.3 1.7 %copy.38 = bf16[256,256]{0,1:T(8,128)(2,1)} copy(bf16[256,256]{1,0:T(8,128)(2,1)} %get-tuple-element.25) | data formatting | bytes 262144
  18.0 1.7 %copy.39 = bf16[256,256]{0,1:T(8,128)(2,1)} copy(bf16[256,256]{1,0:T(8,128)(2,1)} %get-tuple-element.24) | data formatting | bytes 262144
  19.6 0.8 copy.40
  20.4 0.8 copy.37
  22.1 1.0 reshape_reshape.6.own_ref
  23.1 0.5 pad_convert_fusion.live_ref
  23.7 0.6 add_select_fusion.pick_ref
  24.3 1.3 %collective-permute-start.20 = (bf16[96,1024]{1,0:T(8,128)(2,1)S(1)}, bf16[96,1024]{1,0:T(8,128)(2,1)S(1)}, u32[]{:S(2)}, u32[]{:S(2)}) collective-permute-start(bf16[96,1024]{1,0:T(8,128)(2,1)S(1)} %bitcast.157), channel_id=1, source_target_pairs={{0,24},{4,28},{8,16},{12,20},{16,8},{20,12},{24,0},{28,4},{1,25},{... | collective-permute-start | bytes 589832 | tf_op jit(solution)/shard_map/ppermute | solution.py:118
  25.6 1.2 %collective-permute-start.9 = (bf16[1,96,1024]{2,1,0:T(8,128)(2,1)S(1)}, bf16[1,96,1024]{2,1,0:T(8,128)(2,1)S(1)}, u32[]{:S(2)}, u32[]{:S(2)}) collective-permute-start(bf16[1,96,1024]{2,1,0:T(8,128)(2,1)S(1)} %bitcast.143), channel_id=1, source_target_pairs={{0,2},{1,3},{2,0},{3,1},{4,6},{5,7},{6,4},{7,5},{8,10},{9,11},{10,... | collective-permute-start | bytes 589832 | tf_op jit(solution)/shard_map/ppermute | solution.py:27
  27.1 1.0 %fusion.37 = (bf16[1,96,1024]{2,1,0:T(8,128)(2,1)S(1)}, bf16[1,96,1024]{2,1,0:T(8,128)(2,1)S(1)}) fusion(bf16[2,96,1024]{2,1,0:T(8,128)(2,1)} %collective-permute-done), kind=kLoop, calls=%fused_computation.96 | loop fusion | bytes 786432 | tf_op jit(solution)/shard_map/slice | solution.py:152
  28.1 1.1 %collective-permute-start.23 = (bf16[96,1024]{1,0:T(8,128)(2,1)S(1)}, bf16[96,1024]{1,0:T(8,128)(2,1)S(1)}, u32[]{:S(2)}, u32[]{:S(2)}) collective-permute-start(bf16[96,1024]{1,0:T(8,128)(2,1)S(1)} %bitcast.158), channel_id=1, source_target_pairs={{0,28},{4,24},{8,20},{12,16},{16,12},{20,8},{24,4},{28,0},{1,29},{... | collective-permute-start | bytes 589832 | tf_op jit(solution)/shard_map/ppermute | solution.py:118
  29.2 1.2 %collective-permute-done.9 = bf16[1,96,1024]{2,1,0:T(8,128)(2,1)S(1)} collective-permute-done((bf16[1,96,1024]{2,1,0:T(8,128)(2,1)S(1)}, bf16[1,96,1024]{2,1,0:T(8,128)(2,1)S(1)}, u32[]{:S(2)}, u32[]{:S(2)}) %collective-permute-start.9) | collective-permute-done | bytes 196640 | tf_op jit(solution)/shard_map/ppermute | solution.py:27
  30.4 1.2 %collective-permute-start.15 = (bf16[1,96,1024]{2,1,0:T(8,128)(2,1)S(1)}, bf16[1,96,1024]{2,1,0:T(8,128)(2,1)S(1)}, u32[]{:S(2)}, u32[]{:S(2)}) collective-permute-start(bf16[1,96,1024]{2,1,0:T(8,128)(2,1)S(1)} %bitcast.137), channel_id=1, source_target_pairs={{0,2},{1,3},{2,0},{3,1},{4,6},{5,7},{6,4},{7,5},{8,10},{9,11},{10,... | collective-permute-start | bytes 589832 | tf_op jit(solution)/shard_map/ppermute | solution.py:27
  31.7 4.0 %collective-permute-start.2 = (bf16[96,1024]{1,0:T(8,128)(2,1)S(1)}, bf16[96,1024]{1,0:T(8,128)(2,1)S(1)}, u32[]{:S(2)}, u32[]{:S(2)}) collective-permute-start(bf16[96,1024]{1,0:T(8,128)(2,1)S(1)} %bitcast.159), channel_id=1, source_target_pairs={{4,8},{12,16},{20,24},{8,4},{16,12},{24,20},{5,9},{13,17},{21,25},... | collective-permute-start | bytes 589832 | tf_op jit(solution)/shard_map/ppermute | solution.py:109
  36.5 5.9 %collective-permute-start.5 = (bf16[256,256]{0,1:T(8,128)(2,1)S(1)}, bf16[256,256]{0,1:T(8,128)(2,1)S(1)}, u32[]{:S(2)}, u32[]{:S(2)}) collective-permute-start(bf16[256,256]{0,1:T(8,128)(2,1)S(1)} %copy-done.6), channel_id=1, source_target_pairs={{0,1},{1,0},{2,3},{3,2},{4,5},{5,4},{6,7},{7,6},{8,9},{9,8},{10,11... | collective-permute-start | bytes 393224 | tf_op jit(solution)/shard_map/ppermute | solution.py:27
  42.8 1.4 %collective-permute-start.21 = (bf16[1,96,1024]{2,1,0:T(8,128)(2,1)S(1)}, bf16[1,96,1024]{2,1,0:T(8,128)(2,1)S(1)}, u32[]{:S(2)}, u32[]{:S(2)}) collective-permute-start(bf16[1,96,1024]{2,1,0:T(8,128)(2,1)S(1)} %bitcast.146), channel_id=1, source_target_pairs={{0,2},{1,3},{2,0},{3,1},{4,6},{5,7},{6,4},{7,5},{8,10},{9,11},{10,... | collective-permute-start | bytes 589832 | tf_op jit(solution)/shard_map/ppermute | solution.py:27
  44.3 4.7 %collective-permute-start.1 = (bf16[2,96,1024]{2,1,0:T(8,128)(2,1)}, bf16[2,96,1024]{2,1,0:T(8,128)(2,1)S(1)}, u32[]{:S(2)}, u32[]{:S(2)}) collective-permute-start(bf16[2,96,1024]{2,1,0:T(8,128)(2,1)} %collective-permute-done), channel_id=1, source_target_pairs={{0,1},{1,0},{2,3},{3,2},{4,5},{5,4},{6,7},{7,6},{8,9},{9,8},{10,11... | collective-permute-start | bytes 1179656 | tf_op jit(solution)/shard_map/ppermute | solution.py:27
  49.7 0.9 collective-permute-start.3
  50.6 3.2 %collective-permute-done.24 = bf16[1,96,1024]{2,1,0:T(8,128)(2,1)S(1)} collective-permute-done((bf16[1,96,1024]{2,1,0:T(8,128)(2,1)S(1)}, bf16[1,96,1024]{2,1,0:T(8,128)(2,1)S(1)}, u32[]{:S(2)}, u32[]{:S(2)}) %collective-permute-start.24) | collective-permute-done | bytes 196640 | tf_op jit(solution)/shard_map/ppermute | solution.py:27
  53.9 3.5 %collective-permute-start.10 = (bf16[2,96,1024]{2,1,0:T(8,128)(2,1)S(1)}, bf16[2,96,1024]{2,1,0:T(8,128)(2,1)S(1)}, u32[]{:S(2)}, u32[]{:S(2)}) collective-permute-start(bf16[2,96,1024]{2,1,0:T(8,128)(2,1)S(1)} %pad_maximum_fusion.4), channel_id=1, source_target_pairs={{0,1},{1,0},{2,3},{3,2},{4,5},{5,4},{6,7},{7,6},{8,9},{9,8},{10,11... | collective-permute-start | bytes 1179656 | tf_op jit(solution)/shard_map/ppermute | solution.py:27
  57.5 3.4 %collective-permute-done.3 = bf16[1,96,1024]{2,1,0:T(8,128)(2,1)S(1)} collective-permute-done((bf16[1,96,1024]{2,1,0:T(8,128)(2,1)S(1)}, bf16[1,96,1024]{2,1,0:T(8,128)(2,1)S(1)}, u32[]{:S(2)}, u32[]{:S(2)}) %collective-permute-start.3) | collective-permute-done | bytes 196640 | tf_op jit(solution)/shard_map/ppermute | solution.py:27
  60.9 2.1 %collective-permute-start.7 = (bf16[256,256]{0,1:T(8,128)(2,1)S(1)}, bf16[256,256]{0,1:T(8,128)(2,1)S(1)}, u32[]{:S(2)}, u32[]{:S(2)}) collective-permute-start(bf16[256,256]{0,1:T(8,128)(2,1)S(1)} %copy-done.4), channel_id=1, source_target_pairs={{0,3},{1,2},{2,1},{3,0},{4,7},{5,6},{6,5},{7,4},{8,11},{9,10},{10,... | collective-permute-start | bytes 393224 | tf_op jit(solution)/shard_map/ppermute | solution.py:27
  63.2 0.6 collective-permute-start.16
  63.8 1.1 %collective-permute-done.13 = bf16[2,96,1024]{2,1,0:T(8,128)(2,1)S(1)} collective-permute-done((bf16[2,96,1024]{2,1,0:T(8,128)(2,1)S(1)}, bf16[2,96,1024]{2,1,0:T(8,128)(2,1)S(1)}, u32[]{:S(2)}, u32[]{:S(2)}) %collective-permute-start.13) | collective-permute-done | bytes 393248 | tf_op jit(solution)/shard_map/ppermute | solution.py:27
  65.6 1.0 collective-permute-done.19
  67.3 1.0 collective-permute-done.25
  70.3 0.9 copy.31
  71.3 4.3 %convolution_convert_fusion = bf16[2304,512]{1,0:T(8,128)(2,1)} fusion(bf16[2304,1024]{1,0:T(8,128)(2,1)S(1)} %bitcast.110, bf16[1024,512]{0,1:T(8,128)(2,1)S(1)} %bitcast.133), kind=kOutput, calls=%fused_computation | convolution fusion | flops 2417098752 | bytes 8126464 | tf_op jit(solution)/shard_map/dot_general | solution.py:171
  75.6 10.9 %shard_map.73 = bf16[3,128,256]{2,1,0:T(8,128)(2,1)} custom-call(s32[3,11]{1,0:T(4,128)} %pad_convert_fusion.live_ref, s32[4,3]{1,0:T(4,128)} %add_select_fusion.pick_ref, bf16[3,128,256]{2,1,0:T(8,128)(2,1)} %bitcast.162, bf16[3,128,512]{2,1,0:T(8,128)(2,1)} %reshape_reshape.6.own_ref, bf16[6,3,128,512]{3,2,1,0:T(8,128)(2,1)} %bitcast.173), custom_call_target="tpu_custom_call" | custom-call | flops 1107296256 | bytes 3145728 | tf_op jit(solution)/shard_map/pallas_call | solution.py:238
  86.4 1.3 %collective-permute-start.26 = (bf16[1,384,256]{2,1,0:T(8,128)(2,1)}, bf16[1,384,256]{2,1,0:T(8,128)(2,1)S(1)}, u32[]{:S(2)}, u32[]{:S(2)}) collective-permute-start(bf16[1,384,256]{2,1,0:T(8,128)(2,1)} %bitcast.163), channel_id=1, source_target_pairs={{0,2},{1,3},{2,0},{3,1},{4,6},{5,7},{6,4},{7,5},{8,10},{9,11},{10,... | collective-permute-start | bytes 589832 | tf_op jit(solution)/shard_map/ppermute | solution.py:27
  87.7 5.4 %collective-permute-done.26 = bf16[1,384,256]{2,1,0:T(8,128)(2,1)S(1)} collective-permute-done((bf16[1,384,256]{2,1,0:T(8,128)(2,1)}, bf16[1,384,256]{2,1,0:T(8,128)(2,1)S(1)}, u32[]{:S(2)}, u32[]{:S(2)}) %collective-permute-start.26) | collective-permute-done | bytes 196640 | tf_op jit(solution)/shard_map/ppermute | solution.py:27
  93.1 1.0 pad_maximum_fusion.10
  94.0 1.0 collective-permute-start.27
  95.1 0.9 constant_dynamic-slice_fusion.9
  97.5 1.2 %collective-permute-start.29 = (f32[384,2]{0,1:T(2,128)S(1)}, f32[384,2]{0,1:T(2,128)S(1)}, u32[]{:S(2)}, u32[]{:S(2)}) collective-permute-start(f32[384,2]{0,1:T(2,128)S(1)} %get-tuple-element.48), channel_id=1, source_target_pairs={{0,2},{1,3},{2,0},{3,1},{4,6},{5,7},{6,4},{7,5},{8,10},{9,11},{10,... | collective-permute-start | bytes 9224 | tf_op jit(solution)/shard_map/ppermute | solution.py:27
  98.7 0.6 collective-permute-start.30
  99.3 0.7 collective-permute-done.29
  100.0 1.8 %collective-permute-done.30 = f32[384,2]{0,1:T(2,128)S(1)} collective-permute-done((f32[384,2]{0,1:T(2,128)S(1)}, f32[384,2]{0,1:T(2,128)S(1)}, u32[]{:S(2)}, u32[]{:S(2)}) %collective-permute-start.30) | collective-permute-done | bytes 3104 | tf_op jit(solution)/shard_map/ppermute | solution.py:27
  102.1 0.8 copy.33
  (116 shorter events, 8.9 us)
Async XLA Ops:
  0.0 8.0 %copy-start.7 = (s32[4,3]{1,0:T(4,128)S(1)}, s32[4,3]{1,0:T(4,128)}, u32[]{:S(2)}) copy-start(s32[4,3]{1,0:T(4,128)} %param.13) | copy-start | bytes 148
  0.0 8.3 %copy-start = (bf16[1024,3,256]{2,0,1:T(8,128)(2,1)S(1)}, bf16[1024,3,256]{2,0,1:T(8,128)(2,1)}, u32[]{:S(2)}) copy-start(bf16[1024,3,256]{2,0,1:T(8,128)(2,1)} %param.8) | copy-start | bytes 4718596
  1.2 23.1 %collective-permute-start.8 = (bf16[96,1024]{1,0:T(8,128)(2,1)S(1)}, bf16[96,1024]{1,0:T(8,128)(2,1)S(1)}, u32[]{:S(2)}, u32[]{:S(2)}) collective-permute-start(bf16[96,1024]{1,0:T(8,128)(2,1)S(1)} %bitcast.152), channel_id=1, source_target_pairs={{0,8},{4,12},{8,0},{12,4},{16,24},{20,28},{24,16},{28,20},{1,9},{5... | collective-permute-start | bytes 589832 | tf_op jit(solution)/shard_map/ppermute | solution.py:118
  1.3 24.3 %collective-permute-start.11 = (bf16[96,1024]{1,0:T(8,128)(2,1)S(1)}, bf16[96,1024]{1,0:T(8,128)(2,1)S(1)}, u32[]{:S(2)}, u32[]{:S(2)}) collective-permute-start(bf16[96,1024]{1,0:T(8,128)(2,1)S(1)} %bitcast.153), channel_id=1, source_target_pairs={{0,12},{4,8},{8,4},{12,0},{16,28},{20,24},{24,20},{28,16},{1,13},{... | collective-permute-start | bytes 589832 | tf_op jit(solution)/shard_map/ppermute | solution.py:118
  3.7 24.5 %collective-permute-start.14 = (bf16[96,1024]{1,0:T(8,128)(2,1)S(1)}, bf16[96,1024]{1,0:T(8,128)(2,1)S(1)}, u32[]{:S(2)}, u32[]{:S(2)}) collective-permute-start(bf16[96,1024]{1,0:T(8,128)(2,1)S(1)} %bitcast.154), channel_id=1, source_target_pairs={{0,16},{4,20},{8,24},{12,28},{16,0},{20,4},{24,8},{28,12},{1,17},{... | collective-permute-start | bytes 589832 | tf_op jit(solution)/shard_map/ppermute | solution.py:118
  6.0 25.7 %collective-permute-start.17 = (bf16[96,1024]{1,0:T(8,128)(2,1)S(1)}, bf16[96,1024]{1,0:T(8,128)(2,1)S(1)}, u32[]{:S(2)}, u32[]{:S(2)}) collective-permute-start(bf16[96,1024]{1,0:T(8,128)(2,1)S(1)} %bitcast.155), channel_id=1, source_target_pairs={{0,20},{4,16},{8,28},{12,24},{16,4},{20,0},{24,12},{28,8},{1,21},{... | collective-permute-start | bytes 589832 | tf_op jit(solution)/shard_map/ppermute | solution.py:118
  6.8 20.0 %collective-permute-start = (bf16[2,96,1024]{2,1,0:T(8,128)(2,1)}, bf16[2,96,1024]{2,1,0:T(8,128)(2,1)}, u32[]{:S(2)}, u32[]{:S(2)}) collective-permute-start(bf16[2,96,1024]{2,1,0:T(8,128)(2,1)} %pad_maximum_fusion.2), channel_id=1, source_target_pairs={{0,4},{4,0},{8,12},{12,8},{16,20},{20,16},{24,28},{28,24},{1,5},{5... | collective-permute-start | bytes 1179656 | tf_op jit(solution)/shard_map/ppermute | solution.py:114
  8.3 2.0 %copy-start.8 = (s32[3,7]{1,0:T(4,128)S(1)}, s32[3,7]{1,0:T(4,128)}, u32[]{:S(2)}) copy-start(s32[3,7]{1,0:T(4,128)} %param.12) | copy-start | bytes 256
  10.2 2.8 %copy-start.1 = (bf16[384,3,256]{2,0,1:T(8,128)(2,1)}, bf16[384,3,256]{2,0,1:T(8,128)(2,1)S(1)}, u32[]{:S(2)}) copy-start(bf16[384,3,256]{2,0,1:T(8,128)(2,1)S(1)} %convolution_convert_fusion.1) | copy-start | bytes 1769476
  13.0 8.2 %slice-start = ((bf16[1024,3,256]{2,0,1:T(8,128)(2,1)}), bf16[1024,2,256]{2,0,1:T(8,128)(2,1)S(1)}, s32[]{:S(2)}) async-start(bf16[1024,3,256]{2,0,1:T(8,128)(2,1)} %param.8), calls=%async_computation | async-start | bytes 2097152 | tf_op jit(solution)/shard_map/slice | solution.py:281
  16.3 5.5 %slice-start.1 = ((bf16[384,3,256]{2,0,1:T(8,128)(2,1)}), bf16[384,2,256]{2,0,1:T(8,128)(2,1)S(1)}, s32[]{:S(2)}) async-start(bf16[384,3,256]{2,0,1:T(8,128)(2,1)} %copy-done.1), calls=%async_computation.1 | async-start | bytes 786432 | tf_op jit(solution)/shard_map/slice | solution.py:276
  22.1 14.4 %copy-start.6 = (bf16[256,256]{0,1:T(8,128)(2,1)S(1)}, bf16[256,256]{0,1:T(8,128)(2,1)}, u32[]{:S(2)}) copy-start(bf16[256,256]{0,1:T(8,128)(2,1)} %copy.38) | copy-start | bytes 393220
  24.3 12.2 %collective-permute-start.20 = (bf16[96,1024]{1,0:T(8,128)(2,1)S(1)}, bf16[96,1024]{1,0:T(8,128)(2,1)S(1)}, u32[]{:S(2)}, u32[]{:S(2)}) collective-permute-start(bf16[96,1024]{1,0:T(8,128)(2,1)S(1)} %bitcast.157), channel_id=1, source_target_pairs={{0,24},{4,28},{8,16},{12,20},{16,8},{20,12},{24,0},{28,4},{1,25},{... | collective-permute-start | bytes 589832 | tf_op jit(solution)/shard_map/ppermute | solution.py:118
  25.6 4.8 %collective-permute-start.9 = (bf16[1,96,1024]{2,1,0:T(8,128)(2,1)S(1)}, bf16[1,96,1024]{2,1,0:T(8,128)(2,1)S(1)}, u32[]{:S(2)}, u32[]{:S(2)}) collective-permute-start(bf16[1,96,1024]{2,1,0:T(8,128)(2,1)S(1)} %bitcast.143), channel_id=1, source_target_pairs={{0,2},{1,3},{2,0},{3,1},{4,6},{5,7},{6,4},{7,5},{8,10},{9,11},{10,... | collective-permute-start | bytes 589832 | tf_op jit(solution)/shard_map/ppermute | solution.py:27
  26.8 8.9 %collective-permute-start.12 = (bf16[1,96,1024]{2,1,0:T(8,128)(2,1)S(1)}, bf16[1,96,1024]{2,1,0:T(8,128)(2,1)S(1)}, u32[]{:S(2)}, u32[]{:S(2)}) collective-permute-start(bf16[1,96,1024]{2,1,0:T(8,128)(2,1)S(1)} %bitcast.140), channel_id=1, source_target_pairs={{0,2},{1,3},{2,0},{3,1},{4,6},{5,7},{6,4},{7,5},{8,10},{9,11},{10,... | collective-permute-start | bytes 589832 | tf_op jit(solution)/shard_map/ppermute | solution.py:27
  28.1 14.7 %collective-permute-start.23 = (bf16[96,1024]{1,0:T(8,128)(2,1)S(1)}, bf16[96,1024]{1,0:T(8,128)(2,1)S(1)}, u32[]{:S(2)}, u32[]{:S(2)}) collective-permute-start(bf16[96,1024]{1,0:T(8,128)(2,1)S(1)} %bitcast.158), channel_id=1, source_target_pairs={{0,28},{4,24},{8,20},{12,16},{16,12},{20,8},{24,4},{28,0},{1,29},{... | collective-permute-start | bytes 589832 | tf_op jit(solution)/shard_map/ppermute | solution.py:118
  30.4 18.6 %copy-start.5 = (bf16[256,256]{0,1:T(8,128)(2,1)S(1)}, bf16[256,256]{0,1:T(8,128)(2,1)}, u32[]{:S(2)}) copy-start(bf16[256,256]{0,1:T(8,128)(2,1)} %copy.39) | copy-start | bytes 393220
  30.4 13.7 %collective-permute-start.15 = (bf16[1,96,1024]{2,1,0:T(8,128)(2,1)S(1)}, bf16[1,96,1024]{2,1,0:T(8,128)(2,1)S(1)}, u32[]{:S(2)}, u32[]{:S(2)}) collective-permute-start(bf16[1,96,1024]{2,1,0:T(8,128)(2,1)S(1)} %bitcast.137), channel_id=1, source_target_pairs={{0,2},{1,3},{2,0},{3,1},{4,6},{5,7},{6,4},{7,5},{8,10},{9,11},{10,... | collective-permute-start | bytes 589832 | tf_op jit(solution)/shard_map/ppermute | solution.py:27
  31.7 17.4 %collective-permute-start.2 = (bf16[96,1024]{1,0:T(8,128)(2,1)S(1)}, bf16[96,1024]{1,0:T(8,128)(2,1)S(1)}, u32[]{:S(2)}, u32[]{:S(2)}) collective-permute-start(bf16[96,1024]{1,0:T(8,128)(2,1)S(1)} %bitcast.159), channel_id=1, source_target_pairs={{4,8},{12,16},{20,24},{8,4},{16,12},{24,20},{5,9},{13,17},{21,25},... | collective-permute-start | bytes 589832 | tf_op jit(solution)/shard_map/ppermute | solution.py:109
  35.7 8.6 %collective-permute-start.18 = (bf16[1,96,1024]{2,1,0:T(8,128)(2,1)S(1)}, bf16[1,96,1024]{2,1,0:T(8,128)(2,1)S(1)}, u32[]{:S(2)}, u32[]{:S(2)}) collective-permute-start(bf16[1,96,1024]{2,1,0:T(8,128)(2,1)S(1)} %bitcast.134), channel_id=1, source_target_pairs={{0,2},{1,3},{2,0},{3,1},{4,6},{5,7},{6,4},{7,5},{8,10},{9,11},{10,... | collective-permute-start | bytes 589832 | tf_op jit(solution)/shard_map/ppermute | solution.py:27
  36.5 32.6 %collective-permute-start.5 = (bf16[256,256]{0,1:T(8,128)(2,1)S(1)}, bf16[256,256]{0,1:T(8,128)(2,1)S(1)}, u32[]{:S(2)}, u32[]{:S(2)}) collective-permute-start(bf16[256,256]{0,1:T(8,128)(2,1)S(1)} %copy-done.6), channel_id=1, source_target_pairs={{0,1},{1,0},{2,3},{3,2},{4,5},{5,4},{6,7},{7,6},{8,9},{9,8},{10,11... | collective-permute-start | bytes 393224 | tf_op jit(solution)/shard_map/ppermute | solution.py:27
  42.8 6.9 %collective-permute-start.21 = (bf16[1,96,1024]{2,1,0:T(8,128)(2,1)S(1)}, bf16[1,96,1024]{2,1,0:T(8,128)(2,1)S(1)}, u32[]{:S(2)}, u32[]{:S(2)}) collective-permute-start(bf16[1,96,1024]{2,1,0:T(8,128)(2,1)S(1)} %bitcast.146), channel_id=1, source_target_pairs={{0,2},{1,3},{2,0},{3,1},{4,6},{5,7},{6,4},{7,5},{8,10},{9,11},{10,... | collective-permute-start | bytes 589832 | tf_op jit(solution)/shard_map/ppermute | solution.py:27
  44.2 16.7 %copy-start.4 = (bf16[256,256]{0,1:T(8,128)(2,1)S(1)}, bf16[256,256]{0,1:T(8,128)(2,1)}, u32[]{:S(2)}) copy-start(bf16[256,256]{0,1:T(8,128)(2,1)} %copy.40) | copy-start | bytes 393220
  44.2 9.7 %collective-permute-start.24 = (bf16[1,96,1024]{2,1,0:T(8,128)(2,1)S(1)}, bf16[1,96,1024]{2,1,0:T(8,128)(2,1)S(1)}, u32[]{:S(2)}, u32[]{:S(2)}) collective-permute-start(bf16[1,96,1024]{2,1,0:T(8,128)(2,1)S(1)} %bitcast.149), channel_id=1, source_target_pairs={{0,2},{1,3},{2,0},{3,1},{4,6},{5,7},{6,4},{7,5},{8,10},{9,11},{10,... | collective-permute-start | bytes 589832 | tf_op jit(solution)/shard_map/ppermute | solution.py:27
  44.3 18.7 %collective-permute-start.1 = (bf16[2,96,1024]{2,1,0:T(8,128)(2,1)}, bf16[2,96,1024]{2,1,0:T(8,128)(2,1)S(1)}, u32[]{:S(2)}, u32[]{:S(2)}) collective-permute-start(bf16[2,96,1024]{2,1,0:T(8,128)(2,1)} %collective-permute-done), channel_id=1, source_target_pairs={{0,1},{1,0},{2,3},{3,2},{4,5},{5,4},{6,7},{7,6},{8,9},{9,8},{10,11... | collective-permute-start | bytes 1179656 | tf_op jit(solution)/shard_map/ppermute | solution.py:27
  49.1 20.1 %collective-permute-start.6 = (bf16[256,256]{0,1:T(8,128)(2,1)S(1)}, bf16[256,256]{0,1:T(8,128)(2,1)S(1)}, u32[]{:S(2)}, u32[]{:S(2)}) collective-permute-start(bf16[256,256]{0,1:T(8,128)(2,1)S(1)} %copy-done.5), channel_id=1, source_target_pairs={{0,2},{1,3},{2,0},{3,1},{4,6},{5,7},{6,4},{7,5},{8,10},{9,11},{10,... | collective-permute-start | bytes 393224 | tf_op jit(solution)/shard_map/ppermute | solution.py:27
  49.7 11.2 %collective-permute-start.3 = (bf16[1,96,1024]{2,1,0:T(8,128)(2,1)S(1)}, bf16[1,96,1024]{2,1,0:T(8,128)(2,1)S(1)}, u32[]{:S(2)}, u32[]{:S(2)}) collective-permute-start(bf16[1,96,1024]{2,1,0:T(8,128)(2,1)S(1)} %bitcast.123), channel_id=1, source_target_pairs={{0,2},{1,3},{2,0},{3,1},{4,6},{5,7},{6,4},{7,5},{8,10},{9,11},{10,... | collective-permute-start | bytes 589832 | tf_op jit(solution)/shard_map/ppermute | solution.py:27
  53.9 9.3 %collective-permute-start.10 = (bf16[2,96,1024]{2,1,0:T(8,128)(2,1)S(1)}, bf16[2,96,1024]{2,1,0:T(8,128)(2,1)S(1)}, u32[]{:S(2)}, u32[]{:S(2)}) collective-permute-start(bf16[2,96,1024]{2,1,0:T(8,128)(2,1)S(1)} %pad_maximum_fusion.4), channel_id=1, source_target_pairs={{0,1},{1,0},{2,3},{3,2},{4,5},{5,4},{6,7},{7,6},{8,9},{9,8},{10,11... | collective-permute-start | bytes 1179656 | tf_op jit(solution)/shard_map/ppermute | solution.py:27
  60.9 8.3 %collective-permute-start.7 = (bf16[256,256]{0,1:T(8,128)(2,1)S(1)}, bf16[256,256]{0,1:T(8,128)(2,1)S(1)}, u32[]{:S(2)}, u32[]{:S(2)}) collective-permute-start(bf16[256,256]{0,1:T(8,128)(2,1)S(1)} %copy-done.4), channel_id=1, source_target_pairs={{0,3},{1,2},{2,1},{3,0},{4,7},{5,6},{6,5},{7,4},{8,11},{9,10},{10,... | collective-permute-start | bytes 393224 | tf_op jit(solution)/shard_map/ppermute | solution.py:27
  63.1 1.8 %collective-permute-start.13 = (bf16[2,96,1024]{2,1,0:T(8,128)(2,1)S(1)}, bf16[2,96,1024]{2,1,0:T(8,128)(2,1)S(1)}, u32[]{:S(2)}, u32[]{:S(2)}) collective-permute-start(bf16[2,96,1024]{2,1,0:T(8,128)(2,1)S(1)} %pad_maximum_fusion.5), channel_id=1, source_target_pairs={{0,1},{1,0},{2,3},{3,2},{4,5},{5,4},{6,7},{7,6},{8,9},{9,8},{10,11... | collective-permute-start | bytes 1179656 | tf_op jit(solution)/shard_map/ppermute | solution.py:27
  63.2 2.2 %collective-permute-start.16 = (bf16[2,96,1024]{2,1,0:T(8,128)(2,1)S(1)}, bf16[2,96,1024]{2,1,0:T(8,128)(2,1)S(1)}, u32[]{:S(2)}, u32[]{:S(2)}) collective-permute-start(bf16[2,96,1024]{2,1,0:T(8,128)(2,1)S(1)} %pad_maximum_fusion.6), channel_id=1, source_target_pairs={{0,1},{1,0},{2,3},{3,2},{4,5},{5,4},{6,7},{7,6},{8,9},{9,8},{10,11... | collective-permute-start | bytes 1179656 | tf_op jit(solution)/shard_map/ppermute | solution.py:27
  64.8 1.7 %collective-permute-start.19 = (bf16[2,96,1024]{2,1,0:T(8,128)(2,1)S(1)}, bf16[2,96,1024]{2,1,0:T(8,128)(2,1)S(1)}, u32[]{:S(2)}, u32[]{:S(2)}) collective-permute-start(bf16[2,96,1024]{2,1,0:T(8,128)(2,1)S(1)} %pad_maximum_fusion.7), channel_id=1, source_target_pairs={{0,1},{1,0},{2,3},{3,2},{4,5},{5,4},{6,7},{7,6},{8,9},{9,8},{10,11... | collective-permute-start | bytes 1179656 | tf_op jit(solution)/shard_map/ppermute | solution.py:27
  65.4 1.7 %collective-permute-start.22 = (bf16[2,96,1024]{2,1,0:T(8,128)(2,1)S(1)}, bf16[2,96,1024]{2,1,0:T(8,128)(2,1)S(1)}, u32[]{:S(2)}, u32[]{:S(2)}) collective-permute-start(bf16[2,96,1024]{2,1,0:T(8,128)(2,1)S(1)} %pad_maximum_fusion.8), channel_id=1, source_target_pairs={{0,1},{1,0},{2,3},{3,2},{4,5},{5,4},{6,7},{7,6},{8,9},{9,8},{10,11... | collective-permute-start | bytes 1179656 | tf_op jit(solution)/shard_map/ppermute | solution.py:27
  66.6 1.7 %collective-permute-start.25 = (bf16[2,96,1024]{2,1,0:T(8,128)(2,1)S(1)}, bf16[2,96,1024]{2,1,0:T(8,128)(2,1)S(1)}, u32[]{:S(2)}, u32[]{:S(2)}) collective-permute-start(bf16[2,96,1024]{2,1,0:T(8,128)(2,1)S(1)} %pad_maximum_fusion.9), channel_id=1, source_target_pairs={{0,1},{1,0},{2,3},{3,2},{4,5},{5,4},{6,7},{7,6},{8,9},{9,8},{10,11... | collective-permute-start | bytes 1179656 | tf_op jit(solution)/shard_map/ppermute | solution.py:27
  67.1 2.0 %collective-permute-start.4 = (bf16[2,96,1024]{2,1,0:T(8,128)(2,1)S(1)}, bf16[2,96,1024]{2,1,0:T(8,128)(2,1)S(1)}, u32[]{:S(2)}, u32[]{:S(2)}) collective-permute-start(bf16[2,96,1024]{2,1,0:T(8,128)(2,1)S(1)} %pad_maximum_fusion.3), channel_id=1, source_target_pairs={{0,1},{1,0},{2,3},{3,2},{4,5},{5,4},{6,7},{7,6},{8,9},{9,8},{10,11... | collective-permute-start | bytes 1179656 | tf_op jit(solution)/shard_map/ppermute | solution.py:27
  69.2 0.6 copy-start.11
  86.4 10.0 %copy-start.2 = (bf16[3,128,256]{2,1,0:T(8,128)(2,1)S(1)}, bf16[3,128,256]{2,1,0:T(8,128)(2,1)}, u32[]{:S(2)}) copy-start(bf16[3,128,256]{2,1,0:T(8,128)(2,1)} %shard_map.73) | copy-start | bytes 589828
  86.4 10.0 %copy-start.3 = (bf16[256,256]{0,1:T(8,128)(2,1)S(1)}, bf16[256,256]{0,1:T(8,128)(2,1)}, u32[]{:S(2)}) copy-start(bf16[256,256]{0,1:T(8,128)(2,1)} %copy.37) | copy-start | bytes 393220
  86.4 10.0 %copy-start.12 = (bf16[256,256]{0,1:T(8,128)(2,1)S(1)}, bf16[256,256]{0,1:T(8,128)(2,1)}, u32[]{:S(2)}) copy-start(bf16[256,256]{0,1:T(8,128)(2,1)} %copy-done.11) | copy-start | bytes 393220
  86.4 6.6 %collective-permute-start.26 = (bf16[1,384,256]{2,1,0:T(8,128)(2,1)}, bf16[1,384,256]{2,1,0:T(8,128)(2,1)S(1)}, u32[]{:S(2)}, u32[]{:S(2)}) collective-permute-start(bf16[1,384,256]{2,1,0:T(8,128)(2,1)} %bitcast.163), channel_id=1, source_target_pairs={{0,2},{1,3},{2,0},{3,1},{4,6},{5,7},{6,4},{7,5},{8,10},{9,11},{10,... | collective-permute-start | bytes 589832 | tf_op jit(solution)/shard_map/ppermute | solution.py:27
  94.0 2.4 %collective-permute-start.27 = (bf16[2,384,256]{2,1,0:T(8,128)(2,1)S(1)}, bf16[2,384,256]{2,1,0:T(8,128)(2,1)S(1)}, u32[]{:S(2)}, u32[]{:S(2)}) collective-permute-start(bf16[2,384,256]{2,1,0:T(8,128)(2,1)S(1)} %pad_maximum_fusion.10), channel_id=1, source_target_pairs={{0,1},{1,0},{2,3},{3,2},{4,5},{5,4},{6,7},{7,6},{8,9},{9,8},{10,11... | collective-permute-start | bytes 1179656 | tf_op jit(solution)/shard_map/ppermute | solution.py:27
  96.5 5.4 %copy-start.9 = (f32[256]{0:T(256)S(1)}, f32[256]{0:T(256)}, u32[]{:S(2)}) copy-start(f32[256]{0:T(256)} %param.11) | copy-start | bytes 3076
  96.5 5.4 %copy-start.10 = (f32[256]{0:T(256)S(1)}, f32[256]{0:T(256)}, u32[]{:S(2)}) copy-start(f32[256]{0:T(256)} %param.10) | copy-start | bytes 3076
  97.1 2.2 %collective-permute-start.28 = (f32[384,2]{0,1:T(2,128)S(1)}, f32[384,2]{0,1:T(2,128)S(1)}, u32[]{:S(2)}, u32[]{:S(2)}) collective-permute-start(f32[384,2]{0,1:T(2,128)S(1)} %get-tuple-element.48), channel_id=1, source_target_pairs={{0,1},{1,0},{2,3},{3,2},{4,5},{5,4},{6,7},{7,6},{8,9},{9,8},{10,11... | collective-permute-start | bytes 9224 | tf_op jit(solution)/shard_map/ppermute | solution.py:27
  97.5 2.4 %collective-permute-start.29 = (f32[384,2]{0,1:T(2,128)S(1)}, f32[384,2]{0,1:T(2,128)S(1)}, u32[]{:S(2)}, u32[]{:S(2)}) collective-permute-start(f32[384,2]{0,1:T(2,128)S(1)} %get-tuple-element.48), channel_id=1, source_target_pairs={{0,2},{1,3},{2,0},{3,1},{4,6},{5,7},{6,4},{7,5},{8,10},{9,11},{10,... | collective-permute-start | bytes 9224 | tf_op jit(solution)/shard_map/ppermute | solution.py:27
  98.7 3.1 %collective-permute-start.30 = (f32[384,2]{0,1:T(2,128)S(1)}, f32[384,2]{0,1:T(2,128)S(1)}, u32[]{:S(2)}, u32[]{:S(2)}) collective-permute-start(f32[384,2]{0,1:T(2,128)S(1)} %get-tuple-element.48), channel_id=1, source_target_pairs={{0,3},{1,2},{2,1},{3,0},{4,7},{5,6},{6,5},{7,4},{8,11},{9,10},{10,... | collective-permute-start | bytes 9224 | tf_op jit(solution)/shard_map/ppermute | solution.py:27

commit v11 on v10

--- a/solution.py
+++ b/solution.py
@@ -13,7 +13,7 @@
 LANES = 128
 GATHER_GROUPS = 16
 STATIC_GROUPS = 8
-NEAR_SHIFTS = 2
+NEAR_SHIFTS = 3
 
 
 NORM_EPS = 1e-05

time: 105 us -> 107 us (1.019)
  waiting for transfers between devices: 21.1 us -> 26.1 us
  local copies, waits for them, and re-layouts: 16.4 us -> 13.7 us
    ppermute x6 -> x5, waiting for transfers between devices: 0.82 us -> 5.78 us  [static_keys(): lax.ppermute(mine, 'node', [(i, i ^ shift) for i in range(groups)])]
    ppermute x23 -> x22, starting transfers between devices: 27.4 us -> 24.2 us  [flip_heads(): return lax.ppermute(array, 'head', [(i, i ^ flip) for i in range(devices)])]
    unnamed x34, local copies, waits for them, and re-layouts: 5.27 us -> 2.85 us
    ppermute x1, starting transfers between devices: 4.05 us -> 6.03 us  [static_keys(): other = spread_stack(lax.ppermute(mine, 'node', far), heads_axis)]
    slice x2 -> x4, local copies, waits for them, and re-layouts: 1.07 us -> 2.15 us  [pair_stack(): return jnp.stack([received[0], beside[0], received[1], beside[1]])]
    ppermute x6 -> x5, starting transfers between devices: 7.17 us -> 8.22 us  [static_keys(): lax.ppermute(mine, 'node', [(i, i ^ shift) for i in range(groups)])]
    ppermute x23 -> x22, waiting for transfers between devices: 20.3 us -> 20.3 us  [flip_heads(): return lax.ppermute(array, 'head', [(i, i ^ flip) for i in range(devices)])]
  transfers between devices with their start and end apart: 31 -> 30, of which waited for: 15 -> 13; matrix products, arithmetic and copies ran while one was open for 17% -> 13% of each run, Pallas kernels for 0% -> 0%
where the time goes in v11:
time: 107 us; the launch traced here: 105 us
  starting transfers between devices  39.9 us (37%)
  waiting for transfers between devices  26.1 us (24%)
  local copies, waits for them, and re-layouts  13.7 us (13%)
  Pallas kernels  10.9 us (10%)
  matrix products  6.69 us (6%)
  other arithmetic  4.78 us (4%)
  between operations  3.15 us (3%)
    ppermute x22, starting transfers between devices, flip_heads(): return lax.ppermute(array, 'head', [(i, i ^ flip) for i in range(devices)])  24.2 us
    ppermute x22, waiting for transfers between devices, flip_heads(): return lax.ppermute(array, 'head', [(i, i ^ flip) for i in range(devices)])  20.3 us
    pallas_call x1, Pallas kernels, attention(): pl.pallas_call(attention_kernel, out_shape=jax.ShapeDtypeStruct(query.sha...  10.9 us
    ppermute x5, starting transfers between devices, static_keys(): lax.ppermute(mine, 'node', [(i, i ^ shift) for i in range(groups)])  8.22 us
    ppermute x1, starting transfers between devices, static_keys(): other = spread_stack(lax.ppermute(mine, 'node', far), heads_axis)  6.03 us
    ppermute x5, waiting for transfers between devices, static_keys(): lax.ppermute(mine, 'node', [(i, i ^ shift) for i in range(groups)])  5.78 us
    dot_general x1, matrix products, kv_of_spread(): jnp.dot(rows, w_kv, preferred_element_type=jnp.float32).astype(jnp.bfloat16)  4.28 us
    unnamed x34, local copies, waits for them, and re-layouts  2.85 us
  transfers between devices with their start and end apart: 30, of which 13 were waited for; matrix products, arithmetic and copies ran while one was open for 13% of the time, Pallas kernels for 0%

profile of v11, /device:TPU:9, one launch (start us, length us, event | category | flops | bytes accessed | tf_op | source)
XLA Modules:
  0.0 105.1 jit_solution(7239661071201635139)
XLA Ops:
  0.0 1.2 %constant_dynamic-slice_fusion.7 = (bf16[3,1,32,1024]{3,2,1,0:T(8,128)(2,1)S(1)}, bf16[3,1,32,1024]{3,2,1,0:T(8,128)(2,1)S(1)}) fusion(bf16[3,4,32,1024]{3,2,1,0:T(8,128)(2,1)} %bitcast.156, s32[]{:T(128)S(6)} %select_n.63, s32[]{:T(128)S(6)} %select_n.62), kind=kLoop, calls=%fused_computation.67 | loop fusion | bytes 786440 | tf_op jit(solution)/shard_map/jit(dynamic_index_in_dim)/dynamic_slice | solution.py:142
  1.2 0.8 pad_maximum_fusion.2
  2.0 1.2 %collective-permute-start = (bf16[2,96,1024]{2,1,0:T(8,128)(2,1)}, bf16[2,96,1024]{2,1,0:T(8,128)(2,1)}, u32[]{:S(2)}, u32[]{:S(2)}) collective-permute-start(bf16[2,96,1024]{2,1,0:T(8,128)(2,1)} %pad_maximum_fusion.2), channel_id=1, source_target_pairs={{0,4},{4,0},{8,12},{12,8},{16,20},{20,16},{24,28},{28,24},{1,5},{5... | collective-permute-start | bytes 1179656 | tf_op jit(solution)/shard_map/ppermute | solution.py:114
  3.4 1.2 %collective-permute-start.10 = (bf16[96,1024]{1,0:T(8,128)(2,1)S(1)}, bf16[96,1024]{1,0:T(8,128)(2,1)S(1)}, u32[]{:S(2)}, u32[]{:S(2)}) collective-permute-start(bf16[96,1024]{1,0:T(8,128)(2,1)S(1)} %bitcast.149), channel_id=1, source_target_pairs={{0,12},{4,8},{8,4},{12,0},{16,28},{20,24},{24,20},{28,16},{1,13},{... | collective-permute-start | bytes 589832 | tf_op jit(solution)/shard_map/ppermute | solution.py:118
  4.6 2.3 %collective-permute-start.13 = (bf16[96,1024]{1,0:T(8,128)(2,1)S(1)}, bf16[96,1024]{1,0:T(8,128)(2,1)S(1)}, u32[]{:S(2)}, u32[]{:S(2)}) collective-permute-start(bf16[96,1024]{1,0:T(8,128)(2,1)S(1)} %bitcast.150), channel_id=1, source_target_pairs={{0,16},{4,20},{8,24},{12,28},{16,0},{20,4},{24,8},{28,12},{1,17},{... | collective-permute-start | bytes 589832 | tf_op jit(solution)/shard_map/ppermute | solution.py:118
  6.9 1.0 collective-permute-start.16
  8.2 0.6 add_select_fusion.pick_ref
  8.8 1.9 %convolution_convert_fusion.1 = bf16[384,3,256]{2,0,1:T(8,128)(2,1)S(1)} fusion(bf16[1024,3,256]{2,0,1:T(8,128)(2,1)S(1)} %copy-done, bf16[384,1024]{1,0:T(8,128)(2,1)} %param.7), kind=kOutput, calls=%fused_computation.1 | convolution fusion | flops 604274688 | bytes 2949120 | tf_op jit(solution)/shard_map/nd,dtf->ntf/dot_general | solution.py:272
  10.8 1.3 %constant_dynamic-slice_fusion.3 = (bf16[256,256]{1,0:T(8,128)(2,1)S(1)}, bf16[256,256]{1,0:T(8,128)(2,1)S(1)}, bf16[256,256]{1,0:T(8,128)(2,1)S(1)}, bf16[256,256]{1,0:T(8,128)(2,1)S(1)}) fusion(bf16[256,1024]{1,0:T(8,128)(2,1)} %param.9, s32[]{:T(128)S(6)} %select_n.68, s32[]{:T(128)S(6)} %select_n.67, s32[]{:T(128)S(6)} %select_n.66, s32[]{:T(128)S(6)} %select_n.58), kind=kLoop, calls=%fused_computation.63 | loop fusion | bytes 1048592 | tf_op jit(solution)/shard_map/dynamic_slice | solution.py:266
  12.1 0.7 fusion.41
  12.7 0.7 slice.129
  16.0 0.8 copy.38
  16.8 0.8 copy.39
  18.8 1.0 reshape_reshape.6.own_ref
  19.8 0.6 pad_convert_fusion.live_ref
  20.4 1.3 %collective-permute-start.19 = (bf16[96,1024]{1,0:T(8,128)(2,1)S(1)}, bf16[96,1024]{1,0:T(8,128)(2,1)S(1)}, u32[]{:S(2)}, u32[]{:S(2)}) collective-permute-start(bf16[96,1024]{1,0:T(8,128)(2,1)S(1)} %bitcast.152), channel_id=1, source_target_pairs={{0,24},{4,28},{8,16},{12,20},{16,8},{20,12},{24,0},{28,4},{1,25},{... | collective-permute-start | bytes 589832 | tf_op jit(solution)/shard_map/ppermute | solution.py:118
  21.7 1.0 fusion.38
  22.7 1.0 collective-permute-done.10
  23.7 2.4 %collective-permute-start.22 = (bf16[96,1024]{1,0:T(8,128)(2,1)S(1)}, bf16[96,1024]{1,0:T(8,128)(2,1)S(1)}, u32[]{:S(2)}, u32[]{:S(2)}) collective-permute-start(bf16[96,1024]{1,0:T(8,128)(2,1)S(1)} %bitcast.153), channel_id=1, source_target_pairs={{0,28},{4,24},{8,20},{12,16},{16,12},{20,8},{24,4},{28,0},{1,29},{... | collective-permute-start | bytes 589832 | tf_op jit(solution)/shard_map/ppermute | solution.py:118
  26.1 1.2 %collective-permute-start.11 = (bf16[1,96,1024]{2,1,0:T(8,128)(2,1)S(1)}, bf16[1,96,1024]{2,1,0:T(8,128)(2,1)S(1)}, u32[]{:S(2)}, u32[]{:S(2)}) collective-permute-start(bf16[1,96,1024]{2,1,0:T(8,128)(2,1)S(1)} %bitcast.139), channel_id=1, source_target_pairs={{0,2},{1,3},{2,0},{3,1},{4,6},{5,7},{6,4},{7,5},{8,10},{9,11},{10,... | collective-permute-start | bytes 589832 | tf_op jit(solution)/shard_map/ppermute | solution.py:27
  27.5 1.0 fusion.36
  28.6 6.0 %collective-permute-start.2 = (bf16[96,1024]{1,0:T(8,128)(2,1)S(1)}, bf16[96,1024]{1,0:T(8,128)(2,1)S(1)}, u32[]{:S(2)}, u32[]{:S(2)}) collective-permute-start(bf16[96,1024]{1,0:T(8,128)(2,1)S(1)} %bitcast.154), channel_id=1, source_target_pairs={{4,8},{12,16},{20,24},{8,4},{16,12},{24,20},{5,9},{13,17},{21,25},... | collective-permute-start | bytes 589832 | tf_op jit(solution)/shard_map/ppermute | solution.py:109
  34.6 1.3 %collective-permute-start.17 = (bf16[1,96,1024]{2,1,0:T(8,128)(2,1)S(1)}, bf16[1,96,1024]{2,1,0:T(8,128)(2,1)S(1)}, u32[]{:S(2)}, u32[]{:S(2)}) collective-permute-start(bf16[1,96,1024]{2,1,0:T(8,128)(2,1)S(1)} %bitcast.133), channel_id=1, source_target_pairs={{0,2},{1,3},{2,0},{3,1},{4,6},{5,7},{6,4},{7,5},{8,10},{9,11},{10,... | collective-permute-start | bytes 589832 | tf_op jit(solution)/shard_map/ppermute | solution.py:27
  36.0 4.8 %collective-permute-done.19 = bf16[96,1024]{1,0:T(8,128)(2,1)S(1)} collective-permute-done((bf16[96,1024]{1,0:T(8,128)(2,1)S(1)}, bf16[96,1024]{1,0:T(8,128)(2,1)S(1)}, u32[]{:S(2)}, u32[]{:S(2)}) %collective-permute-start.19) | collective-permute-done | bytes 196640 | tf_op jit(solution)/shard_map/ppermute | solution.py:118
  40.8 4.8 %collective-permute-start.5 = (bf16[256,256]{0,1:T(8,128)(2,1)S(1)}, bf16[256,256]{0,1:T(8,128)(2,1)S(1)}, u32[]{:S(2)}, u32[]{:S(2)}) collective-permute-start(bf16[256,256]{0,1:T(8,128)(2,1)S(1)} %copy-done.4), channel_id=1, source_target_pairs={{0,1},{1,0},{2,3},{3,2},{4,5},{5,4},{6,7},{7,6},{8,9},{9,8},{10,11... | collective-permute-start | bytes 393224 | tf_op jit(solution)/shard_map/ppermute | solution.py:27
  45.5 0.6 collective-permute-start.20
  46.1 0.9 collective-permute-start.23
  47.1 3.4 %collective-permute-start.1 = (bf16[2,96,1024]{2,1,0:T(8,128)(2,1)}, bf16[2,96,1024]{2,1,0:T(8,128)(2,1)S(1)}, u32[]{:S(2)}, u32[]{:S(2)}) collective-permute-start(bf16[2,96,1024]{2,1,0:T(8,128)(2,1)} %collective-permute-done), channel_id=1, source_target_pairs={{0,1},{1,0},{2,3},{3,2},{4,5},{5,4},{6,7},{7,6},{8,9},{9,8},{10,11... | collective-permute-start | bytes 1179656 | tf_op jit(solution)/shard_map/ppermute | solution.py:27
  50.5 2.0 %collective-permute-start.6 = (bf16[256,256]{0,1:T(8,128)(2,1)S(1)}, bf16[256,256]{0,1:T(8,128)(2,1)S(1)}, u32[]{:S(2)}, u32[]{:S(2)}) collective-permute-start(bf16[256,256]{0,1:T(8,128)(2,1)S(1)} %copy-done.3), channel_id=1, source_target_pairs={{0,2},{1,3},{2,0},{3,1},{4,6},{5,7},{6,4},{7,5},{8,10},{9,11},{10,... | collective-permute-start | bytes 393224 | tf_op jit(solution)/shard_map/ppermute | solution.py:27
  53.0 3.7 %collective-permute-done.23 = bf16[1,96,1024]{2,1,0:T(8,128)(2,1)S(1)} collective-permute-done((bf16[1,96,1024]{2,1,0:T(8,128)(2,1)S(1)}, bf16[1,96,1024]{2,1,0:T(8,128)(2,1)S(1)}, u32[]{:S(2)}, u32[]{:S(2)}) %collective-permute-start.23) | collective-permute-done | bytes 196640 | tf_op jit(solution)/shard_map/ppermute | solution.py:27
  56.7 2.2 %collective-permute-start.9 = (bf16[2,96,1024]{2,1,0:T(8,128)(2,1)}, bf16[2,96,1024]{2,1,0:T(8,128)(2,1)S(1)}, u32[]{:S(2)}, u32[]{:S(2)}) collective-permute-start(bf16[2,96,1024]{2,1,0:T(8,128)(2,1)} %collective-permute-done.8), channel_id=1, source_target_pairs={{0,1},{1,0},{2,3},{3,2},{4,5},{5,4},{6,7},{7,6},{8,9},{9,8},{10,11... | collective-permute-start | bytes 1179656 | tf_op jit(solution)/shard_map/ppermute | solution.py:27
  58.9 4.8 %collective-permute-done.3 = bf16[1,96,1024]{2,1,0:T(8,128)(2,1)S(1)} collective-permute-done((bf16[1,96,1024]{2,1,0:T(8,128)(2,1)S(1)}, bf16[1,96,1024]{2,1,0:T(8,128)(2,1)S(1)}, u32[]{:S(2)}, u32[]{:S(2)}) %collective-permute-start.3) | collective-permute-done | bytes 196640 | tf_op jit(solution)/shard_map/ppermute | solution.py:27
  63.7 2.4 %collective-permute-start.7 = (bf16[256,256]{0,1:T(8,128)(2,1)S(1)}, bf16[256,256]{0,1:T(8,128)(2,1)S(1)}, u32[]{:S(2)}, u32[]{:S(2)}) collective-permute-start(bf16[256,256]{0,1:T(8,128)(2,1)S(1)} %copy.40), channel_id=1, source_target_pairs={{0,3},{1,2},{2,1},{3,0},{4,7},{5,6},{6,5},{7,4},{8,11},{9,10},{10,... | collective-permute-start | bytes 393224 | tf_op jit(solution)/shard_map/ppermute | solution.py:27
  66.3 0.6 collective-permute-start.15
  66.9 1.1 %collective-permute-done.12 = bf16[2,96,1024]{2,1,0:T(8,128)(2,1)S(1)} collective-permute-done((bf16[2,96,1024]{2,1,0:T(8,128)(2,1)S(1)}, bf16[2,96,1024]{2,1,0:T(8,128)(2,1)S(1)}, u32[]{:S(2)}, u32[]{:S(2)}) %collective-permute-start.12) | collective-permute-done | bytes 393248 | tf_op jit(solution)/shard_map/ppermute | solution.py:27
  68.7 1.0 collective-permute-done.18
  70.4 1.0 collective-permute-done.24
  73.5 0.9 copy.31
  74.4 4.3 %convolution_convert_fusion = bf16[2304,512]{1,0:T(8,128)(2,1)} fusion(bf16[2304,1024]{1,0:T(8,128)(2,1)S(1)} %bitcast.109, bf16[1024,512]{0,1:T(8,128)(2,1)S(1)} %bitcast.132), kind=kOutput, calls=%fused_computation | convolution fusion | flops 2417098752 | bytes 8126464 | tf_op jit(solution)/shard_map/dot_general | solution.py:171
  78.7 10.9 %shard_map.73 = bf16[3,128,256]{2,1,0:T(8,128)(2,1)} custom-call(s32[3,11]{1,0:T(4,128)} %pad_convert_fusion.live_ref, s32[4,3]{1,0:T(4,128)} %add_select_fusion.pick_ref, bf16[3,128,256]{2,1,0:T(8,128)(2,1)} %bitcast.157, bf16[3,128,512]{2,1,0:T(8,128)(2,1)} %reshape_reshape.6.own_ref, bf16[6,3,128,512]{3,2,1,0:T(8,128)(2,1)} %bitcast.168), custom_call_target="tpu_custom_call" | custom-call | flops 1107296256 | bytes 3145728 | tf_op jit(solution)/shard_map/pallas_call | solution.py:238
  89.9 6.3 %collective-permute-done.25 = bf16[1,384,256]{2,1,0:T(8,128)(2,1)S(1)} collective-permute-done((bf16[1,384,256]{2,1,0:T(8,128)(2,1)}, bf16[1,384,256]{2,1,0:T(8,128)(2,1)S(1)}, u32[]{:S(2)}, u32[]{:S(2)}) %collective-permute-start.25) | collective-permute-done | bytes 196640 | tf_op jit(solution)/shard_map/ppermute | solution.py:27
  96.2 1.0 pad_maximum_fusion.9
  97.2 1.0 collective-permute-start.26
  98.2 0.9 constant_dynamic-slice_fusion.9
  100.9 1.5 %collective-permute-start.29 = (f32[384,2]{0,1:T(2,128)S(1)}, f32[384,2]{0,1:T(2,128)S(1)}, u32[]{:S(2)}, u32[]{:S(2)}) collective-permute-start(f32[384,2]{0,1:T(2,128)S(1)} %get-tuple-element.50), channel_id=1, source_target_pairs={{0,3},{1,2},{2,1},{3,0},{4,7},{5,6},{6,5},{7,4},{8,11},{9,10},{10,... | collective-permute-start | bytes 9224 | tf_op jit(solution)/shard_map/ppermute | solution.py:27
  102.5 0.7 collective-permute-done.28
  103.1 0.9 collective-permute-done.29
  104.3 0.8 copy.33
  (114 shorter events, 8.4 us)
Async XLA Ops:
  0.0 7.9 %copy-start.5 = (s32[4,3]{1,0:T(4,128)S(1)}, s32[4,3]{1,0:T(4,128)}, u32[]{:S(2)}) copy-start(s32[4,3]{1,0:T(4,128)} %param.13) | copy-start | bytes 148
  0.0 8.8 %copy-start = (bf16[1024,3,256]{2,0,1:T(8,128)(2,1)S(1)}, bf16[1024,3,256]{2,0,1:T(8,128)(2,1)}, u32[]{:S(2)}) copy-start(bf16[1024,3,256]{2,0,1:T(8,128)(2,1)} %param.8) | copy-start | bytes 4718596
  2.0 18.4 %collective-permute-start = (bf16[2,96,1024]{2,1,0:T(8,128)(2,1)}, bf16[2,96,1024]{2,1,0:T(8,128)(2,1)}, u32[]{:S(2)}, u32[]{:S(2)}) collective-permute-start(bf16[2,96,1024]{2,1,0:T(8,128)(2,1)} %pad_maximum_fusion.2), channel_id=1, source_target_pairs={{0,4},{4,0},{8,12},{12,8},{16,20},{20,16},{24,28},{28,24},{1,5},{5... | collective-permute-start | bytes 1179656 | tf_op jit(solution)/shard_map/ppermute | solution.py:114
  3.2 24.1 %collective-permute-start.8 = (bf16[2,96,1024]{2,1,0:T(8,128)(2,1)}, bf16[2,96,1024]{2,1,0:T(8,128)(2,1)}, u32[]{:S(2)}, u32[]{:S(2)}) collective-permute-start(bf16[2,96,1024]{2,1,0:T(8,128)(2,1)} %pad_maximum_fusion.2), channel_id=1, source_target_pairs={{0,8},{4,12},{8,0},{12,4},{16,24},{20,28},{24,16},{28,20},{1,9},{5... | collective-permute-start | bytes 1179656 | tf_op jit(solution)/shard_map/ppermute | solution.py:114
  3.4 20.3 %collective-permute-start.10 = (bf16[96,1024]{1,0:T(8,128)(2,1)S(1)}, bf16[96,1024]{1,0:T(8,128)(2,1)S(1)}, u32[]{:S(2)}, u32[]{:S(2)}) collective-permute-start(bf16[96,1024]{1,0:T(8,128)(2,1)S(1)} %bitcast.149), channel_id=1, source_target_pairs={{0,12},{4,8},{8,4},{12,0},{16,28},{20,24},{24,20},{28,16},{1,13},{... | collective-permute-start | bytes 589832 | tf_op jit(solution)/shard_map/ppermute | solution.py:118
  4.6 21.4 %collective-permute-start.13 = (bf16[96,1024]{1,0:T(8,128)(2,1)S(1)}, bf16[96,1024]{1,0:T(8,128)(2,1)S(1)}, u32[]{:S(2)}, u32[]{:S(2)}) collective-permute-start(bf16[96,1024]{1,0:T(8,128)(2,1)S(1)} %bitcast.150), channel_id=1, source_target_pairs={{0,16},{4,20},{8,24},{12,28},{16,0},{20,4},{24,8},{28,12},{1,17},{... | collective-permute-start | bytes 589832 | tf_op jit(solution)/shard_map/ppermute | solution.py:118
  6.9 21.7 %collective-permute-start.16 = (bf16[96,1024]{1,0:T(8,128)(2,1)S(1)}, bf16[96,1024]{1,0:T(8,128)(2,1)S(1)}, u32[]{:S(2)}, u32[]{:S(2)}) collective-permute-start(bf16[96,1024]{1,0:T(8,128)(2,1)S(1)} %bitcast.151), channel_id=1, source_target_pairs={{0,20},{4,16},{8,28},{12,24},{16,4},{20,0},{24,12},{28,8},{1,21},{... | collective-permute-start | bytes 589832 | tf_op jit(solution)/shard_map/ppermute | solution.py:118
  8.8 1.9 %copy-start.6 = (s32[3,7]{1,0:T(4,128)S(1)}, s32[3,7]{1,0:T(4,128)}, u32[]{:S(2)}) copy-start(s32[3,7]{1,0:T(4,128)} %param.12) | copy-start | bytes 256
  10.7 2.0 %copy-start.1 = (bf16[384,3,256]{2,0,1:T(8,128)(2,1)}, bf16[384,3,256]{2,0,1:T(8,128)(2,1)S(1)}, u32[]{:S(2)}) copy-start(bf16[384,3,256]{2,0,1:T(8,128)(2,1)S(1)} %convolution_convert_fusion.1) | copy-start | bytes 1769476
  12.7 5.0 %slice-start = ((bf16[1024,3,256]{2,0,1:T(8,128)(2,1)}), bf16[1024,2,256]{2,0,1:T(8,128)(2,1)S(1)}, s32[]{:S(2)}) async-start(bf16[1024,3,256]{2,0,1:T(8,128)(2,1)} %param.8), calls=%async_computation | async-start | bytes 2097152 | tf_op jit(solution)/shard_map/slice | solution.py:281
  16.0 2.3 %slice-start.1 = ((bf16[384,3,256]{2,0,1:T(8,128)(2,1)}), bf16[384,2,256]{2,0,1:T(8,128)(2,1)S(1)}, s32[]{:S(2)}) async-start(bf16[384,3,256]{2,0,1:T(8,128)(2,1)} %copy-done.1), calls=%async_computation.1 | async-start | bytes 786432 | tf_op jit(solution)/shard_map/slice | solution.py:276
  18.8 22.0 %copy-start.4 = (bf16[256,256]{0,1:T(8,128)(2,1)S(1)}, bf16[256,256]{0,1:T(8,128)(2,1)}, u32[]{:S(2)}) copy-start(bf16[256,256]{0,1:T(8,128)(2,1)} %copy.38) | copy-start | bytes 393220
  20.4 20.4 %collective-permute-start.19 = (bf16[96,1024]{1,0:T(8,128)(2,1)S(1)}, bf16[96,1024]{1,0:T(8,128)(2,1)S(1)}, u32[]{:S(2)}, u32[]{:S(2)}) collective-permute-start(bf16[96,1024]{1,0:T(8,128)(2,1)S(1)} %bitcast.152), channel_id=1, source_target_pairs={{0,24},{4,28},{8,16},{12,20},{16,8},{20,12},{24,0},{28,4},{1,25},{... | collective-permute-start | bytes 589832 | tf_op jit(solution)/shard_map/ppermute | solution.py:118
  23.7 21.8 %collective-permute-start.22 = (bf16[96,1024]{1,0:T(8,128)(2,1)S(1)}, bf16[96,1024]{1,0:T(8,128)(2,1)S(1)}, u32[]{:S(2)}, u32[]{:S(2)}) collective-permute-start(bf16[96,1024]{1,0:T(8,128)(2,1)S(1)} %bitcast.153), channel_id=1, source_target_pairs={{0,28},{4,24},{8,20},{12,16},{16,12},{20,8},{24,4},{28,0},{1,29},{... | collective-permute-start | bytes 589832 | tf_op jit(solution)/shard_map/ppermute | solution.py:118
  26.1 8.6 %collective-permute-start.11 = (bf16[1,96,1024]{2,1,0:T(8,128)(2,1)S(1)}, bf16[1,96,1024]{2,1,0:T(8,128)(2,1)S(1)}, u32[]{:S(2)}, u32[]{:S(2)}) collective-permute-start(bf16[1,96,1024]{2,1,0:T(8,128)(2,1)S(1)} %bitcast.139), channel_id=1, source_target_pairs={{0,2},{1,3},{2,0},{3,1},{4,6},{5,7},{6,4},{7,5},{8,10},{9,11},{10,... | collective-permute-start | bytes 589832 | tf_op jit(solution)/shard_map/ppermute | solution.py:27
  27.3 23.2 %copy-start.3 = (bf16[256,256]{0,1:T(8,128)(2,1)S(1)}, bf16[256,256]{0,1:T(8,128)(2,1)}, u32[]{:S(2)}) copy-start(bf16[256,256]{0,1:T(8,128)(2,1)} %copy.39) | copy-start | bytes 393220
  27.3 18.8 %collective-permute-start.14 = (bf16[1,96,1024]{2,1,0:T(8,128)(2,1)S(1)}, bf16[1,96,1024]{2,1,0:T(8,128)(2,1)S(1)}, u32[]{:S(2)}, u32[]{:S(2)}) collective-permute-start(bf16[1,96,1024]{2,1,0:T(8,128)(2,1)S(1)} %bitcast.136), channel_id=1, source_target_pairs={{0,2},{1,3},{2,0},{3,1},{4,6},{5,7},{6,4},{7,5},{8,10},{9,11},{10,... | collective-permute-start | bytes 589832 | tf_op jit(solution)/shard_map/ppermute | solution.py:27
  28.6 21.9 %collective-permute-start.2 = (bf16[96,1024]{1,0:T(8,128)(2,1)S(1)}, bf16[96,1024]{1,0:T(8,128)(2,1)S(1)}, u32[]{:S(2)}, u32[]{:S(2)}) collective-permute-start(bf16[96,1024]{1,0:T(8,128)(2,1)S(1)} %bitcast.154), channel_id=1, source_target_pairs={{4,8},{12,16},{20,24},{8,4},{16,12},{24,20},{5,9},{13,17},{21,25},... | collective-permute-start | bytes 589832 | tf_op jit(solution)/shard_map/ppermute | solution.py:109
  34.6 12.4 %collective-permute-start.17 = (bf16[1,96,1024]{2,1,0:T(8,128)(2,1)S(1)}, bf16[1,96,1024]{2,1,0:T(8,128)(2,1)S(1)}, u32[]{:S(2)}, u32[]{:S(2)}) collective-permute-start(bf16[1,96,1024]{2,1,0:T(8,128)(2,1)S(1)} %bitcast.133), channel_id=1, source_target_pairs={{0,2},{1,3},{2,0},{3,1},{4,6},{5,7},{6,4},{7,5},{8,10},{9,11},{10,... | collective-permute-start | bytes 589832 | tf_op jit(solution)/shard_map/ppermute | solution.py:27
  40.8 31.4 %collective-permute-start.5 = (bf16[256,256]{0,1:T(8,128)(2,1)S(1)}, bf16[256,256]{0,1:T(8,128)(2,1)S(1)}, u32[]{:S(2)}, u32[]{:S(2)}) collective-permute-start(bf16[256,256]{0,1:T(8,128)(2,1)S(1)} %copy-done.4), channel_id=1, source_target_pairs={{0,1},{1,0},{2,3},{3,2},{4,5},{5,4},{6,7},{7,6},{8,9},{9,8},{10,11... | collective-permute-start | bytes 393224 | tf_op jit(solution)/shard_map/ppermute | solution.py:27
  45.5 7.0 %collective-permute-start.20 = (bf16[1,96,1024]{2,1,0:T(8,128)(2,1)S(1)}, bf16[1,96,1024]{2,1,0:T(8,128)(2,1)S(1)}, u32[]{:S(2)}, u32[]{:S(2)}) collective-permute-start(bf16[1,96,1024]{2,1,0:T(8,128)(2,1)S(1)} %bitcast.142), channel_id=1, source_target_pairs={{0,2},{1,3},{2,0},{3,1},{4,6},{5,7},{6,4},{7,5},{8,10},{9,11},{10,... | collective-permute-start | bytes 589832 | tf_op jit(solution)/shard_map/ppermute | solution.py:27
  46.1 10.6 %collective-permute-start.23 = (bf16[1,96,1024]{2,1,0:T(8,128)(2,1)S(1)}, bf16[1,96,1024]{2,1,0:T(8,128)(2,1)S(1)}, u32[]{:S(2)}, u32[]{:S(2)}) collective-permute-start(bf16[1,96,1024]{2,1,0:T(8,128)(2,1)S(1)} %bitcast.145), channel_id=1, source_target_pairs={{0,2},{1,3},{2,0},{3,1},{4,6},{5,7},{6,4},{7,5},{8,10},{9,11},{10,... | collective-permute-start | bytes 589832 | tf_op jit(solution)/shard_map/ppermute | solution.py:27
  47.1 19.1 %collective-permute-start.1 = (bf16[2,96,1024]{2,1,0:T(8,128)(2,1)}, bf16[2,96,1024]{2,1,0:T(8,128)(2,1)S(1)}, u32[]{:S(2)}, u32[]{:S(2)}) collective-permute-start(bf16[2,96,1024]{2,1,0:T(8,128)(2,1)} %collective-permute-done), channel_id=1, source_target_pairs={{0,1},{1,0},{2,3},{3,2},{4,5},{5,4},{6,7},{7,6},{8,9},{9,8},{10,11... | collective-permute-start | bytes 1179656 | tf_op jit(solution)/shard_map/ppermute | solution.py:27
  50.5 21.7 %collective-permute-start.6 = (bf16[256,256]{0,1:T(8,128)(2,1)S(1)}, bf16[256,256]{0,1:T(8,128)(2,1)S(1)}, u32[]{:S(2)}, u32[]{:S(2)}) collective-permute-start(bf16[256,256]{0,1:T(8,128)(2,1)S(1)} %copy-done.3), channel_id=1, source_target_pairs={{0,2},{1,3},{2,0},{3,1},{4,6},{5,7},{6,4},{7,5},{8,10},{9,11},{10,... | collective-permute-start | bytes 393224 | tf_op jit(solution)/shard_map/ppermute | solution.py:27
  52.5 11.2 %collective-permute-start.3 = (bf16[1,96,1024]{2,1,0:T(8,128)(2,1)S(1)}, bf16[1,96,1024]{2,1,0:T(8,128)(2,1)S(1)}, u32[]{:S(2)}, u32[]{:S(2)}) collective-permute-start(bf16[1,96,1024]{2,1,0:T(8,128)(2,1)S(1)} %bitcast.122), channel_id=1, source_target_pairs={{0,2},{1,3},{2,0},{3,1},{4,6},{5,7},{6,4},{7,5},{8,10},{9,11},{10,... | collective-permute-start | bytes 589832 | tf_op jit(solution)/shard_map/ppermute | solution.py:27
  56.7 9.6 %collective-permute-start.9 = (bf16[2,96,1024]{2,1,0:T(8,128)(2,1)}, bf16[2,96,1024]{2,1,0:T(8,128)(2,1)S(1)}, u32[]{:S(2)}, u32[]{:S(2)}) collective-permute-start(bf16[2,96,1024]{2,1,0:T(8,128)(2,1)} %collective-permute-done.8), channel_id=1, source_target_pairs={{0,1},{1,0},{2,3},{3,2},{4,5},{5,4},{6,7},{7,6},{8,9},{9,8},{10,11... | collective-permute-start | bytes 1179656 | tf_op jit(solution)/shard_map/ppermute | solution.py:27
  63.7 8.5 %collective-permute-start.7 = (bf16[256,256]{0,1:T(8,128)(2,1)S(1)}, bf16[256,256]{0,1:T(8,128)(2,1)S(1)}, u32[]{:S(2)}, u32[]{:S(2)}) collective-permute-start(bf16[256,256]{0,1:T(8,128)(2,1)S(1)} %copy.40), channel_id=1, source_target_pairs={{0,3},{1,2},{2,1},{3,0},{4,7},{5,6},{6,5},{7,4},{8,11},{9,10},{10,... | collective-permute-start | bytes 393224 | tf_op jit(solution)/shard_map/ppermute | solution.py:27
  66.2 1.8 %collective-permute-start.12 = (bf16[2,96,1024]{2,1,0:T(8,128)(2,1)S(1)}, bf16[2,96,1024]{2,1,0:T(8,128)(2,1)S(1)}, u32[]{:S(2)}, u32[]{:S(2)}) collective-permute-start(bf16[2,96,1024]{2,1,0:T(8,128)(2,1)S(1)} %pad_maximum_fusion.4), channel_id=1, source_target_pairs={{0,1},{1,0},{2,3},{3,2},{4,5},{5,4},{6,7},{7,6},{8,9},{9,8},{10,11... | collective-permute-start | bytes 1179656 | tf_op jit(solution)/shard_map/ppermute | solution.py:27
  66.3 2.2 %collective-permute-start.15 = (bf16[2,96,1024]{2,1,0:T(8,128)(2,1)S(1)}, bf16[2,96,1024]{2,1,0:T(8,128)(2,1)S(1)}, u32[]{:S(2)}, u32[]{:S(2)}) collective-permute-start(bf16[2,96,1024]{2,1,0:T(8,128)(2,1)S(1)} %pad_maximum_fusion.5), channel_id=1, source_target_pairs={{0,1},{1,0},{2,3},{3,2},{4,5},{5,4},{6,7},{7,6},{8,9},{9,8},{10,11... | collective-permute-start | bytes 1179656 | tf_op jit(solution)/shard_map/ppermute | solution.py:27
  68.0 1.7 %collective-permute-start.18 = (bf16[2,96,1024]{2,1,0:T(8,128)(2,1)S(1)}, bf16[2,96,1024]{2,1,0:T(8,128)(2,1)S(1)}, u32[]{:S(2)}, u32[]{:S(2)}) collective-permute-start(bf16[2,96,1024]{2,1,0:T(8,128)(2,1)S(1)} %pad_maximum_fusion.6), channel_id=1, source_target_pairs={{0,1},{1,0},{2,3},{3,2},{4,5},{5,4},{6,7},{7,6},{8,9},{9,8},{10,11... | collective-permute-start | bytes 1179656 | tf_op jit(solution)/shard_map/ppermute | solution.py:27
  68.5 1.7 %collective-permute-start.21 = (bf16[2,96,1024]{2,1,0:T(8,128)(2,1)S(1)}, bf16[2,96,1024]{2,1,0:T(8,128)(2,1)S(1)}, u32[]{:S(2)}, u32[]{:S(2)}) collective-permute-start(bf16[2,96,1024]{2,1,0:T(8,128)(2,1)S(1)} %pad_maximum_fusion.7), channel_id=1, source_target_pairs={{0,1},{1,0},{2,3},{3,2},{4,5},{5,4},{6,7},{7,6},{8,9},{9,8},{10,11... | collective-permute-start | bytes 1179656 | tf_op jit(solution)/shard_map/ppermute | solution.py:27
  69.7 1.7 %collective-permute-start.24 = (bf16[2,96,1024]{2,1,0:T(8,128)(2,1)S(1)}, bf16[2,96,1024]{2,1,0:T(8,128)(2,1)S(1)}, u32[]{:S(2)}, u32[]{:S(2)}) collective-permute-start(bf16[2,96,1024]{2,1,0:T(8,128)(2,1)S(1)} %pad_maximum_fusion.8), channel_id=1, source_target_pairs={{0,1},{1,0},{2,3},{3,2},{4,5},{5,4},{6,7},{7,6},{8,9},{9,8},{10,11... | collective-permute-start | bytes 1179656 | tf_op jit(solution)/shard_map/ppermute | solution.py:27
  70.2 2.0 %collective-permute-start.4 = (bf16[2,96,1024]{2,1,0:T(8,128)(2,1)S(1)}, bf16[2,96,1024]{2,1,0:T(8,128)(2,1)S(1)}, u32[]{:S(2)}, u32[]{:S(2)}) collective-permute-start(bf16[2,96,1024]{2,1,0:T(8,128)(2,1)S(1)} %pad_maximum_fusion.3), channel_id=1, source_target_pairs={{0,1},{1,0},{2,3},{3,2},{4,5},{5,4},{6,7},{7,6},{8,9},{9,8},{10,11... | collective-permute-start | bytes 1179656 | tf_op jit(solution)/shard_map/ppermute | solution.py:27
  72.2 0.6 copy-start.9
  72.2 0.7 copy-start.11
  89.6 10.0 %copy-start.2 = (bf16[3,128,256]{2,1,0:T(8,128)(2,1)S(1)}, bf16[3,128,256]{2,1,0:T(8,128)(2,1)}, u32[]{:S(2)}) copy-start(bf16[3,128,256]{2,1,0:T(8,128)(2,1)} %shard_map.73) | copy-start | bytes 589828
  89.6 10.0 %copy-start.10 = (bf16[256,256]{0,1:T(8,128)(2,1)S(1)}, bf16[256,256]{0,1:T(8,128)(2,1)}, u32[]{:S(2)}) copy-start(bf16[256,256]{0,1:T(8,128)(2,1)} %copy-done.9) | copy-start | bytes 393220
  89.6 10.0 %copy-start.12 = (bf16[256,256]{0,1:T(8,128)(2,1)S(1)}, bf16[256,256]{0,1:T(8,128)(2,1)}, u32[]{:S(2)}) copy-start(bf16[256,256]{0,1:T(8,128)(2,1)} %copy-done.11) | copy-start | bytes 393220
  89.6 6.6 %collective-permute-start.25 = (bf16[1,384,256]{2,1,0:T(8,128)(2,1)}, bf16[1,384,256]{2,1,0:T(8,128)(2,1)S(1)}, u32[]{:S(2)}, u32[]{:S(2)}) collective-permute-start(bf16[1,384,256]{2,1,0:T(8,128)(2,1)} %bitcast.158), channel_id=1, source_target_pairs={{0,2},{1,3},{2,0},{3,1},{4,6},{5,7},{6,4},{7,5},{8,10},{9,11},{10,... | collective-permute-start | bytes 589832 | tf_op jit(solution)/shard_map/ppermute | solution.py:27
  97.2 2.4 %collective-permute-start.26 = (bf16[2,384,256]{2,1,0:T(8,128)(2,1)S(1)}, bf16[2,384,256]{2,1,0:T(8,128)(2,1)S(1)}, u32[]{:S(2)}, u32[]{:S(2)}) collective-permute-start(bf16[2,384,256]{2,1,0:T(8,128)(2,1)S(1)} %pad_maximum_fusion.9), channel_id=1, source_target_pairs={{0,1},{1,0},{2,3},{3,2},{4,5},{5,4},{6,7},{7,6},{8,9},{9,8},{10,11... | collective-permute-start | bytes 1179656 | tf_op jit(solution)/shard_map/ppermute | solution.py:27
  99.6 4.5 %copy-start.7 = (f32[256]{0:T(256)S(1)}, f32[256]{0:T(256)}, u32[]{:S(2)}) copy-start(f32[256]{0:T(256)} %param.11) | copy-start | bytes 3076
  99.6 4.5 %copy-start.8 = (f32[256]{0:T(256)S(1)}, f32[256]{0:T(256)}, u32[]{:S(2)}) copy-start(f32[256]{0:T(256)} %param.10) | copy-start | bytes 3076
  100.2 2.2 %collective-permute-start.27 = (f32[384,2]{0,1:T(2,128)S(1)}, f32[384,2]{0,1:T(2,128)S(1)}, u32[]{:S(2)}, u32[]{:S(2)}) collective-permute-start(f32[384,2]{0,1:T(2,128)S(1)} %get-tuple-element.50), channel_id=1, source_target_pairs={{0,1},{1,0},{2,3},{3,2},{4,5},{5,4},{6,7},{7,6},{8,9},{9,8},{10,11... | collective-permute-start | bytes 9224 | tf_op jit(solution)/shard_map/ppermute | solution.py:27
  100.7 2.4 %collective-permute-start.28 = (f32[384,2]{0,1:T(2,128)S(1)}, f32[384,2]{0,1:T(2,128)S(1)}, u32[]{:S(2)}, u32[]{:S(2)}) collective-permute-start(f32[384,2]{0,1:T(2,128)S(1)} %get-tuple-element.50), channel_id=1, source_target_pairs={{0,2},{1,3},{2,0},{3,1},{4,6},{5,7},{6,4},{7,5},{8,10},{9,11},{10,... | collective-permute-start | bytes 9224 | tf_op jit(solution)/shard_map/ppermute | solution.py:27
  100.9 3.1 %collective-permute-start.29 = (f32[384,2]{0,1:T(2,128)S(1)}, f32[384,2]{0,1:T(2,128)S(1)}, u32[]{:S(2)}, u32[]{:S(2)}) collective-permute-start(f32[384,2]{0,1:T(2,128)S(1)} %get-tuple-element.50), channel_id=1, source_target_pairs={{0,3},{1,2},{2,1},{3,0},{4,7},{5,6},{6,5},{7,4},{8,11},{9,10},{10,... | collective-permute-start | bytes 9224 | tf_op jit(solution)/shard_map/ppermute | solution.py:27

commit v12 on v8

--- a/solution.py
+++ b/solution.py
@@ -13,7 +13,7 @@
 LANES = 128
 GATHER_GROUPS = 16
 STATIC_GROUPS = 8
-NEAR_SHIFTS = 4
+NEAR_SHIFTS = 2
 
 
 NORM_EPS = 1e-05

time: 107 us -> 111 us (1.037)
  the two profiles are of different devices: /device:TPU:13 before, /device:TPU:9 now
where the time goes in v12:
time: 111 us; the launch traced here: 110 us
  starting transfers between devices  35.3 us (32%)
  waiting for transfers between devices  35.2 us (32%)
  local copies, waits for them, and re-layouts  13.7 us (12%)
  Pallas kernels  10.9 us (10%)
  matrix products  6.5 us (6%)
  other arithmetic  4.79 us (4%)
  between operations  3.17 us (3%)
    ppermute x22, starting transfers between devices, flip_heads(): return lax.ppermute(array, 'head', [(i, i ^ flip) for i in range(devices)])  25.4 us
    ppermute x22, waiting for transfers between devices, flip_heads(): return lax.ppermute(array, 'head', [(i, i ^ flip) for i in range(devices)])  14.9 us
    ppermute x6, waiting for transfers between devices, static_keys(): lax.ppermute(mine, 'node', [(i, i ^ shift) for i in range(groups)])  13.3 us
    pallas_call x1, Pallas kernels, attention(): pl.pallas_call(attention_kernel, out_shape=jax.ShapeDtypeStruct(query.sha...  10.9 us
    ppermute x1, waiting for transfers between devices, static_keys(): lax.ppermute(near, 'node', [(i, i ^ shift) for i in range(groups)])  7.09 us
    ppermute x6, starting transfers between devices, static_keys(): lax.ppermute(mine, 'node', [(i, i ^ shift) for i in range(groups)])  6.6 us
    dot_general x1, matrix products, kv_of_spread(): jnp.dot(rows, w_kv, preferred_element_type=jnp.float32).astype(jnp.bfloat16)  4.1 us
    ppermute x1, starting transfers between devices, static_keys(): other = pair_stack(lax.ppermute(near, 'node', far), heads_axis)  3.02 us
  transfers between devices with their start and end apart: 30, of which 14 were waited for; matrix products, arithmetic and copies ran while one was open for 14% of the time, Pallas kernels for 0%

profile of v12, /device:TPU:9, one launch (start us, length us, event | category | flops | bytes accessed | tf_op | source)
XLA Modules:
  0.0 109.5 jit_solution(8186277984913134725)
XLA Ops:
  0.0 1.2 %constant_dynamic-slice_fusion.8 = (bf16[3,1,32,1024]{3,2,1,0:T(8,128)(2,1)S(1)}, bf16[3,1,32,1024]{3,2,1,0:T(8,128)(2,1)S(1)}) fusion(bf16[3,4,32,1024]{3,2,1,0:T(8,128)(2,1)} %bitcast.157, s32[]{:T(128)S(6)} %select_n.62, s32[]{:T(128)S(6)} %select_n.63), kind=kLoop, calls=%fused_computation.68 | loop fusion | bytes 786440 | tf_op jit(solution)/shard_map/jit(dynamic_index_in_dim)/dynamic_slice | solution.py:145
  1.3 2.4 %collective-permute-start.10 = (bf16[96,1024]{1,0:T(8,128)(2,1)S(1)}, bf16[96,1024]{1,0:T(8,128)(2,1)S(1)}, u32[]{:S(2)}, u32[]{:S(2)}) collective-permute-start(bf16[96,1024]{1,0:T(8,128)(2,1)S(1)} %bitcast.150), channel_id=1, source_target_pairs={{0,12},{4,8},{8,4},{12,0},{16,28},{20,24},{24,20},{28,16},{1,13},{... | collective-permute-start | bytes 589832 | tf_op jit(solution)/shard_map/ppermute | solution.py:121
  3.7 2.3 %collective-permute-start.13 = (bf16[96,1024]{1,0:T(8,128)(2,1)S(1)}, bf16[96,1024]{1,0:T(8,128)(2,1)S(1)}, u32[]{:S(2)}, u32[]{:S(2)}) collective-permute-start(bf16[96,1024]{1,0:T(8,128)(2,1)S(1)} %bitcast.151), channel_id=1, source_target_pairs={{0,16},{4,20},{8,24},{12,28},{16,0},{20,4},{24,8},{28,12},{1,17},{... | collective-permute-start | bytes 589832 | tf_op jit(solution)/shard_map/ppermute | solution.py:121
  6.0 0.8 pad_maximum_fusion.2
  7.0 3.0 %collective-permute-start.2 = (bf16[2,96,1024]{2,1,0:T(8,128)(2,1)}, bf16[2,96,1024]{2,1,0:T(8,128)(2,1)}, u32[]{:S(2)}, u32[]{:S(2)}) collective-permute-start(bf16[2,96,1024]{2,1,0:T(8,128)(2,1)} %pad_maximum_fusion.2), channel_id=1, source_target_pairs={{4,8},{12,16},{20,24},{8,4},{16,12},{24,20},{5,9},{13,17},{21,25},... | collective-permute-start | bytes 1179656 | tf_op jit(solution)/shard_map/ppermute | solution.py:111
  10.3 0.6 add_select_fusion.pick_ref
  10.9 1.9 %convolution_convert_fusion.1 = bf16[384,3,256]{2,0,1:T(8,128)(2,1)S(1)} fusion(bf16[1024,3,256]{2,0,1:T(8,128)(2,1)S(1)} %copy-done, bf16[384,1024]{1,0:T(8,128)(2,1)} %param.7), kind=kOutput, calls=%fused_computation.1 | convolution fusion | flops 604274688 | bytes 2949120 | tf_op jit(solution)/shard_map/nd,dtf->ntf/dot_general | solution.py:275
  12.9 1.3 %constant_dynamic-slice_fusion.3 = (bf16[256,256]{1,0:T(8,128)(2,1)S(1)}, bf16[256,256]{1,0:T(8,128)(2,1)S(1)}, bf16[256,256]{1,0:T(8,128)(2,1)S(1)}, bf16[256,256]{1,0:T(8,128)(2,1)S(1)}) fusion(bf16[256,1024]{1,0:T(8,128)(2,1)} %param.9, s32[]{:T(128)S(6)} %select_n.68, s32[]{:T(128)S(6)} %select_n.67, s32[]{:T(128)S(6)} %select_n.66, s32[]{:T(128)S(6)} %select_n.58), kind=kLoop, calls=%fused_computation.63 | loop fusion | bytes 1048592 | tf_op jit(solution)/shard_map/dynamic_slice | solution.py:269
  14.2 0.7 fusion.41
  14.8 0.7 slice.129
  18.1 0.8 copy.38
  18.9 0.8 copy.39
  19.9 0.5 copy.41
  20.9 1.0 reshape_reshape.6.own_ref
  21.9 0.6 pad_convert_fusion.live_ref
  22.5 7.1 %collective-permute-done = bf16[2,96,1024]{2,1,0:T(8,128)(2,1)} collective-permute-done((bf16[2,96,1024]{2,1,0:T(8,128)(2,1)}, bf16[2,96,1024]{2,1,0:T(8,128)(2,1)}, u32[]{:S(2)}, u32[]{:S(2)}) %collective-permute-start) | collective-permute-done | bytes 393248 | tf_op jit(solution)/shard_map/ppermute | solution.py:117
  29.5 1.0 fusion.37
  30.6 0.5 collective-permute-start.19
  31.1 1.1 %collective-permute-start.8 = (bf16[1,96,1024]{2,1,0:T(8,128)(2,1)S(1)}, bf16[1,96,1024]{2,1,0:T(8,128)(2,1)S(1)}, u32[]{:S(2)}, u32[]{:S(2)}) collective-permute-start(bf16[1,96,1024]{2,1,0:T(8,128)(2,1)S(1)} %bitcast.137), channel_id=1, source_target_pairs={{0,2},{1,3},{2,0},{3,1},{4,6},{5,7},{6,4},{7,5},{8,10},{9,11},{10,... | collective-permute-start | bytes 589832 | tf_op jit(solution)/shard_map/ppermute | solution.py:27
  32.6 1.0 fusion.39
  33.7 1.3 %collective-permute-start.22 = (bf16[96,1024]{1,0:T(8,128)(2,1)S(1)}, bf16[96,1024]{1,0:T(8,128)(2,1)S(1)}, u32[]{:S(2)}, u32[]{:S(2)}) collective-permute-start(bf16[96,1024]{1,0:T(8,128)(2,1)S(1)} %bitcast.155), channel_id=1, source_target_pairs={{0,28},{4,24},{8,20},{12,16},{16,12},{20,8},{24,4},{28,0},{1,29},{... | collective-permute-start | bytes 589832 | tf_op jit(solution)/shard_map/ppermute | solution.py:121
  35.0 1.0 collective-permute-done.8
  36.0 1.1 %collective-permute-start.14 = (bf16[1,96,1024]{2,1,0:T(8,128)(2,1)S(1)}, bf16[1,96,1024]{2,1,0:T(8,128)(2,1)S(1)}, u32[]{:S(2)}, u32[]{:S(2)}) collective-permute-start(bf16[1,96,1024]{2,1,0:T(8,128)(2,1)S(1)} %bitcast.131), channel_id=1, source_target_pairs={{0,2},{1,3},{2,0},{3,1},{4,6},{5,7},{6,4},{7,5},{8,10},{9,11},{10,... | collective-permute-start | bytes 589832 | tf_op jit(solution)/shard_map/ppermute | solution.py:27
  37.1 9.6 %collective-permute-done.16 = bf16[96,1024]{1,0:T(8,128)(2,1)S(1)} collective-permute-done((bf16[96,1024]{1,0:T(8,128)(2,1)S(1)}, bf16[96,1024]{1,0:T(8,128)(2,1)S(1)}, u32[]{:S(2)}, u32[]{:S(2)}) %collective-permute-start.16) | collective-permute-done | bytes 196640 | tf_op jit(solution)/shard_map/ppermute | solution.py:121
  46.7 0.6 collective-permute-start.4
  47.3 3.6 %collective-permute-done.19 = bf16[96,1024]{1,0:T(8,128)(2,1)S(1)} collective-permute-done((bf16[96,1024]{1,0:T(8,128)(2,1)S(1)}, bf16[96,1024]{1,0:T(8,128)(2,1)S(1)}, u32[]{:S(2)}, u32[]{:S(2)}) %collective-permute-start.19) | collective-permute-done | bytes 196640 | tf_op jit(solution)/shard_map/ppermute | solution.py:121
  51.0 1.1 %collective-permute-start.17 = (bf16[1,96,1024]{2,1,0:T(8,128)(2,1)S(1)}, bf16[1,96,1024]{2,1,0:T(8,128)(2,1)S(1)}, u32[]{:S(2)}, u32[]{:S(2)}) collective-permute-start(bf16[1,96,1024]{2,1,0:T(8,128)(2,1)S(1)} %bitcast.140), channel_id=1, source_target_pairs={{0,2},{1,3},{2,0},{3,1},{4,6},{5,7},{6,4},{7,5},{8,10},{9,11},{10,... | collective-permute-start | bytes 589832 | tf_op jit(solution)/shard_map/ppermute | solution.py:27
  52.5 4.4 %collective-permute-start.1 = (bf16[2,96,1024]{2,1,0:T(8,128)(2,1)}, bf16[2,96,1024]{2,1,0:T(8,128)(2,1)S(1)}, u32[]{:S(2)}, u32[]{:S(2)}) collective-permute-start(bf16[2,96,1024]{2,1,0:T(8,128)(2,1)} %collective-permute-done), channel_id=1, source_target_pairs={{0,1},{1,0},{2,3},{3,2},{4,5},{5,4},{6,7},{7,6},{8,9},{9,8},{10,11... | collective-permute-start | bytes 1179656 | tf_op jit(solution)/shard_map/ppermute | solution.py:27
  56.9 1.3 %collective-permute-start.5 = (bf16[256,256]{0,1:T(8,128)(2,1)S(1)}, bf16[256,256]{0,1:T(8,128)(2,1)S(1)}, u32[]{:S(2)}, u32[]{:S(2)}) collective-permute-start(bf16[256,256]{0,1:T(8,128)(2,1)S(1)} %copy-done.3), channel_id=1, source_target_pairs={{0,2},{1,3},{2,0},{3,1},{4,6},{5,7},{6,4},{7,5},{8,10},{9,11},{10,... | collective-permute-start | bytes 393224 | tf_op jit(solution)/shard_map/ppermute | solution.py:27
  58.5 6.3 %collective-permute-start.9 = (bf16[2,96,1024]{2,1,0:T(8,128)(2,1)S(1)}, bf16[2,96,1024]{2,1,0:T(8,128)(2,1)S(1)}, u32[]{:S(2)}, u32[]{:S(2)}) collective-permute-start(bf16[2,96,1024]{2,1,0:T(8,128)(2,1)S(1)} %pad_maximum_fusion.3), channel_id=1, source_target_pairs={{0,1},{1,0},{2,3},{3,2},{4,5},{5,4},{6,7},{7,6},{8,9},{9,8},{10,11... | collective-permute-start | bytes 1179656 | tf_op jit(solution)/shard_map/ppermute | solution.py:27
  64.9 1.9 %collective-permute-done.23 = bf16[1,96,1024]{2,1,0:T(8,128)(2,1)S(1)} collective-permute-done((bf16[1,96,1024]{2,1,0:T(8,128)(2,1)S(1)}, bf16[1,96,1024]{2,1,0:T(8,128)(2,1)S(1)}, u32[]{:S(2)}, u32[]{:S(2)}) %collective-permute-start.23) | collective-permute-done | bytes 196640 | tf_op jit(solution)/shard_map/ppermute | solution.py:27
  66.8 3.8 %collective-permute-start.6 = (bf16[256,256]{0,1:T(8,128)(2,1)S(1)}, bf16[256,256]{0,1:T(8,128)(2,1)S(1)}, u32[]{:S(2)}, u32[]{:S(2)}) collective-permute-start(bf16[256,256]{0,1:T(8,128)(2,1)S(1)} %copy.40), channel_id=1, source_target_pairs={{0,3},{1,2},{2,1},{3,0},{4,7},{5,6},{6,5},{7,4},{8,11},{9,10},{10,... | collective-permute-start | bytes 393224 | tf_op jit(solution)/shard_map/ppermute | solution.py:27
  70.8 0.6 collective-permute-start.15
  71.4 1.1 collective-permute-done.12
  73.2 1.0 collective-permute-done.18
  74.9 1.0 collective-permute-done.24
  78.1 0.9 copy.31
  79.0 4.1 %convolution_convert_fusion = bf16[2304,512]{1,0:T(8,128)(2,1)} fusion(bf16[2304,1024]{1,0:T(8,128)(2,1)S(1)} %bitcast.109, bf16[1024,512]{0,1:T(8,128)(2,1)S(1)} %bitcast.130), kind=kOutput, calls=%fused_computation | convolution fusion | flops 2417098752 | bytes 8126464 | tf_op jit(solution)/shard_map/dot_general | solution.py:174
  83.1 10.9 %shard_map.73 = bf16[3,128,256]{2,1,0:T(8,128)(2,1)} custom-call(s32[3,11]{1,0:T(4,128)} %pad_convert_fusion.live_ref, s32[4,3]{1,0:T(4,128)} %add_select_fusion.pick_ref, bf16[3,128,256]{2,1,0:T(8,128)(2,1)} %bitcast.158, bf16[3,128,512]{2,1,0:T(8,128)(2,1)} %reshape_reshape.6.own_ref, bf16[6,3,128,512]{3,2,1,0:T(8,128)(2,1)} %bitcast.169), custom_call_target="tpu_custom_call" | custom-call | flops 1107296256 | bytes 3145728 | tf_op jit(solution)/shard_map/pallas_call | solution.py:241
  94.3 6.3 %collective-permute-done.25 = bf16[1,384,256]{2,1,0:T(8,128)(2,1)S(1)} collective-permute-done((bf16[1,384,256]{2,1,0:T(8,128)(2,1)}, bf16[1,384,256]{2,1,0:T(8,128)(2,1)S(1)}, u32[]{:S(2)}, u32[]{:S(2)}) %collective-permute-start.25) | collective-permute-done | bytes 196640 | tf_op jit(solution)/shard_map/ppermute | solution.py:27
  100.6 1.0 pad_maximum_fusion.9
  101.6 1.0 collective-permute-start.26
  102.6 0.9 constant_dynamic-slice_fusion.9
  104.0 0.5 fusion.42
  105.3 1.5 %collective-permute-start.29 = (f32[384,2]{0,1:T(2,128)S(1)}, f32[384,2]{0,1:T(2,128)S(1)}, u32[]{:S(2)}, u32[]{:S(2)}) collective-permute-start(f32[384,2]{0,1:T(2,128)S(1)} %get-tuple-element.50), channel_id=1, source_target_pairs={{0,3},{1,2},{2,1},{3,0},{4,7},{5,6},{6,5},{7,4},{8,11},{9,10},{10,... | collective-permute-start | bytes 9224 | tf_op jit(solution)/shard_map/ppermute | solution.py:27
  106.9 0.7 collective-permute-done.28
  107.5 0.9 collective-permute-done.29
  108.7 0.8 copy.33
  (114 shorter events, 7.8 us)
Async XLA Ops:
  0.0 10.0 %copy-start.5 = (s32[4,3]{1,0:T(4,128)S(1)}, s32[4,3]{1,0:T(4,128)}, u32[]{:S(2)}) copy-start(s32[4,3]{1,0:T(4,128)} %param.13) | copy-start | bytes 148
  0.0 10.9 %copy-start = (bf16[1024,3,256]{2,0,1:T(8,128)(2,1)S(1)}, bf16[1024,3,256]{2,0,1:T(8,128)(2,1)}, u32[]{:S(2)}) copy-start(bf16[1024,3,256]{2,0,1:T(8,128)(2,1)} %param.8) | copy-start | bytes 4718596
  1.2 29.4 %collective-permute-start.7 = (bf16[96,1024]{1,0:T(8,128)(2,1)S(1)}, bf16[96,1024]{1,0:T(8,128)(2,1)S(1)}, u32[]{:S(2)}, u32[]{:S(2)}) collective-permute-start(bf16[96,1024]{1,0:T(8,128)(2,1)S(1)} %bitcast.149), channel_id=1, source_target_pairs={{0,8},{4,12},{8,0},{12,4},{16,24},{20,28},{24,16},{28,20},{1,9},{5... | collective-permute-start | bytes 589832 | tf_op jit(solution)/shard_map/ppermute | solution.py:121
  1.3 29.9 %collective-permute-start.10 = (bf16[96,1024]{1,0:T(8,128)(2,1)S(1)}, bf16[96,1024]{1,0:T(8,128)(2,1)S(1)}, u32[]{:S(2)}, u32[]{:S(2)}) collective-permute-start(bf16[96,1024]{1,0:T(8,128)(2,1)S(1)} %bitcast.150), channel_id=1, source_target_pairs={{0,12},{4,8},{8,4},{12,0},{16,28},{20,24},{24,20},{28,16},{1,13},{... | collective-permute-start | bytes 589832 | tf_op jit(solution)/shard_map/ppermute | solution.py:121
  3.7 30.0 %collective-permute-start.13 = (bf16[96,1024]{1,0:T(8,128)(2,1)S(1)}, bf16[96,1024]{1,0:T(8,128)(2,1)S(1)}, u32[]{:S(2)}, u32[]{:S(2)}) collective-permute-start(bf16[96,1024]{1,0:T(8,128)(2,1)S(1)} %bitcast.151), channel_id=1, source_target_pairs={{0,16},{4,20},{8,24},{12,28},{16,0},{20,4},{24,8},{28,12},{1,17},{... | collective-permute-start | bytes 589832 | tf_op jit(solution)/shard_map/ppermute | solution.py:121
  6.8 22.8 %collective-permute-start = (bf16[2,96,1024]{2,1,0:T(8,128)(2,1)}, bf16[2,96,1024]{2,1,0:T(8,128)(2,1)}, u32[]{:S(2)}, u32[]{:S(2)}) collective-permute-start(bf16[2,96,1024]{2,1,0:T(8,128)(2,1)} %pad_maximum_fusion.2), channel_id=1, source_target_pairs={{0,4},{4,0},{8,12},{12,8},{16,20},{20,16},{24,28},{28,24},{1,5},{5... | collective-permute-start | bytes 1179656 | tf_op jit(solution)/shard_map/ppermute | solution.py:117
  7.0 25.3 %collective-permute-start.2 = (bf16[2,96,1024]{2,1,0:T(8,128)(2,1)}, bf16[2,96,1024]{2,1,0:T(8,128)(2,1)}, u32[]{:S(2)}, u32[]{:S(2)}) collective-permute-start(bf16[2,96,1024]{2,1,0:T(8,128)(2,1)} %pad_maximum_fusion.2), channel_id=1, source_target_pairs={{4,8},{12,16},{20,24},{8,4},{16,12},{24,20},{5,9},{13,17},{21,25},... | collective-permute-start | bytes 1179656 | tf_op jit(solution)/shard_map/ppermute | solution.py:111
  10.9 1.9 %copy-start.6 = (s32[3,7]{1,0:T(4,128)S(1)}, s32[3,7]{1,0:T(4,128)}, u32[]{:S(2)}) copy-start(s32[3,7]{1,0:T(4,128)} %param.12) | copy-start | bytes 256
  12.8 2.0 %copy-start.1 = (bf16[384,3,256]{2,0,1:T(8,128)(2,1)}, bf16[384,3,256]{2,0,1:T(8,128)(2,1)S(1)}, u32[]{:S(2)}) copy-start(bf16[384,3,256]{2,0,1:T(8,128)(2,1)S(1)} %convolution_convert_fusion.1) | copy-start | bytes 1769476
  14.8 5.0 %slice-start = ((bf16[1024,3,256]{2,0,1:T(8,128)(2,1)}), bf16[1024,2,256]{2,0,1:T(8,128)(2,1)S(1)}, s32[]{:S(2)}) async-start(bf16[1024,3,256]{2,0,1:T(8,128)(2,1)} %param.8), calls=%async_computation | async-start | bytes 2097152 | tf_op jit(solution)/shard_map/slice | solution.py:284
  18.1 2.3 %slice-start.1 = ((bf16[384,3,256]{2,0,1:T(8,128)(2,1)}), bf16[384,2,256]{2,0,1:T(8,128)(2,1)S(1)}, s32[]{:S(2)}) async-start(bf16[384,3,256]{2,0,1:T(8,128)(2,1)} %copy-done.1), calls=%async_computation.1 | async-start | bytes 786432 | tf_op jit(solution)/shard_map/slice | solution.py:279
  20.8 25.9 %copy-start.4 = (bf16[256,256]{0,1:T(8,128)(2,1)S(1)}, bf16[256,256]{0,1:T(8,128)(2,1)}, u32[]{:S(2)}) copy-start(bf16[256,256]{0,1:T(8,128)(2,1)} %copy.38) | copy-start | bytes 393220
  29.5 17.2 %collective-permute-start.16 = (bf16[96,1024]{1,0:T(8,128)(2,1)S(1)}, bf16[96,1024]{1,0:T(8,128)(2,1)S(1)}, u32[]{:S(2)}, u32[]{:S(2)}) collective-permute-start(bf16[96,1024]{1,0:T(8,128)(2,1)S(1)} %bitcast.153), channel_id=1, source_target_pairs={{0,20},{4,16},{8,28},{12,24},{16,4},{20,0},{24,12},{28,8},{1,21},{... | collective-permute-start | bytes 589832 | tf_op jit(solution)/shard_map/ppermute | solution.py:121
  30.6 20.3 %collective-permute-start.19 = (bf16[96,1024]{1,0:T(8,128)(2,1)S(1)}, bf16[96,1024]{1,0:T(8,128)(2,1)S(1)}, u32[]{:S(2)}, u32[]{:S(2)}) collective-permute-start(bf16[96,1024]{1,0:T(8,128)(2,1)S(1)} %bitcast.154), channel_id=1, source_target_pairs={{0,24},{4,28},{8,16},{12,20},{16,8},{20,12},{24,0},{28,4},{1,25},{... | collective-permute-start | bytes 589832 | tf_op jit(solution)/shard_map/ppermute | solution.py:121
  31.1 4.8 %collective-permute-start.8 = (bf16[1,96,1024]{2,1,0:T(8,128)(2,1)S(1)}, bf16[1,96,1024]{2,1,0:T(8,128)(2,1)S(1)}, u32[]{:S(2)}, u32[]{:S(2)}) collective-permute-start(bf16[1,96,1024]{2,1,0:T(8,128)(2,1)S(1)} %bitcast.137), channel_id=1, source_target_pairs={{0,2},{1,3},{2,0},{3,1},{4,6},{5,7},{6,4},{7,5},{8,10},{9,11},{10,... | collective-permute-start | bytes 589832 | tf_op jit(solution)/shard_map/ppermute | solution.py:27
  32.3 24.7 %copy-start.3 = (bf16[256,256]{0,1:T(8,128)(2,1)S(1)}, bf16[256,256]{0,1:T(8,128)(2,1)}, u32[]{:S(2)}) copy-start(bf16[256,256]{0,1:T(8,128)(2,1)} %copy.39) | copy-start | bytes 393220
  32.3 19.8 %collective-permute-start.11 = (bf16[1,96,1024]{2,1,0:T(8,128)(2,1)S(1)}, bf16[1,96,1024]{2,1,0:T(8,128)(2,1)S(1)}, u32[]{:S(2)}, u32[]{:S(2)}) collective-permute-start(bf16[1,96,1024]{2,1,0:T(8,128)(2,1)S(1)} %bitcast.134), channel_id=1, source_target_pairs={{0,2},{1,3},{2,0},{3,1},{4,6},{5,7},{6,4},{7,5},{8,10},{9,11},{10,... | collective-permute-start | bytes 589832 | tf_op jit(solution)/shard_map/ppermute | solution.py:27
  33.7 23.2 %collective-permute-start.22 = (bf16[96,1024]{1,0:T(8,128)(2,1)S(1)}, bf16[96,1024]{1,0:T(8,128)(2,1)S(1)}, u32[]{:S(2)}, u32[]{:S(2)}) collective-permute-start(bf16[96,1024]{1,0:T(8,128)(2,1)S(1)} %bitcast.155), channel_id=1, source_target_pairs={{0,28},{4,24},{8,20},{12,16},{16,12},{20,8},{24,4},{28,0},{1,29},{... | collective-permute-start | bytes 589832 | tf_op jit(solution)/shard_map/ppermute | solution.py:121
  36.0 16.5 %collective-permute-start.14 = (bf16[1,96,1024]{2,1,0:T(8,128)(2,1)S(1)}, bf16[1,96,1024]{2,1,0:T(8,128)(2,1)S(1)}, u32[]{:S(2)}, u32[]{:S(2)}) collective-permute-start(bf16[1,96,1024]{2,1,0:T(8,128)(2,1)S(1)} %bitcast.131), channel_id=1, source_target_pairs={{0,2},{1,3},{2,0},{3,1},{4,6},{5,7},{6,4},{7,5},{8,10},{9,11},{10,... | collective-permute-start | bytes 589832 | tf_op jit(solution)/shard_map/ppermute | solution.py:27
  46.7 30.0 %collective-permute-start.4 = (bf16[256,256]{0,1:T(8,128)(2,1)S(1)}, bf16[256,256]{0,1:T(8,128)(2,1)S(1)}, u32[]{:S(2)}, u32[]{:S(2)}) collective-permute-start(bf16[256,256]{0,1:T(8,128)(2,1)S(1)} %copy-done.4), channel_id=1, source_target_pairs={{0,1},{1,0},{2,3},{3,2},{4,5},{5,4},{6,7},{7,6},{8,9},{9,8},{10,11... | collective-permute-start | bytes 393224 | tf_op jit(solution)/shard_map/ppermute | solution.py:27
  51.0 7.3 %collective-permute-start.17 = (bf16[1,96,1024]{2,1,0:T(8,128)(2,1)S(1)}, bf16[1,96,1024]{2,1,0:T(8,128)(2,1)S(1)}, u32[]{:S(2)}, u32[]{:S(2)}) collective-permute-start(bf16[1,96,1024]{2,1,0:T(8,128)(2,1)S(1)} %bitcast.140), channel_id=1, source_target_pairs={{0,2},{1,3},{2,0},{3,1},{4,6},{5,7},{6,4},{7,5},{8,10},{9,11},{10,... | collective-permute-start | bytes 589832 | tf_op jit(solution)/shard_map/ppermute | solution.py:27
  52.1 6.4 %collective-permute-start.20 = (bf16[1,96,1024]{2,1,0:T(8,128)(2,1)S(1)}, bf16[1,96,1024]{2,1,0:T(8,128)(2,1)S(1)}, u32[]{:S(2)}, u32[]{:S(2)}) collective-permute-start(bf16[1,96,1024]{2,1,0:T(8,128)(2,1)S(1)} %bitcast.143), channel_id=1, source_target_pairs={{0,2},{1,3},{2,0},{3,1},{4,6},{5,7},{6,4},{7,5},{8,10},{9,11},{10,... | collective-permute-start | bytes 589832 | tf_op jit(solution)/shard_map/ppermute | solution.py:27
  52.5 18.2 %collective-permute-start.1 = (bf16[2,96,1024]{2,1,0:T(8,128)(2,1)}, bf16[2,96,1024]{2,1,0:T(8,128)(2,1)S(1)}, u32[]{:S(2)}, u32[]{:S(2)}) collective-permute-start(bf16[2,96,1024]{2,1,0:T(8,128)(2,1)} %collective-permute-done), channel_id=1, source_target_pairs={{0,1},{1,0},{2,3},{3,2},{4,5},{5,4},{6,7},{7,6},{8,9},{9,8},{10,11... | collective-permute-start | bytes 1179656 | tf_op jit(solution)/shard_map/ppermute | solution.py:27
  56.9 19.8 %collective-permute-start.5 = (bf16[256,256]{0,1:T(8,128)(2,1)S(1)}, bf16[256,256]{0,1:T(8,128)(2,1)S(1)}, u32[]{:S(2)}, u32[]{:S(2)}) collective-permute-start(bf16[256,256]{0,1:T(8,128)(2,1)S(1)} %copy-done.3), channel_id=1, source_target_pairs={{0,2},{1,3},{2,0},{3,1},{4,6},{5,7},{6,4},{7,5},{8,10},{9,11},{10,... | collective-permute-start | bytes 393224 | tf_op jit(solution)/shard_map/ppermute | solution.py:27
  58.2 8.6 %collective-permute-start.23 = (bf16[1,96,1024]{2,1,0:T(8,128)(2,1)S(1)}, bf16[1,96,1024]{2,1,0:T(8,128)(2,1)S(1)}, u32[]{:S(2)}, u32[]{:S(2)}) collective-permute-start(bf16[1,96,1024]{2,1,0:T(8,128)(2,1)S(1)} %bitcast.146), channel_id=1, source_target_pairs={{0,2},{1,3},{2,0},{3,1},{4,6},{5,7},{6,4},{7,5},{8,10},{9,11},{10,... | collective-permute-start | bytes 589832 | tf_op jit(solution)/shard_map/ppermute | solution.py:27
  58.5 12.3 %collective-permute-start.9 = (bf16[2,96,1024]{2,1,0:T(8,128)(2,1)S(1)}, bf16[2,96,1024]{2,1,0:T(8,128)(2,1)S(1)}, u32[]{:S(2)}, u32[]{:S(2)}) collective-permute-start(bf16[2,96,1024]{2,1,0:T(8,128)(2,1)S(1)} %pad_maximum_fusion.3), channel_id=1, source_target_pairs={{0,1},{1,0},{2,3},{3,2},{4,5},{5,4},{6,7},{7,6},{8,9},{9,8},{10,11... | collective-permute-start | bytes 1179656 | tf_op jit(solution)/shard_map/ppermute | solution.py:27
  66.8 10.0 %collective-permute-start.6 = (bf16[256,256]{0,1:T(8,128)(2,1)S(1)}, bf16[256,256]{0,1:T(8,128)(2,1)S(1)}, u32[]{:S(2)}, u32[]{:S(2)}) collective-permute-start(bf16[256,256]{0,1:T(8,128)(2,1)S(1)} %copy.40), channel_id=1, source_target_pairs={{0,3},{1,2},{2,1},{3,0},{4,7},{5,6},{6,5},{7,4},{8,11},{9,10},{10,... | collective-permute-start | bytes 393224 | tf_op jit(solution)/shard_map/ppermute | solution.py:27
  70.7 1.8 %collective-permute-start.12 = (bf16[2,96,1024]{2,1,0:T(8,128)(2,1)S(1)}, bf16[2,96,1024]{2,1,0:T(8,128)(2,1)S(1)}, u32[]{:S(2)}, u32[]{:S(2)}) collective-permute-start(bf16[2,96,1024]{2,1,0:T(8,128)(2,1)S(1)} %pad_maximum_fusion.4), channel_id=1, source_target_pairs={{0,1},{1,0},{2,3},{3,2},{4,5},{5,4},{6,7},{7,6},{8,9},{9,8},{10,11... | collective-permute-start | bytes 1179656 | tf_op jit(solution)/shard_map/ppermute | solution.py:27
  70.8 2.2 %collective-permute-start.15 = (bf16[2,96,1024]{2,1,0:T(8,128)(2,1)S(1)}, bf16[2,96,1024]{2,1,0:T(8,128)(2,1)S(1)}, u32[]{:S(2)}, u32[]{:S(2)}) collective-permute-start(bf16[2,96,1024]{2,1,0:T(8,128)(2,1)S(1)} %pad_maximum_fusion.5), channel_id=1, source_target_pairs={{0,1},{1,0},{2,3},{3,2},{4,5},{5,4},{6,7},{7,6},{8,9},{9,8},{10,11... | collective-permute-start | bytes 1179656 | tf_op jit(solution)/shard_map/ppermute | solution.py:27
  72.5 1.7 %collective-permute-start.18 = (bf16[2,96,1024]{2,1,0:T(8,128)(2,1)S(1)}, bf16[2,96,1024]{2,1,0:T(8,128)(2,1)S(1)}, u32[]{:S(2)}, u32[]{:S(2)}) collective-permute-start(bf16[2,96,1024]{2,1,0:T(8,128)(2,1)S(1)} %pad_maximum_fusion.6), channel_id=1, source_target_pairs={{0,1},{1,0},{2,3},{3,2},{4,5},{5,4},{6,7},{7,6},{8,9},{9,8},{10,11... | collective-permute-start | bytes 1179656 | tf_op jit(solution)/shard_map/ppermute | solution.py:27
  73.0 1.7 %collective-permute-start.21 = (bf16[2,96,1024]{2,1,0:T(8,128)(2,1)S(1)}, bf16[2,96,1024]{2,1,0:T(8,128)(2,1)S(1)}, u32[]{:S(2)}, u32[]{:S(2)}) collective-permute-start(bf16[2,96,1024]{2,1,0:T(8,128)(2,1)S(1)} %pad_maximum_fusion.7), channel_id=1, source_target_pairs={{0,1},{1,0},{2,3},{3,2},{4,5},{5,4},{6,7},{7,6},{8,9},{9,8},{10,11... | collective-permute-start | bytes 1179656 | tf_op jit(solution)/shard_map/ppermute | solution.py:27
  74.2 1.7 %collective-permute-start.24 = (bf16[2,96,1024]{2,1,0:T(8,128)(2,1)S(1)}, bf16[2,96,1024]{2,1,0:T(8,128)(2,1)S(1)}, u32[]{:S(2)}, u32[]{:S(2)}) collective-permute-start(bf16[2,96,1024]{2,1,0:T(8,128)(2,1)S(1)} %pad_maximum_fusion.8), channel_id=1, source_target_pairs={{0,1},{1,0},{2,3},{3,2},{4,5},{5,4},{6,7},{7,6},{8,9},{9,8},{10,11... | collective-permute-start | bytes 1179656 | tf_op jit(solution)/shard_map/ppermute | solution.py:27
  74.7 2.1 %collective-permute-start.3 = (bf16[2,96,1024]{2,1,0:T(8,128)(2,1)}, bf16[2,96,1024]{2,1,0:T(8,128)(2,1)S(1)}, u32[]{:S(2)}, u32[]{:S(2)}) collective-permute-start(bf16[2,96,1024]{2,1,0:T(8,128)(2,1)} %collective-permute-done.2), channel_id=1, source_target_pairs={{0,1},{1,0},{2,3},{3,2},{4,5},{5,4},{6,7},{7,6},{8,9},{9,8},{10,11... | collective-permute-start | bytes 1179656 | tf_op jit(solution)/shard_map/ppermute | solution.py:27
  76.8 0.6 copy-start.9
  76.8 0.7 copy-start.11
  94.0 10.0 %copy-start.2 = (bf16[3,128,256]{2,1,0:T(8,128)(2,1)S(1)}, bf16[3,128,256]{2,1,0:T(8,128)(2,1)}, u32[]{:S(2)}) copy-start(bf16[3,128,256]{2,1,0:T(8,128)(2,1)} %shard_map.73) | copy-start | bytes 589828
  94.0 10.0 %copy-start.10 = (bf16[256,256]{0,1:T(8,128)(2,1)S(1)}, bf16[256,256]{0,1:T(8,128)(2,1)}, u32[]{:S(2)}) copy-start(bf16[256,256]{0,1:T(8,128)(2,1)} %copy-done.9) | copy-start | bytes 393220
  94.0 10.0 %copy-start.12 = (bf16[256,256]{0,1:T(8,128)(2,1)S(1)}, bf16[256,256]{0,1:T(8,128)(2,1)}, u32[]{:S(2)}) copy-start(bf16[256,256]{0,1:T(8,128)(2,1)} %copy-done.11) | copy-start | bytes 393220
  94.0 6.6 %collective-permute-start.25 = (bf16[1,384,256]{2,1,0:T(8,128)(2,1)}, bf16[1,384,256]{2,1,0:T(8,128)(2,1)S(1)}, u32[]{:S(2)}, u32[]{:S(2)}) collective-permute-start(bf16[1,384,256]{2,1,0:T(8,128)(2,1)} %bitcast.159), channel_id=1, source_target_pairs={{0,2},{1,3},{2,0},{3,1},{4,6},{5,7},{6,4},{7,5},{8,10},{9,11},{10,... | collective-permute-start | bytes 589832 | tf_op jit(solution)/shard_map/ppermute | solution.py:27
  101.6 2.4 %collective-permute-start.26 = (bf16[2,384,256]{2,1,0:T(8,128)(2,1)S(1)}, bf16[2,384,256]{2,1,0:T(8,128)(2,1)S(1)}, u32[]{:S(2)}, u32[]{:S(2)}) collective-permute-start(bf16[2,384,256]{2,1,0:T(8,128)(2,1)S(1)} %pad_maximum_fusion.9), channel_id=1, source_target_pairs={{0,1},{1,0},{2,3},{3,2},{4,5},{5,4},{6,7},{7,6},{8,9},{9,8},{10,11... | collective-permute-start | bytes 1179656 | tf_op jit(solution)/shard_map/ppermute | solution.py:27
  104.0 4.5 %copy-start.7 = (f32[256]{0:T(256)S(1)}, f32[256]{0:T(256)}, u32[]{:S(2)}) copy-start(f32[256]{0:T(256)} %param.11) | copy-start | bytes 3076
  104.0 4.5 %copy-start.8 = (f32[256]{0:T(256)S(1)}, f32[256]{0:T(256)}, u32[]{:S(2)}) copy-start(f32[256]{0:T(256)} %param.10) | copy-start | bytes 3076
  104.6 2.2 %collective-permute-start.27 = (f32[384,2]{0,1:T(2,128)S(1)}, f32[384,2]{0,1:T(2,128)S(1)}, u32[]{:S(2)}, u32[]{:S(2)}) collective-permute-start(f32[384,2]{0,1:T(2,128)S(1)} %get-tuple-element.50), channel_id=1, source_target_pairs={{0,1},{1,0},{2,3},{3,2},{4,5},{5,4},{6,7},{7,6},{8,9},{9,8},{10,11... | collective-permute-start | bytes 9224 | tf_op jit(solution)/shard_map/ppermute | solution.py:27
  105.1 2.4 %collective-permute-start.28 = (f32[384,2]{0,1:T(2,128)S(1)}, f32[384,2]{0,1:T(2,128)S(1)}, u32[]{:S(2)}, u32[]{:S(2)}) collective-permute-start(f32[384,2]{0,1:T(2,128)S(1)} %get-tuple-element.50), channel_id=1, source_target_pairs={{0,2},{1,3},{2,0},{3,1},{4,6},{5,7},{6,4},{7,5},{8,10},{9,11},{10,... | collective-permute-start | bytes 9224 | tf_op jit(solution)/shard_map/ppermute | solution.py:27
  105.3 3.1 %collective-permute-start.29 = (f32[384,2]{0,1:T(2,128)S(1)}, f32[384,2]{0,1:T(2,128)S(1)}, u32[]{:S(2)}, u32[]{:S(2)}) collective-permute-start(f32[384,2]{0,1:T(2,128)S(1)} %get-tuple-element.50), channel_id=1, source_target_pairs={{0,3},{1,2},{2,1},{3,0},{4,7},{5,6},{6,5},{7,4},{8,11},{9,10},{10,... | collective-permute-start | bytes 9224 | tf_op jit(solution)/shard_map/ppermute | solution.py:27

commit v13 on v11

--- a/solution.py
+++ b/solution.py
@@ -13,7 +13,7 @@
 LANES = 128
 GATHER_GROUPS = 16
 STATIC_GROUPS = 8
-NEAR_SHIFTS = 3
+NEAR_SHIFTS = (1, 3)
 
 
 NORM_EPS = 1e-05
@@ -113,7 +113,7 @@
             pair_stack(
                 lax.ppermute(near, "node", [(i, i ^ shift) for i in range(groups)]), heads_axis
             )
-            if shift < NEAR_SHIFTS and heads_axis == 4
+            if shift in NEAR_SHIFTS and heads_axis == 4
             else spread_stack(
                 lax.ppermute(mine, "node", [(i, i ^ shift) for i in range(groups)]), heads_axis
             )

time: 107 us -> 106 us (level); the launches traced: 105 us -> 106 us
  waiting for transfers between devices: 26.1 us -> 32.9 us
  starting transfers between devices: 39.9 us -> 34.1 us
    ppermute x22, starting transfers between devices: 24.2 us -> 18.3 us  [flip_heads(): return lax.ppermute(array, 'head', [(i, i ^ flip) for i in range(devices)])]
    ppermute x5, waiting for transfers between devices: 5.78 us -> 11.4 us  [static_keys(): lax.ppermute(mine, 'node', [(i, i ^ shift) for i in range(groups)])]
  transfers between devices with their start and end apart: 30 -> 30, of which waited for: 13 -> 16; matrix products, arithmetic and copies ran while one was open for 13% -> 13% of each run, Pallas kernels for 0% -> 0%
where the time goes in v13:
time: 106 us
  starting transfers between devices  34.1 us (32%)
  waiting for transfers between devices  32.9 us (31%)
  local copies, waits for them, and re-layouts  13.7 us (13%)
  Pallas kernels  10.9 us (10%)
  matrix products  6.69 us (6%)
  other arithmetic  4.78 us (5%)
  between operations  3.15 us (3%)
    ppermute x22, waiting for transfers between devices, flip_heads(): return lax.ppermute(array, 'head', [(i, i ^ flip) for i in range(devices)])  21.2 us
    ppermute x22, starting transfers between devices, flip_heads(): return lax.ppermute(array, 'head', [(i, i ^ flip) for i in range(devices)])  18.3 us
    ppermute x5, waiting for transfers between devices, static_keys(): lax.ppermute(mine, 'node', [(i, i ^ shift) for i in range(groups)])  11.4 us
    pallas_call x1, Pallas kernels, attention(): pl.pallas_call(attention_kernel, out_shape=jax.ShapeDtypeStruct(query.sha...  10.9 us
    ppermute x5, starting transfers between devices, static_keys(): lax.ppermute(mine, 'node', [(i, i ^ shift) for i in range(groups)])  9.15 us
    ppermute x1, starting transfers between devices, static_keys(): other = spread_stack(lax.ppermute(mine, 'node', far), heads_axis)  5.34 us
    dot_general x1, matrix products, kv_of_spread(): jnp.dot(rows, w_kv, preferred_element_type=jnp.float32).astype(jnp.bfloat16)  4.28 us
    unnamed x34, local copies, waits for them, and re-layouts  2.85 us
  transfers between devices with their start and end apart: 30, of which 16 were waited for; matrix products, arithmetic and copies ran while one was open for 13% of the time, Pallas kernels for 0%

profile of v13, /device:TPU:9, one launch (start us, length us, event | category | flops | bytes accessed | tf_op | source)
XLA Modules:
  0.0 106.1 jit_solution(3669146373510829428)
XLA Ops:
  0.0 1.2 %constant_dynamic-slice_fusion.7 = (bf16[3,1,32,1024]{3,2,1,0:T(8,128)(2,1)S(1)}, bf16[3,1,32,1024]{3,2,1,0:T(8,128)(2,1)S(1)}) fusion(bf16[3,4,32,1024]{3,2,1,0:T(8,128)(2,1)} %bitcast.156, s32[]{:T(128)S(6)} %select_n.63, s32[]{:T(128)S(6)} %select_n.62), kind=kLoop, calls=%fused_computation.67 | loop fusion | bytes 786440 | tf_op jit(solution)/shard_map/jit(dynamic_index_in_dim)/dynamic_slice | solution.py:142
  1.2 0.8 pad_maximum_fusion.2
  2.0 1.2 %collective-permute-start = (bf16[2,96,1024]{2,1,0:T(8,128)(2,1)}, bf16[2,96,1024]{2,1,0:T(8,128)(2,1)}, u32[]{:S(2)}, u32[]{:S(2)}) collective-permute-start(bf16[2,96,1024]{2,1,0:T(8,128)(2,1)} %pad_maximum_fusion.2), channel_id=1, source_target_pairs={{0,4},{4,0},{8,12},{12,8},{16,20},{20,16},{24,28},{28,24},{1,5},{5... | collective-permute-start | bytes 1179656 | tf_op jit(solution)/shard_map/ppermute | solution.py:114
  3.2 1.4 %collective-permute-start.8 = (bf16[96,1024]{1,0:T(8,128)(2,1)S(1)}, bf16[96,1024]{1,0:T(8,128)(2,1)S(1)}, u32[]{:S(2)}, u32[]{:S(2)}) collective-permute-start(bf16[96,1024]{1,0:T(8,128)(2,1)S(1)} %bitcast.149), channel_id=1, source_target_pairs={{0,8},{4,12},{8,0},{12,4},{16,24},{20,28},{24,16},{28,20},{1,9},{5... | collective-permute-start | bytes 589832 | tf_op jit(solution)/shard_map/ppermute | solution.py:118
  4.6 2.3 %collective-permute-start.13 = (bf16[96,1024]{1,0:T(8,128)(2,1)S(1)}, bf16[96,1024]{1,0:T(8,128)(2,1)S(1)}, u32[]{:S(2)}, u32[]{:S(2)}) collective-permute-start(bf16[96,1024]{1,0:T(8,128)(2,1)S(1)} %bitcast.150), channel_id=1, source_target_pairs={{0,16},{4,20},{8,24},{12,28},{16,0},{20,4},{24,8},{28,12},{1,17},{... | collective-permute-start | bytes 589832 | tf_op jit(solution)/shard_map/ppermute | solution.py:118
  6.9 1.0 collective-permute-start.16
  8.8 1.9 %convolution_convert_fusion.1 = bf16[384,3,256]{2,0,1:T(8,128)(2,1)S(1)} fusion(bf16[1024,3,256]{2,0,1:T(8,128)(2,1)S(1)} %copy-done, bf16[384,1024]{1,0:T(8,128)(2,1)} %param.7), kind=kOutput, calls=%fused_computation.1 | convolution fusion | flops 604274688 | bytes 2949120 | tf_op jit(solution)/shard_map/nd,dtf->ntf/dot_general | solution.py:272
  10.8 1.3 %constant_dynamic-slice_fusion.3 = (bf16[256,256]{1,0:T(8,128)(2,1)S(1)}, bf16[256,256]{1,0:T(8,128)(2,1)S(1)}, bf16[256,256]{1,0:T(8,128)(2,1)S(1)}, bf16[256,256]{1,0:T(8,128)(2,1)S(1)}) fusion(bf16[256,1024]{1,0:T(8,128)(2,1)} %param.9, s32[]{:T(128)S(6)} %select_n.68, s32[]{:T(128)S(6)} %select_n.67, s32[]{:T(128)S(6)} %select_n.66, s32[]{:T(128)S(6)} %select_n.58), kind=kLoop, calls=%fused_computation.63 | loop fusion | bytes 1048592 | tf_op jit(solution)/shard_map/dynamic_slice | solution.py:266
  12.1 0.7 fusion.41
  12.7 0.7 slice.129
  16.0 0.8 copy.38
  16.8 0.8 copy.39
  18.8 1.0 reshape_reshape.6.own_ref
  19.8 0.6 pad_convert_fusion.live_ref
  20.7 1.3 %collective-permute-start.19 = (bf16[96,1024]{1,0:T(8,128)(2,1)S(1)}, bf16[96,1024]{1,0:T(8,128)(2,1)S(1)}, u32[]{:S(2)}, u32[]{:S(2)}) collective-permute-start(bf16[96,1024]{1,0:T(8,128)(2,1)S(1)} %bitcast.152), channel_id=1, source_target_pairs={{0,24},{4,28},{8,16},{12,20},{16,8},{20,12},{24,0},{28,4},{1,25},{... | collective-permute-start | bytes 589832 | tf_op jit(solution)/shard_map/ppermute | solution.py:118
  22.0 1.0 fusion.38
  23.0 1.0 collective-permute-done.8
  24.0 3.1 %collective-permute-start.22 = (bf16[96,1024]{1,0:T(8,128)(2,1)S(1)}, bf16[96,1024]{1,0:T(8,128)(2,1)S(1)}, u32[]{:S(2)}, u32[]{:S(2)}) collective-permute-start(bf16[96,1024]{1,0:T(8,128)(2,1)S(1)} %bitcast.153), channel_id=1, source_target_pairs={{0,28},{4,24},{8,20},{12,16},{16,12},{20,8},{24,4},{28,0},{1,29},{... | collective-permute-start | bytes 589832 | tf_op jit(solution)/shard_map/ppermute | solution.py:118
  27.1 1.2 %collective-permute-start.9 = (bf16[1,96,1024]{2,1,0:T(8,128)(2,1)S(1)}, bf16[1,96,1024]{2,1,0:T(8,128)(2,1)S(1)}, u32[]{:S(2)}, u32[]{:S(2)}) collective-permute-start(bf16[1,96,1024]{2,1,0:T(8,128)(2,1)S(1)} %bitcast.139), channel_id=1, source_target_pairs={{0,2},{1,3},{2,0},{3,1},{4,6},{5,7},{6,4},{7,5},{8,10},{9,11},{10,... | collective-permute-start | bytes 589832 | tf_op jit(solution)/shard_map/ppermute | solution.py:27
  28.6 1.0 fusion.35
  29.7 5.3 %collective-permute-start.2 = (bf16[96,1024]{1,0:T(8,128)(2,1)S(1)}, bf16[96,1024]{1,0:T(8,128)(2,1)S(1)}, u32[]{:S(2)}, u32[]{:S(2)}) collective-permute-start(bf16[96,1024]{1,0:T(8,128)(2,1)S(1)} %bitcast.154), channel_id=1, source_target_pairs={{4,8},{12,16},{20,24},{8,4},{16,12},{24,20},{5,9},{13,17},{21,25},... | collective-permute-start | bytes 589832 | tf_op jit(solution)/shard_map/ppermute | solution.py:109
  35.0 1.3 %collective-permute-start.17 = (bf16[1,96,1024]{2,1,0:T(8,128)(2,1)S(1)}, bf16[1,96,1024]{2,1,0:T(8,128)(2,1)S(1)}, u32[]{:S(2)}, u32[]{:S(2)}) collective-permute-start(bf16[1,96,1024]{2,1,0:T(8,128)(2,1)S(1)} %bitcast.133), channel_id=1, source_target_pairs={{0,2},{1,3},{2,0},{3,1},{4,6},{5,7},{6,4},{7,5},{8,10},{9,11},{10,... | collective-permute-start | bytes 589832 | tf_op jit(solution)/shard_map/ppermute | solution.py:27
  36.4 4.4 %collective-permute-done.19 = bf16[96,1024]{1,0:T(8,128)(2,1)S(1)} collective-permute-done((bf16[96,1024]{1,0:T(8,128)(2,1)S(1)}, bf16[96,1024]{1,0:T(8,128)(2,1)S(1)}, u32[]{:S(2)}, u32[]{:S(2)}) %collective-permute-start.19) | collective-permute-done | bytes 196640 | tf_op jit(solution)/shard_map/ppermute | solution.py:118
  40.7 0.6 collective-permute-start.5
  41.3 6.0 %collective-permute-done.22 = bf16[96,1024]{1,0:T(8,128)(2,1)S(1)} collective-permute-done((bf16[96,1024]{1,0:T(8,128)(2,1)S(1)}, bf16[96,1024]{1,0:T(8,128)(2,1)S(1)}, u32[]{:S(2)}, u32[]{:S(2)}) %collective-permute-start.22) | collective-permute-done | bytes 196640 | tf_op jit(solution)/shard_map/ppermute | solution.py:118
  47.4 1.2 %collective-permute-start.20 = (bf16[1,96,1024]{2,1,0:T(8,128)(2,1)S(1)}, bf16[1,96,1024]{2,1,0:T(8,128)(2,1)S(1)}, u32[]{:S(2)}, u32[]{:S(2)}) collective-permute-start(bf16[1,96,1024]{2,1,0:T(8,128)(2,1)S(1)} %bitcast.142), channel_id=1, source_target_pairs={{0,2},{1,3},{2,0},{3,1},{4,6},{5,7},{6,4},{7,5},{8,10},{9,11},{10,... | collective-permute-start | bytes 589832 | tf_op jit(solution)/shard_map/ppermute | solution.py:27
  48.9 1.2 %collective-permute-start.1 = (bf16[2,96,1024]{2,1,0:T(8,128)(2,1)}, bf16[2,96,1024]{2,1,0:T(8,128)(2,1)S(1)}, u32[]{:S(2)}, u32[]{:S(2)}) collective-permute-start(bf16[2,96,1024]{2,1,0:T(8,128)(2,1)} %collective-permute-done), channel_id=1, source_target_pairs={{0,1},{1,0},{2,3},{3,2},{4,5},{5,4},{6,7},{7,6},{8,9},{9,8},{10,11... | collective-permute-start | bytes 1179656 | tf_op jit(solution)/shard_map/ppermute | solution.py:27
  50.1 1.3 %collective-permute-start.6 = (bf16[256,256]{0,1:T(8,128)(2,1)S(1)}, bf16[256,256]{0,1:T(8,128)(2,1)S(1)}, u32[]{:S(2)}, u32[]{:S(2)}) collective-permute-start(bf16[256,256]{0,1:T(8,128)(2,1)S(1)} %copy-done.3), channel_id=1, source_target_pairs={{0,2},{1,3},{2,0},{3,1},{4,6},{5,7},{6,4},{7,5},{8,10},{9,11},{10,... | collective-permute-start | bytes 393224 | tf_op jit(solution)/shard_map/ppermute | solution.py:27
  51.4 1.9 %collective-permute-done.20 = bf16[1,96,1024]{2,1,0:T(8,128)(2,1)S(1)} collective-permute-done((bf16[1,96,1024]{2,1,0:T(8,128)(2,1)S(1)}, bf16[1,96,1024]{2,1,0:T(8,128)(2,1)S(1)}, u32[]{:S(2)}, u32[]{:S(2)}) %collective-permute-start.20) | collective-permute-done | bytes 196640 | tf_op jit(solution)/shard_map/ppermute | solution.py:27
  53.3 1.2 %collective-permute-start.3 = (bf16[1,96,1024]{2,1,0:T(8,128)(2,1)S(1)}, bf16[1,96,1024]{2,1,0:T(8,128)(2,1)S(1)}, u32[]{:S(2)}, u32[]{:S(2)}) collective-permute-start(bf16[1,96,1024]{2,1,0:T(8,128)(2,1)S(1)} %bitcast.122), channel_id=1, source_target_pairs={{0,2},{1,3},{2,0},{3,1},{4,6},{5,7},{6,4},{7,5},{8,10},{9,11},{10,... | collective-permute-start | bytes 589832 | tf_op jit(solution)/shard_map/ppermute | solution.py:27
  54.5 3.0 %collective-permute-done.23 = bf16[1,96,1024]{2,1,0:T(8,128)(2,1)S(1)} collective-permute-done((bf16[1,96,1024]{2,1,0:T(8,128)(2,1)S(1)}, bf16[1,96,1024]{2,1,0:T(8,128)(2,1)S(1)}, u32[]{:S(2)}, u32[]{:S(2)}) %collective-permute-start.23) | collective-permute-done | bytes 196640 | tf_op jit(solution)/shard_map/ppermute | solution.py:27
  57.5 2.4 %collective-permute-start.10 = (bf16[2,96,1024]{2,1,0:T(8,128)(2,1)S(1)}, bf16[2,96,1024]{2,1,0:T(8,128)(2,1)S(1)}, u32[]{:S(2)}, u32[]{:S(2)}) collective-permute-start(bf16[2,96,1024]{2,1,0:T(8,128)(2,1)S(1)} %pad_maximum_fusion.4), channel_id=1, source_target_pairs={{0,1},{1,0},{2,3},{3,2},{4,5},{5,4},{6,7},{7,6},{8,9},{9,8},{10,11... | collective-permute-start | bytes 1179656 | tf_op jit(solution)/shard_map/ppermute | solution.py:27
  59.9 4.6 %collective-permute-done.3 = bf16[1,96,1024]{2,1,0:T(8,128)(2,1)S(1)} collective-permute-done((bf16[1,96,1024]{2,1,0:T(8,128)(2,1)S(1)}, bf16[1,96,1024]{2,1,0:T(8,128)(2,1)S(1)}, u32[]{:S(2)}, u32[]{:S(2)}) %collective-permute-start.3) | collective-permute-done | bytes 196640 | tf_op jit(solution)/shard_map/ppermute | solution.py:27
  64.5 2.5 %collective-permute-start.7 = (bf16[256,256]{0,1:T(8,128)(2,1)S(1)}, bf16[256,256]{0,1:T(8,128)(2,1)S(1)}, u32[]{:S(2)}, u32[]{:S(2)}) collective-permute-start(bf16[256,256]{0,1:T(8,128)(2,1)S(1)} %copy.40), channel_id=1, source_target_pairs={{0,3},{1,2},{2,1},{3,0},{4,7},{5,6},{6,5},{7,4},{8,11},{9,10},{10,... | collective-permute-start | bytes 393224 | tf_op jit(solution)/shard_map/ppermute | solution.py:27
  67.8 1.3 %collective-permute-done.12 = bf16[2,96,1024]{2,1,0:T(8,128)(2,1)S(1)} collective-permute-done((bf16[2,96,1024]{2,1,0:T(8,128)(2,1)}, bf16[2,96,1024]{2,1,0:T(8,128)(2,1)S(1)}, u32[]{:S(2)}, u32[]{:S(2)}) %collective-permute-start.12) | collective-permute-done | bytes 393248 | tf_op jit(solution)/shard_map/ppermute | solution.py:27
  69.7 1.1 %collective-permute-done.18 = bf16[2,96,1024]{2,1,0:T(8,128)(2,1)S(1)} collective-permute-done((bf16[2,96,1024]{2,1,0:T(8,128)(2,1)S(1)}, bf16[2,96,1024]{2,1,0:T(8,128)(2,1)S(1)}, u32[]{:S(2)}, u32[]{:S(2)}) %collective-permute-start.18) | collective-permute-done | bytes 393248 | tf_op jit(solution)/shard_map/ppermute | solution.py:27
  71.6 0.9 collective-permute-done.24
  74.5 0.9 copy.31
  75.4 4.3 %convolution_convert_fusion = bf16[2304,512]{1,0:T(8,128)(2,1)} fusion(bf16[2304,1024]{1,0:T(8,128)(2,1)S(1)} %bitcast.109, bf16[1024,512]{0,1:T(8,128)(2,1)S(1)} %bitcast.132), kind=kOutput, calls=%fused_computation | convolution fusion | flops 2417098752 | bytes 8126464 | tf_op jit(solution)/shard_map/dot_general | solution.py:171
  79.7 10.9 %shard_map.73 = bf16[3,128,256]{2,1,0:T(8,128)(2,1)} custom-call(s32[3,11]{1,0:T(4,128)} %pad_convert_fusion.live_ref, s32[4,3]{1,0:T(4,128)} %add_select_fusion.pick_ref, bf16[3,128,256]{2,1,0:T(8,128)(2,1)} %bitcast.157, bf16[3,128,512]{2,1,0:T(8,128)(2,1)} %reshape_reshape.6.own_ref, bf16[6,3,128,512]{3,2,1,0:T(8,128)(2,1)} %bitcast.168), custom_call_target="tpu_custom_call" | custom-call | flops 1107296256 | bytes 3145728 | tf_op jit(solution)/shard_map/pallas_call | solution.py:238
  90.9 6.3 %collective-permute-done.25 = bf16[1,384,256]{2,1,0:T(8,128)(2,1)S(1)} collective-permute-done((bf16[1,384,256]{2,1,0:T(8,128)(2,1)}, bf16[1,384,256]{2,1,0:T(8,128)(2,1)S(1)}, u32[]{:S(2)}, u32[]{:S(2)}) %collective-permute-start.25) | collective-permute-done | bytes 196640 | tf_op jit(solution)/shard_map/ppermute | solution.py:27
  97.2 1.0 pad_maximum_fusion.9
  98.2 1.0 collective-permute-start.26
  99.2 0.9 constant_dynamic-slice_fusion.9
  102.0 1.5 %collective-permute-start.29 = (f32[384,2]{0,1:T(2,128)S(1)}, f32[384,2]{0,1:T(2,128)S(1)}, u32[]{:S(2)}, u32[]{:S(2)}) collective-permute-start(f32[384,2]{0,1:T(2,128)S(1)} %get-tuple-element.50), channel_id=1, source_target_pairs={{0,3},{1,2},{2,1},{3,0},{4,7},{5,6},{6,5},{7,4},{8,11},{9,10},{10,... | collective-permute-start | bytes 9224 | tf_op jit(solution)/shard_map/ppermute | solution.py:27
  103.5 0.7 collective-permute-done.28
  104.2 0.9 collective-permute-done.29
  105.3 0.8 copy.33
  (114 shorter events, 9.4 us)
Async XLA Ops:
  0.0 7.9 %copy-start.5 = (s32[4,3]{1,0:T(4,128)S(1)}, s32[4,3]{1,0:T(4,128)}, u32[]{:S(2)}) copy-start(s32[4,3]{1,0:T(4,128)} %param.13) | copy-start | bytes 148
  0.0 8.8 %copy-start = (bf16[1024,3,256]{2,0,1:T(8,128)(2,1)S(1)}, bf16[1024,3,256]{2,0,1:T(8,128)(2,1)}, u32[]{:S(2)}) copy-start(bf16[1024,3,256]{2,0,1:T(8,128)(2,1)} %param.8) | copy-start | bytes 4718596
  2.0 18.7 %collective-permute-start = (bf16[2,96,1024]{2,1,0:T(8,128)(2,1)}, bf16[2,96,1024]{2,1,0:T(8,128)(2,1)}, u32[]{:S(2)}, u32[]{:S(2)}) collective-permute-start(bf16[2,96,1024]{2,1,0:T(8,128)(2,1)} %pad_maximum_fusion.2), channel_id=1, source_target_pairs={{0,4},{4,0},{8,12},{12,8},{16,20},{20,16},{24,28},{28,24},{1,5},{5... | collective-permute-start | bytes 1179656 | tf_op jit(solution)/shard_map/ppermute | solution.py:114
  3.2 25.2 %collective-permute-start.11 = (bf16[2,96,1024]{2,1,0:T(8,128)(2,1)}, bf16[2,96,1024]{2,1,0:T(8,128)(2,1)}, u32[]{:S(2)}, u32[]{:S(2)}) collective-permute-start(bf16[2,96,1024]{2,1,0:T(8,128)(2,1)} %pad_maximum_fusion.2), channel_id=1, source_target_pairs={{0,12},{4,8},{8,4},{12,0},{16,28},{20,24},{24,20},{28,16},{1,13},{... | collective-permute-start | bytes 1179656 | tf_op jit(solution)/shard_map/ppermute | solution.py:114
  3.2 20.8 %collective-permute-start.8 = (bf16[96,1024]{1,0:T(8,128)(2,1)S(1)}, bf16[96,1024]{1,0:T(8,128)(2,1)S(1)}, u32[]{:S(2)}, u32[]{:S(2)}) collective-permute-start(bf16[96,1024]{1,0:T(8,128)(2,1)S(1)} %bitcast.149), channel_id=1, source_target_pairs={{0,8},{4,12},{8,0},{12,4},{16,24},{20,28},{24,16},{28,20},{1,9},{5... | collective-permute-start | bytes 589832 | tf_op jit(solution)/shard_map/ppermute | solution.py:118
  4.6 22.5 %collective-permute-start.13 = (bf16[96,1024]{1,0:T(8,128)(2,1)S(1)}, bf16[96,1024]{1,0:T(8,128)(2,1)S(1)}, u32[]{:S(2)}, u32[]{:S(2)}) collective-permute-start(bf16[96,1024]{1,0:T(8,128)(2,1)S(1)} %bitcast.150), channel_id=1, source_target_pairs={{0,16},{4,20},{8,24},{12,28},{16,0},{20,4},{24,8},{28,12},{1,17},{... | collective-permute-start | bytes 589832 | tf_op jit(solution)/shard_map/ppermute | solution.py:118
  6.9 22.7 %collective-permute-start.16 = (bf16[96,1024]{1,0:T(8,128)(2,1)S(1)}, bf16[96,1024]{1,0:T(8,128)(2,1)S(1)}, u32[]{:S(2)}, u32[]{:S(2)}) collective-permute-start(bf16[96,1024]{1,0:T(8,128)(2,1)S(1)} %bitcast.151), channel_id=1, source_target_pairs={{0,20},{4,16},{8,28},{12,24},{16,4},{20,0},{24,12},{28,8},{1,21},{... | collective-permute-start | bytes 589832 | tf_op jit(solution)/shard_map/ppermute | solution.py:118
  8.8 1.9 %copy-start.6 = (s32[3,7]{1,0:T(4,128)S(1)}, s32[3,7]{1,0:T(4,128)}, u32[]{:S(2)}) copy-start(s32[3,7]{1,0:T(4,128)} %param.12) | copy-start | bytes 256
  10.7 2.0 %copy-start.1 = (bf16[384,3,256]{2,0,1:T(8,128)(2,1)}, bf16[384,3,256]{2,0,1:T(8,128)(2,1)S(1)}, u32[]{:S(2)}) copy-start(bf16[384,3,256]{2,0,1:T(8,128)(2,1)S(1)} %convolution_convert_fusion.1) | copy-start | bytes 1769476
  12.7 5.0 %slice-start = ((bf16[1024,3,256]{2,0,1:T(8,128)(2,1)}), bf16[1024,2,256]{2,0,1:T(8,128)(2,1)S(1)}, s32[]{:S(2)}) async-start(bf16[1024,3,256]{2,0,1:T(8,128)(2,1)} %param.8), calls=%async_computation | async-start | bytes 2097152 | tf_op jit(solution)/shard_map/slice | solution.py:281
  16.0 2.3 %slice-start.1 = ((bf16[384,3,256]{2,0,1:T(8,128)(2,1)}), bf16[384,2,256]{2,0,1:T(8,128)(2,1)S(1)}, s32[]{:S(2)}) async-start(bf16[384,3,256]{2,0,1:T(8,128)(2,1)} %copy-done.1), calls=%async_computation.1 | async-start | bytes 786432 | tf_op jit(solution)/shard_map/slice | solution.py:276
  18.8 22.0 %copy-start.4 = (bf16[256,256]{0,1:T(8,128)(2,1)S(1)}, bf16[256,256]{0,1:T(8,128)(2,1)}, u32[]{:S(2)}) copy-start(bf16[256,256]{0,1:T(8,128)(2,1)} %copy.38) | copy-start | bytes 393220
  20.7 20.0 %collective-permute-start.19 = (bf16[96,1024]{1,0:T(8,128)(2,1)S(1)}, bf16[96,1024]{1,0:T(8,128)(2,1)S(1)}, u32[]{:S(2)}, u32[]{:S(2)}) collective-permute-start(bf16[96,1024]{1,0:T(8,128)(2,1)S(1)} %bitcast.152), channel_id=1, source_target_pairs={{0,24},{4,28},{8,16},{12,20},{16,8},{20,12},{24,0},{28,4},{1,25},{... | collective-permute-start | bytes 589832 | tf_op jit(solution)/shard_map/ppermute | solution.py:118
  24.0 23.3 %collective-permute-start.22 = (bf16[96,1024]{1,0:T(8,128)(2,1)S(1)}, bf16[96,1024]{1,0:T(8,128)(2,1)S(1)}, u32[]{:S(2)}, u32[]{:S(2)}) collective-permute-start(bf16[96,1024]{1,0:T(8,128)(2,1)S(1)} %bitcast.153), channel_id=1, source_target_pairs={{0,28},{4,24},{8,20},{12,16},{16,12},{20,8},{24,4},{28,0},{1,29},{... | collective-permute-start | bytes 589832 | tf_op jit(solution)/shard_map/ppermute | solution.py:118
  27.1 7.9 %collective-permute-start.9 = (bf16[1,96,1024]{2,1,0:T(8,128)(2,1)S(1)}, bf16[1,96,1024]{2,1,0:T(8,128)(2,1)S(1)}, u32[]{:S(2)}, u32[]{:S(2)}) collective-permute-start(bf16[1,96,1024]{2,1,0:T(8,128)(2,1)S(1)} %bitcast.139), channel_id=1, source_target_pairs={{0,2},{1,3},{2,0},{3,1},{4,6},{5,7},{6,4},{7,5},{8,10},{9,11},{10,... | collective-permute-start | bytes 589832 | tf_op jit(solution)/shard_map/ppermute | solution.py:27
  28.4 21.7 %copy-start.3 = (bf16[256,256]{0,1:T(8,128)(2,1)S(1)}, bf16[256,256]{0,1:T(8,128)(2,1)}, u32[]{:S(2)}) copy-start(bf16[256,256]{0,1:T(8,128)(2,1)} %copy.39) | copy-start | bytes 393220
  28.4 20.2 %collective-permute-start.14 = (bf16[1,96,1024]{2,1,0:T(8,128)(2,1)S(1)}, bf16[1,96,1024]{2,1,0:T(8,128)(2,1)S(1)}, u32[]{:S(2)}, u32[]{:S(2)}) collective-permute-start(bf16[1,96,1024]{2,1,0:T(8,128)(2,1)S(1)} %bitcast.136), channel_id=1, source_target_pairs={{0,2},{1,3},{2,0},{3,1},{4,6},{5,7},{6,4},{7,5},{8,10},{9,11},{10,... | collective-permute-start | bytes 589832 | tf_op jit(solution)/shard_map/ppermute | solution.py:27
  29.7 20.4 %collective-permute-start.2 = (bf16[96,1024]{1,0:T(8,128)(2,1)S(1)}, bf16[96,1024]{1,0:T(8,128)(2,1)S(1)}, u32[]{:S(2)}, u32[]{:S(2)}) collective-permute-start(bf16[96,1024]{1,0:T(8,128)(2,1)S(1)} %bitcast.154), channel_id=1, source_target_pairs={{4,8},{12,16},{20,24},{8,4},{16,12},{24,20},{5,9},{13,17},{21,25},... | collective-permute-start | bytes 589832 | tf_op jit(solution)/shard_map/ppermute | solution.py:109
  35.0 13.8 %collective-permute-start.17 = (bf16[1,96,1024]{2,1,0:T(8,128)(2,1)S(1)}, bf16[1,96,1024]{2,1,0:T(8,128)(2,1)S(1)}, u32[]{:S(2)}, u32[]{:S(2)}) collective-permute-start(bf16[1,96,1024]{2,1,0:T(8,128)(2,1)S(1)} %bitcast.133), channel_id=1, source_target_pairs={{0,2},{1,3},{2,0},{3,1},{4,6},{5,7},{6,4},{7,5},{8,10},{9,11},{10,... | collective-permute-start | bytes 589832 | tf_op jit(solution)/shard_map/ppermute | solution.py:27
  40.7 32.5 %collective-permute-start.5 = (bf16[256,256]{0,1:T(8,128)(2,1)S(1)}, bf16[256,256]{0,1:T(8,128)(2,1)S(1)}, u32[]{:S(2)}, u32[]{:S(2)}) collective-permute-start(bf16[256,256]{0,1:T(8,128)(2,1)S(1)} %copy-done.4), channel_id=1, source_target_pairs={{0,1},{1,0},{2,3},{3,2},{4,5},{5,4},{6,7},{7,6},{8,9},{9,8},{10,11... | collective-permute-start | bytes 393224 | tf_op jit(solution)/shard_map/ppermute | solution.py:27
  47.4 5.9 %collective-permute-start.20 = (bf16[1,96,1024]{2,1,0:T(8,128)(2,1)S(1)}, bf16[1,96,1024]{2,1,0:T(8,128)(2,1)S(1)}, u32[]{:S(2)}, u32[]{:S(2)}) collective-permute-start(bf16[1,96,1024]{2,1,0:T(8,128)(2,1)S(1)} %bitcast.142), channel_id=1, source_target_pairs={{0,2},{1,3},{2,0},{3,1},{4,6},{5,7},{6,4},{7,5},{8,10},{9,11},{10,... | collective-permute-start | bytes 589832 | tf_op jit(solution)/shard_map/ppermute | solution.py:27
  48.6 8.9 %collective-permute-start.23 = (bf16[1,96,1024]{2,1,0:T(8,128)(2,1)S(1)}, bf16[1,96,1024]{2,1,0:T(8,128)(2,1)S(1)}, u32[]{:S(2)}, u32[]{:S(2)}) collective-permute-start(bf16[1,96,1024]{2,1,0:T(8,128)(2,1)S(1)} %bitcast.145), channel_id=1, source_target_pairs={{0,2},{1,3},{2,0},{3,1},{4,6},{5,7},{6,4},{7,5},{8,10},{9,11},{10,... | collective-permute-start | bytes 589832 | tf_op jit(solution)/shard_map/ppermute | solution.py:27
  48.9 18.2 %collective-permute-start.1 = (bf16[2,96,1024]{2,1,0:T(8,128)(2,1)}, bf16[2,96,1024]{2,1,0:T(8,128)(2,1)S(1)}, u32[]{:S(2)}, u32[]{:S(2)}) collective-permute-start(bf16[2,96,1024]{2,1,0:T(8,128)(2,1)} %collective-permute-done), channel_id=1, source_target_pairs={{0,1},{1,0},{2,3},{3,2},{4,5},{5,4},{6,7},{7,6},{8,9},{9,8},{10,11... | collective-permute-start | bytes 1179656 | tf_op jit(solution)/shard_map/ppermute | solution.py:27
  50.1 23.1 %collective-permute-start.6 = (bf16[256,256]{0,1:T(8,128)(2,1)S(1)}, bf16[256,256]{0,1:T(8,128)(2,1)S(1)}, u32[]{:S(2)}, u32[]{:S(2)}) collective-permute-start(bf16[256,256]{0,1:T(8,128)(2,1)S(1)} %copy-done.3), channel_id=1, source_target_pairs={{0,2},{1,3},{2,0},{3,1},{4,6},{5,7},{6,4},{7,5},{8,10},{9,11},{10,... | collective-permute-start | bytes 393224 | tf_op jit(solution)/shard_map/ppermute | solution.py:27
  53.3 11.2 %collective-permute-start.3 = (bf16[1,96,1024]{2,1,0:T(8,128)(2,1)S(1)}, bf16[1,96,1024]{2,1,0:T(8,128)(2,1)S(1)}, u32[]{:S(2)}, u32[]{:S(2)}) collective-permute-start(bf16[1,96,1024]{2,1,0:T(8,128)(2,1)S(1)} %bitcast.122), channel_id=1, source_target_pairs={{0,2},{1,3},{2,0},{3,1},{4,6},{5,7},{6,4},{7,5},{8,10},{9,11},{10,... | collective-permute-start | bytes 589832 | tf_op jit(solution)/shard_map/ppermute | solution.py:27
  57.5 9.7 %collective-permute-start.10 = (bf16[2,96,1024]{2,1,0:T(8,128)(2,1)S(1)}, bf16[2,96,1024]{2,1,0:T(8,128)(2,1)S(1)}, u32[]{:S(2)}, u32[]{:S(2)}) collective-permute-start(bf16[2,96,1024]{2,1,0:T(8,128)(2,1)S(1)} %pad_maximum_fusion.4), channel_id=1, source_target_pairs={{0,1},{1,0},{2,3},{3,2},{4,5},{5,4},{6,7},{7,6},{8,9},{9,8},{10,11... | collective-permute-start | bytes 1179656 | tf_op jit(solution)/shard_map/ppermute | solution.py:27
  64.5 8.7 %collective-permute-start.7 = (bf16[256,256]{0,1:T(8,128)(2,1)S(1)}, bf16[256,256]{0,1:T(8,128)(2,1)S(1)}, u32[]{:S(2)}, u32[]{:S(2)}) collective-permute-start(bf16[256,256]{0,1:T(8,128)(2,1)S(1)} %copy.40), channel_id=1, source_target_pairs={{0,3},{1,2},{2,1},{3,0},{4,7},{5,6},{6,5},{7,4},{8,11},{9,10},{10,... | collective-permute-start | bytes 393224 | tf_op jit(solution)/shard_map/ppermute | solution.py:27
  67.1 2.0 %collective-permute-start.12 = (bf16[2,96,1024]{2,1,0:T(8,128)(2,1)}, bf16[2,96,1024]{2,1,0:T(8,128)(2,1)S(1)}, u32[]{:S(2)}, u32[]{:S(2)}) collective-permute-start(bf16[2,96,1024]{2,1,0:T(8,128)(2,1)} %collective-permute-done.11), channel_id=1, source_target_pairs={{0,1},{1,0},{2,3},{3,2},{4,5},{5,4},{6,7},{7,6},{8,9},{9,8},{10,11... | collective-permute-start | bytes 1179656 | tf_op jit(solution)/shard_map/ppermute | solution.py:27
  67.2 2.2 %collective-permute-start.15 = (bf16[2,96,1024]{2,1,0:T(8,128)(2,1)S(1)}, bf16[2,96,1024]{2,1,0:T(8,128)(2,1)S(1)}, u32[]{:S(2)}, u32[]{:S(2)}) collective-permute-start(bf16[2,96,1024]{2,1,0:T(8,128)(2,1)S(1)} %pad_maximum_fusion.5), channel_id=1, source_target_pairs={{0,1},{1,0},{2,3},{3,2},{4,5},{5,4},{6,7},{7,6},{8,9},{9,8},{10,11... | collective-permute-start | bytes 1179656 | tf_op jit(solution)/shard_map/ppermute | solution.py:27
  69.1 1.7 %collective-permute-start.18 = (bf16[2,96,1024]{2,1,0:T(8,128)(2,1)S(1)}, bf16[2,96,1024]{2,1,0:T(8,128)(2,1)S(1)}, u32[]{:S(2)}, u32[]{:S(2)}) collective-permute-start(bf16[2,96,1024]{2,1,0:T(8,128)(2,1)S(1)} %pad_maximum_fusion.6), channel_id=1, source_target_pairs={{0,1},{1,0},{2,3},{3,2},{4,5},{5,4},{6,7},{7,6},{8,9},{9,8},{10,11... | collective-permute-start | bytes 1179656 | tf_op jit(solution)/shard_map/ppermute | solution.py:27
  69.4 1.9 %collective-permute-start.21 = (bf16[2,96,1024]{2,1,0:T(8,128)(2,1)S(1)}, bf16[2,96,1024]{2,1,0:T(8,128)(2,1)S(1)}, u32[]{:S(2)}, u32[]{:S(2)}) collective-permute-start(bf16[2,96,1024]{2,1,0:T(8,128)(2,1)S(1)} %pad_maximum_fusion.7), channel_id=1, source_target_pairs={{0,1},{1,0},{2,3},{3,2},{4,5},{5,4},{6,7},{7,6},{8,9},{9,8},{10,11... | collective-permute-start | bytes 1179656 | tf_op jit(solution)/shard_map/ppermute | solution.py:27
  70.8 1.7 %collective-permute-start.24 = (bf16[2,96,1024]{2,1,0:T(8,128)(2,1)S(1)}, bf16[2,96,1024]{2,1,0:T(8,128)(2,1)S(1)}, u32[]{:S(2)}, u32[]{:S(2)}) collective-permute-start(bf16[2,96,1024]{2,1,0:T(8,128)(2,1)S(1)} %pad_maximum_fusion.8), channel_id=1, source_target_pairs={{0,1},{1,0},{2,3},{3,2},{4,5},{5,4},{6,7},{7,6},{8,9},{9,8},{10,11... | collective-permute-start | bytes 1179656 | tf_op jit(solution)/shard_map/ppermute | solution.py:27
  71.3 1.9 %collective-permute-start.4 = (bf16[2,96,1024]{2,1,0:T(8,128)(2,1)S(1)}, bf16[2,96,1024]{2,1,0:T(8,128)(2,1)S(1)}, u32[]{:S(2)}, u32[]{:S(2)}) collective-permute-start(bf16[2,96,1024]{2,1,0:T(8,128)(2,1)S(1)} %pad_maximum_fusion.3), channel_id=1, source_target_pairs={{0,1},{1,0},{2,3},{3,2},{4,5},{5,4},{6,7},{7,6},{8,9},{9,8},{10,11... | collective-permute-start | bytes 1179656 | tf_op jit(solution)/shard_map/ppermute | solution.py:27
  73.2 0.6 copy-start.9
  73.2 0.7 copy-start.11
  90.6 10.0 %copy-start.2 = (bf16[3,128,256]{2,1,0:T(8,128)(2,1)S(1)}, bf16[3,128,256]{2,1,0:T(8,128)(2,1)}, u32[]{:S(2)}) copy-start(bf16[3,128,256]{2,1,0:T(8,128)(2,1)} %shard_map.73) | copy-start | bytes 589828
  90.6 10.0 %copy-start.10 = (bf16[256,256]{0,1:T(8,128)(2,1)S(1)}, bf16[256,256]{0,1:T(8,128)(2,1)}, u32[]{:S(2)}) copy-start(bf16[256,256]{0,1:T(8,128)(2,1)} %copy-done.9) | copy-start | bytes 393220
  90.6 10.0 %copy-start.12 = (bf16[256,256]{0,1:T(8,128)(2,1)S(1)}, bf16[256,256]{0,1:T(8,128)(2,1)}, u32[]{:S(2)}) copy-start(bf16[256,256]{0,1:T(8,128)(2,1)} %copy-done.11) | copy-start | bytes 393220
  90.6 6.6 %collective-permute-start.25 = (bf16[1,384,256]{2,1,0:T(8,128)(2,1)}, bf16[1,384,256]{2,1,0:T(8,128)(2,1)S(1)}, u32[]{:S(2)}, u32[]{:S(2)}) collective-permute-start(bf16[1,384,256]{2,1,0:T(8,128)(2,1)} %bitcast.158), channel_id=1, source_target_pairs={{0,2},{1,3},{2,0},{3,1},{4,6},{5,7},{6,4},{7,5},{8,10},{9,11},{10,... | collective-permute-start | bytes 589832 | tf_op jit(solution)/shard_map/ppermute | solution.py:27
  98.2 2.4 %collective-permute-start.26 = (bf16[2,384,256]{2,1,0:T(8,128)(2,1)S(1)}, bf16[2,384,256]{2,1,0:T(8,128)(2,1)S(1)}, u32[]{:S(2)}, u32[]{:S(2)}) collective-permute-start(bf16[2,384,256]{2,1,0:T(8,128)(2,1)S(1)} %pad_maximum_fusion.9), channel_id=1, source_target_pairs={{0,1},{1,0},{2,3},{3,2},{4,5},{5,4},{6,7},{7,6},{8,9},{9,8},{10,11... | collective-permute-start | bytes 1179656 | tf_op jit(solution)/shard_map/ppermute | solution.py:27
  100.6 4.5 %copy-start.7 = (f32[256]{0:T(256)S(1)}, f32[256]{0:T(256)}, u32[]{:S(2)}) copy-start(f32[256]{0:T(256)} %param.11) | copy-start | bytes 3076
  100.6 4.5 %copy-start.8 = (f32[256]{0:T(256)S(1)}, f32[256]{0:T(256)}, u32[]{:S(2)}) copy-start(f32[256]{0:T(256)} %param.10) | copy-start | bytes 3076
  101.3 2.2 %collective-permute-start.27 = (f32[384,2]{0,1:T(2,128)S(1)}, f32[384,2]{0,1:T(2,128)S(1)}, u32[]{:S(2)}, u32[]{:S(2)}) collective-permute-start(f32[384,2]{0,1:T(2,128)S(1)} %get-tuple-element.50), channel_id=1, source_target_pairs={{0,1},{1,0},{2,3},{3,2},{4,5},{5,4},{6,7},{7,6},{8,9},{9,8},{10,11... | collective-permute-start | bytes 9224 | tf_op jit(solution)/shard_map/ppermute | solution.py:27
  101.7 2.4 %collective-permute-start.28 = (f32[384,2]{0,1:T(2,128)S(1)}, f32[384,2]{0,1:T(2,128)S(1)}, u32[]{:S(2)}, u32[]{:S(2)}) collective-permute-start(f32[384,2]{0,1:T(2,128)S(1)} %get-tuple-element.50), channel_id=1, source_target_pairs={{0,2},{1,3},{2,0},{3,1},{4,6},{5,7},{6,4},{7,5},{8,10},{9,11},{10,... | collective-permute-start | bytes 9224 | tf_op jit(solution)/shard_map/ppermute | solution.py:27
  102.0 3.1 %collective-permute-start.29 = (f32[384,2]{0,1:T(2,128)S(1)}, f32[384,2]{0,1:T(2,128)S(1)}, u32[]{:S(2)}, u32[]{:S(2)}) collective-permute-start(f32[384,2]{0,1:T(2,128)S(1)} %get-tuple-element.50), channel_id=1, source_target_pairs={{0,3},{1,2},{2,1},{3,0},{4,7},{5,6},{6,5},{7,4},{8,11},{9,10},{10,... | collective-permute-start | bytes 9224 | tf_op jit(solution)/shard_map/ppermute | solution.py:27
